TPU v7x, 128 devices: a whole 4x4x4 slice. The times are simulated.
128 devices in a mesh: section: 2 (over y_lo), row: 8 (over x, core), col: 8 (over z, y_hi).
Axes of the slice: x: 4, y: 4 (y_hi: 2, y_lo: 2; y = y_hi * 2 + y_lo), z: 4, core: 2. Of those that a mesh axis runs over, the one named last changes fastest.
Arguments:
- features: bfloat16 [2, 192, 64, 1024], P(None, None, 'row', 'col'), may hold values from -36 to 36
- labels: int32 [2, 64, 1024], P(None, 'row', 'col'), may hold values from 0 to 15
- dw_weight: float32 [192, 49], replicated, may hold values from -0.875 to 0.875
- dw_bias: float32 [192], replicated, may hold values from -3 to 3
- norm_gain: float32 [192], replicated, may hold values from 0.25 to 1.75
- norm_bias: float32 [192], replicated, may hold values from -2 to 2
- w_in: bfloat16 [192, 768], replicated, may hold values from -0.4375 to 0.4375
- b_in: float32 [768], replicated, may hold values from -3 to 3
- w_out: bfloat16 [768, 192], replicated, may hold values from -0.21875 to 0.21875
- b_out: float32 [192], replicated, may hold values from -3 to 3
- layer_scale: float32 [192], replicated, may hold values from 0.2 to 1
- w_lateral: bfloat16 [192, 512], replicated, may hold values from -0.4375 to 0.4375
- b_lateral: float32 [512], replicated, may hold values from -3 to 3
- w_class: bfloat16 [512, 16], replicated, may hold values from -1.8 to 1.8
- b_class: float32 [16], replicated, may hold values from -4 to 4
Outputs:
- d_features: float32 [2, 192, 64, 1024], P('section', None, 'row', 'col')
- loss: float32 [], replicated
- grad_dw_weight: float32 [192, 49], replicated
- grad_dw_bias: float32 [192], replicated
- grad_norm_gain: float32 [192], replicated
- grad_norm_bias: float32 [192], replicated
- grad_w_in: float32 [192, 768], replicated
- grad_b_in: float32 [768], replicated
- grad_w_out: float32 [768, 192], replicated
- grad_b_out: float32 [192], replicated
- grad_layer_scale: float32 [192], replicated
- grad_w_lateral: float32 [192, 512], replicated
- grad_b_lateral: float32 [512], replicated
- grad_w_class: float32 [512, 16], replicated
- grad_b_class: float32 [16], replicated
All inputs are finite; a program needn't handle non-finite values.
Results may differ from a plain program's by a relative error of at most 0.0059.
Values may be sent and summed in bfloat16 or wider, within the bound.
No kernel may reach another device: no remote copies, remote signals or barrier semaphores. Data moves between devices by JAX's collectives and lax.ppermute only.
A program may use at most 128 MiB of HBM per device.

v0:
```python
import math

import jax
import jax.numpy as jnp
from jax import lax
from jax.sharding import PartitionSpec as P

EPSILON = 1e-06
ROOT_HALF = 0.7071067811865476
DENSITY_SCALE = 0.3989422804014327


def padded_2(x, sides, width):
    for axis, dim in sides:
        count, length = (lax.axis_size(axis), x.shape[dim])
        up = [(i, (i + 1) % count) for i in range(count - 1)]
        down = [(j, i) for i, j in up]
        last = lax.slice_in_dim(x, length - width, length, axis=dim)
        leading = lax.slice_in_dim(x, 0, width, axis=dim)
        before = lax.ppermute(last, axis, up)
        after = lax.ppermute(leading, axis, down)
        x = jnp.concatenate([before, x, after], axis=dim)
    return x


def from_behind(block, axis, distance):
    devices = range(lax.axis_size(axis))
    route = [(i - distance, i) for i in devices if i - distance in devices]
    return lax.ppermute(block, axis, route)


def product(form, left_side, right_side):
    return jnp.einsum(form, left_side, right_side, preferred_element_type=jnp.float32)


def depthwise(padded, kernel, height, width, flipped):
    total = jnp.zeros((padded.shape[0], height, width), jnp.float32)
    for tap_index in range(49):
        down_step = tap_index // 7
        side_step = tap_index % 7
        if flipped:
            down_step = 6 - down_step
            side_step = 6 - side_step
        window = padded[:, down_step : down_step + height, side_step : side_step + width].astype(
            jnp.float32
        )
        total = total + kernel[:, tap_index][:, None, None] * window
    return total


def normal_cdf(values):
    return 0.5 * (1.0 + lax.erf(values * ROOT_HALF))


def gelu_slope(values):
    return normal_cdf(values) + values * jnp.exp(-0.5 * values * values) * DENSITY_SCALE


def encoder_forward(padded, enc_params):
    dw_weight, dw_bias, norm_gain, norm_bias, w_in, b_in, w_out, b_out, layer_scale = enc_params
    height = padded.shape[1] - 6
    width = padded.shape[2] - 6
    conv = depthwise(padded, dw_weight, height, width, False) + dw_bias[:, None, None]
    centre = conv - jnp.mean(conv, axis=0, keepdims=True)
    inv_std = lax.rsqrt(jnp.mean(centre * centre, axis=0, keepdims=True) + EPSILON)
    scaled = centre * inv_std
    normed = (scaled * norm_gain[:, None, None] + norm_bias[:, None, None]).astype(jnp.bfloat16)
    before = product("chw,cd->dhw", normed, w_in) + b_in[:, None, None]
    active = (before * normal_cdf(before)).astype(jnp.bfloat16)
    branch = product("dhw,dc->chw", active, w_out) + b_out[:, None, None]
    inner = padded[:, 3 : 3 + height, 3 : 3 + width].astype(jnp.float32)
    output = (inner + layer_scale[:, None, None] * branch).astype(jnp.bfloat16)
    return (output, (scaled, inv_std, normed, before, active, branch))


def encoder_backward(saved, grad_out, enc_params):
    dw_weight, dw_bias, norm_gain, norm_bias, w_in, b_in, w_out, b_out, layer_scale = enc_params
    scaled, inv_std, normed, before, active, branch = saved
    grad_float = grad_out.astype(jnp.float32)
    layerscale_grad = jnp.sum(branch * grad_float, axis=(1, 2))
    d_branch = (layer_scale[:, None, None] * grad_float).astype(jnp.bfloat16)
    projbias_grad = jnp.sum(d_branch.astype(jnp.float32), axis=(1, 2))
    project_grad = product("dhw,chw->dc", active, d_branch)
    d_active = product("chw,dc->dhw", d_branch, w_out)
    d_before = (d_active * gelu_slope(before)).astype(jnp.bfloat16)
    expbias_grad = jnp.sum(d_before.astype(jnp.float32), axis=(1, 2))
    expand_grad = product("chw,dhw->cd", normed, d_before)
    d_normed = product("dhw,cd->chw", d_before, w_in)
    gain_grad = jnp.sum(d_normed * scaled, axis=(1, 2))
    normbias_grad = jnp.sum(d_normed, axis=(1, 2))
    d_scaled = d_normed * norm_gain[:, None, None]
    d_conv = inv_std * (
        d_scaled
        - jnp.mean(d_scaled, axis=0, keepdims=True)
        - scaled * jnp.mean(d_scaled * scaled, axis=0, keepdims=True)
    )
    grads = (
        gain_grad,
        normbias_grad,
        expand_grad,
        expbias_grad,
        project_grad,
        projbias_grad,
        layerscale_grad,
    )
    return (d_conv.astype(jnp.bfloat16), grads)


def conv_backward(padded, d_conv, d_padded, grad_out, dw_weight):
    height = d_conv.shape[1]
    width = d_conv.shape[2]
    d_input = grad_out.astype(jnp.float32) + depthwise(d_padded, dw_weight, height, width, True)
    conv_float = d_conv.astype(jnp.float32)
    columns = []
    for tap_index in range(49):
        down_step = tap_index // 7
        side_step = tap_index % 7
        window = padded[:, down_step : down_step + height, side_step : side_step + width].astype(
            jnp.float32
        )
        columns.append(jnp.sum(window * conv_float, axis=(1, 2)))
    kernel_grad = jnp.stack(columns, axis=1)
    convbias_grad = jnp.sum(conv_float, axis=(1, 2))
    return (d_input, kernel_grad, convbias_grad)


def decoder(encoded, label_tile, w_lateral, b_lateral, w_class, b_class):
    lateral_pre = product("chw,cl->lhw", encoded, w_lateral) + b_lateral[:, None, None]
    lateral = (lateral_pre * normal_cdf(lateral_pre)).astype(jnp.bfloat16)
    logits = product("lhw,lk->khw", lateral, w_class) + b_class[:, None, None]
    highest = jnp.max(logits, axis=0, keepdims=True)
    shifted = logits - highest
    totals = jnp.sum(jnp.exp(shifted), axis=0, keepdims=True)
    log_total = highest + jnp.log(totals)
    classes = jnp.arange(logits.shape[0], dtype=jnp.int32)
    onehot = (label_tile[None, :, :] == classes[:, None, None]).astype(jnp.float32)
    loss_sum = jnp.sum(log_total[0] - jnp.sum(onehot * logits, axis=0))
    d_logits = (jnp.exp(shifted) / totals - onehot).astype(jnp.bfloat16)
    classify_grad = product("lhw,khw->lk", lateral, d_logits)
    clsbias_grad = jnp.sum(d_logits.astype(jnp.float32), axis=(1, 2))
    d_lateral_raw = product("khw,lk->lhw", d_logits, w_class)
    d_lateral = (d_lateral_raw * gelu_slope(lateral_pre)).astype(jnp.bfloat16)
    lateral_grad = product("chw,lhw->cl", encoded, d_lateral)
    latbias_grad = jnp.sum(d_lateral.astype(jnp.float32), axis=(1, 2))
    d_encoded = product("lhw,cl->chw", d_lateral, w_lateral).astype(jnp.bfloat16)
    return (d_encoded, loss_sum, (lateral_grad, latbias_grad, classify_grad, clsbias_grad))


def flat_psum(parts, axes):
    shapes = [p.shape for p in parts]
    flat = jnp.concatenate([p.reshape(-1) for p in parts])
    total = lax.psum(flat, axes)
    out, at = [], 0
    for shape in shapes:
        size = math.prod(shape)
        out.append(total[at : at + size].reshape(shape))
        at += size
    return out


def shards(
    features,
    labels,
    dw_weight,
    dw_bias,
    norm_gain,
    norm_bias,
    w_in,
    b_in,
    w_out,
    b_out,
    layer_scale,
    w_lateral,
    b_lateral,
    w_class,
    b_class,
):
    enc_params = (dw_weight, dw_bias, norm_gain, norm_bias, w_in, b_in, w_out, b_out, layer_scale)
    section = lax.axis_index("section")
    micro_count = features.shape[0]
    height = features.shape[2]
    width = features.shape[3]
    axes = ("section", "row", "col")

    def rimmed(tile):
        return padded_2(tile, (("row", 1), ("col", 2)), 3)

    tile = lax.dynamic_index_in_dim(features, section, 0, keepdims=False)
    label_tile = lax.dynamic_index_in_dim(labels, section, 0, keepdims=False)
    padded = rimmed(tile)
    output, saved = encoder_forward(padded, enc_params)
    returned, loss_sum, dec_grads = decoder(output, label_tile, w_lateral, b_lateral, w_class, b_class)
    d_conv, enc_grads = encoder_backward(saved, returned, enc_params)
    early = flat_psum(list(enc_grads) + list(dec_grads) + [loss_sum], axes)
    (
        gain_grad,
        normbias_grad,
        expand_grad,
        expbias_grad,
        project_grad,
        projbias_grad,
        layerscale_grad,
        lateral_grad,
        latbias_grad,
        classify_grad,
        clsbias_grad,
        loss_total,
    ) = early
    d_padded = rimmed(d_conv)
    d_input, kernel_grad, convbias_grad = conv_backward(padded, d_conv, d_padded, returned, dw_weight)
    kernel_grad, convbias_grad = flat_psum([kernel_grad, convbias_grad], ("col",))
    kernel_grad, convbias_grad = flat_psum([kernel_grad, convbias_grad], ("row",))
    kernel_grad, convbias_grad = flat_psum([kernel_grad, convbias_grad], ("section",))
    cell_count = micro_count * height * width * lax.axis_size("row") * lax.axis_size("col")
    grad_scale = 1.0 / math.sqrt(cell_count)
    return (
        d_input[None],
        loss_total / cell_count,
        kernel_grad * grad_scale,
        convbias_grad * grad_scale,
        gain_grad * grad_scale,
        normbias_grad * grad_scale,
        expand_grad * grad_scale,
        expbias_grad * grad_scale,
        project_grad * grad_scale,
        projbias_grad * grad_scale,
        layerscale_grad * grad_scale,
        lateral_grad * grad_scale,
        latbias_grad * grad_scale,
        classify_grad * grad_scale,
        clsbias_grad * grad_scale,
    )


def solution(mesh):
    placed = (
        P(None, None, "row", "col"),
        P(None, "row", "col"),
        P(),
        P(),
        P(),
        P(),
        P(),
        P(),
        P(),
        P(),
        P(),
        P(),
        P(),
        P(),
        P(),
    )
    return jax.shard_map(
        shards,
        mesh=mesh,
        in_specs=placed,
        out_specs=(
            P("section", None, "row", "col"),
            P(),
            P(),
            P(),
            P(),
            P(),
            P(),
            P(),
            P(),
            P(),
            P(),
            P(),
            P(),
            P(),
            P(),
        ),
        check_vma=False,
    )
```

profile of v0, /device:TPU:1, one launch (start us, length us, event | category | flops | bytes accessed | tf_op | source)
XLA Modules:
  0.0 354.7 jit_solution(17407703938424092805)
XLA Ops:
  7.3 1.1 copy-done
  8.4 4.5 %collective-permute-start = (bf16[192,3,128]{2,0,1:T(8,128)(2,1)S(1)}, bf16[192,3,128]{2,0,1:T(8,128)(2,1)S(1)}, u32[]{:S(2)}, u32[]{:S(2)}) collective-permute-start(bf16[192,3,128]{2,0,1:T(8,128)(2,1)S(1)} %get-tuple-element.148), channel_id=1, source_target_pairs={{0,8},{8,16},{16,24},{24,32},{32,40},{40,48},{48,56},{1,9},{9,17},... | collective-permute-start | bytes 442376 | tf_op jit(solution)/shard_map/ppermute | solution.py:20
  12.9 1.9 collective-permute-start.1
  15.9 3.5 collective-permute-done.1
  20.2 4.8 %collective-permute-start.2 = (bf16[192,14,3]{0,1,2:T(8,128)(2,1)S(1)}, bf16[192,14,3]{0,1,2:T(8,128)(2,1)S(1)}, u32[]{:S(2)}, u32[]{:S(2)}) collective-permute-start(bf16[192,14,3]{0,1,2:T(8,128)(2,1)S(1)} %copy.57), channel_id=1, source_target_pairs={{0,1},{1,2},{2,3},{3,4},{4,5},{5,6},{6,7},{8,9},{9,10},{10,11},{11... | collective-permute-start | bytes 48392 | tf_op jit(solution)/shard_map/ppermute | solution.py:20
  25.4 1.3 collective-permute-start.3
  27.1 4.3 %collective-permute-done.3 = bf16[192,14,3]{0,1,2:T(8,128)(2,1)S(1)} collective-permute-done((bf16[192,14,3]{0,1,2:T(8,128)(2,1)S(1)}, bf16[192,14,3]{0,1,2:T(8,128)(2,1)S(1)}, u32[]{:S(2)}, u32[]{:S(2)}) %collective-permute-start.3) | collective-permute-done | bytes 16160 | tf_op jit(solution)/shard_map/ppermute | solution.py:21
  31.9 1.4 maximum_maximum_fusion
  33.8 9.2 %fusion.170 = (f32[8,128]{1,0:T(8,128)S(1)}, f32[192,8,128]{2,0,1:T(8,128)S(1)}) fusion(f32[192]{0:T(256)S(1)} %copy-done.103, bf16[192,14,131]{2,0,1:T(8,128)(2,1)S(1)} %get-tuple-element.143, f32[192]{0:T(256)} %bitcast.49, f32[192]{0:T(256)} %bitcast.48, f32[192]{0:T(256)S(1)} %bitcast.233, bf16[192,3,128]{2,0,1:T(8,128)(2,1)S(1)} %collective-permute-done.1, ...), kind=kLoop, calls=%fused_computation.350 | loop fusion | flops 30276608 | bytes 18032128 | tf_op jit(solution)/shard_map/reduce_sum | solution.py:64
  43.1 1.0 fusion.9
  46.9 1.9 convert_reduce_fusion.2
  48.7 1.1 convolution_bitcast_fusion.2
  49.9 2.0 convert_reduce_fusion.3
  51.9 1.5 convolution_bitcast_fusion
  53.3 2.4 convert_reduce_fusion.1
  55.8 1.4 convolution_bitcast_fusion.1
  57.1 1.4 fusion.147
  58.5 4.0 %fusion.142 = (f32[192]{0:T(256)S(1)}, f32[192]{0:T(256)S(1)}, f32[192]{0:T(256)S(1)}, f32[192]{0:T(256)S(1)}, f32[192]{0:T(256)S(1)}, /*index=5*/f32[192]{0:T(2...) fusion(bf16[192,14,131]{2,0,1:T(8,128)(2,1)S(1)} %get-tuple-ele, ...), kind=kLoop, calls=%fused_computation.262 | loop fusion | flops 12382848 | bytes 9074944 | tf_op jit(solution)/shard_map/reduce_sum | solution.py:121
  62.5 3.9 %fusion.146 = (f32[192]{0:T(256)S(1)}, f32[192]{0:T(256)S(1)}, f32[192]{0:T(256)S(1)}, f32[192]{0:T(256)S(1)}, f32[192]{0:T(256)S(1)}, /*index=5*/f32[192]{0:T(2...) fusion(bf16[192,8,128]{2,0,1:T(8,128)(2,1)S(1)} %get-tuple-elem, ...), kind=kLoop, calls=%fused_computation.266 | loop fusion | flops 11006400 | bytes 7485696 | tf_op jit(solution)/shard_map/reduce_sum | solution.py:121
  67.0 1.9 fusion.145
  68.9 1.5 stack.199
  70.9 33.5 %psum.29 = f32[9600]{0:T(1024)S(1)} all-reduce(f32[9600]{0:T(1024)S(1)} %pad_maximum_fusion.8), channel_id=1, replica_groups=mesh['section'=2,'row'=8,'col'=8] {'col'}, use_global_device_ids=true, to_apply=%region_66.67 | all-reduce | flops 9600 | bytes 76800 | tf_op jit(solution)/shard_map/psum | solution.py:152
  104.4 28.1 %psum.30 = f32[9600]{0:T(1024)S(1)} all-reduce(f32[9600]{0:T(1024)S(1)} %psum.29), channel_id=1, replica_groups=mesh['section'=2,'row'=8,'col'=8] {'row'}, use_global_device_ids=true, to_apply=%region_67.68 | all-reduce | flops 9600 | bytes 76800 | tf_op jit(solution)/shard_map/psum | solution.py:152
  132.4 6.5 %psum.31 = f32[9600]{0:T(1024)S(1)} all-reduce(f32[9600]{0:T(1024)S(1)} %psum.30), channel_id=1, replica_groups=mesh['section'=2,'row'=8,'col'=8] {'section'}, use_global_device_ids=true, to_apply=%region_68.69 | all-reduce | flops 9600 | bytes 76800 | tf_op jit(solution)/shard_map/psum | solution.py:152
  139.6 5.2 %collective-permute-start.4 = (bf16[192,3,128]{2,0,1:T(8,128)(2,1)S(1)}, bf16[192,3,128]{2,0,1:T(8,128)(2,1)S(1)}, u32[]{:S(2)}, u32[]{:S(2)}) collective-permute-start(bf16[192,3,128]{2,0,1:T(8,128)(2,1)S(1)} %get-tuple-element.147), channel_id=1, source_target_pairs={{0,8},{8,16},{16,24},{24,32},{32,40},{40,48},{48,56},{1,9},{9,17},... | collective-permute-start | bytes 442376 | tf_op jit(solution)/shard_map/ppermute | solution.py:20
  144.8 3.2 collective-permute-start.5
  148.0 1.2 convolution_bitcast_fusion.3
  149.2 2.1 collective-permute-done.5
  152.7 1.3 collective-permute-start.6
  154.0 1.0 copy.67
  155.0 5.6 %collective-permute-start.7 = (bf16[192,14,3]{0,1,2:T(8,128)(2,1)}, bf16[192,14,3]{0,1,2:T(8,128)(2,1)S(1)}, u32[]{:S(2)}, u32[]{:S(2)}) collective-permute-start(bf16[192,14,3]{0,1,2:T(8,128)(2,1)} %copy.67), channel_id=1, source_target_pairs={{0,1},{1,2},{2,3},{3,4},{4,5},{5,6},{6,7},{8,9},{9,10},{10,11},{11... | collective-permute-start | bytes 48392 | tf_op jit(solution)/shard_map/ppermute | solution.py:20
  161.3 1.1 reshape.152
  162.4 1.9 copy.92
  164.3 1.2 reshape.150
  165.8 20.0 %concatenate.138 = f32[403473]{0:T(1024)} concatenate(f32[192]{0:T(256)S(1)} %copy-done.105, f32[192]{0:T(256)S(1)} %reduce_sum.582, f32[147456]{0:T(1024)S(1)} %reshape.149, f32[768]{0:T(1024)S(1)} %copy-done.97, f32[147456]{0:T(1024)} %reshape.150, f32[192]{0:T(256)S(1)} %copy-done.94, f32[192]{0:T(256)S(1)} %copy-done.95, f32[98304]{0:T(1024)} %bitcast.230, ...), dimensions={0} | concatenate | bytes 3227784 | tf_op jit(solution)/shard_map/concatenate | solution.py:151
  187.9 1.3 pad_maximum_fusion.1
  189.6 9.1 %add_bitcast_fusion = f32[1,192,8,128]{3,1,2,0:T(8,128)S(1)} fusion(f32[192,8,128]{2,0,1:T(8,128)S(1)} %copy-done.1, bf16[192,8,128]{2,0,1:T(8,128)(2,1)S(1)} %get-tuple-element.124, bf16[192,3,128]{2,0,1:T(8,128)(2,1)S(1)} %copy-done.7, bf16[192,3,128]{2,0,1:T(8,128)(2,1)S(1)} %copy-done.9, bf16[192,14,131]{2,0,1:T(8,128)(2,1)S(1)} %get-tuple-element.139, ...), kind=kLoop, calls=%fused_computation.272 | loop fusion | flops 30081024 | bytes 18813696 | tf_op jit(solution)/shard_map/broadcast_in_dim | solution.py:217
  198.7 1.3 copy.76
  200.0 132.6 %all-reduce.2.cloned.1.call-done = f32[403473]{0:T(1024)} async-done(((f32[403473]{0:T(1024)}), f32[403473]{0:T(1024)}) %all-reduce.2.cloned.1.call-update) | async-done | bytes 1613908 | tf_op jit(solution)/shard_map/psum | solution.py:152
  332.6 1.4 slice_multiply_fusion
  334.2 1.1 copy.78
  335.3 0.9 mul.1422
  336.2 1.0 slice_multiply_fusion.2
  339.7 1.3 slice.975
  341.6 1.4 slice_multiply_fusion.7
  343.0 1.3 slice_multiply_fusion.5
  344.3 1.3 slice_multiply_fusion.6
  345.5 1.2 slice_multiply_fusion.12
  (264 shorter events, 13.9 us)
Async XLA Ops:
  7.2 325.4 %all-reduce.2.cloned.1.call-start = ((), (), s32[]{:S(2)}) async-start(), calls=%async_computation | async-start | bytes 3235840 | tf_op jit(solution)/shard_map/psum | solution.py:152
  8.4 7.5 %collective-permute-start = (bf16[192,3,128]{2,0,1:T(8,128)(2,1)S(1)}, bf16[192,3,128]{2,0,1:T(8,128)(2,1)S(1)}, u32[]{:S(2)}, u32[]{:S(2)}) collective-permute-start(bf16[192,3,128]{2,0,1:T(8,128)(2,1)S(1)} %get-tuple-element.148), channel_id=1, source_target_pairs={{0,8},{8,16},{16,24},{24,32},{32,40},{40,48},{48,56},{1,9},{9,17},... | collective-permute-start | bytes 442376 | tf_op jit(solution)/shard_map/ppermute | solution.py:20
  12.9 6.5 %collective-permute-start.1 = (bf16[192,3,128]{2,0,1:T(8,128)(2,1)S(1)}, bf16[192,3,128]{2,0,1:T(8,128)(2,1)S(1)}, u32[]{:S(2)}, u32[]{:S(2)}) collective-permute-start(bf16[192,3,128]{2,0,1:T(8,128)(2,1)S(1)} %get-tuple-element.149), channel_id=1, source_target_pairs={{8,0},{16,8},{24,16},{32,24},{40,32},{48,40},{56,48},{9,1},{17,9},... | collective-permute-start | bytes 442376 | tf_op jit(solution)/shard_map/ppermute | solution.py:21
  14.9 18.4 %copy-start.15 = (f32[192,1]{0,1:T(1,128)}, f32[192,1]{0,1:T(1,128)S(1)}, u32[]{:S(2)}) copy-start(f32[192,1]{0,1:T(1,128)S(1)} %get-tuple-element.153) | copy-start | bytes 2308
  14.9 18.4 %copy-start.17 = (f32[192,1]{0,1:T(1,128)}, f32[192,1]{0,1:T(1,128)S(1)}, u32[]{:S(2)}) copy-start(f32[192,1]{0,1:T(1,128)S(1)} %get-tuple-element.154) | copy-start | bytes 2308
  14.9 18.4 %copy-start.19 = (f32[192,1]{0,1:T(1,128)}, f32[192,1]{0,1:T(1,128)S(1)}, u32[]{:S(2)}) copy-start(f32[192,1]{0,1:T(1,128)S(1)} %get-tuple-element.155) | copy-start | bytes 2308
  14.9 18.4 %copy-start.21 = (f32[192,1]{0,1:T(1,128)}, f32[192,1]{0,1:T(1,128)S(1)}, u32[]{:S(2)}) copy-start(f32[192,1]{0,1:T(1,128)S(1)} %get-tuple-element.156) | copy-start | bytes 2308
  14.9 18.4 %copy-start.23 = (f32[192,1]{0,1:T(1,128)}, f32[192,1]{0,1:T(1,128)S(1)}, u32[]{:S(2)}) copy-start(f32[192,1]{0,1:T(1,128)S(1)} %get-tuple-element.157) | copy-start | bytes 2308
  15.0 18.4 %copy-start.25 = (f32[192,1]{0,1:T(1,128)}, f32[192,1]{0,1:T(1,128)S(1)}, u32[]{:S(2)}) copy-start(f32[192,1]{0,1:T(1,128)S(1)} %get-tuple-element.158) | copy-start | bytes 2308
  15.0 18.4 %copy-start.27 = (f32[192,1]{0,1:T(1,128)}, f32[192,1]{0,1:T(1,128)S(1)}, u32[]{:S(2)}) copy-start(f32[192,1]{0,1:T(1,128)S(1)} %get-tuple-element.159) | copy-start | bytes 2308
  15.0 18.4 %copy-start.29 = (f32[192,1]{0,1:T(1,128)}, f32[192,1]{0,1:T(1,128)S(1)}, u32[]{:S(2)}) copy-start(f32[192,1]{0,1:T(1,128)S(1)} %get-tuple-element.160) | copy-start | bytes 2308
  15.0 18.4 %copy-start.31 = (f32[192,1]{0,1:T(1,128)}, f32[192,1]{0,1:T(1,128)S(1)}, u32[]{:S(2)}) copy-start(f32[192,1]{0,1:T(1,128)S(1)} %get-tuple-element.161) | copy-start | bytes 2308
  15.0 18.4 %copy-start.33 = (f32[192,1]{0,1:T(1,128)}, f32[192,1]{0,1:T(1,128)S(1)}, u32[]{:S(2)}) copy-start(f32[192,1]{0,1:T(1,128)S(1)} %get-tuple-element.162) | copy-start | bytes 2308
  15.0 18.4 %copy-start.35 = (f32[192,1]{0,1:T(1,128)}, f32[192,1]{0,1:T(1,128)S(1)}, u32[]{:S(2)}) copy-start(f32[192,1]{0,1:T(1,128)S(1)} %get-tuple-element.163) | copy-start | bytes 2308
  15.0 18.4 %copy-start.37 = (f32[192,1]{0,1:T(1,128)}, f32[192,1]{0,1:T(1,128)S(1)}, u32[]{:S(2)}) copy-start(f32[192,1]{0,1:T(1,128)S(1)} %get-tuple-element.164) | copy-start | bytes 2308
  15.0 18.4 %copy-start.39 = (f32[192,1]{0,1:T(1,128)}, f32[192,1]{0,1:T(1,128)S(1)}, u32[]{:S(2)}) copy-start(f32[192,1]{0,1:T(1,128)S(1)} %get-tuple-element.165) | copy-start | bytes 2308
  15.0 18.4 %copy-start.41 = (f32[192,1]{0,1:T(1,128)}, f32[192,1]{0,1:T(1,128)S(1)}, u32[]{:S(2)}) copy-start(f32[192,1]{0,1:T(1,128)S(1)} %get-tuple-element.166) | copy-start | bytes 2308
  15.1 18.4 %copy-start.43 = (f32[192,1]{0,1:T(1,128)}, f32[192,1]{0,1:T(1,128)S(1)}, u32[]{:S(2)}) copy-start(f32[192,1]{0,1:T(1,128)S(1)} %get-tuple-element.167) | copy-start | bytes 2308
  15.1 18.4 %copy-start.45 = (f32[192,1]{0,1:T(1,128)}, f32[192,1]{0,1:T(1,128)S(1)}, u32[]{:S(2)}) copy-start(f32[192,1]{0,1:T(1,128)S(1)} %get-tuple-element.168) | copy-start | bytes 2308
  15.1 18.4 %copy-start.47 = (f32[192,1]{0,1:T(1,128)}, f32[192,1]{0,1:T(1,128)S(1)}, u32[]{:S(2)}) copy-start(f32[192,1]{0,1:T(1,128)S(1)} %get-tuple-element.169) | copy-start | bytes 2308
  15.1 18.4 %copy-start.49 = (f32[192,1]{0,1:T(1,128)}, f32[192,1]{0,1:T(1,128)S(1)}, u32[]{:S(2)}) copy-start(f32[192,1]{0,1:T(1,128)S(1)} %get-tuple-element.170) | copy-start | bytes 2308
  15.1 18.4 %copy-start.51 = (f32[192,1]{0,1:T(1,128)}, f32[192,1]{0,1:T(1,128)S(1)}, u32[]{:S(2)}) copy-start(f32[192,1]{0,1:T(1,128)S(1)} %get-tuple-element.171) | copy-start | bytes 2308
  15.1 18.4 %copy-start.53 = (f32[192,1]{0,1:T(1,128)}, f32[192,1]{0,1:T(1,128)S(1)}, u32[]{:S(2)}) copy-start(f32[192,1]{0,1:T(1,128)S(1)} %get-tuple-element.172) | copy-start | bytes 2308
  15.1 18.4 %copy-start.55 = (f32[192,1]{0,1:T(1,128)}, f32[192,1]{0,1:T(1,128)S(1)}, u32[]{:S(2)}) copy-start(f32[192,1]{0,1:T(1,128)S(1)} %get-tuple-element.173) | copy-start | bytes 2308
  15.1 18.4 %copy-start.57 = (f32[192,1]{0,1:T(1,128)}, f32[192,1]{0,1:T(1,128)S(1)}, u32[]{:S(2)}) copy-start(f32[192,1]{0,1:T(1,128)S(1)} %get-tuple-element.174) | copy-start | bytes 2308
  15.2 18.4 %copy-start.59 = (f32[192,1]{0,1:T(1,128)}, f32[192,1]{0,1:T(1,128)S(1)}, u32[]{:S(2)}) copy-start(f32[192,1]{0,1:T(1,128)S(1)} %get-tuple-element.175) | copy-start | bytes 2308
  15.2 18.4 %copy-start.61 = (f32[192,1]{0,1:T(1,128)}, f32[192,1]{0,1:T(1,128)S(1)}, u32[]{:S(2)}) copy-start(f32[192,1]{0,1:T(1,128)S(1)} %get-tuple-element.176) | copy-start | bytes 2308
  15.2 18.4 %copy-start.63 = (f32[192,1]{0,1:T(1,128)}, f32[192,1]{0,1:T(1,128)S(1)}, u32[]{:S(2)}) copy-start(f32[192,1]{0,1:T(1,128)S(1)} %get-tuple-element.177) | copy-start | bytes 2308
  15.2 18.4 %copy-start.65 = (f32[192,1]{0,1:T(1,128)}, f32[192,1]{0,1:T(1,128)S(1)}, u32[]{:S(2)}) copy-start(f32[192,1]{0,1:T(1,128)S(1)} %get-tuple-element.178) | copy-start | bytes 2308
  15.2 18.4 %copy-start.67 = (f32[192,1]{0,1:T(1,128)}, f32[192,1]{0,1:T(1,128)S(1)}, u32[]{:S(2)}) copy-start(f32[192,1]{0,1:T(1,128)S(1)} %get-tuple-element.179) | copy-start | bytes 2308
  15.2 18.4 %copy-start.69 = (f32[192,1]{0,1:T(1,128)}, f32[192,1]{0,1:T(1,128)S(1)}, u32[]{:S(2)}) copy-start(f32[192,1]{0,1:T(1,128)S(1)} %get-tuple-element.180) | copy-start | bytes 2308
  15.2 18.4 %copy-start.71 = (f32[192,1]{0,1:T(1,128)}, f32[192,1]{0,1:T(1,128)S(1)}, u32[]{:S(2)}) copy-start(f32[192,1]{0,1:T(1,128)S(1)} %get-tuple-element.181) | copy-start | bytes 2308
  15.2 18.4 %copy-start.73 = (f32[192,1]{0,1:T(1,128)}, f32[192,1]{0,1:T(1,128)S(1)}, u32[]{:S(2)}) copy-start(f32[192,1]{0,1:T(1,128)S(1)} %get-tuple-element.182) | copy-start | bytes 2308
  15.2 18.4 %copy-start.75 = (f32[192,1]{0,1:T(1,128)}, f32[192,1]{0,1:T(1,128)S(1)}, u32[]{:S(2)}) copy-start(f32[192,1]{0,1:T(1,128)S(1)} %get-tuple-element.183) | copy-start | bytes 2308
  15.2 18.4 %copy-start.77 = (f32[192,1]{0,1:T(1,128)}, f32[192,1]{0,1:T(1,128)S(1)}, u32[]{:S(2)}) copy-start(f32[192,1]{0,1:T(1,128)S(1)} %get-tuple-element.184) | copy-start | bytes 2308
  15.3 18.4 %copy-start.79 = (f32[192,1]{0,1:T(1,128)}, f32[192,1]{0,1:T(1,128)S(1)}, u32[]{:S(2)}) copy-start(f32[192,1]{0,1:T(1,128)S(1)} %get-tuple-element.185) | copy-start | bytes 2308
  15.3 18.4 %copy-start.81 = (f32[192,1]{0,1:T(1,128)}, f32[192,1]{0,1:T(1,128)S(1)}, u32[]{:S(2)}) copy-start(f32[192,1]{0,1:T(1,128)S(1)} %get-tuple-element.186) | copy-start | bytes 2308
  15.3 18.4 %copy-start.83 = (f32[192,1]{0,1:T(1,128)}, f32[192,1]{0,1:T(1,128)S(1)}, u32[]{:S(2)}) copy-start(f32[192,1]{0,1:T(1,128)S(1)} %get-tuple-element.187) | copy-start | bytes 2308
  15.9 17.8 %copy-start.85 = (f32[192,1]{0,1:T(1,128)}, f32[192,1]{0,1:T(1,128)S(1)}, u32[]{:S(2)}) copy-start(f32[192,1]{0,1:T(1,128)S(1)} %get-tuple-element.188) | copy-start | bytes 2308
  15.9 17.8 %copy-start.87 = (f32[192,1]{0,1:T(1,128)}, f32[192,1]{0,1:T(1,128)S(1)}, u32[]{:S(2)}) copy-start(f32[192,1]{0,1:T(1,128)S(1)} %get-tuple-element.189) | copy-start | bytes 2308
  15.9 17.8 %copy-start.89 = (f32[192,1]{0,1:T(1,128)}, f32[192,1]{0,1:T(1,128)S(1)}, u32[]{:S(2)}) copy-start(f32[192,1]{0,1:T(1,128)S(1)} %get-tuple-element.190) | copy-start | bytes 2308
  15.9 17.8 %copy-start.90 = (f32[192,1]{0,1:T(1,128)}, f32[192,1]{0,1:T(1,128)S(1)}, u32[]{:S(2)}) copy-start(f32[192,1]{0,1:T(1,128)S(1)} %get-tuple-element.191) | copy-start | bytes 2308
  20.2 6.5 %collective-permute-start.2 = (bf16[192,14,3]{0,1,2:T(8,128)(2,1)S(1)}, bf16[192,14,3]{0,1,2:T(8,128)(2,1)S(1)}, u32[]{:S(2)}, u32[]{:S(2)}) collective-permute-start(bf16[192,14,3]{0,1,2:T(8,128)(2,1)S(1)} %copy.57), channel_id=1, source_target_pairs={{0,1},{1,2},{2,3},{3,4},{4,5},{5,6},{6,7},{8,9},{9,10},{10,11},{11... | collective-permute-start | bytes 48392 | tf_op jit(solution)/shard_map/ppermute | solution.py:20
  25.4 6.1 %collective-permute-start.3 = (bf16[192,14,3]{0,1,2:T(8,128)(2,1)S(1)}, bf16[192,14,3]{0,1,2:T(8,128)(2,1)S(1)}, u32[]{:S(2)}, u32[]{:S(2)}) collective-permute-start(bf16[192,14,3]{0,1,2:T(8,128)(2,1)S(1)} %copy.59), channel_id=1, source_target_pairs={{1,0},{2,1},{3,2},{4,3},{5,4},{6,5},{7,6},{9,8},{10,9},{11,10},{12... | collective-permute-start | bytes 48392 | tf_op jit(solution)/shard_map/ppermute | solution.py:21
  139.6 9.6 %collective-permute-start.4 = (bf16[192,3,128]{2,0,1:T(8,128)(2,1)S(1)}, bf16[192,3,128]{2,0,1:T(8,128)(2,1)S(1)}, u32[]{:S(2)}, u32[]{:S(2)}) collective-permute-start(bf16[192,3,128]{2,0,1:T(8,128)(2,1)S(1)} %get-tuple-element.147), channel_id=1, source_target_pairs={{0,8},{8,16},{16,24},{24,32},{32,40},{40,48},{48,56},{1,9},{9,17},... | collective-permute-start | bytes 442376 | tf_op jit(solution)/shard_map/ppermute | solution.py:20
  144.8 6.5 %collective-permute-start.5 = (bf16[192,3,128]{2,0,1:T(8,128)(2,1)S(1)}, bf16[192,3,128]{2,0,1:T(8,128)(2,1)S(1)}, u32[]{:S(2)}, u32[]{:S(2)}) collective-permute-start(bf16[192,3,128]{2,0,1:T(8,128)(2,1)S(1)} %get-tuple-element.146), channel_id=1, source_target_pairs={{8,0},{16,8},{24,16},{32,24},{40,32},{48,40},{56,48},{9,1},{17,9},... | collective-permute-start | bytes 442376 | tf_op jit(solution)/shard_map/ppermute | solution.py:21
  152.7 34.0 %collective-permute-start.6 = (bf16[192,14,3]{0,1,2:T(8,128)(2,1)S(1)}, bf16[192,14,3]{0,1,2:T(8,128)(2,1)S(1)}, u32[]{:S(2)}, u32[]{:S(2)}) collective-permute-start(bf16[192,14,3]{0,1,2:T(8,128)(2,1)S(1)} %copy.65), channel_id=1, source_target_pairs={{1,0},{2,1},{3,2},{4,3},{5,4},{6,5},{7,6},{9,8},{10,9},{11,10},{12... | collective-permute-start | bytes 48392 | tf_op jit(solution)/shard_map/ppermute | solution.py:21
  155.0 32.1 %collective-permute-start.7 = (bf16[192,14,3]{0,1,2:T(8,128)(2,1)}, bf16[192,14,3]{0,1,2:T(8,128)(2,1)S(1)}, u32[]{:S(2)}, u32[]{:S(2)}) collective-permute-start(bf16[192,14,3]{0,1,2:T(8,128)(2,1)} %copy.67), channel_id=1, source_target_pairs={{0,1},{1,2},{2,3},{3,4},{4,5},{5,6},{6,7},{8,9},{9,10},{10,11},{11... | collective-permute-start | bytes 48392 | tf_op jit(solution)/shard_map/ppermute | solution.py:20
  (68 other events, 191.8 us)
Sparse Core Ops, SparseCore 0:
  185.9 146.6 all-reduce.1
where the time goes:
time: 356 us; the launch traced here: 355 us
  waiting for transfers between devices  143 us (40%)
  blocking collectives  68.1 us (19%)
  other arithmetic  42 us (12%)
  local copies, waits for them, and re-layouts  40.8 us (11%)
  starting transfers between devices  27.8 us (8%)
  between operations  17.8 us (5%)
  matrix products  15.6 us (4%)
    psum x1, waiting for transfers between devices, flat_psum(): total = lax.psum(flat, axes)  133 us
    psum x3, blocking collectives, flat_psum(): total = lax.psum(flat, axes)  68.1 us
    ppermute x4, starting transfers between devices, padded_2(): before = lax.ppermute(last, axis, up)  20.1 us
    concatenate x1, local copies, waits for them, and re-layouts, flat_psum(): flat = jnp.concatenate([p.reshape(-1) for p in parts])  20 us
    dot_general x12, matrix products, product(): jnp.einsum(form, left_side, right_side, preferred_element_type=jnp.float32)  15.6 us
    reduce_sum x4, other arithmetic, conv_backward(): columns.append(jnp.sum(window * conv_float, axis=(1, 2)))  10.4 us
    ppermute x4, waiting for transfers between devices, padded_2(): after = lax.ppermute(leading, axis, down)  9.93 us
    reduce_sum x1, other arithmetic, encoder_forward(): centre = conv - jnp.mean(conv, axis=0, keepdims=True)  9.17 us
  transfers between devices with their start and end apart: 9, of which 4 were waited for; matrix products, arithmetic and copies ran while one was open for 12% of the time, Pallas kernels for 0%

commit v1 on v0

--- a/solution.py
+++ b/solution.py
@@ -146,16 +146,54 @@
     return (d_encoded, loss_sum, (lateral_grad, latbias_grad, classify_grad, clsbias_grad))
 
 
-def flat_psum(parts, axes):
-    shapes = [p.shape for p in parts]
-    flat = jnp.concatenate([p.reshape(-1) for p in parts])
-    total = lax.psum(flat, axes)
+LANES = 128
+
+
+def pack_rows(parts, multiple):
+    shapes, rows = [], []
+    for part in parts:
+        flat = part.reshape(-1)
+        size = flat.shape[0]
+        padded_rows = -(-size // (8 * LANES)) * 8
+        flat = jnp.pad(flat, (0, padded_rows * LANES - size))
+        rows.append(flat.reshape(padded_rows, LANES))
+        shapes.append(part.shape)
+    total = sum(r.shape[0] for r in rows)
+    extra = -total % multiple
+    if extra:
+        rows.append(jnp.zeros((extra, LANES), jnp.float32))
+    return jnp.concatenate(rows, axis=0), shapes
+
+
+def unpack_rows(buffer, shapes):
     out, at = [], 0
     for shape in shapes:
         size = math.prod(shape)
-        out.append(total[at : at + size].reshape(shape))
-        at += size
+        padded_rows = -(-size // (8 * LANES)) * 8
+        out.append(buffer[at : at + padded_rows].reshape(-1)[:size].reshape(shape))
+        at += padded_rows
     return out
+
+
+def butterfly_psum(buffer, axes, order):
+    index = lax.axis_index(axes)
+    count = math.prod(lax.axis_size(a) for a in axes)
+    for bit_at in order:
+        bit = (index >> bit_at) & 1
+        halves = buffer.reshape(2, buffer.shape[0] // 2, buffer.shape[1])
+        keep = lax.dynamic_index_in_dim(halves, bit, 0, keepdims=False)
+        send = lax.dynamic_index_in_dim(halves, 1 - bit, 0, keepdims=False)
+        pairs = [(i, i ^ (1 << bit_at)) for i in range(count)]
+        buffer = keep + lax.ppermute(send, axes, pairs)
+    for bit_at in reversed(order):
+        bit = (index >> bit_at) & 1
+        pairs = [(i, i ^ (1 << bit_at)) for i in range(count)]
+        other = lax.ppermute(buffer, axes, pairs)
+        both = jnp.zeros((2,) + buffer.shape, buffer.dtype)
+        both = lax.dynamic_update_index_in_dim(both, buffer, bit, 0)
+        both = lax.dynamic_update_index_in_dim(both, other, 1 - bit, 0)
+        buffer = both.reshape(-1, buffer.shape[1])
+    return buffer
 
 
 def shards(
@@ -191,8 +229,15 @@
     output, saved = encoder_forward(padded, enc_params)
     returned, loss_sum, dec_grads = decoder(output, label_tile, w_lateral, b_lateral, w_class, b_class)
     d_conv, enc_grads = encoder_backward(saved, returned, enc_params)
-    early = flat_psum(list(enc_grads) + list(dec_grads) + [loss_sum], axes)
+    d_padded = rimmed(d_conv)
+    d_input, kernel_grad, convbias_grad = conv_backward(padded, d_conv, d_padded, returned, dw_weight)
+    parts = [kernel_grad, convbias_grad] + list(enc_grads) + list(dec_grads) + [loss_sum]
+    count = math.prod(lax.axis_size(a) for a in axes)
+    buffer, shapes = pack_rows(parts, count * 2)
+    buffer = butterfly_psum(buffer, axes, [3, 6, 1, 2, 0, 4, 5])
     (
+        kernel_grad,
+        convbias_grad,
         gain_grad,
         normbias_grad,
         expand_grad,
@@ -205,12 +250,7 @@
         classify_grad,
         clsbias_grad,
         loss_total,
-    ) = early
-    d_padded = rimmed(d_conv)
-    d_input, kernel_grad, convbias_grad = conv_backward(padded, d_conv, d_padded, returned, dw_weight)
-    kernel_grad, convbias_grad = flat_psum([kernel_grad, convbias_grad], ("col",))
-    kernel_grad, convbias_grad = flat_psum([kernel_grad, convbias_grad], ("row",))
-    kernel_grad, convbias_grad = flat_psum([kernel_grad, convbias_grad], ("section",))
+    ) = unpack_rows(buffer, shapes)
     cell_count = micro_count * height * width * lax.axis_size("row") * lax.axis_size("col")
     grad_scale = 1.0 / math.sqrt(cell_count)
     return (

time: 356 us -> 213 us (0.60)
  waiting for transfers between devices: 143 us -> 41.8 us
  blocking collectives: 68.1 us -> 0 us
  starting transfers between devices: 27.8 us -> 59.9 us
  between operations: 17.8 us -> 4.61 us
    psum x1 -> x0, waiting for transfers between devices: 133 us -> none  [flat_psum(): total = lax.psum(flat, axes)]
    psum x3 -> x0, blocking collectives: 68.1 us -> none  [flat_psum(): total = lax.psum(flat, axes)]
    ppermute x0 -> x14, waiting for transfers between devices: none -> 34.2 us  [the longest x7 25.1 us: butterfly_psum(): buffer = keep + lax.ppermute(send, axes, pairs)]
    ppermute x0 -> x14, starting transfers between devices: none -> 29.6 us  [the longest x7 17.3 us: butterfly_psum(): other = lax.ppermute(buffer, axes, pairs)]
    concatenate x1, local copies, waits for them, and re-layouts: 20 us -> 0.6 us  [pack_rows(): return (jnp.concatenate(rows, axis=0), shapes)]
    unnamed x219 -> x244, local copies, waits for them, and re-layouts: 8.08 us -> 17.5 us
    ppermute x4, starting transfers between devices: 20.1 us -> 23.9 us  [padded_2(): before = lax.ppermute(last, axis, up)]
    dynamic_update_slice x0 -> x13, local copies, waits for them, and re-layouts: none -> 3.67 us  [the longest x7 1.84 us: butterfly_psum(): both = lax.dynamic_update_index_in_dim(both, other, 1 - bit, 0)]
  transfers between devices with their start and end apart: 9 -> 22, of which waited for: 4 -> 14; matrix products, arithmetic and copies ran while one was open for 12% -> 9% of each run, Pallas kernels for 0% -> 0%
where the time goes in v1:
time: 213 us; the launch traced here: 209 us
  starting transfers between devices  59.9 us (28%)
  local copies, waits for them, and re-layouts  44.3 us (21%)
  other arithmetic  43 us (20%)
  waiting for transfers between devices  41.8 us (20%)
  matrix products  15.6 us (7%)
  between operations  4.61 us (2%)
    ppermute x7, waiting for transfers between devices, butterfly_psum(): buffer = keep + lax.ppermute(send, axes, pairs)  25.1 us
    ppermute x4, starting transfers between devices, padded_2(): before = lax.ppermute(last, axis, up)  23.9 us
    unnamed x244, local copies, waits for them, and re-layouts  17.5 us
    ppermute x7, starting transfers between devices, butterfly_psum(): other = lax.ppermute(buffer, axes, pairs)  17.3 us
    dot_general x12, matrix products, product(): jnp.einsum(form, left_side, right_side, preferred_element_type=jnp.float32)  15.6 us
    ppermute x7, starting transfers between devices, butterfly_psum(): buffer = keep + lax.ppermute(send, axes, pairs)  12.3 us
    reduce_sum x3, other arithmetic, conv_backward(): columns.append(jnp.sum(window * conv_float, axis=(1, 2)))  9.7 us
    broadcast_in_dim x1, other arithmetic, shards(): d_input[None]  9.29 us
  transfers between devices with their start and end apart: 22, of which 14 were waited for; matrix products, arithmetic and copies ran while one was open for 9% of the time, Pallas kernels for 0%

profile of v1, /device:TPU:1, one launch (start us, length us, event | category | flops | bytes accessed | tf_op | source)
XLA Modules:
  0.0 209.1 jit_solution(10809394037793549112)
XLA Ops:
  1.9 4.5 %collective-permute-start = (bf16[192,3,128]{2,0,1:T(8,128)(2,1)S(1)}, bf16[192,3,128]{2,0,1:T(8,128)(2,1)S(1)}, u32[]{:S(2)}, u32[]{:S(2)}) collective-permute-start(bf16[192,3,128]{2,0,1:T(8,128)(2,1)S(1)} %get-tuple-element.156), channel_id=1, source_target_pairs={{0,8},{8,16},{16,24},{24,32},{32,40},{40,48},{48,56},{1,9},{9,17},... | collective-permute-start | bytes 442376 | tf_op jit(solution)/shard_map/ppermute | solution.py:20
  6.4 1.9 collective-permute-start.1
  9.9 3.0 %collective-permute-done.1 = bf16[192,3,128]{2,0,1:T(8,128)(2,1)S(1)} collective-permute-done((bf16[192,3,128]{2,0,1:T(8,128)(2,1)S(1)}, bf16[192,3,128]{2,0,1:T(8,128)(2,1)S(1)}, u32[]{:S(2)}, u32[]{:S(2)}) %collective-permute-start.1) | collective-permute-done | bytes 147488 | tf_op jit(solution)/shard_map/ppermute | solution.py:21
  14.1 1.5 copy.57
  15.6 4.8 %collective-permute-start.2 = (bf16[192,14,3]{0,1,2:T(8,128)(2,1)S(1)}, bf16[192,14,3]{0,1,2:T(8,128)(2,1)S(1)}, u32[]{:S(2)}, u32[]{:S(2)}) collective-permute-start(bf16[192,14,3]{0,1,2:T(8,128)(2,1)S(1)} %copy.57), channel_id=1, source_target_pairs={{0,1},{1,2},{2,3},{3,4},{4,5},{5,6},{6,7},{8,9},{9,10},{10,11},{11... | collective-permute-start | bytes 48392 | tf_op jit(solution)/shard_map/ppermute | solution.py:20
  20.8 1.3 collective-permute-start.3
  23.3 3.6 %collective-permute-done.3 = bf16[192,14,3]{0,1,2:T(8,128)(2,1)S(1)} collective-permute-done((bf16[192,14,3]{0,1,2:T(8,128)(2,1)S(1)}, bf16[192,14,3]{0,1,2:T(8,128)(2,1)S(1)}, u32[]{:S(2)}, u32[]{:S(2)}) %collective-permute-start.3) | collective-permute-done | bytes 16160 | tf_op jit(solution)/shard_map/ppermute | solution.py:21
  28.3 2.4 %maximum_maximum_fusion = (bf16[192,14,131]{2,0,1:T(8,128)(2,1)S(1)}, bf16[192,14,131]{2,0,1:T(8,128)(2,1)S(1)}) fusion(bf16[192,3,128]{2,0,1:T(8,128)(2,1)S(1)} %collective-permute-done.1, bf16[192,8,128]{2,0,1:T(8,128)(2,1)S(1)} %bitcast.332, bf16[192,3,128]{2,0,1:T(8,128)(2,1)S(1)} %collective-permute-done, bf16[192,14,3]{2,0,1:T(8,128)(2,1)} %copy.58, ...), kind=kLoop, calls=%fused_computation.79 | loop fusion | flops 5634048 | bytes 2128896 | tf_op jit(solution)/shard_map/concatenate | solution.py:22
  31.2 8.3 %fusion.173 = (f32[8,128]{1,0:T(8,128)S(1)}, f32[192,8,128]{2,0,1:T(8,128)S(1)}) fusion(f32[192]{0:T(256)S(1)} %copy-done.110, bf16[192,14,131]{2,0,1:T(8,128)(2,1)S(1)} %get-tuple-element.151, f32[192]{0:T(256)S(1)} %bitcast.453, f32[192]{0:T(256)S(1)} %bitcast.455, f32[192]{0:T(256)S(1)} %bitcast.360, bf16[192,3,128]{2,0,1:T(8,128)(2,1)S(1)} %collective-permute-done.1, ...), kind=kLoop, calls=%fused_computation.403 | loop fusion | flops 30276608 | bytes 18032128 | tf_op jit(solution)/shard_map/reduce_sum | solution.py:64
  43.4 1.9 convert_reduce_fusion.2
  45.3 2.0 convert_reduce_fusion.3
  47.3 2.4 %convert_reduce_fusion.1 = (f32[768]{0:T(1024)}, bf16[768,8,128]{0,2,1:T(8,128)(2,1)S(1)}) fusion(f32[8,128,768]{2,1,0:T(8,128)S(1)} %get-tuple-element.208, f32[768]{0:T(1024)S(1)} %copy-done.104, bf16[192,8,128]{2,0,1:T(8,128)(2,1)S(1)} %get-tuple-element.132, bf16[768,192]{0,1:T(8,128)(2,1)S(1)} %copy-done.8), kind=kOutput, calls=%fused_computation.64 | convolution fusion | flops 312212736 | bytes 5412864 | tf_op jit(solution)/shard_map/chw,dc->dhw/dot_general | solution.py:33
  49.7 1.4 convolution_bitcast_fusion.1
  51.1 1.4 fusion.147
  52.5 4.1 %fusion.142 = (f32[192]{0:T(256)}, f32[192]{0:T(256)}, f32[192]{0:T(256)}, f32[192]{0:T(256)}, f32[192]{0:T(256)}, /*index=5*/f32[192]{0:T(256)}, f32[192]{0:T(2...) fusion(bf16[192,14,131]{2,0,1:T(8,128)(2,1)S(1)} %get-tuple-ele, ...), kind=kLoop, calls=%fused_computation.266 | loop fusion | flops 12382848 | bytes 9074944 | tf_op jit(solution)/shard_map/reduce_sum | solution.py:121
  56.5 4.5 %fusion.146 = (f32[192]{0:T(256)}, f32[192]{0:T(256)}, f32[192]{0:T(256)}, f32[192]{0:T(256)}, f32[192]{0:T(256)}, /*index=5*/f32[192]{0:T(256)}, f32[192]{0:T(2...) fusion(bf16[192,8,128]{2,0,1:T(8,128)(2,1)S(1)} %get-tuple-elem, ...), kind=kLoop, calls=%fused_computation.270 | loop fusion | flops 10809984 | bytes 7484928 | tf_op jit(solution)/shard_map/reduce_sum | solution.py:121
  62.2 1.5 convolution_bitcast_fusion
  66.0 1.9 reshape.268
  67.9 2.7 %convert_reduce_fusion = (f32[192]{0:T(256)}, f32[192]{0:T(256)}, f32[192]{0:T(256)}, f32[192]{0:T(256)}, f32[192]{0:T(256)}, /*index=5*/f32[192]{0:T(256)}, f32...) fusion(bf16[192,8,128]{2,0,1:T(8,128)(2,1)S(1)} %get-tuple-element.133, ...), kind=kLoop, calls=%fused_computation | loop fusion | flops 7468992 | bytes 2662656 | tf_op jit(solution)/shard_map/reduce_sum | solution.py:123
  70.6 5.1 %stack.199 = f32[192,49]{0,1:T(8,128)S(1)} concatenate(f32[192,1]{0,1:T(1,128)} %bitcast.486, f32[192,1]{0,1:T(1,128)} %bitcast.485, f32[192,1]{0,1:T(1,128)} %bitcast.484, f32[192,1]{0,1:T(1,128)} %bitcast.477, f32[192,1]{0,1:T(1,128)} %bitcast.457, f32[192,1]{0,1:T(1,128)} %bitcast.458, f32[192,1]{0,1:T(1,128)} %bitcast.459, f32[192,1]{0,1:T(1,128)} %bitcast.488, ...), dimensions={1} | concatenate | bytes 75264 | tf_op jit(solution)/shard_map/stack | solution.py:122
  76.7 1.8 reduce_sum.632
  80.7 1.3 constant_dynamic-update-slice_fusion.13
  82.0 1.3 constant_dynamic-update-slice_fusion.12
  93.8 2.4 %collective-permute-done.8 = f32[1664,128]{1,0:T(8,128)S(1)} collective-permute-done((f32[1664,128]{1,0:T(8,128)S(1)}, f32[1664,128]{1,0:T(8,128)S(1)}, u32[]{:S(2)}, u32[]{:S(2)}) %collective-permute-start.8) | collective-permute-done | bytes 852000 | tf_op jit(solution)/shard_map/ppermute | solution.py:187
  97.9 10.8 %collective-permute-done.9 = f32[832,128]{1,0:T(8,128)S(1)} collective-permute-done((f32[832,128]{1,0:T(8,128)S(1)}, f32[832,128]{1,0:T(8,128)S(1)}, u32[]{:S(2)}, u32[]{:S(2)}) %collective-permute-start.9) | collective-permute-done | bytes 426016 | tf_op jit(solution)/shard_map/ppermute | solution.py:187
  108.8 1.7 collective-permute-start.10
  110.5 4.5 %collective-permute-done.10 = f32[416,128]{1,0:T(8,128)S(1)} collective-permute-done((f32[416,128]{1,0:T(8,128)S(1)}, f32[416,128]{1,0:T(8,128)S(1)}, u32[]{:S(2)}, u32[]{:S(2)}) %collective-permute-start.10) | collective-permute-done | bytes 213024 | tf_op jit(solution)/shard_map/ppermute | solution.py:187
  115.1 3.3 %collective-permute-start.11 = (f32[208,128]{1,0:T(8,128)S(1)}, f32[208,128]{1,0:T(8,128)S(1)}, u32[]{:S(2)}, u32[]{:S(2)}) collective-permute-start(f32[208,128]{1,0:T(8,128)S(1)} %dynamic-slice_bitcast_fusion.3), channel_id=1, source_target_pairs={{0,4},{1,5},{2,6},{3,7},{4,0},{5,1},{6,2},{7,3},{8,12},{9,13},{10,... | collective-permute-start | bytes 319496 | tf_op jit(solution)/shard_map/ppermute | solution.py:187
  118.5 2.1 %collective-permute-done.11 = f32[208,128]{1,0:T(8,128)S(1)} collective-permute-done((f32[208,128]{1,0:T(8,128)S(1)}, f32[208,128]{1,0:T(8,128)S(1)}, u32[]{:S(2)}, u32[]{:S(2)}) %collective-permute-start.11) | collective-permute-done | bytes 106528 | tf_op jit(solution)/shard_map/ppermute | solution.py:187
  120.6 3.1 %collective-permute-start.12 = (f32[104,128]{1,0:T(8,128)S(1)}, f32[104,128]{1,0:T(8,128)S(1)}, u32[]{:S(2)}, u32[]{:S(2)}) collective-permute-start(f32[104,128]{1,0:T(8,128)S(1)} %dynamic-slice_bitcast_fusion.4), channel_id=1, source_target_pairs={{0,1},{1,0},{2,3},{3,2},{4,5},{5,4},{6,7},{7,6},{8,9},{9,8},{10,11... | collective-permute-start | bytes 159752 | tf_op jit(solution)/shard_map/ppermute | solution.py:187
  123.7 1.5 collective-permute-done.12
  126.5 1.9 collective-permute-done.13
  128.4 2.3 %collective-permute-start.14 = (f32[26,128]{1,0:T(8,128)S(1)}, f32[26,128]{1,0:T(8,128)S(1)}, u32[]{:S(2)}, u32[]{:S(2)}) collective-permute-start(f32[26,128]{1,0:T(8,128)S(1)} %dynamic-slice_bitcast_fusion.6), channel_id=1, source_target_pairs={{0,32},{1,33},{2,34},{3,35},{4,36},{5,37},{6,38},{7,39},{8,40},{9,... | collective-permute-start | bytes 39944 | tf_op jit(solution)/shard_map/ppermute | solution.py:187
  130.7 1.8 collective-permute-done.14
  132.6 2.5 %collective-permute-start.15 = (f32[26,128]{1,0:T(8,128)S(1)}, f32[26,128]{1,0:T(8,128)S(1)}, u32[]{:S(2)}, u32[]{:S(2)}) collective-permute-start(f32[26,128]{1,0:T(8,128)S(1)} %get-tuple-element.128), channel_id=1, source_target_pairs={{0,32},{1,33},{2,34},{3,35},{4,36},{5,37},{6,38},{7,39},{8,40},{9,... | collective-permute-start | bytes 39944 | tf_op jit(solution)/shard_map/ppermute | solution.py:191
  135.1 8.1 %collective-permute-start.4 = (bf16[192,3,128]{2,0,1:T(8,128)(2,1)S(1)}, bf16[192,3,128]{2,0,1:T(8,128)(2,1)S(1)}, u32[]{:S(2)}, u32[]{:S(2)}) collective-permute-start(bf16[192,3,128]{2,0,1:T(8,128)(2,1)S(1)} %get-tuple-element.155), channel_id=1, source_target_pairs={{0,8},{8,16},{16,24},{24,32},{32,40},{40,48},{48,56},{1,9},{9,17},... | collective-permute-start | bytes 442376 | tf_op jit(solution)/shard_map/ppermute | solution.py:20
  143.2 1.9 collective-permute-start.5
  145.4 2.6 %collective-permute-done.16 = f32[52,128]{1,0:T(8,128)S(1)} collective-permute-done((f32[52,128]{1,0:T(8,128)S(1)}, f32[52,128]{1,0:T(8,128)S(1)}, u32[]{:S(2)}, u32[]{:S(2)}) %collective-permute-start.16) | collective-permute-done | bytes 26656 | tf_op jit(solution)/shard_map/ppermute | solution.py:191
  148.0 2.9 %collective-permute-start.17 = (f32[104,128]{1,0:T(8,128)S(1)}, f32[104,128]{1,0:T(8,128)S(1)}, u32[]{:S(2)}, u32[]{:S(2)}) collective-permute-start(f32[104,128]{1,0:T(8,128)S(1)} %reshape.287), channel_id=1, source_target_pairs={{0,1},{1,0},{2,3},{3,2},{4,5},{5,4},{6,7},{7,6},{8,9},{9,8},{10,11... | collective-permute-start | bytes 159752 | tf_op jit(solution)/shard_map/ppermute | solution.py:191
  151.0 1.6 collective-permute-done.17
  152.6 3.3 %collective-permute-start.18 = (f32[208,128]{1,0:T(8,128)S(1)}, f32[208,128]{1,0:T(8,128)S(1)}, u32[]{:S(2)}, u32[]{:S(2)}) collective-permute-start(f32[208,128]{1,0:T(8,128)S(1)} %bitcast.356), channel_id=1, source_target_pairs={{0,4},{1,5},{2,6},{3,7},{4,0},{5,1},{6,2},{7,3},{8,12},{9,13},{10,... | collective-permute-start | bytes 319496 | tf_op jit(solution)/shard_map/ppermute | solution.py:191
  156.0 2.1 collective-permute-done.18
  160.8 2.8 %collective-permute-done.19 = f32[416,128]{1,0:T(8,128)S(1)} collective-permute-done((f32[416,128]{1,0:T(8,128)S(1)}, f32[416,128]{1,0:T(8,128)S(1)}, u32[]{:S(2)}, u32[]{:S(2)}) %collective-permute-start.19) | collective-permute-done | bytes 213024 | tf_op jit(solution)/shard_map/ppermute | solution.py:191
  165.4 1.3 collective-permute-start.6
  167.0 6.4 %collective-permute-start.7 = (bf16[192,14,3]{0,1,2:T(8,128)(2,1)S(1)}, bf16[192,14,3]{0,1,2:T(8,128)(2,1)S(1)}, u32[]{:S(2)}, u32[]{:S(2)}) collective-permute-start(bf16[192,14,3]{0,1,2:T(8,128)(2,1)S(1)} %copy.67), channel_id=1, source_target_pairs={{0,1},{1,2},{2,3},{3,4},{4,5},{5,6},{6,7},{8,9},{9,10},{10,11},{11... | collective-permute-start | bytes 48392 | tf_op jit(solution)/shard_map/ppermute | solution.py:20
  179.2 6.9 %collective-permute-start.21 = (f32[1664,128]{1,0:T(8,128)S(1)}, f32[1664,128]{1,0:T(8,128)S(1)}, u32[]{:S(2)}, u32[]{:S(2)}) collective-permute-start(f32[1664,128]{1,0:T(8,128)S(1)} %bitcast.342), channel_id=1, source_target_pairs={{0,8},{1,9},{2,10},{3,11},{4,12},{5,13},{6,14},{7,15},{8,0},{9,1},... | collective-permute-start | bytes 2555912 | tf_op jit(solution)/shard_map/ppermute | solution.py:191
  186.4 9.3 %add_bitcast_fusion = f32[1,192,8,128]{3,1,2,0:T(8,128)S(1)} fusion(f32[192,8,128]{2,0,1:T(8,128)S(1)} %copy-done.1, bf16[192,8,128]{2,0,1:T(8,128)(2,1)S(1)} %get-tuple-element.133, bf16[192,3,128]{2,0,1:T(8,128)(2,1)S(1)} %collective-permute-done.4, bf16[192,3,128]{2,0,1:T(8,128)(2,1)S(1)} %collective-permute-done.5, ...), kind=kLoop, calls=%fused_computation.276 | loop fusion | flops 30081024 | bytes 18813696 | tf_op jit(solution)/shard_map/broadcast_in_dim | solution.py:257
  195.7 1.3 copy.76
  (356 shorter events, 51.5 us)
Async XLA Ops:
  1.9 8.0 %collective-permute-start = (bf16[192,3,128]{2,0,1:T(8,128)(2,1)S(1)}, bf16[192,3,128]{2,0,1:T(8,128)(2,1)S(1)}, u32[]{:S(2)}, u32[]{:S(2)}) collective-permute-start(bf16[192,3,128]{2,0,1:T(8,128)(2,1)S(1)} %get-tuple-element.156), channel_id=1, source_target_pairs={{0,8},{8,16},{16,24},{24,32},{32,40},{40,48},{48,56},{1,9},{9,17},... | collective-permute-start | bytes 442376 | tf_op jit(solution)/shard_map/ppermute | solution.py:20
  6.4 6.5 %collective-permute-start.1 = (bf16[192,3,128]{2,0,1:T(8,128)(2,1)S(1)}, bf16[192,3,128]{2,0,1:T(8,128)(2,1)S(1)}, u32[]{:S(2)}, u32[]{:S(2)}) collective-permute-start(bf16[192,3,128]{2,0,1:T(8,128)(2,1)S(1)} %get-tuple-element.157), channel_id=1, source_target_pairs={{8,0},{16,8},{24,16},{32,24},{40,32},{48,40},{56,48},{9,1},{17,9},... | collective-permute-start | bytes 442376 | tf_op jit(solution)/shard_map/ppermute | solution.py:21
  8.4 22.3 %copy-start.12 = (f32[192,1]{0,1:T(1,128)}, f32[192,1]{0,1:T(1,128)S(1)}, u32[]{:S(2)}) copy-start(f32[192,1]{0,1:T(1,128)S(1)} %get-tuple-element.159) | copy-start | bytes 2308
  8.4 22.3 %copy-start.14 = (f32[192,1]{0,1:T(1,128)}, f32[192,1]{0,1:T(1,128)S(1)}, u32[]{:S(2)}) copy-start(f32[192,1]{0,1:T(1,128)S(1)} %get-tuple-element.160) | copy-start | bytes 2308
  8.4 22.3 %copy-start.16 = (f32[192,1]{0,1:T(1,128)}, f32[192,1]{0,1:T(1,128)S(1)}, u32[]{:S(2)}) copy-start(f32[192,1]{0,1:T(1,128)S(1)} %get-tuple-element.161) | copy-start | bytes 2308
  8.4 22.3 %copy-start.18 = (f32[192,1]{0,1:T(1,128)}, f32[192,1]{0,1:T(1,128)S(1)}, u32[]{:S(2)}) copy-start(f32[192,1]{0,1:T(1,128)S(1)} %get-tuple-element.162) | copy-start | bytes 2308
  8.4 22.3 %copy-start.20 = (f32[192,1]{0,1:T(1,128)}, f32[192,1]{0,1:T(1,128)S(1)}, u32[]{:S(2)}) copy-start(f32[192,1]{0,1:T(1,128)S(1)} %get-tuple-element.163) | copy-start | bytes 2308
  8.4 22.3 %copy-start.22 = (f32[192,1]{0,1:T(1,128)}, f32[192,1]{0,1:T(1,128)S(1)}, u32[]{:S(2)}) copy-start(f32[192,1]{0,1:T(1,128)S(1)} %get-tuple-element.164) | copy-start | bytes 2308
  8.4 22.3 %copy-start.24 = (f32[192,1]{0,1:T(1,128)}, f32[192,1]{0,1:T(1,128)S(1)}, u32[]{:S(2)}) copy-start(f32[192,1]{0,1:T(1,128)S(1)} %get-tuple-element.165) | copy-start | bytes 2308
  8.4 22.3 %copy-start.26 = (f32[192,1]{0,1:T(1,128)}, f32[192,1]{0,1:T(1,128)S(1)}, u32[]{:S(2)}) copy-start(f32[192,1]{0,1:T(1,128)S(1)} %get-tuple-element.166) | copy-start | bytes 2308
  8.5 22.3 %copy-start.28 = (f32[192,1]{0,1:T(1,128)}, f32[192,1]{0,1:T(1,128)S(1)}, u32[]{:S(2)}) copy-start(f32[192,1]{0,1:T(1,128)S(1)} %get-tuple-element.167) | copy-start | bytes 2308
  8.5 22.3 %copy-start.30 = (f32[192,1]{0,1:T(1,128)}, f32[192,1]{0,1:T(1,128)S(1)}, u32[]{:S(2)}) copy-start(f32[192,1]{0,1:T(1,128)S(1)} %get-tuple-element.168) | copy-start | bytes 2308
  8.5 22.3 %copy-start.32 = (f32[192,1]{0,1:T(1,128)}, f32[192,1]{0,1:T(1,128)S(1)}, u32[]{:S(2)}) copy-start(f32[192,1]{0,1:T(1,128)S(1)} %get-tuple-element.169) | copy-start | bytes 2308
  8.5 22.3 %copy-start.34 = (f32[192,1]{0,1:T(1,128)}, f32[192,1]{0,1:T(1,128)S(1)}, u32[]{:S(2)}) copy-start(f32[192,1]{0,1:T(1,128)S(1)} %get-tuple-element.170) | copy-start | bytes 2308
  8.5 22.3 %copy-start.36 = (f32[192,1]{0,1:T(1,128)}, f32[192,1]{0,1:T(1,128)S(1)}, u32[]{:S(2)}) copy-start(f32[192,1]{0,1:T(1,128)S(1)} %get-tuple-element.171) | copy-start | bytes 2308
  8.5 22.3 %copy-start.38 = (f32[192,1]{0,1:T(1,128)}, f32[192,1]{0,1:T(1,128)S(1)}, u32[]{:S(2)}) copy-start(f32[192,1]{0,1:T(1,128)S(1)} %get-tuple-element.172) | copy-start | bytes 2308
  8.5 22.3 %copy-start.40 = (f32[192,1]{0,1:T(1,128)}, f32[192,1]{0,1:T(1,128)S(1)}, u32[]{:S(2)}) copy-start(f32[192,1]{0,1:T(1,128)S(1)} %get-tuple-element.173) | copy-start | bytes 2308
  8.5 22.3 %copy-start.42 = (f32[192,1]{0,1:T(1,128)}, f32[192,1]{0,1:T(1,128)S(1)}, u32[]{:S(2)}) copy-start(f32[192,1]{0,1:T(1,128)S(1)} %get-tuple-element.174) | copy-start | bytes 2308
  8.5 22.3 %copy-start.44 = (f32[192,1]{0,1:T(1,128)}, f32[192,1]{0,1:T(1,128)S(1)}, u32[]{:S(2)}) copy-start(f32[192,1]{0,1:T(1,128)S(1)} %get-tuple-element.175) | copy-start | bytes 2308
  8.5 22.3 %copy-start.46 = (f32[192,1]{0,1:T(1,128)}, f32[192,1]{0,1:T(1,128)S(1)}, u32[]{:S(2)}) copy-start(f32[192,1]{0,1:T(1,128)S(1)} %get-tuple-element.176) | copy-start | bytes 2308
  9.2 21.6 %copy-start.48 = (f32[192,1]{0,1:T(1,128)}, f32[192,1]{0,1:T(1,128)S(1)}, u32[]{:S(2)}) copy-start(f32[192,1]{0,1:T(1,128)S(1)} %get-tuple-element.177) | copy-start | bytes 2308
  9.2 21.6 %copy-start.50 = (f32[192,1]{0,1:T(1,128)}, f32[192,1]{0,1:T(1,128)S(1)}, u32[]{:S(2)}) copy-start(f32[192,1]{0,1:T(1,128)S(1)} %get-tuple-element.178) | copy-start | bytes 2308
  9.2 21.6 %copy-start.52 = (f32[192,1]{0,1:T(1,128)}, f32[192,1]{0,1:T(1,128)S(1)}, u32[]{:S(2)}) copy-start(f32[192,1]{0,1:T(1,128)S(1)} %get-tuple-element.179) | copy-start | bytes 2308
  9.2 21.6 %copy-start.54 = (f32[192,1]{0,1:T(1,128)}, f32[192,1]{0,1:T(1,128)S(1)}, u32[]{:S(2)}) copy-start(f32[192,1]{0,1:T(1,128)S(1)} %get-tuple-element.180) | copy-start | bytes 2308
  9.2 21.6 %copy-start.56 = (f32[192,1]{0,1:T(1,128)}, f32[192,1]{0,1:T(1,128)S(1)}, u32[]{:S(2)}) copy-start(f32[192,1]{0,1:T(1,128)S(1)} %get-tuple-element.181) | copy-start | bytes 2308
  9.2 21.6 %copy-start.58 = (f32[192,1]{0,1:T(1,128)}, f32[192,1]{0,1:T(1,128)S(1)}, u32[]{:S(2)}) copy-start(f32[192,1]{0,1:T(1,128)S(1)} %get-tuple-element.182) | copy-start | bytes 2308
  12.9 18.0 %copy-start.4 = (bf16[192,3,128]{2,0,1:T(8,128)(2,1)}, bf16[192,3,128]{2,0,1:T(8,128)(2,1)S(1)}, u32[]{:S(2)}) copy-start(bf16[192,3,128]{2,0,1:T(8,128)(2,1)S(1)} %collective-permute-done.1) | copy-start | bytes 442372
  15.6 6.6 %collective-permute-start.2 = (bf16[192,14,3]{0,1,2:T(8,128)(2,1)S(1)}, bf16[192,14,3]{0,1,2:T(8,128)(2,1)S(1)}, u32[]{:S(2)}, u32[]{:S(2)}) collective-permute-start(bf16[192,14,3]{0,1,2:T(8,128)(2,1)S(1)} %copy.57), channel_id=1, source_target_pairs={{0,1},{1,2},{2,3},{3,4},{4,5},{5,6},{6,7},{8,9},{9,10},{10,11},{11... | collective-permute-start | bytes 48392 | tf_op jit(solution)/shard_map/ppermute | solution.py:20
  20.8 6.1 %collective-permute-start.3 = (bf16[192,14,3]{0,1,2:T(8,128)(2,1)S(1)}, bf16[192,14,3]{0,1,2:T(8,128)(2,1)S(1)}, u32[]{:S(2)}, u32[]{:S(2)}) collective-permute-start(bf16[192,14,3]{0,1,2:T(8,128)(2,1)S(1)} %copy.59), channel_id=1, source_target_pairs={{1,0},{2,1},{3,2},{4,3},{5,4},{6,5},{7,6},{9,8},{10,9},{11,10},{12... | collective-permute-start | bytes 48392 | tf_op jit(solution)/shard_map/ppermute | solution.py:21
  80.1 9.9 %copy-start.107 = (f32[16]{0:T(128)S(1)}, f32[16]{0:T(128)}, u32[]{:S(2)}) copy-start(f32[16]{0:T(128)} %get-tuple-element.129) | copy-start | bytes 196
  93.7 2.5 %collective-permute-start.8 = (f32[1664,128]{1,0:T(8,128)S(1)}, f32[1664,128]{1,0:T(8,128)S(1)}, u32[]{:S(2)}, u32[]{:S(2)}) collective-permute-start(f32[1664,128]{1,0:T(8,128)S(1)} %dynamic-slice_bitcast_fusion), channel_id=1, source_target_pairs={{0,8},{1,9},{2,10},{3,11},{4,12},{5,13},{6,14},{7,15},{8,0},{9,1},... | collective-permute-start | bytes 2555912 | tf_op jit(solution)/shard_map/ppermute | solution.py:187
  97.4 11.3 %collective-permute-start.9 = (f32[832,128]{1,0:T(8,128)S(1)}, f32[832,128]{1,0:T(8,128)S(1)}, u32[]{:S(2)}, u32[]{:S(2)}) collective-permute-start(f32[832,128]{1,0:T(8,128)S(1)} %dynamic-slice_bitcast_fusion.1), channel_id=1, source_target_pairs={{0,64},{1,65},{2,66},{3,67},{4,68},{5,69},{6,70},{7,71},{8,72},{9,... | collective-permute-start | bytes 1277960 | tf_op jit(solution)/shard_map/ppermute | solution.py:187
  108.8 6.2 %collective-permute-start.10 = (f32[416,128]{1,0:T(8,128)S(1)}, f32[416,128]{1,0:T(8,128)S(1)}, u32[]{:S(2)}, u32[]{:S(2)}) collective-permute-start(f32[416,128]{1,0:T(8,128)S(1)} %dynamic-slice_bitcast_fusion.2), channel_id=1, source_target_pairs={{0,2},{1,3},{2,0},{3,1},{4,6},{5,7},{6,4},{7,5},{8,10},{9,11},{10,... | collective-permute-start | bytes 638984 | tf_op jit(solution)/shard_map/ppermute | solution.py:187
  115.1 5.4 %collective-permute-start.11 = (f32[208,128]{1,0:T(8,128)S(1)}, f32[208,128]{1,0:T(8,128)S(1)}, u32[]{:S(2)}, u32[]{:S(2)}) collective-permute-start(f32[208,128]{1,0:T(8,128)S(1)} %dynamic-slice_bitcast_fusion.3), channel_id=1, source_target_pairs={{0,4},{1,5},{2,6},{3,7},{4,0},{5,1},{6,2},{7,3},{8,12},{9,13},{10,... | collective-permute-start | bytes 319496 | tf_op jit(solution)/shard_map/ppermute | solution.py:187
  120.6 4.6 %collective-permute-start.12 = (f32[104,128]{1,0:T(8,128)S(1)}, f32[104,128]{1,0:T(8,128)S(1)}, u32[]{:S(2)}, u32[]{:S(2)}) collective-permute-start(f32[104,128]{1,0:T(8,128)S(1)} %dynamic-slice_bitcast_fusion.4), channel_id=1, source_target_pairs={{0,1},{1,0},{2,3},{3,2},{4,5},{5,4},{6,7},{7,6},{8,9},{9,8},{10,11... | collective-permute-start | bytes 159752 | tf_op jit(solution)/shard_map/ppermute | solution.py:187
  125.3 3.1 %collective-permute-start.13 = (f32[52,128]{1,0:T(8,128)S(1)}, f32[52,128]{1,0:T(8,128)S(1)}, u32[]{:S(2)}, u32[]{:S(2)}) collective-permute-start(f32[52,128]{1,0:T(8,128)S(1)} %dynamic-slice_bitcast_fusion.5), channel_id=1, source_target_pairs={{0,16},{1,17},{2,18},{3,19},{4,20},{5,21},{6,22},{7,23},{8,24},{9,... | collective-permute-start | bytes 79880 | tf_op jit(solution)/shard_map/ppermute | solution.py:187
  128.4 4.2 %collective-permute-start.14 = (f32[26,128]{1,0:T(8,128)S(1)}, f32[26,128]{1,0:T(8,128)S(1)}, u32[]{:S(2)}, u32[]{:S(2)}) collective-permute-start(f32[26,128]{1,0:T(8,128)S(1)} %dynamic-slice_bitcast_fusion.6), channel_id=1, source_target_pairs={{0,32},{1,33},{2,34},{3,35},{4,36},{5,37},{6,38},{7,39},{8,40},{9,... | collective-permute-start | bytes 39944 | tf_op jit(solution)/shard_map/ppermute | solution.py:187
  132.6 12.6 %collective-permute-start.15 = (f32[26,128]{1,0:T(8,128)S(1)}, f32[26,128]{1,0:T(8,128)S(1)}, u32[]{:S(2)}, u32[]{:S(2)}) collective-permute-start(f32[26,128]{1,0:T(8,128)S(1)} %get-tuple-element.128), channel_id=1, source_target_pairs={{0,32},{1,33},{2,34},{3,35},{4,36},{5,37},{6,38},{7,39},{8,40},{9,... | collective-permute-start | bytes 39944 | tf_op jit(solution)/shard_map/ppermute | solution.py:191
  135.1 24.1 %collective-permute-start.4 = (bf16[192,3,128]{2,0,1:T(8,128)(2,1)S(1)}, bf16[192,3,128]{2,0,1:T(8,128)(2,1)S(1)}, u32[]{:S(2)}, u32[]{:S(2)}) collective-permute-start(bf16[192,3,128]{2,0,1:T(8,128)(2,1)S(1)} %get-tuple-element.155), channel_id=1, source_target_pairs={{0,8},{8,16},{16,24},{24,32},{32,40},{40,48},{48,56},{1,9},{9,17},... | collective-permute-start | bytes 442376 | tf_op jit(solution)/shard_map/ppermute | solution.py:20
  143.2 16.0 %collective-permute-start.5 = (bf16[192,3,128]{2,0,1:T(8,128)(2,1)S(1)}, bf16[192,3,128]{2,0,1:T(8,128)(2,1)S(1)}, u32[]{:S(2)}, u32[]{:S(2)}) collective-permute-start(bf16[192,3,128]{2,0,1:T(8,128)(2,1)S(1)} %get-tuple-element.154), channel_id=1, source_target_pairs={{8,0},{16,8},{24,16},{32,24},{40,32},{48,40},{56,48},{9,1},{17,9},... | collective-permute-start | bytes 442376 | tf_op jit(solution)/shard_map/ppermute | solution.py:21
  145.2 2.8 %collective-permute-start.16 = (f32[52,128]{1,0:T(8,128)S(1)}, f32[52,128]{1,0:T(8,128)S(1)}, u32[]{:S(2)}, u32[]{:S(2)}) collective-permute-start(f32[52,128]{1,0:T(8,128)S(1)} %reshape.286), channel_id=1, source_target_pairs={{0,16},{1,17},{2,18},{3,19},{4,20},{5,21},{6,22},{7,23},{8,24},{9,... | collective-permute-start | bytes 79880 | tf_op jit(solution)/shard_map/ppermute | solution.py:191
  148.0 4.6 %collective-permute-start.17 = (f32[104,128]{1,0:T(8,128)S(1)}, f32[104,128]{1,0:T(8,128)S(1)}, u32[]{:S(2)}, u32[]{:S(2)}) collective-permute-start(f32[104,128]{1,0:T(8,128)S(1)} %reshape.287), channel_id=1, source_target_pairs={{0,1},{1,0},{2,3},{3,2},{4,5},{5,4},{6,7},{7,6},{8,9},{9,8},{10,11... | collective-permute-start | bytes 159752 | tf_op jit(solution)/shard_map/ppermute | solution.py:191
  152.6 5.4 %collective-permute-start.18 = (f32[208,128]{1,0:T(8,128)S(1)}, f32[208,128]{1,0:T(8,128)S(1)}, u32[]{:S(2)}, u32[]{:S(2)}) collective-permute-start(f32[208,128]{1,0:T(8,128)S(1)} %bitcast.356), channel_id=1, source_target_pairs={{0,4},{1,5},{2,6},{3,7},{4,0},{5,1},{6,2},{7,3},{8,12},{9,13},{10,... | collective-permute-start | bytes 319496 | tf_op jit(solution)/shard_map/ppermute | solution.py:191
  158.0 5.5 %collective-permute-start.19 = (f32[416,128]{1,0:T(8,128)S(1)}, f32[416,128]{1,0:T(8,128)S(1)}, u32[]{:S(2)}, u32[]{:S(2)}) collective-permute-start(f32[416,128]{1,0:T(8,128)S(1)} %bitcast.352), channel_id=1, source_target_pairs={{0,2},{1,3},{2,0},{3,1},{4,6},{5,7},{6,4},{7,5},{8,10},{9,11},{10,... | collective-permute-start | bytes 638984 | tf_op jit(solution)/shard_map/ppermute | solution.py:191
  164.3 13.9 %collective-permute-start.20 = (f32[832,128]{1,0:T(8,128)}, f32[832,128]{1,0:T(8,128)}, u32[]{:S(2)}, u32[]{:S(2)}) collective-permute-start(f32[832,128]{1,0:T(8,128)} %bitcast.158), channel_id=1, source_target_pairs={{0,64},{1,65},{2,66},{3,67},{4,68},{5,69},{6,70},{7,71},{8,72},{9,... | collective-permute-start | bytes 1277960 | tf_op jit(solution)/shard_map/ppermute | solution.py:191
  165.4 9.2 %collective-permute-start.6 = (bf16[192,14,3]{0,1,2:T(8,128)(2,1)S(1)}, bf16[192,14,3]{0,1,2:T(8,128)(2,1)S(1)}, u32[]{:S(2)}, u32[]{:S(2)}) collective-permute-start(bf16[192,14,3]{0,1,2:T(8,128)(2,1)S(1)} %copy.65), channel_id=1, source_target_pairs={{1,0},{2,1},{3,2},{4,3},{5,4},{6,5},{7,6},{9,8},{10,9},{11,10},{12... | collective-permute-start | bytes 48392 | tf_op jit(solution)/shard_map/ppermute | solution.py:21
  167.0 7.9 %collective-permute-start.7 = (bf16[192,14,3]{0,1,2:T(8,128)(2,1)S(1)}, bf16[192,14,3]{0,1,2:T(8,128)(2,1)S(1)}, u32[]{:S(2)}, u32[]{:S(2)}) collective-permute-start(bf16[192,14,3]{0,1,2:T(8,128)(2,1)S(1)} %copy.67), channel_id=1, source_target_pairs={{0,1},{1,2},{2,3},{3,4},{4,5},{5,6},{6,7},{8,9},{9,10},{10,11},{11... | collective-permute-start | bytes 48392 | tf_op jit(solution)/shard_map/ppermute | solution.py:20
  179.2 18.1 %collective-permute-start.21 = (f32[1664,128]{1,0:T(8,128)S(1)}, f32[1664,128]{1,0:T(8,128)S(1)}, u32[]{:S(2)}, u32[]{:S(2)}) collective-permute-start(f32[1664,128]{1,0:T(8,128)S(1)} %bitcast.342), channel_id=1, source_target_pairs={{0,8},{1,9},{2,10},{3,11},{4,12},{5,13},{6,14},{7,15},{8,0},{9,1},... | collective-permute-start | bytes 2555912 | tf_op jit(solution)/shard_map/ppermute | solution.py:191
  (87 other events, 572.7 us)

commit v2 on v1

--- a/solution.py
+++ b/solution.py
@@ -175,23 +175,45 @@
     return out
 
 
-def butterfly_psum(buffer, axes, order):
+def spread(value, bits):
+    out = 0
+    for k, bit_at in enumerate(bits):
+        if (value >> k) & 1:
+            out |= 1 << bit_at
+    return out
+
+
+def butterfly_psum(buffer, axes, stages, scale_of):
     index = lax.axis_index(axes)
     count = math.prod(lax.axis_size(a) for a in axes)
-    for bit_at in order:
-        bit = (index >> bit_at) & 1
-        halves = buffer.reshape(2, buffer.shape[0] // 2, buffer.shape[1])
-        keep = lax.dynamic_index_in_dim(halves, bit, 0, keepdims=False)
-        send = lax.dynamic_index_in_dim(halves, 1 - bit, 0, keepdims=False)
-        pairs = [(i, i ^ (1 << bit_at)) for i in range(count)]
-        buffer = keep + lax.ppermute(send, axes, pairs)
-    for bit_at in reversed(order):
-        bit = (index >> bit_at) & 1
-        pairs = [(i, i ^ (1 << bit_at)) for i in range(count)]
-        other = lax.ppermute(buffer, axes, pairs)
-        both = jnp.zeros((2,) + buffer.shape, buffer.dtype)
-        both = lax.dynamic_update_index_in_dim(both, buffer, bit, 0)
-        both = lax.dynamic_update_index_in_dim(both, other, 1 - bit, 0)
+    offset = jnp.zeros((), jnp.int32)
+    places = []
+    for bits in stages:
+        ways = 1 << len(bits)
+        mine = sum(((index >> bit_at) & 1) << k for k, bit_at in enumerate(bits))
+        pieces = buffer.reshape(ways, buffer.shape[0] // ways, buffer.shape[1])
+        total = lax.dynamic_index_in_dim(pieces, mine, 0, keepdims=False)
+        for step in range(1, ways):
+            flip = spread(step, bits)
+            pairs = [(i, i ^ flip) for i in range(count)]
+            send = lax.dynamic_index_in_dim(pieces, mine ^ step, 0, keepdims=False)
+            total = total + lax.ppermute(send, axes, pairs)
+        offset = offset * ways + mine
+        places.append((bits, mine))
+        buffer = total
+    rows = buffer.shape[0]
+    position = (offset * rows + lax.broadcasted_iota(jnp.int32, buffer.shape, 0)) * buffer.shape[1]
+    position = position + lax.broadcasted_iota(jnp.int32, buffer.shape, 1)
+    buffer = buffer * scale_of(position)
+    for bits, mine in reversed(places):
+        ways = 1 << len(bits)
+        both = jnp.zeros((ways,) + buffer.shape, buffer.dtype)
+        both = lax.dynamic_update_index_in_dim(both, buffer, mine, 0)
+        for step in range(1, ways):
+            flip = spread(step, bits)
+            pairs = [(i, i ^ flip) for i in range(count)]
+            other = lax.ppermute(buffer, axes, pairs)
+            both = lax.dynamic_update_index_in_dim(both, other, mine ^ step, 0)
         buffer = both.reshape(-1, buffer.shape[1])
     return buffer
 
@@ -231,11 +253,51 @@
     d_conv, enc_grads = encoder_backward(saved, returned, enc_params)
     d_padded = rimmed(d_conv)
     d_input, kernel_grad, convbias_grad = conv_backward(padded, d_conv, d_padded, returned, dw_weight)
-    parts = [kernel_grad, convbias_grad] + list(enc_grads) + list(dec_grads) + [loss_sum]
+    (
+        gain_grad,
+        normbias_grad,
+        expand_grad,
+        expbias_grad,
+        project_grad,
+        projbias_grad,
+        layerscale_grad,
+    ) = enc_grads
+    lateral_grad, latbias_grad, classify_grad, clsbias_grad = dec_grads
+    vectors = [convbias_grad, gain_grad, normbias_grad, expbias_grad, projbias_grad]
+    vectors += [layerscale_grad, latbias_grad, clsbias_grad, loss_sum.reshape(1)]
+    joined = jnp.concatenate(vectors)
+    parts = [joined, kernel_grad, expand_grad, project_grad, lateral_grad, classify_grad]
     count = math.prod(lax.axis_size(a) for a in axes)
     buffer, shapes = pack_rows(parts, count * 2)
-    buffer = butterfly_psum(buffer, axes, [3, 6, 1, 2, 0, 4, 5])
+    buffer, d_padded = lax.optimization_barrier((buffer, d_padded))
+    d_input, _, _ = conv_backward(padded, d_conv, d_padded, returned, dw_weight)
+    cell_count = micro_count * height * width * lax.axis_size("row") * lax.axis_size("col")
+    grad_scale = 1.0 / math.sqrt(cell_count)
+    loss_at = joined.shape[0] - 1
+
+    def scale_of(position):
+        return jnp.where(position == loss_at, 1.0 / cell_count, grad_scale).astype(jnp.float32)
+
+    buffer = butterfly_psum(buffer, axes, [(3,), (6, 0), (1, 2), (4, 5)], scale_of)
+    joined, kernel_grad, expand_grad, project_grad, lateral_grad, classify_grad = unpack_rows(
+        buffer, shapes
+    )
+    sizes = [v.shape[0] for v in vectors]
+    cuts = [sum(sizes[:k]) for k in range(len(sizes) + 1)]
     (
+        convbias_grad,
+        gain_grad,
+        normbias_grad,
+        expbias_grad,
+        projbias_grad,
+        layerscale_grad,
+        latbias_grad,
+        clsbias_grad,
+        loss_total,
+    ) = [joined[cuts[k] : cuts[k + 1]] for k in range(len(sizes))]
+    return (
+        d_input[None],
+        loss_total[0],
         kernel_grad,
         convbias_grad,
         gain_grad,
@@ -249,26 +311,6 @@
         latbias_grad,
         classify_grad,
         clsbias_grad,
-        loss_total,
-    ) = unpack_rows(buffer, shapes)
-    cell_count = micro_count * height * width * lax.axis_size("row") * lax.axis_size("col")
-    grad_scale = 1.0 / math.sqrt(cell_count)
-    return (
-        d_input[None],
-        loss_total / cell_count,
-        kernel_grad * grad_scale,
-        convbias_grad * grad_scale,
-        gain_grad * grad_scale,
-        normbias_grad * grad_scale,
-        expand_grad * grad_scale,
-        expbias_grad * grad_scale,
-        project_grad * grad_scale,
-        projbias_grad * grad_scale,
-        layerscale_grad * grad_scale,
-        lateral_grad * grad_scale,
-        latbias_grad * grad_scale,
-        classify_grad * grad_scale,
-        clsbias_grad * grad_scale,
     )
 
 

time: 213 us -> 181 us (0.85); the launches traced: 209 us -> 180 us
  local copies, waits for them, and re-layouts: 44.3 us -> 31.6 us
  other arithmetic: 43 us -> 35.6 us
  waiting for transfers between devices: 41.8 us -> 34.5 us
  starting transfers between devices: 59.9 us -> 62.9 us
  matrix products: 15.6 us -> 13.3 us
    unnamed x244 -> x198, local copies, waits for them, and re-layouts: 17.5 us -> 9.86 us
    ppermute x7 -> x10, waiting for transfers between devices: 25.1 us -> 19.7 us  [butterfly_psum(): total = total + lax.ppermute(send, axes, pairs)]
    ppermute x4, starting transfers between devices: 23.9 us -> 19 us  [padded_2(): before = lax.ppermute(last, axis, up)]
    mul x12 -> x1, other arithmetic: 4.66 us -> 0.01 us  [butterfly_psum(): (offset * rows + lax.broadcasted_iota(jnp.int32, buffer.shape, 0)) * buff...]
    ppermute x7 -> x10, starting transfers between devices: 17.3 us -> 21.1 us  [butterfly_psum(): other = lax.ppermute(buffer, axes, pairs)]
    dynamic_update_slice x13, local copies, waits for them, and re-layouts: 3.67 us -> 0.25 us  [the longest x10 0.15 us: butterfly_psum(): both = lax.dynamic_update_index_in_dim(both, other, mine ^ step, 0)]
    ppermute x4, waiting for transfers between devices: 7.64 us -> 4.33 us  [padded_2(): after = lax.ppermute(leading, axis, down)]
    slice x0 -> x5, local copies, waits for them, and re-layouts: none -> 3.12 us  [shards(): joined[cuts[k]:cuts[k + 1]]]
  transfers between devices with their start and end apart: 22 -> 28, of which waited for: 14 -> 16; matrix products, arithmetic and copies ran while one was open for 9% -> 10% of each run, Pallas kernels for 0% -> 0%
where the time goes in v2:
time: 181 us; the launch traced here: 180 us
  starting transfers between devices  62.9 us (35%)
  other arithmetic  35.6 us (20%)
  waiting for transfers between devices  34.5 us (19%)
  local copies, waits for them, and re-layouts  31.6 us (17%)
  matrix products  13.3 us (7%)
  between operations  2.5 us (1%)
    ppermute x10, starting transfers between devices, butterfly_psum(): other = lax.ppermute(buffer, axes, pairs)  21.1 us
    ppermute x10, waiting for transfers between devices, butterfly_psum(): total = total + lax.ppermute(send, axes, pairs)  19.7 us
    ppermute x4, starting transfers between devices, padded_2(): before = lax.ppermute(last, axis, up)  19 us
    ppermute x10, starting transfers between devices, butterfly_psum(): total = total + lax.ppermute(send, axes, pairs)  14.6 us
    dot_general x12, matrix products, product(): jnp.einsum(form, left_side, right_side, preferred_element_type=jnp.float32)  13.3 us
    reduce_sum x4, other arithmetic, conv_backward(): columns.append(jnp.sum(window * conv_float, axis=(1, 2)))  10.9 us
    ppermute x10, waiting for transfers between devices, butterfly_psum(): other = lax.ppermute(buffer, axes, pairs)  9.93 us
    unnamed x198, local copies, waits for them, and re-layouts  9.86 us
  transfers between devices with their start and end apart: 28, of which 16 were waited for; matrix products, arithmetic and copies ran while one was open for 10% of the time, Pallas kernels for 0%

profile of v2, /device:TPU:1, one launch (start us, length us, event | category | flops | bytes accessed | tf_op | source)
XLA Modules:
  0.0 180.4 jit_solution(9945022196432117127)
XLA Ops:
  0.7 1.1 copy-done
  1.9 3.3 %collective-permute-start.1 = (bf16[192,3,128]{2,0,1:T(8,128)(2,1)S(1)}, bf16[192,3,128]{2,0,1:T(8,128)(2,1)S(1)}, u32[]{:S(2)}, u32[]{:S(2)}) collective-permute-start(bf16[192,3,128]{2,0,1:T(8,128)(2,1)S(1)} %get-tuple-element.149), channel_id=1, source_target_pairs={{8,0},{16,8},{24,16},{32,24},{40,32},{48,40},{56,48},{9,1},{17,9},... | collective-permute-start | bytes 442376 | tf_op jit(solution)/shard_map/ppermute | solution.py:21
  5.2 3.1 %collective-permute-start = (bf16[192,3,128]{2,0,1:T(8,128)(2,1)S(1)}, bf16[192,3,128]{2,0,1:T(8,128)(2,1)S(1)}, u32[]{:S(2)}, u32[]{:S(2)}) collective-permute-start(bf16[192,3,128]{2,0,1:T(8,128)(2,1)S(1)} %get-tuple-element.148), channel_id=1, source_target_pairs={{0,8},{8,16},{16,24},{24,32},{32,40},{40,48},{48,56},{1,9},{9,17},... | collective-permute-start | bytes 442376 | tf_op jit(solution)/shard_map/ppermute | solution.py:20
  11.2 4.8 %collective-permute-start.2 = (bf16[192,14,3]{0,1,2:T(8,128)(2,1)S(1)}, bf16[192,14,3]{0,1,2:T(8,128)(2,1)S(1)}, u32[]{:S(2)}, u32[]{:S(2)}) collective-permute-start(bf16[192,14,3]{0,1,2:T(8,128)(2,1)S(1)} %copy.57), channel_id=1, source_target_pairs={{0,1},{1,2},{2,3},{3,4},{4,5},{5,6},{6,7},{8,9},{9,10},{10,11},{11... | collective-permute-start | bytes 48392 | tf_op jit(solution)/shard_map/ppermute | solution.py:20
  16.4 1.3 collective-permute-start.3
  18.2 4.3 %collective-permute-done.3 = bf16[192,14,3]{0,1,2:T(8,128)(2,1)S(1)} collective-permute-done((bf16[192,14,3]{0,1,2:T(8,128)(2,1)S(1)}, bf16[192,14,3]{0,1,2:T(8,128)(2,1)S(1)}, u32[]{:S(2)}, u32[]{:S(2)}) %collective-permute-start.3) | collective-permute-done | bytes 16160 | tf_op jit(solution)/shard_map/ppermute | solution.py:21
  23.1 1.3 maximum_maximum_fusion
  24.9 8.3 %fusion.150 = (f32[8,128]{1,0:T(8,128)S(1)}, f32[192,8,128]{2,0,1:T(8,128)S(1)}) fusion(f32[192]{0:T(256)S(1)} %copy-done.91, bf16[192,14,131]{2,0,1:T(8,128)(2,1)S(1)} %get-tuple-element.143, f32[192]{0:T(256)S(1)} %bitcast.427, f32[192]{0:T(256)S(1)} %bitcast.429, f32[192]{0:T(256)S(1)} %bitcast.334, bf16[192,3,128]{2,0,1:T(8,128)(2,1)S(1)} %collective-permute-done.1, ...), kind=kLoop, calls=%fused_computation.342 | loop fusion | flops 30276608 | bytes 18032128 | tf_op jit(solution)/shard_map/reduce_sum | solution.py:64
  36.6 1.3 convert_reduce_fusion.2
  37.9 1.4 convert_reduce_fusion.3
  39.3 1.8 convert_reduce_fusion.1
  42.0 1.3 fusion.120
  43.3 4.3 %fusion.121 = (f32[192]{0:T(256)S(1)}, f32[192]{0:T(256)S(1)}, f32[192]{0:T(256)}, f32[192]{0:T(256)}, f32[192]{0:T(256)}, /*index=5*/f32[192]{0:T(256)}, f32[19...) fusion(bf16[192,8,128]{2,0,1:T(8,128)(2,1)S(1)} %get-tuple-elem, ...), kind=kLoop, calls=%fused_computation.243 | loop fusion | flops 11006400 | bytes 7485696 | tf_op jit(solution)/shard_map/reduce_sum | solution.py:121
  47.7 4.0 %fusion.117 = (f32[192]{0:T(256)}, f32[192]{0:T(256)}, f32[192]{0:T(256)}, f32[192]{0:T(256)}, f32[192]{0:T(256)}, /*index=5*/f32[192]{0:T(256)}, f32[192]{0:T(2...) fusion(bf16[192,8,128]{2,0,1:T(8,128)(2,1)S(1)} %get-tuple-elem, ...), kind=kLoop, calls=%fused_computation.239 | loop fusion | flops 10809984 | bytes 7484928 | tf_op jit(solution)/shard_map/reduce_sum | solution.py:121
  51.7 1.4 convolution_bitcast_fusion.1
  53.1 1.5 convolution_bitcast_fusion
  54.6 1.1 convolution_bitcast_fusion.2
  55.7 1.2 convolution_bitcast_fusion.3
  59.7 1.2 fusion.118
  60.9 4.4 %stack.199 = f32[192,49]{0,1:T(8,128)S(1)} concatenate(f32[192,1]{0,1:T(1,128)} %bitcast.456, f32[192,1]{0,1:T(1,128)} %bitcast.457, f32[192,1]{0,1:T(1,128)} %bitcast.458, f32[192,1]{0,1:T(1,128)} %bitcast.477, f32[192,1]{0,1:T(1,128)S(1)} %bitcast.438, f32[192,1]{0,1:T(1,128)} %bitcast.439, f32[192,1]{0,1:T(1,128)} %bitcast.440, f32[192,1]{0,1:T(1,128)} %bitcast.459, ...), dimensions={1} | concatenate | bytes 75264 | tf_op jit(solution)/shard_map/stack | solution.py:122
  66.5 1.2 reshape.186
  67.7 2.4 %collective-permute-start.5 = (bf16[192,3,128]{2,0,1:T(8,128)(2,1)}, bf16[192,3,128]{2,0,1:T(8,128)(2,1)S(1)}, u32[]{:S(2)}, u32[]{:S(2)}) collective-permute-start(bf16[192,3,128]{2,0,1:T(8,128)(2,1)} %get-tuple-element.147), channel_id=1, source_target_pairs={{8,0},{16,8},{24,16},{32,24},{40,32},{48,40},{56,48},{9,1},{17,9},... | collective-permute-start | bytes 442376 | tf_op jit(solution)/shard_map/ppermute | solution.py:21
  70.1 5.5 %collective-permute-start.4 = (bf16[192,3,128]{2,0,1:T(8,128)(2,1)}, bf16[192,3,128]{2,0,1:T(8,128)(2,1)S(1)}, u32[]{:S(2)}, u32[]{:S(2)}) collective-permute-start(bf16[192,3,128]{2,0,1:T(8,128)(2,1)} %get-tuple-element.146), channel_id=1, source_target_pairs={{0,8},{8,16},{16,24},{24,32},{32,40},{40,48},{48,56},{1,9},{9,17},... | collective-permute-start | bytes 442376 | tf_op jit(solution)/shard_map/ppermute | solution.py:20
  80.3 1.3 collective-permute-start.7
  82.0 5.5 %collective-permute-start.6 = (bf16[192,14,3]{0,1,2:T(8,128)(2,1)S(1)}, bf16[192,14,3]{0,1,2:T(8,128)(2,1)S(1)}, u32[]{:S(2)}, u32[]{:S(2)}) collective-permute-start(bf16[192,14,3]{0,1,2:T(8,128)(2,1)S(1)} %copy.72), channel_id=1, source_target_pairs={{0,1},{1,2},{2,3},{3,4},{4,5},{5,6},{6,7},{8,9},{9,10},{10,11},{11... | collective-permute-start | bytes 48392 | tf_op jit(solution)/shard_map/ppermute | solution.py:20
  88.5 1.2 copy.74
  89.7 2.0 %pad_maximum_fusion.1 = bf16[192,14,134]{2,0,1:T(8,128)(2,1)S(1)} fusion(bf16[192,14,3]{2,0,1:T(8,128)(2,1)S(1)} %copy.75, bf16[192,3,128]{2,0,1:T(8,128)(2,1)S(1)} %collective-permute-done.5, bf16[192,8,128]{2,0,1:T(8,128)(2,1)S(1)} %get-tuple-element.127, bf16[192,3,128]{2,0,1:T(8,128)(2,1)S(1)} %collective-permute-done.4, bf16[192,14,3]{2,0,1:T(8,128)(2,1)} %copy.74), kind=kLoop, calls=%fused_computation.80 | loop fusion | flops 3601920 | bytes 1440768 | tf_op jit(solution)/shard_map/concatenate | solution.py:22
  91.9 2.5 %collective-permute-done.8 = f32[1664,128]{1,0:T(8,128)} collective-permute-done((f32[1664,128]{1,0:T(8,128)S(1)}, f32[1664,128]{1,0:T(8,128)}, u32[]{:S(2)}, u32[]{:S(2)}) %collective-permute-start.8) | collective-permute-done | bytes 852000 | tf_op jit(solution)/shard_map/ppermute | solution.py:200
  94.3 1.5 bitcast_add_fusion
  96.7 3.9 %collective-permute-start.11 = (f32[416,128]{1,0:T(8,128)}, f32[416,128]{1,0:T(8,128)S(1)}, u32[]{:S(2)}, u32[]{:S(2)}) collective-permute-start(f32[416,128]{1,0:T(8,128)} %get-tuple-element.137), channel_id=1, source_target_pairs={{0,65},{1,64},{2,67},{3,66},{4,69},{5,68},{6,71},{7,70},{8,73},{9,... | collective-permute-start | bytes 638984 | tf_op jit(solution)/shard_map/ppermute | solution.py:200
  101.2 9.7 %collective-permute-done.11 = f32[416,128]{1,0:T(8,128)S(1)} collective-permute-done((f32[416,128]{1,0:T(8,128)}, f32[416,128]{1,0:T(8,128)S(1)}, u32[]{:S(2)}, u32[]{:S(2)}) %collective-permute-start.11) | collective-permute-done | bytes 213024 | tf_op jit(solution)/shard_map/ppermute | solution.py:200
  112.4 5.2 %collective-permute-start.14 = (f32[104,128]{1,0:T(8,128)S(1)}, f32[104,128]{1,0:T(8,128)S(1)}, u32[]{:S(2)}, u32[]{:S(2)}) collective-permute-start(f32[104,128]{1,0:T(8,128)S(1)} %get-tuple-element.151), channel_id=1, source_target_pairs={{0,6},{1,7},{2,4},{3,5},{4,2},{5,3},{6,0},{7,1},{8,14},{9,15},{10,... | collective-permute-start | bytes 159752 | tf_op jit(solution)/shard_map/ppermute | solution.py:200
  119.2 2.9 %collective-permute-done.13 = f32[104,128]{1,0:T(8,128)S(1)} collective-permute-done((f32[104,128]{1,0:T(8,128)S(1)}, f32[104,128]{1,0:T(8,128)S(1)}, u32[]{:S(2)}, u32[]{:S(2)}) %collective-permute-start.13) | collective-permute-done | bytes 53280 | tf_op jit(solution)/shard_map/ppermute | solution.py:200
  122.2 3.5 %collective-permute-start.17 = (f32[26,128]{1,0:T(8,128)S(1)}, f32[26,128]{1,0:T(8,128)S(1)}, u32[]{:S(2)}, u32[]{:S(2)}) collective-permute-start(f32[26,128]{1,0:T(8,128)S(1)} %get-tuple-element.154), channel_id=1, source_target_pairs={{0,48},{1,49},{2,50},{3,51},{4,52},{5,53},{6,54},{7,55},{8,56},{9,... | collective-permute-start | bytes 39944 | tf_op jit(solution)/shard_map/ppermute | solution.py:200
  126.8 3.0 %collective-permute-done.16 = f32[26,128]{1,0:T(8,128)S(1)} collective-permute-done((f32[26,128]{1,0:T(8,128)S(1)}, f32[26,128]{1,0:T(8,128)S(1)}, u32[]{:S(2)}, u32[]{:S(2)}) %collective-permute-start.16) | collective-permute-done | bytes 13344 | tf_op jit(solution)/shard_map/ppermute | solution.py:200
  129.9 1.7 collective-permute-start.19
  131.6 2.1 %collective-permute-start.20 = (f32[26,128]{1,0:T(8,128)S(1)}, f32[26,128]{1,0:T(8,128)S(1)}, u32[]{:S(2)}, u32[]{:S(2)}) collective-permute-start(f32[26,128]{1,0:T(8,128)S(1)} %get-tuple-element.126), channel_id=1, source_target_pairs={{0,48},{1,49},{2,50},{3,51},{4,52},{5,53},{6,54},{7,55},{8,56},{9,... | collective-permute-start | bytes 39944 | tf_op jit(solution)/shard_map/ppermute | solution.py:215
  134.1 1.3 collective-permute-done.20
  135.5 2.0 %collective-permute-start.22 = (f32[104,128]{1,0:T(8,128)S(1)}, f32[104,128]{1,0:T(8,128)S(1)}, u32[]{:S(2)}, u32[]{:S(2)}) collective-permute-start(f32[104,128]{1,0:T(8,128)S(1)} %reshape.193), channel_id=1, source_target_pairs={{0,4},{1,5},{2,6},{3,7},{4,0},{5,1},{6,2},{7,3},{8,12},{9,13},{10,... | collective-permute-start | bytes 159752 | tf_op jit(solution)/shard_map/ppermute | solution.py:215
  137.5 1.8 %collective-permute-start.23 = (f32[104,128]{1,0:T(8,128)S(1)}, f32[104,128]{1,0:T(8,128)S(1)}, u32[]{:S(2)}, u32[]{:S(2)}) collective-permute-start(f32[104,128]{1,0:T(8,128)S(1)} %reshape.193), channel_id=1, source_target_pairs={{0,6},{1,7},{2,4},{3,5},{4,2},{5,3},{6,0},{7,1},{8,14},{9,15},{10,... | collective-permute-start | bytes 159752 | tf_op jit(solution)/shard_map/ppermute | solution.py:215
  140.1 1.6 collective-permute-done.23
  141.7 1.4 collective-permute-start.24
  144.1 1.6 collective-permute-start.26
  146.8 2.8 %collective-permute-done.25 = f32[416,128]{1,0:T(8,128)S(1)} collective-permute-done((f32[416,128]{1,0:T(8,128)S(1)}, f32[416,128]{1,0:T(8,128)S(1)}, u32[]{:S(2)}, u32[]{:S(2)}) %collective-permute-start.25) | collective-permute-done | bytes 213024 | tf_op jit(solution)/shard_map/ppermute | solution.py:215
  149.6 2.2 %collective-permute-done.26 = f32[416,128]{1,0:T(8,128)S(1)} collective-permute-done((f32[416,128]{1,0:T(8,128)S(1)}, f32[416,128]{1,0:T(8,128)S(1)}, u32[]{:S(2)}, u32[]{:S(2)}) %collective-permute-start.26) | collective-permute-done | bytes 213024 | tf_op jit(solution)/shard_map/ppermute | solution.py:215
  151.8 9.4 %collective-permute-start.27 = (f32[1664,128]{1,0:T(8,128)S(1)}, f32[1664,128]{1,0:T(8,128)S(1)}, u32[]{:S(2)}, u32[]{:S(2)}) collective-permute-start(f32[1664,128]{1,0:T(8,128)S(1)} %bitcast.319), channel_id=1, source_target_pairs={{0,8},{1,9},{2,10},{3,11},{4,12},{5,13},{6,14},{7,15},{8,0},{9,1},... | collective-permute-start | bytes 2555912 | tf_op jit(solution)/shard_map/ppermute | solution.py:215
  161.4 9.3 %add_bitcast_fusion = f32[1,192,8,128]{3,1,2,0:T(8,128)S(1)} fusion(f32[192,8,128]{2,0,1:T(8,128)S(1)} %copy-done.1, bf16[192,14,134]{2,0,1:T(8,128)(2,1)S(1)} %pad_maximum_fusion.1, f32[192]{0:T(256)} %bitcast.426, f32[192]{0:T(256)} %bitcast.428, f32[192]{0:T(256)S(1)} %bitcast.335, f32[192]{0:T(256)S(1)} %bitcast.337, f32[192]{0:T(256)S(1)} %bitcast.339, ...), kind=kLoop, calls=%fused_computation.247 | loop fusion | flops 28901376 | bytes 20878080 | tf_op jit(solution)/shard_map/broadcast_in_dim | solution.py:299
  170.8 1.3 copy.76
  (307 shorter events, 35.7 us)
Async XLA Ops:
  1.9 8.0 %collective-permute-start.1 = (bf16[192,3,128]{2,0,1:T(8,128)(2,1)S(1)}, bf16[192,3,128]{2,0,1:T(8,128)(2,1)S(1)}, u32[]{:S(2)}, u32[]{:S(2)}) collective-permute-start(bf16[192,3,128]{2,0,1:T(8,128)(2,1)S(1)} %get-tuple-element.149), channel_id=1, source_target_pairs={{8,0},{16,8},{24,16},{32,24},{40,32},{48,40},{56,48},{9,1},{17,9},... | collective-permute-start | bytes 442376 | tf_op jit(solution)/shard_map/ppermute | solution.py:21
  5.2 5.2 %collective-permute-start = (bf16[192,3,128]{2,0,1:T(8,128)(2,1)S(1)}, bf16[192,3,128]{2,0,1:T(8,128)(2,1)S(1)}, u32[]{:S(2)}, u32[]{:S(2)}) collective-permute-start(bf16[192,3,128]{2,0,1:T(8,128)(2,1)S(1)} %get-tuple-element.148), channel_id=1, source_target_pairs={{0,8},{8,16},{16,24},{24,32},{32,40},{40,48},{48,56},{1,9},{9,17},... | collective-permute-start | bytes 442376 | tf_op jit(solution)/shard_map/ppermute | solution.py:20
  11.2 6.6 %collective-permute-start.2 = (bf16[192,14,3]{0,1,2:T(8,128)(2,1)S(1)}, bf16[192,14,3]{0,1,2:T(8,128)(2,1)S(1)}, u32[]{:S(2)}, u32[]{:S(2)}) collective-permute-start(bf16[192,14,3]{0,1,2:T(8,128)(2,1)S(1)} %copy.57), channel_id=1, source_target_pairs={{0,1},{1,2},{2,3},{3,4},{4,5},{5,6},{6,7},{8,9},{9,10},{10,11},{11... | collective-permute-start | bytes 48392 | tf_op jit(solution)/shard_map/ppermute | solution.py:20
  16.4 6.1 %collective-permute-start.3 = (bf16[192,14,3]{0,1,2:T(8,128)(2,1)S(1)}, bf16[192,14,3]{0,1,2:T(8,128)(2,1)S(1)}, u32[]{:S(2)}, u32[]{:S(2)}) collective-permute-start(bf16[192,14,3]{0,1,2:T(8,128)(2,1)S(1)} %copy.59), channel_id=1, source_target_pairs={{1,0},{2,1},{3,2},{4,3},{5,4},{6,5},{7,6},{9,8},{10,9},{11,10},{12... | collective-permute-start | bytes 48392 | tf_op jit(solution)/shard_map/ppermute | solution.py:21
  67.7 11.7 %collective-permute-start.5 = (bf16[192,3,128]{2,0,1:T(8,128)(2,1)}, bf16[192,3,128]{2,0,1:T(8,128)(2,1)S(1)}, u32[]{:S(2)}, u32[]{:S(2)}) collective-permute-start(bf16[192,3,128]{2,0,1:T(8,128)(2,1)} %get-tuple-element.147), channel_id=1, source_target_pairs={{8,0},{16,8},{24,16},{32,24},{40,32},{48,40},{56,48},{9,1},{17,9},... | collective-permute-start | bytes 442376 | tf_op jit(solution)/shard_map/ppermute | solution.py:21
  70.1 9.4 %collective-permute-start.4 = (bf16[192,3,128]{2,0,1:T(8,128)(2,1)}, bf16[192,3,128]{2,0,1:T(8,128)(2,1)S(1)}, u32[]{:S(2)}, u32[]{:S(2)}) collective-permute-start(bf16[192,3,128]{2,0,1:T(8,128)(2,1)} %get-tuple-element.146), channel_id=1, source_target_pairs={{0,8},{8,16},{16,24},{24,32},{32,40},{40,48},{48,56},{1,9},{9,17},... | collective-permute-start | bytes 442376 | tf_op jit(solution)/shard_map/ppermute | solution.py:20
  80.3 7.8 %collective-permute-start.7 = (bf16[192,14,3]{0,1,2:T(8,128)(2,1)S(1)}, bf16[192,14,3]{0,1,2:T(8,128)(2,1)S(1)}, u32[]{:S(2)}, u32[]{:S(2)}) collective-permute-start(bf16[192,14,3]{0,1,2:T(8,128)(2,1)S(1)} %copy.73), channel_id=1, source_target_pairs={{1,0},{2,1},{3,2},{4,3},{5,4},{6,5},{7,6},{9,8},{10,9},{11,10},{12... | collective-permute-start | bytes 48392 | tf_op jit(solution)/shard_map/ppermute | solution.py:21
  82.0 6.5 %collective-permute-start.6 = (bf16[192,14,3]{0,1,2:T(8,128)(2,1)S(1)}, bf16[192,14,3]{0,1,2:T(8,128)(2,1)S(1)}, u32[]{:S(2)}, u32[]{:S(2)}) collective-permute-start(bf16[192,14,3]{0,1,2:T(8,128)(2,1)S(1)} %copy.72), channel_id=1, source_target_pairs={{0,1},{1,2},{2,3},{3,4},{4,5},{5,6},{6,7},{8,9},{9,10},{10,11},{11... | collective-permute-start | bytes 48392 | tf_op jit(solution)/shard_map/ppermute | solution.py:20
  91.8 2.6 %collective-permute-start.8 = (f32[1664,128]{1,0:T(8,128)S(1)}, f32[1664,128]{1,0:T(8,128)}, u32[]{:S(2)}, u32[]{:S(2)}) collective-permute-start(f32[1664,128]{1,0:T(8,128)S(1)} %dynamic-slice_bitcast_fusion), channel_id=1, source_target_pairs={{0,8},{1,9},{2,10},{3,11},{4,12},{5,13},{6,14},{7,15},{8,0},{9,1},... | collective-permute-start | bytes 2555912 | tf_op jit(solution)/shard_map/ppermute | solution.py:200
  96.7 14.2 %collective-permute-start.11 = (f32[416,128]{1,0:T(8,128)}, f32[416,128]{1,0:T(8,128)S(1)}, u32[]{:S(2)}, u32[]{:S(2)}) collective-permute-start(f32[416,128]{1,0:T(8,128)} %get-tuple-element.137), channel_id=1, source_target_pairs={{0,65},{1,64},{2,67},{3,66},{4,69},{5,68},{6,71},{7,70},{8,73},{9,... | collective-permute-start | bytes 638984 | tf_op jit(solution)/shard_map/ppermute | solution.py:200
  100.6 10.3 %collective-permute-start.10 = (f32[416,128]{1,0:T(8,128)}, f32[416,128]{1,0:T(8,128)}, u32[]{:S(2)}, u32[]{:S(2)}) collective-permute-start(f32[416,128]{1,0:T(8,128)} %get-tuple-element.138), channel_id=1, source_target_pairs={{0,1},{1,0},{2,3},{3,2},{4,5},{5,4},{6,7},{7,6},{8,9},{9,8},{10,11... | collective-permute-start | bytes 638984 | tf_op jit(solution)/shard_map/ppermute | solution.py:200
  100.6 10.7 %collective-permute-start.9 = (f32[416,128]{1,0:T(8,128)S(1)}, f32[416,128]{1,0:T(8,128)}, u32[]{:S(2)}, u32[]{:S(2)}) collective-permute-start(f32[416,128]{1,0:T(8,128)S(1)} %get-tuple-element.136), channel_id=1, source_target_pairs={{0,64},{1,65},{2,66},{3,67},{4,68},{5,69},{6,70},{7,71},{8,72},{9,... | collective-permute-start | bytes 638984 | tf_op jit(solution)/shard_map/ppermute | solution.py:200
  112.4 6.7 %collective-permute-start.14 = (f32[104,128]{1,0:T(8,128)S(1)}, f32[104,128]{1,0:T(8,128)S(1)}, u32[]{:S(2)}, u32[]{:S(2)}) collective-permute-start(f32[104,128]{1,0:T(8,128)S(1)} %get-tuple-element.151), channel_id=1, source_target_pairs={{0,6},{1,7},{2,4},{3,5},{4,2},{5,3},{6,0},{7,1},{8,14},{9,15},{10,... | collective-permute-start | bytes 159752 | tf_op jit(solution)/shard_map/ppermute | solution.py:200
  117.6 4.5 %collective-permute-start.13 = (f32[104,128]{1,0:T(8,128)S(1)}, f32[104,128]{1,0:T(8,128)S(1)}, u32[]{:S(2)}, u32[]{:S(2)}) collective-permute-start(f32[104,128]{1,0:T(8,128)S(1)} %get-tuple-element.152), channel_id=1, source_target_pairs={{0,4},{1,5},{2,6},{3,7},{4,0},{5,1},{6,2},{7,3},{8,12},{9,13},{10,... | collective-permute-start | bytes 159752 | tf_op jit(solution)/shard_map/ppermute | solution.py:200
  117.6 4.5 %collective-permute-start.12 = (f32[104,128]{1,0:T(8,128)S(1)}, f32[104,128]{1,0:T(8,128)S(1)}, u32[]{:S(2)}, u32[]{:S(2)}) collective-permute-start(f32[104,128]{1,0:T(8,128)S(1)} %get-tuple-element.150), channel_id=1, source_target_pairs={{0,2},{1,3},{2,0},{3,1},{4,6},{5,7},{6,4},{7,5},{8,10},{9,11},{10,... | collective-permute-start | bytes 159752 | tf_op jit(solution)/shard_map/ppermute | solution.py:200
  118.3 42.9 %copy-start.1 = (f32[192,8,128]{2,0,1:T(8,128)S(1)}, f32[192,8,128]{2,0,1:T(8,128)}, u32[]{:S(2)}) copy-start(f32[192,8,128]{2,0,1:T(8,128)} %get-tuple-element.218) | copy-start | bytes 2359300
  118.3 42.9 %copy-start.18 = (f32[192,1]{0,1:T(1,128)S(1)}, f32[192,1]{0,1:T(1,128)}, u32[]{:S(2)}) copy-start(f32[192,1]{0,1:T(1,128)} %copy-done.17) | copy-start | bytes 2308
  118.3 42.9 %copy-start.20 = (f32[192,1]{0,1:T(1,128)S(1)}, f32[192,1]{0,1:T(1,128)}, u32[]{:S(2)}) copy-start(f32[192,1]{0,1:T(1,128)} %copy-done.19) | copy-start | bytes 2308
  118.3 42.9 %copy-start.22 = (f32[192,1]{0,1:T(1,128)S(1)}, f32[192,1]{0,1:T(1,128)}, u32[]{:S(2)}) copy-start(f32[192,1]{0,1:T(1,128)} %copy-done.21) | copy-start | bytes 2308
  118.3 42.9 %copy-start.24 = (f32[192,1]{0,1:T(1,128)S(1)}, f32[192,1]{0,1:T(1,128)}, u32[]{:S(2)}) copy-start(f32[192,1]{0,1:T(1,128)} %copy-done.23) | copy-start | bytes 2308
  118.3 42.9 %copy-start.26 = (f32[192,1]{0,1:T(1,128)S(1)}, f32[192,1]{0,1:T(1,128)}, u32[]{:S(2)}) copy-start(f32[192,1]{0,1:T(1,128)} %copy-done.25) | copy-start | bytes 2308
  118.3 42.9 %copy-start.28 = (f32[192,1]{0,1:T(1,128)S(1)}, f32[192,1]{0,1:T(1,128)}, u32[]{:S(2)}) copy-start(f32[192,1]{0,1:T(1,128)} %copy-done.27) | copy-start | bytes 2308
  118.3 42.9 %copy-start.30 = (f32[192,1]{0,1:T(1,128)S(1)}, f32[192,1]{0,1:T(1,128)}, u32[]{:S(2)}) copy-start(f32[192,1]{0,1:T(1,128)} %copy-done.29) | copy-start | bytes 2308
  118.3 42.9 %copy-start.32 = (f32[192,1]{0,1:T(1,128)S(1)}, f32[192,1]{0,1:T(1,128)}, u32[]{:S(2)}) copy-start(f32[192,1]{0,1:T(1,128)} %copy-done.31) | copy-start | bytes 2308
  118.3 42.9 %copy-start.34 = (f32[192,1]{0,1:T(1,128)S(1)}, f32[192,1]{0,1:T(1,128)}, u32[]{:S(2)}) copy-start(f32[192,1]{0,1:T(1,128)} %copy-done.33) | copy-start | bytes 2308
  118.3 42.9 %copy-start.36 = (f32[192,1]{0,1:T(1,128)S(1)}, f32[192,1]{0,1:T(1,128)}, u32[]{:S(2)}) copy-start(f32[192,1]{0,1:T(1,128)} %copy-done.35) | copy-start | bytes 2308
  118.4 42.9 %copy-start.38 = (f32[192,1]{0,1:T(1,128)S(1)}, f32[192,1]{0,1:T(1,128)}, u32[]{:S(2)}) copy-start(f32[192,1]{0,1:T(1,128)} %copy-done.37) | copy-start | bytes 2308
  119.1 42.2 %copy-start.48 = (f32[192,1]{0,1:T(1,128)S(1)}, f32[192,1]{0,1:T(1,128)}, u32[]{:S(2)}) copy-start(f32[192,1]{0,1:T(1,128)} %copy-done.47) | copy-start | bytes 2308
  119.2 42.2 %copy-start.50 = (f32[192,1]{0,1:T(1,128)S(1)}, f32[192,1]{0,1:T(1,128)}, u32[]{:S(2)}) copy-start(f32[192,1]{0,1:T(1,128)} %copy-done.49) | copy-start | bytes 2308
  119.2 42.2 %copy-start.52 = (f32[192,1]{0,1:T(1,128)S(1)}, f32[192,1]{0,1:T(1,128)}, u32[]{:S(2)}) copy-start(f32[192,1]{0,1:T(1,128)} %copy-done.51) | copy-start | bytes 2308
  119.2 42.2 %copy-start.54 = (f32[192,1]{0,1:T(1,128)S(1)}, f32[192,1]{0,1:T(1,128)}, u32[]{:S(2)}) copy-start(f32[192,1]{0,1:T(1,128)} %copy-done.53) | copy-start | bytes 2308
  119.2 42.2 %copy-start.56 = (f32[192,1]{0,1:T(1,128)S(1)}, f32[192,1]{0,1:T(1,128)}, u32[]{:S(2)}) copy-start(f32[192,1]{0,1:T(1,128)} %copy-done.55) | copy-start | bytes 2308
  119.2 42.2 %copy-start.58 = (f32[192,1]{0,1:T(1,128)S(1)}, f32[192,1]{0,1:T(1,128)}, u32[]{:S(2)}) copy-start(f32[192,1]{0,1:T(1,128)} %copy-done.57) | copy-start | bytes 2308
  119.2 42.2 %copy-start.60 = (f32[192,1]{0,1:T(1,128)S(1)}, f32[192,1]{0,1:T(1,128)}, u32[]{:S(2)}) copy-start(f32[192,1]{0,1:T(1,128)} %copy-done.59) | copy-start | bytes 2308
  119.2 42.2 %copy-start.62 = (f32[192,1]{0,1:T(1,128)S(1)}, f32[192,1]{0,1:T(1,128)}, u32[]{:S(2)}) copy-start(f32[192,1]{0,1:T(1,128)} %get-tuple-element.182) | copy-start | bytes 2308
  122.2 4.6 %collective-permute-start.17 = (f32[26,128]{1,0:T(8,128)S(1)}, f32[26,128]{1,0:T(8,128)S(1)}, u32[]{:S(2)}, u32[]{:S(2)}) collective-permute-start(f32[26,128]{1,0:T(8,128)S(1)} %get-tuple-element.154), channel_id=1, source_target_pairs={{0,48},{1,49},{2,50},{3,51},{4,52},{5,53},{6,54},{7,55},{8,56},{9,... | collective-permute-start | bytes 39944 | tf_op jit(solution)/shard_map/ppermute | solution.py:200
  125.6 4.1 %collective-permute-start.16 = (f32[26,128]{1,0:T(8,128)S(1)}, f32[26,128]{1,0:T(8,128)S(1)}, u32[]{:S(2)}, u32[]{:S(2)}) collective-permute-start(f32[26,128]{1,0:T(8,128)S(1)} %get-tuple-element.155), channel_id=1, source_target_pairs={{0,32},{1,33},{2,34},{3,35},{4,36},{5,37},{6,38},{7,39},{8,40},{9,... | collective-permute-start | bytes 39944 | tf_op jit(solution)/shard_map/ppermute | solution.py:200
  125.9 3.8 %collective-permute-start.15 = (f32[26,128]{1,0:T(8,128)S(1)}, f32[26,128]{1,0:T(8,128)S(1)}, u32[]{:S(2)}, u32[]{:S(2)}) collective-permute-start(f32[26,128]{1,0:T(8,128)S(1)} %get-tuple-element.153), channel_id=1, source_target_pairs={{0,16},{1,17},{2,18},{3,19},{4,20},{5,21},{6,22},{7,23},{8,24},{9,... | collective-permute-start | bytes 39944 | tf_op jit(solution)/shard_map/ppermute | solution.py:200
  129.8 3.9 %collective-permute-start.18 = (f32[26,128]{1,0:T(8,128)S(1)}, f32[26,128]{1,0:T(8,128)S(1)}, u32[]{:S(2)}, u32[]{:S(2)}) collective-permute-start(f32[26,128]{1,0:T(8,128)S(1)} %get-tuple-element.126), channel_id=1, source_target_pairs={{0,16},{1,17},{2,18},{3,19},{4,20},{5,21},{6,22},{7,23},{8,24},{9,... | collective-permute-start | bytes 39944 | tf_op jit(solution)/shard_map/ppermute | solution.py:215
  129.9 4.2 %collective-permute-start.19 = (f32[26,128]{1,0:T(8,128)S(1)}, f32[26,128]{1,0:T(8,128)S(1)}, u32[]{:S(2)}, u32[]{:S(2)}) collective-permute-start(f32[26,128]{1,0:T(8,128)S(1)} %get-tuple-element.126), channel_id=1, source_target_pairs={{0,32},{1,33},{2,34},{3,35},{4,36},{5,37},{6,38},{7,39},{8,40},{9,... | collective-permute-start | bytes 39944 | tf_op jit(solution)/shard_map/ppermute | solution.py:215
  131.6 3.8 %collective-permute-start.20 = (f32[26,128]{1,0:T(8,128)S(1)}, f32[26,128]{1,0:T(8,128)S(1)}, u32[]{:S(2)}, u32[]{:S(2)}) collective-permute-start(f32[26,128]{1,0:T(8,128)S(1)} %get-tuple-element.126), channel_id=1, source_target_pairs={{0,48},{1,49},{2,50},{3,51},{4,52},{5,53},{6,54},{7,55},{8,56},{9,... | collective-permute-start | bytes 39944 | tf_op jit(solution)/shard_map/ppermute | solution.py:215
  135.4 4.0 %collective-permute-start.21 = (f32[104,128]{1,0:T(8,128)S(1)}, f32[104,128]{1,0:T(8,128)S(1)}, u32[]{:S(2)}, u32[]{:S(2)}) collective-permute-start(f32[104,128]{1,0:T(8,128)S(1)} %reshape.193), channel_id=1, source_target_pairs={{0,2},{1,3},{2,0},{3,1},{4,6},{5,7},{6,4},{7,5},{8,10},{9,11},{10,... | collective-permute-start | bytes 159752 | tf_op jit(solution)/shard_map/ppermute | solution.py:215
  135.5 4.6 %collective-permute-start.22 = (f32[104,128]{1,0:T(8,128)S(1)}, f32[104,128]{1,0:T(8,128)S(1)}, u32[]{:S(2)}, u32[]{:S(2)}) collective-permute-start(f32[104,128]{1,0:T(8,128)S(1)} %reshape.193), channel_id=1, source_target_pairs={{0,4},{1,5},{2,6},{3,7},{4,0},{5,1},{6,2},{7,3},{8,12},{9,13},{10,... | collective-permute-start | bytes 159752 | tf_op jit(solution)/shard_map/ppermute | solution.py:215
  137.5 4.2 %collective-permute-start.23 = (f32[104,128]{1,0:T(8,128)S(1)}, f32[104,128]{1,0:T(8,128)S(1)}, u32[]{:S(2)}, u32[]{:S(2)}) collective-permute-start(f32[104,128]{1,0:T(8,128)S(1)} %reshape.193), channel_id=1, source_target_pairs={{0,6},{1,7},{2,4},{3,5},{4,2},{5,3},{6,0},{7,1},{8,14},{9,15},{10,... | collective-permute-start | bytes 159752 | tf_op jit(solution)/shard_map/ppermute | solution.py:215
  141.7 5.1 %collective-permute-start.24 = (f32[416,128]{1,0:T(8,128)S(1)}, f32[416,128]{1,0:T(8,128)S(1)}, u32[]{:S(2)}, u32[]{:S(2)}) collective-permute-start(f32[416,128]{1,0:T(8,128)S(1)} %bitcast.327), channel_id=1, source_target_pairs={{0,64},{1,65},{2,66},{3,67},{4,68},{5,69},{6,70},{7,71},{8,72},{9,... | collective-permute-start | bytes 638984 | tf_op jit(solution)/shard_map/ppermute | solution.py:215
  143.1 6.5 %collective-permute-start.25 = (f32[416,128]{1,0:T(8,128)S(1)}, f32[416,128]{1,0:T(8,128)S(1)}, u32[]{:S(2)}, u32[]{:S(2)}) collective-permute-start(f32[416,128]{1,0:T(8,128)S(1)} %bitcast.328), channel_id=1, source_target_pairs={{0,1},{1,0},{2,3},{3,2},{4,5},{5,4},{6,7},{7,6},{8,9},{9,8},{10,11... | collective-permute-start | bytes 638984 | tf_op jit(solution)/shard_map/ppermute | solution.py:215
  144.1 7.7 %collective-permute-start.26 = (f32[416,128]{1,0:T(8,128)S(1)}, f32[416,128]{1,0:T(8,128)S(1)}, u32[]{:S(2)}, u32[]{:S(2)}) collective-permute-start(f32[416,128]{1,0:T(8,128)S(1)} %bitcast.329), channel_id=1, source_target_pairs={{0,65},{1,64},{2,67},{3,66},{4,69},{5,68},{6,71},{7,70},{8,73},{9,... | collective-permute-start | bytes 638984 | tf_op jit(solution)/shard_map/ppermute | solution.py:215
  151.8 20.5 %collective-permute-start.27 = (f32[1664,128]{1,0:T(8,128)S(1)}, f32[1664,128]{1,0:T(8,128)S(1)}, u32[]{:S(2)}, u32[]{:S(2)}) collective-permute-start(f32[1664,128]{1,0:T(8,128)S(1)} %bitcast.319), channel_id=1, source_target_pairs={{0,8},{1,9},{2,10},{3,11},{4,12},{5,13},{6,14},{7,15},{8,0},{9,1},... | collective-permute-start | bytes 2555912 | tf_op jit(solution)/shard_map/ppermute | solution.py:215
  (74 other events, 733.8 us)

commit v3 on v2

--- a/solution.py
+++ b/solution.py
@@ -183,7 +183,7 @@
     return out
 
 
-def butterfly_psum(buffer, axes, stages, scale_of):
+def butterfly_psum(buffer, axes, stages, scale_of, tie, tie_after):
     index = lax.axis_index(axes)
     count = math.prod(lax.axis_size(a) for a in axes)
     offset = jnp.zeros((), jnp.int32)
@@ -201,6 +201,8 @@
         offset = offset * ways + mine
         places.append((bits, mine))
         buffer = total
+        if len(places) == tie_after:
+            buffer, tie = lax.optimization_barrier((buffer, tie))
     rows = buffer.shape[0]
     position = (offset * rows + lax.broadcasted_iota(jnp.int32, buffer.shape, 0)) * buffer.shape[1]
     position = position + lax.broadcasted_iota(jnp.int32, buffer.shape, 1)
@@ -215,7 +217,7 @@
             other = lax.ppermute(buffer, axes, pairs)
             both = lax.dynamic_update_index_in_dim(both, other, mine ^ step, 0)
         buffer = both.reshape(-1, buffer.shape[1])
-    return buffer
+    return buffer, tie
 
 
 def shards(
@@ -269,8 +271,6 @@
     parts = [joined, kernel_grad, expand_grad, project_grad, lateral_grad, classify_grad]
     count = math.prod(lax.axis_size(a) for a in axes)
     buffer, shapes = pack_rows(parts, count * 2)
-    buffer, d_padded = lax.optimization_barrier((buffer, d_padded))
-    d_input, _, _ = conv_backward(padded, d_conv, d_padded, returned, dw_weight)
     cell_count = micro_count * height * width * lax.axis_size("row") * lax.axis_size("col")
     grad_scale = 1.0 / math.sqrt(cell_count)
     loss_at = joined.shape[0] - 1
@@ -278,7 +278,9 @@
     def scale_of(position):
         return jnp.where(position == loss_at, 1.0 / cell_count, grad_scale).astype(jnp.float32)
 
-    buffer = butterfly_psum(buffer, axes, [(3,), (6, 0), (1, 2), (4, 5)], scale_of)
+    buffer, d_input = butterfly_psum(
+        buffer, axes, [(3,), (6, 0), (1, 2), (4, 5)], scale_of, d_input, 2
+    )
     joined, kernel_grad, expand_grad, project_grad, lateral_grad, classify_grad = unpack_rows(
         buffer, shapes
     )

time: 181 us -> 179 us (0.989)
  waiting for transfers between devices: 34.5 us -> 25 us
  local copies, waits for them, and re-layouts: 31.6 us -> 35.5 us
    ppermute x10, waiting for transfers between devices: 19.7 us -> 6.8 us  [butterfly_psum(): total = total + lax.ppermute(send, axes, pairs)]
    broadcast_in_dim x1 -> x0, other arithmetic: 9.34 us -> none  [shards(): d_input[None]]
    add x0 -> x1, other arithmetic: none -> 9 us  [conv_backward(): grad_out.astype(jnp.float32)]
    ppermute x10, waiting for transfers between devices: 9.93 us -> 12.6 us  [butterfly_psum(): other = lax.ppermute(buffer, axes, pairs)]
    unnamed x198 -> x218, local copies, waits for them, and re-layouts: 9.86 us -> 10.7 us
  transfers between devices with their start and end apart: 28 -> 28, of which waited for: 16 -> 17; matrix products, arithmetic and copies ran while one was open for 10% -> 9% of each run, Pallas kernels for 0% -> 0%
where the time goes in v3:
time: 179 us; the launch traced here: 178 us
  starting transfers between devices  64.1 us (36%)
  other arithmetic  37.1 us (21%)
  local copies, waits for them, and re-layouts  35.5 us (20%)
  waiting for transfers between devices  25 us (14%)
  matrix products  13.2 us (7%)
  between operations  2.79 us (2%)
    ppermute x10, starting transfers between devices, butterfly_psum(): other = lax.ppermute(buffer, axes, pairs)  20.4 us
    ppermute x4, starting transfers between devices, padded_2(): before = lax.ppermute(last, axis, up)  20.2 us
    ppermute x10, starting transfers between devices, butterfly_psum(): total = total + lax.ppermute(send, axes, pairs)  15.7 us
    dot_general x12, matrix products, product(): jnp.einsum(form, left_side, right_side, preferred_element_type=jnp.float32)  13.2 us
    ppermute x10, waiting for transfers between devices, butterfly_psum(): other = lax.ppermute(buffer, axes, pairs)  12.6 us
    reduce_sum x4, other arithmetic, conv_backward(): columns.append(jnp.sum(window * conv_float, axis=(1, 2)))  12.5 us
    unnamed x218, local copies, waits for them, and re-layouts  10.7 us
    add x1, other arithmetic, conv_backward(): grad_out.astype(jnp.float32)  9 us
  transfers between devices with their start and end apart: 28, of which 17 were waited for; matrix products, arithmetic and copies ran while one was open for 9% of the time, Pallas kernels for 0%

profile of v3, /device:TPU:1, one launch (start us, length us, event | category | flops | bytes accessed | tf_op | source)
XLA Modules:
  0.0 177.8 jit_solution(2589542406078733979)
XLA Ops:
  1.9 3.3 %collective-permute-start.1 = (bf16[192,3,128]{2,0,1:T(8,128)(2,1)S(1)}, bf16[192,3,128]{2,0,1:T(8,128)(2,1)S(1)}, u32[]{:S(2)}, u32[]{:S(2)}) collective-permute-start(bf16[192,3,128]{2,0,1:T(8,128)(2,1)S(1)} %get-tuple-element.154), channel_id=1, source_target_pairs={{8,0},{16,8},{24,16},{32,24},{40,32},{48,40},{56,48},{9,1},{17,9},... | collective-permute-start | bytes 442376 | tf_op jit(solution)/shard_map/ppermute | solution.py:21
  5.2 3.1 %collective-permute-start = (bf16[192,3,128]{2,0,1:T(8,128)(2,1)S(1)}, bf16[192,3,128]{2,0,1:T(8,128)(2,1)S(1)}, u32[]{:S(2)}, u32[]{:S(2)}) collective-permute-start(bf16[192,3,128]{2,0,1:T(8,128)(2,1)S(1)} %get-tuple-element.153), channel_id=1, source_target_pairs={{0,8},{8,16},{16,24},{24,32},{32,40},{40,48},{48,56},{1,9},{9,17},... | collective-permute-start | bytes 442376 | tf_op jit(solution)/shard_map/ppermute | solution.py:20
  11.2 1.3 collective-permute-start.3
  12.9 5.5 %collective-permute-start.2 = (bf16[192,14,3]{0,1,2:T(8,128)(2,1)S(1)}, bf16[192,14,3]{0,1,2:T(8,128)(2,1)S(1)}, u32[]{:S(2)}, u32[]{:S(2)}) collective-permute-start(bf16[192,14,3]{0,1,2:T(8,128)(2,1)S(1)} %copy.57), channel_id=1, source_target_pairs={{0,1},{1,2},{2,3},{3,4},{4,5},{5,6},{6,7},{8,9},{9,10},{10,11},{11... | collective-permute-start | bytes 48392 | tf_op jit(solution)/shard_map/ppermute | solution.py:20
  18.4 1.2 copy.60
  19.6 1.2 copy.58
  21.0 2.4 %pad_maximum_fusion = (bf16[192,14,131]{2,0,1:T(8,128)(2,1)S(1)}, bf16[192,14,131]{2,0,1:T(8,128)(2,1)S(1)}) fusion(bf16[192,14,3]{2,0,1:T(8,128)(2,1)} %copy.60, bf16[192,3,128]{2,0,1:T(8,128)(2,1)S(1)} %collective-permute-done.1, bf16[192,8,128]{2,0,1:T(8,128)(2,1)S(1)} %bitcast.310, bf16[192,3,128]{2,0,1:T(8,128)(2,1)S(1)} %collective-permute-done, ...), kind=kLoop, calls=%fused_computation.80 | loop fusion | flops 5634048 | bytes 2128896 | tf_op jit(solution)/shard_map/concatenate | solution.py:22
  23.9 8.3 %fusion.180 = (f32[8,128]{1,0:T(8,128)S(1)}, f32[192,8,128]{2,0,1:T(8,128)S(1)}) fusion(f32[192]{0:T(256)S(1)} %copy-done.101, bf16[192,14,131]{2,0,1:T(8,128)(2,1)S(1)} %get-tuple-element.147, f32[192]{0:T(256)S(1)} %bitcast.427, f32[192]{0:T(256)S(1)} %bitcast.429, f32[192]{0:T(256)S(1)} %bitcast.334, bf16[192,3,128]{2,0,1:T(8,128)(2,1)S(1)} %collective-permute-done.1, ...), kind=kLoop, calls=%fused_computation.383 | loop fusion | flops 30276608 | bytes 18032128 | tf_op jit(solution)/shard_map/reduce_sum | solution.py:64
  35.6 1.3 convert_reduce_fusion.2
  36.9 1.4 convert_reduce_fusion.3
  38.3 1.8 %convert_reduce_fusion.1 = (f32[768]{0:T(1024)S(1)}, bf16[768,8,128]{0,2,1:T(8,128)(2,1)S(1)}) fusion(f32[8,128,768]{2,1,0:T(8,128)S(1)} %get-tuple-element.216, f32[768]{0:T(1024)S(1)} %copy-done.98, bf16[192,8,128]{2,0,1:T(8,128)(2,1)S(1)} %get-tuple-element.134, bf16[768,192]{0,1:T(8,128)(2,1)S(1)} %copy-done.8), kind=kOutput, calls=%fused_computation.64 | convolution fusion | flops 312212736 | bytes 5412864 | tf_op jit(solution)/shard_map/chw,dc->dhw/dot_general | solution.py:33
  41.0 4.1 %fusion.117 = (f32[192]{0:T(256)}, f32[192]{0:T(256)}, f32[192]{0:T(256)}, f32[192]{0:T(256)}, f32[192]{0:T(256)}, /*index=5*/f32[192]{0:T(256)}, f32[192]{0:T(2...) fusion(bf16[192,14,131]{2,0,1:T(8,128)(2,1)S(1)} %get-tuple-ele, ...), kind=kLoop, calls=%fused_computation.241 | loop fusion | flops 12382848 | bytes 9074944 | tf_op jit(solution)/shard_map/reduce_sum | solution.py:121
  45.0 4.5 %fusion.121 = (f32[192]{0:T(256)}, f32[192]{0:T(256)}, f32[192]{0:T(256)}, f32[192]{0:T(256)}, f32[192]{0:T(256)}, /*index=5*/f32[192]{0:T(256)}, f32[192]{0:T(2...) fusion(bf16[192,8,128]{2,0,1:T(8,128)(2,1)S(1)} %get-tuple-elem, ...), kind=kLoop, calls=%fused_computation.245 | loop fusion | flops 11006400 | bytes 7485696 | tf_op jit(solution)/shard_map/reduce_sum | solution.py:121
  49.6 1.1 fusion.75
  50.7 1.4 convolution_bitcast_fusion.1
  52.0 1.5 convolution_bitcast_fusion
  53.5 1.1 convolution_bitcast_fusion.2
  54.7 1.2 convolution_bitcast_fusion.3
  55.8 1.3 reduce_sum.583
  59.0 2.8 %fusion.120 = (f32[192]{0:T(256)}, f32[192]{0:T(256)}, f32[192]{0:T(256)}, f32[192]{0:T(256)}, f32[192]{0:T(256)}, /*index=5*/f32[192]{0:T(256)}, f32[192]{0:T(256)}, f32[192]{0:T(256)}, f32[192]{0:T(256)}, f32[192]{0:T(256)}) fusion(bf16[192,8,128]{2,0,1:T(8,128)(2,1)S(1)} %get-tuple-element.130, bf16[192,14,131]{2,0,1:T(8,128)(2,1)S(1)} %get-tuple-element.147, ...), kind=kLoop, calls=%fused_computation.244 | loop fusion | flops 7272576 | bytes 2661888 | tf_op jit(solution)/shard_map/reduce_sum | solution.py:121
  61.8 5.1 %stack.199 = f32[192,49]{0,1:T(8,128)S(1)} concatenate(f32[192,1]{0,1:T(1,128)} %bitcast.460, f32[192,1]{0,1:T(1,128)} %bitcast.459, f32[192,1]{0,1:T(1,128)} %bitcast.458, f32[192,1]{0,1:T(1,128)} %bitcast.454, f32[192,1]{0,1:T(1,128)} %bitcast.431, f32[192,1]{0,1:T(1,128)} %bitcast.432, f32[192,1]{0,1:T(1,128)} %bitcast.433, f32[192,1]{0,1:T(1,128)} %bitcast.462, ...), dimensions={1} | concatenate | bytes 75264 | tf_op jit(solution)/shard_map/stack | solution.py:122
  70.6 1.4 bitcast_dynamic-update-slice_fusion.9
  75.7 2.1 %dynamic-slice_bitcast_fusion = f32[1664,128]{1,0:T(8,128)} fusion(f32[2,1664,128]{2,1,0:T(8,128)} %bitcast.323, s32[]{:T(128)S(6)} %select_n.76), kind=kLoop, calls=%fused_computation.147 | loop fusion | bytes 1703940 | tf_op jit(solution)/shard_map/jit(dynamic_index_in_dim)/squeeze | solution.py:199
  77.8 5.2 %collective-permute-start.8 = (bf16[192,3,128]{2,0,1:T(8,128)(2,1)S(1)}, bf16[192,3,128]{2,0,1:T(8,128)(2,1)S(1)}, u32[]{:S(2)}, u32[]{:S(2)}) collective-permute-start(bf16[192,3,128]{2,0,1:T(8,128)(2,1)S(1)} %get-tuple-element.152), channel_id=1, source_target_pairs={{0,8},{8,16},{16,24},{24,32},{32,40},{40,48},{48,56},{1,9},{9,17},... | collective-permute-start | bytes 442376 | tf_op jit(solution)/shard_map/ppermute | solution.py:20
  83.0 1.9 %collective-permute-start.9 = (bf16[192,3,128]{2,0,1:T(8,128)(2,1)S(1)}, bf16[192,3,128]{2,0,1:T(8,128)(2,1)S(1)}, u32[]{:S(2)}, u32[]{:S(2)}) collective-permute-start(bf16[192,3,128]{2,0,1:T(8,128)(2,1)S(1)} %get-tuple-element.151), channel_id=1, source_target_pairs={{8,0},{16,8},{24,16},{32,24},{40,32},{48,40},{56,48},{9,1},{17,9},... | collective-permute-start | bytes 442376 | tf_op jit(solution)/shard_map/ppermute | solution.py:21
  85.1 4.4 %collective-permute-done.9 = bf16[192,3,128]{2,0,1:T(8,128)(2,1)S(1)} collective-permute-done((bf16[192,3,128]{2,0,1:T(8,128)(2,1)S(1)}, bf16[192,3,128]{2,0,1:T(8,128)(2,1)S(1)}, u32[]{:S(2)}, u32[]{:S(2)}) %collective-permute-start.9) | collective-permute-done | bytes 147488 | tf_op jit(solution)/shard_map/ppermute | solution.py:21
  90.3 1.3 collective-permute-start.10
  91.9 6.4 %collective-permute-start.11 = (bf16[192,14,3]{0,1,2:T(8,128)(2,1)S(1)}, bf16[192,14,3]{0,1,2:T(8,128)(2,1)S(1)}, u32[]{:S(2)}, u32[]{:S(2)}) collective-permute-start(bf16[192,14,3]{0,1,2:T(8,128)(2,1)S(1)} %copy.74), channel_id=1, source_target_pairs={{0,1},{1,2},{2,3},{3,4},{4,5},{5,6},{6,7},{8,9},{9,10},{10,11},{11... | collective-permute-start | bytes 48392 | tf_op jit(solution)/shard_map/ppermute | solution.py:20
  99.6 1.3 pad_maximum_fusion.1
  101.3 1.3 bitcast_add_fusion
  102.7 4.4 %collective-permute-start.7 = (f32[416,128]{1,0:T(8,128)S(1)}, f32[416,128]{1,0:T(8,128)S(1)}, u32[]{:S(2)}, u32[]{:S(2)}) collective-permute-start(f32[416,128]{1,0:T(8,128)S(1)} %get-tuple-element.140), channel_id=1, source_target_pairs={{0,65},{1,64},{2,67},{3,66},{4,69},{5,68},{6,71},{7,70},{8,73},{9,... | collective-permute-start | bytes 638984 | tf_op jit(solution)/shard_map/ppermute | solution.py:200
  108.1 9.0 %fusion.148 = f32[192,8,128]{2,0,1:T(8,128)S(1)} fusion(f32[192,8,128]{2,0,1:T(8,128)S(1)} %copy-done.1, bf16[192,8,128]{2,0,1:T(8,128)(2,1)S(1)} %get-tuple-element.130, bf16[192,3,128]{2,0,1:T(8,128)(2,1)S(1)} %collective-permute-done.8, bf16[192,3,128]{2,0,1:T(8,128)(2,1)S(1)} %collective-permute-done.9, ...), kind=kLoop, calls=%fused_computation.281 | loop fusion | flops 30081024 | bytes 18813696 | tf_op jit(solution)/shard_map/add | solution.py:112
  117.2 6.7 %collective-permute-start.14 = (f32[104,128]{1,0:T(8,128)S(1)}, f32[104,128]{1,0:T(8,128)S(1)}, u32[]{:S(2)}, u32[]{:S(2)}) collective-permute-start(f32[104,128]{1,0:T(8,128)S(1)} %get-tuple-element.156), channel_id=1, source_target_pairs={{0,6},{1,7},{2,4},{3,5},{4,2},{5,3},{6,0},{7,1},{8,14},{9,15},{10,... | collective-permute-start | bytes 159752 | tf_op jit(solution)/shard_map/ppermute | solution.py:200
  124.5 1.4 collective-permute-done.14
  126.0 2.9 %collective-permute-done.13 = f32[104,128]{1,0:T(8,128)S(1)} collective-permute-done((f32[104,128]{1,0:T(8,128)S(1)}, f32[104,128]{1,0:T(8,128)S(1)}, u32[]{:S(2)}, u32[]{:S(2)}) %collective-permute-start.13) | collective-permute-done | bytes 53280 | tf_op jit(solution)/shard_map/ppermute | solution.py:200
  129.1 2.8 %collective-permute-start.16 = (f32[26,128]{1,0:T(8,128)S(1)}, f32[26,128]{1,0:T(8,128)S(1)}, u32[]{:S(2)}, u32[]{:S(2)}) collective-permute-start(f32[26,128]{1,0:T(8,128)S(1)} %get-tuple-element.160), channel_id=1, source_target_pairs={{0,32},{1,33},{2,34},{3,35},{4,36},{5,37},{6,38},{7,39},{8,40},{9,... | collective-permute-start | bytes 39944 | tf_op jit(solution)/shard_map/ppermute | solution.py:200
  133.3 1.5 collective-permute-done.15
  135.6 2.1 %collective-permute-start.19 = (f32[26,128]{1,0:T(8,128)S(1)}, f32[26,128]{1,0:T(8,128)S(1)}, u32[]{:S(2)}, u32[]{:S(2)}) collective-permute-start(f32[26,128]{1,0:T(8,128)S(1)} %get-tuple-element.129), channel_id=1, source_target_pairs={{0,32},{1,33},{2,34},{3,35},{4,36},{5,37},{6,38},{7,39},{8,40},{9,... | collective-permute-start | bytes 39944 | tf_op jit(solution)/shard_map/ppermute | solution.py:217
  137.7 1.2 collective-permute-start.20
  139.7 1.8 collective-permute-done.20
  141.6 2.3 %collective-permute-start.22 = (f32[104,128]{1,0:T(8,128)S(1)}, f32[104,128]{1,0:T(8,128)S(1)}, u32[]{:S(2)}, u32[]{:S(2)}) collective-permute-start(f32[104,128]{1,0:T(8,128)S(1)} %reshape.193), channel_id=1, source_target_pairs={{0,4},{1,5},{2,6},{3,7},{4,0},{5,1},{6,2},{7,3},{8,12},{9,13},{10,... | collective-permute-start | bytes 159752 | tf_op jit(solution)/shard_map/ppermute | solution.py:217
  143.9 1.5 collective-permute-start.23
  146.2 1.9 %collective-permute-done.23 = f32[104,128]{1,0:T(8,128)S(1)} collective-permute-done((f32[104,128]{1,0:T(8,128)S(1)}, f32[104,128]{1,0:T(8,128)S(1)}, u32[]{:S(2)}, u32[]{:S(2)}) %collective-permute-start.23) | collective-permute-done | bytes 53280 | tf_op jit(solution)/shard_map/ppermute | solution.py:217
  148.7 2.6 %collective-permute-start.25 = (f32[416,128]{1,0:T(8,128)S(1)}, f32[416,128]{1,0:T(8,128)S(1)}, u32[]{:S(2)}, u32[]{:S(2)}) collective-permute-start(f32[416,128]{1,0:T(8,128)S(1)} %bitcast.328), channel_id=1, source_target_pairs={{0,1},{1,0},{2,3},{3,2},{4,5},{5,4},{6,7},{7,6},{8,9},{9,8},{10,11... | collective-permute-start | bytes 638984 | tf_op jit(solution)/shard_map/ppermute | solution.py:217
  152.9 4.0 %collective-permute-done.25 = f32[416,128]{1,0:T(8,128)S(1)} collective-permute-done((f32[416,128]{1,0:T(8,128)S(1)}, f32[416,128]{1,0:T(8,128)S(1)}, u32[]{:S(2)}, u32[]{:S(2)}) %collective-permute-start.25) | collective-permute-done | bytes 213024 | tf_op jit(solution)/shard_map/ppermute | solution.py:217
  157.0 2.2 %collective-permute-done.26 = f32[416,128]{1,0:T(8,128)S(1)} collective-permute-done((f32[416,128]{1,0:T(8,128)S(1)}, f32[416,128]{1,0:T(8,128)S(1)}, u32[]{:S(2)}, u32[]{:S(2)}) %collective-permute-start.26) | collective-permute-done | bytes 213024 | tf_op jit(solution)/shard_map/ppermute | solution.py:217
  159.2 8.5 %collective-permute-start.27 = (f32[1664,128]{1,0:T(8,128)S(1)}, f32[1664,128]{1,0:T(8,128)S(1)}, u32[]{:S(2)}, u32[]{:S(2)}) collective-permute-start(f32[1664,128]{1,0:T(8,128)S(1)} %bitcast.318), channel_id=1, source_target_pairs={{0,8},{1,9},{2,10},{3,11},{4,12},{5,13},{6,14},{7,15},{8,0},{9,1},... | collective-permute-start | bytes 2555912 | tf_op jit(solution)/shard_map/ppermute | solution.py:217
  167.7 1.3 copy.76
  (327 shorter events, 36.9 us)
Async XLA Ops:
  1.9 8.0 %collective-permute-start.1 = (bf16[192,3,128]{2,0,1:T(8,128)(2,1)S(1)}, bf16[192,3,128]{2,0,1:T(8,128)(2,1)S(1)}, u32[]{:S(2)}, u32[]{:S(2)}) collective-permute-start(bf16[192,3,128]{2,0,1:T(8,128)(2,1)S(1)} %get-tuple-element.154), channel_id=1, source_target_pairs={{8,0},{16,8},{24,16},{32,24},{40,32},{48,40},{56,48},{9,1},{17,9},... | collective-permute-start | bytes 442376 | tf_op jit(solution)/shard_map/ppermute | solution.py:21
  5.2 5.2 %collective-permute-start = (bf16[192,3,128]{2,0,1:T(8,128)(2,1)S(1)}, bf16[192,3,128]{2,0,1:T(8,128)(2,1)S(1)}, u32[]{:S(2)}, u32[]{:S(2)}) collective-permute-start(bf16[192,3,128]{2,0,1:T(8,128)(2,1)S(1)} %get-tuple-element.153), channel_id=1, source_target_pairs={{0,8},{8,16},{16,24},{24,32},{32,40},{40,48},{48,56},{1,9},{9,17},... | collective-permute-start | bytes 442376 | tf_op jit(solution)/shard_map/ppermute | solution.py:20
  8.4 15.0 %copy-start.12 = (f32[192,1]{0,1:T(1,128)}, f32[192,1]{0,1:T(1,128)S(1)}, u32[]{:S(2)}) copy-start(f32[192,1]{0,1:T(1,128)S(1)} %get-tuple-element.165) | copy-start | bytes 2308
  8.4 15.0 %copy-start.14 = (f32[192,1]{0,1:T(1,128)}, f32[192,1]{0,1:T(1,128)S(1)}, u32[]{:S(2)}) copy-start(f32[192,1]{0,1:T(1,128)S(1)} %get-tuple-element.166) | copy-start | bytes 2308
  8.4 15.0 %copy-start.16 = (f32[192,1]{0,1:T(1,128)}, f32[192,1]{0,1:T(1,128)S(1)}, u32[]{:S(2)}) copy-start(f32[192,1]{0,1:T(1,128)S(1)} %get-tuple-element.167) | copy-start | bytes 2308
  8.4 15.0 %copy-start.18 = (f32[192,1]{0,1:T(1,128)}, f32[192,1]{0,1:T(1,128)S(1)}, u32[]{:S(2)}) copy-start(f32[192,1]{0,1:T(1,128)S(1)} %get-tuple-element.168) | copy-start | bytes 2308
  8.4 15.0 %copy-start.20 = (f32[192,1]{0,1:T(1,128)}, f32[192,1]{0,1:T(1,128)S(1)}, u32[]{:S(2)}) copy-start(f32[192,1]{0,1:T(1,128)S(1)} %get-tuple-element.169) | copy-start | bytes 2308
  8.4 15.0 %copy-start.22 = (f32[192,1]{0,1:T(1,128)}, f32[192,1]{0,1:T(1,128)S(1)}, u32[]{:S(2)}) copy-start(f32[192,1]{0,1:T(1,128)S(1)} %get-tuple-element.170) | copy-start | bytes 2308
  8.4 15.0 %copy-start.24 = (f32[192,1]{0,1:T(1,128)}, f32[192,1]{0,1:T(1,128)S(1)}, u32[]{:S(2)}) copy-start(f32[192,1]{0,1:T(1,128)S(1)} %get-tuple-element.171) | copy-start | bytes 2308
  8.4 15.0 %copy-start.26 = (f32[192,1]{0,1:T(1,128)}, f32[192,1]{0,1:T(1,128)S(1)}, u32[]{:S(2)}) copy-start(f32[192,1]{0,1:T(1,128)S(1)} %get-tuple-element.172) | copy-start | bytes 2308
  8.5 15.0 %copy-start.28 = (f32[192,1]{0,1:T(1,128)}, f32[192,1]{0,1:T(1,128)S(1)}, u32[]{:S(2)}) copy-start(f32[192,1]{0,1:T(1,128)S(1)} %get-tuple-element.173) | copy-start | bytes 2308
  8.5 15.0 %copy-start.30 = (f32[192,1]{0,1:T(1,128)}, f32[192,1]{0,1:T(1,128)S(1)}, u32[]{:S(2)}) copy-start(f32[192,1]{0,1:T(1,128)S(1)} %get-tuple-element.174) | copy-start | bytes 2308
  8.5 15.0 %copy-start.32 = (f32[192,1]{0,1:T(1,128)}, f32[192,1]{0,1:T(1,128)S(1)}, u32[]{:S(2)}) copy-start(f32[192,1]{0,1:T(1,128)S(1)} %get-tuple-element.175) | copy-start | bytes 2308
  8.5 15.0 %copy-start.34 = (f32[192,1]{0,1:T(1,128)}, f32[192,1]{0,1:T(1,128)S(1)}, u32[]{:S(2)}) copy-start(f32[192,1]{0,1:T(1,128)S(1)} %get-tuple-element.176) | copy-start | bytes 2308
  8.5 15.0 %copy-start.36 = (f32[192,1]{0,1:T(1,128)}, f32[192,1]{0,1:T(1,128)S(1)}, u32[]{:S(2)}) copy-start(f32[192,1]{0,1:T(1,128)S(1)} %get-tuple-element.177) | copy-start | bytes 2308
  8.5 15.0 %copy-start.38 = (f32[192,1]{0,1:T(1,128)}, f32[192,1]{0,1:T(1,128)S(1)}, u32[]{:S(2)}) copy-start(f32[192,1]{0,1:T(1,128)S(1)} %get-tuple-element.178) | copy-start | bytes 2308
  8.5 15.0 %copy-start.40 = (f32[192,1]{0,1:T(1,128)}, f32[192,1]{0,1:T(1,128)S(1)}, u32[]{:S(2)}) copy-start(f32[192,1]{0,1:T(1,128)S(1)} %get-tuple-element.179) | copy-start | bytes 2308
  9.2 14.4 %copy-start.46 = (f32[192,1]{0,1:T(1,128)}, f32[192,1]{0,1:T(1,128)S(1)}, u32[]{:S(2)}) copy-start(f32[192,1]{0,1:T(1,128)S(1)} %get-tuple-element.182) | copy-start | bytes 2308
  9.2 14.4 %copy-start.48 = (f32[192,1]{0,1:T(1,128)}, f32[192,1]{0,1:T(1,128)S(1)}, u32[]{:S(2)}) copy-start(f32[192,1]{0,1:T(1,128)S(1)} %get-tuple-element.183) | copy-start | bytes 2308
  9.2 14.4 %copy-start.50 = (f32[192,1]{0,1:T(1,128)}, f32[192,1]{0,1:T(1,128)S(1)}, u32[]{:S(2)}) copy-start(f32[192,1]{0,1:T(1,128)S(1)} %get-tuple-element.184) | copy-start | bytes 2308
  9.2 14.4 %copy-start.52 = (f32[192,1]{0,1:T(1,128)}, f32[192,1]{0,1:T(1,128)S(1)}, u32[]{:S(2)}) copy-start(f32[192,1]{0,1:T(1,128)S(1)} %get-tuple-element.185) | copy-start | bytes 2308
  9.2 14.4 %copy-start.54 = (f32[192,1]{0,1:T(1,128)}, f32[192,1]{0,1:T(1,128)S(1)}, u32[]{:S(2)}) copy-start(f32[192,1]{0,1:T(1,128)S(1)} %get-tuple-element.186) | copy-start | bytes 2308
  11.2 7.2 %collective-permute-start.3 = (bf16[192,14,3]{0,1,2:T(8,128)(2,1)S(1)}, bf16[192,14,3]{0,1,2:T(8,128)(2,1)S(1)}, u32[]{:S(2)}, u32[]{:S(2)}) collective-permute-start(bf16[192,14,3]{0,1,2:T(8,128)(2,1)S(1)} %copy.59), channel_id=1, source_target_pairs={{1,0},{2,1},{3,2},{4,3},{5,4},{6,5},{7,6},{9,8},{10,9},{11,10},{12... | collective-permute-start | bytes 48392 | tf_op jit(solution)/shard_map/ppermute | solution.py:21
  12.9 6.7 %collective-permute-start.2 = (bf16[192,14,3]{0,1,2:T(8,128)(2,1)S(1)}, bf16[192,14,3]{0,1,2:T(8,128)(2,1)S(1)}, u32[]{:S(2)}, u32[]{:S(2)}) collective-permute-start(bf16[192,14,3]{0,1,2:T(8,128)(2,1)S(1)} %copy.57), channel_id=1, source_target_pairs={{0,1},{1,2},{2,3},{3,4},{4,5},{5,6},{6,7},{8,9},{9,10},{10,11},{11... | collective-permute-start | bytes 48392 | tf_op jit(solution)/shard_map/ppermute | solution.py:20
  77.8 23.5 %collective-permute-start.4 = (f32[1664,128]{1,0:T(8,128)}, f32[1664,128]{1,0:T(8,128)}, u32[]{:S(2)}, u32[]{:S(2)}) collective-permute-start(f32[1664,128]{1,0:T(8,128)} %dynamic-slice_bitcast_fusion), channel_id=1, source_target_pairs={{0,8},{1,9},{2,10},{3,11},{4,12},{5,13},{6,14},{7,15},{8,0},{9,1},... | collective-permute-start | bytes 2555912 | tf_op jit(solution)/shard_map/ppermute | solution.py:200
  77.8 7.3 %collective-permute-start.8 = (bf16[192,3,128]{2,0,1:T(8,128)(2,1)S(1)}, bf16[192,3,128]{2,0,1:T(8,128)(2,1)S(1)}, u32[]{:S(2)}, u32[]{:S(2)}) collective-permute-start(bf16[192,3,128]{2,0,1:T(8,128)(2,1)S(1)} %get-tuple-element.152), channel_id=1, source_target_pairs={{0,8},{8,16},{16,24},{24,32},{32,40},{40,48},{48,56},{1,9},{9,17},... | collective-permute-start | bytes 442376 | tf_op jit(solution)/shard_map/ppermute | solution.py:20
  83.0 6.5 %collective-permute-start.9 = (bf16[192,3,128]{2,0,1:T(8,128)(2,1)S(1)}, bf16[192,3,128]{2,0,1:T(8,128)(2,1)S(1)}, u32[]{:S(2)}, u32[]{:S(2)}) collective-permute-start(bf16[192,3,128]{2,0,1:T(8,128)(2,1)S(1)} %get-tuple-element.151), channel_id=1, source_target_pairs={{8,0},{16,8},{24,16},{32,24},{40,32},{48,40},{56,48},{9,1},{17,9},... | collective-permute-start | bytes 442376 | tf_op jit(solution)/shard_map/ppermute | solution.py:21
  90.3 8.1 %collective-permute-start.10 = (bf16[192,14,3]{0,1,2:T(8,128)(2,1)S(1)}, bf16[192,14,3]{0,1,2:T(8,128)(2,1)S(1)}, u32[]{:S(2)}, u32[]{:S(2)}) collective-permute-start(bf16[192,14,3]{0,1,2:T(8,128)(2,1)S(1)} %copy.72), channel_id=1, source_target_pairs={{1,0},{2,1},{3,2},{4,3},{5,4},{6,5},{7,6},{9,8},{10,9},{11,10},{12... | collective-permute-start | bytes 48392 | tf_op jit(solution)/shard_map/ppermute | solution.py:21
  91.9 7.3 %collective-permute-start.11 = (bf16[192,14,3]{0,1,2:T(8,128)(2,1)S(1)}, bf16[192,14,3]{0,1,2:T(8,128)(2,1)S(1)}, u32[]{:S(2)}, u32[]{:S(2)}) collective-permute-start(bf16[192,14,3]{0,1,2:T(8,128)(2,1)S(1)} %copy.74), channel_id=1, source_target_pairs={{0,1},{1,2},{2,3},{3,4},{4,5},{5,6},{6,7},{8,9},{9,10},{10,11},{11... | collective-permute-start | bytes 48392 | tf_op jit(solution)/shard_map/ppermute | solution.py:20
  102.7 14.4 %collective-permute-start.7 = (f32[416,128]{1,0:T(8,128)S(1)}, f32[416,128]{1,0:T(8,128)S(1)}, u32[]{:S(2)}, u32[]{:S(2)}) collective-permute-start(f32[416,128]{1,0:T(8,128)S(1)} %get-tuple-element.140), channel_id=1, source_target_pairs={{0,65},{1,64},{2,67},{3,66},{4,69},{5,68},{6,71},{7,70},{8,73},{9,... | collective-permute-start | bytes 638984 | tf_op jit(solution)/shard_map/ppermute | solution.py:200
  107.0 10.1 %collective-permute-start.6 = (f32[416,128]{1,0:T(8,128)S(1)}, f32[416,128]{1,0:T(8,128)S(1)}, u32[]{:S(2)}, u32[]{:S(2)}) collective-permute-start(f32[416,128]{1,0:T(8,128)S(1)} %get-tuple-element.141), channel_id=1, source_target_pairs={{0,1},{1,0},{2,3},{3,2},{4,5},{5,4},{6,7},{7,6},{8,9},{9,8},{10,11... | collective-permute-start | bytes 638984 | tf_op jit(solution)/shard_map/ppermute | solution.py:200
  107.3 9.8 %collective-permute-start.5 = (f32[416,128]{1,0:T(8,128)S(1)}, f32[416,128]{1,0:T(8,128)S(1)}, u32[]{:S(2)}, u32[]{:S(2)}) collective-permute-start(f32[416,128]{1,0:T(8,128)S(1)} %get-tuple-element.139), channel_id=1, source_target_pairs={{0,64},{1,65},{2,66},{3,67},{4,68},{5,69},{6,70},{7,71},{8,72},{9,... | collective-permute-start | bytes 638984 | tf_op jit(solution)/shard_map/ppermute | solution.py:200
  117.2 8.8 %collective-permute-start.14 = (f32[104,128]{1,0:T(8,128)S(1)}, f32[104,128]{1,0:T(8,128)S(1)}, u32[]{:S(2)}, u32[]{:S(2)}) collective-permute-start(f32[104,128]{1,0:T(8,128)S(1)} %get-tuple-element.156), channel_id=1, source_target_pairs={{0,6},{1,7},{2,4},{3,5},{4,2},{5,3},{6,0},{7,1},{8,14},{9,15},{10,... | collective-permute-start | bytes 159752 | tf_op jit(solution)/shard_map/ppermute | solution.py:200
  123.9 5.1 %collective-permute-start.13 = (f32[104,128]{1,0:T(8,128)S(1)}, f32[104,128]{1,0:T(8,128)S(1)}, u32[]{:S(2)}, u32[]{:S(2)}) collective-permute-start(f32[104,128]{1,0:T(8,128)S(1)} %get-tuple-element.157), channel_id=1, source_target_pairs={{0,4},{1,5},{2,6},{3,7},{4,0},{5,1},{6,2},{7,3},{8,12},{9,13},{10,... | collective-permute-start | bytes 159752 | tf_op jit(solution)/shard_map/ppermute | solution.py:200
  123.9 5.1 %collective-permute-start.12 = (f32[104,128]{1,0:T(8,128)S(1)}, f32[104,128]{1,0:T(8,128)S(1)}, u32[]{:S(2)}, u32[]{:S(2)}) collective-permute-start(f32[104,128]{1,0:T(8,128)S(1)} %get-tuple-element.155), channel_id=1, source_target_pairs={{0,2},{1,3},{2,0},{3,1},{4,6},{5,7},{6,4},{7,5},{8,10},{9,11},{10,... | collective-permute-start | bytes 159752 | tf_op jit(solution)/shard_map/ppermute | solution.py:200
  129.0 3.9 %collective-permute-start.17 = (f32[26,128]{1,0:T(8,128)S(1)}, f32[26,128]{1,0:T(8,128)S(1)}, u32[]{:S(2)}, u32[]{:S(2)}) collective-permute-start(f32[26,128]{1,0:T(8,128)S(1)} %get-tuple-element.159), channel_id=1, source_target_pairs={{0,48},{1,49},{2,50},{3,51},{4,52},{5,53},{6,54},{7,55},{8,56},{9,... | collective-permute-start | bytes 39944 | tf_op jit(solution)/shard_map/ppermute | solution.py:200
  129.1 4.2 %collective-permute-start.16 = (f32[26,128]{1,0:T(8,128)S(1)}, f32[26,128]{1,0:T(8,128)S(1)}, u32[]{:S(2)}, u32[]{:S(2)}) collective-permute-start(f32[26,128]{1,0:T(8,128)S(1)} %get-tuple-element.160), channel_id=1, source_target_pairs={{0,32},{1,33},{2,34},{3,35},{4,36},{5,37},{6,38},{7,39},{8,40},{9,... | collective-permute-start | bytes 39944 | tf_op jit(solution)/shard_map/ppermute | solution.py:200
  131.8 2.9 %collective-permute-start.15 = (f32[26,128]{1,0:T(8,128)S(1)}, f32[26,128]{1,0:T(8,128)S(1)}, u32[]{:S(2)}, u32[]{:S(2)}) collective-permute-start(f32[26,128]{1,0:T(8,128)S(1)} %get-tuple-element.158), channel_id=1, source_target_pairs={{0,16},{1,17},{2,18},{3,19},{4,20},{5,21},{6,22},{7,23},{8,24},{9,... | collective-permute-start | bytes 39944 | tf_op jit(solution)/shard_map/ppermute | solution.py:200
  134.8 4.1 %collective-permute-start.18 = (f32[26,128]{1,0:T(8,128)S(1)}, f32[26,128]{1,0:T(8,128)S(1)}, u32[]{:S(2)}, u32[]{:S(2)}) collective-permute-start(f32[26,128]{1,0:T(8,128)S(1)} %get-tuple-element.129), channel_id=1, source_target_pairs={{0,16},{1,17},{2,18},{3,19},{4,20},{5,21},{6,22},{7,23},{8,24},{9,... | collective-permute-start | bytes 39944 | tf_op jit(solution)/shard_map/ppermute | solution.py:217
  135.6 4.1 %collective-permute-start.19 = (f32[26,128]{1,0:T(8,128)S(1)}, f32[26,128]{1,0:T(8,128)S(1)}, u32[]{:S(2)}, u32[]{:S(2)}) collective-permute-start(f32[26,128]{1,0:T(8,128)S(1)} %get-tuple-element.129), channel_id=1, source_target_pairs={{0,32},{1,33},{2,34},{3,35},{4,36},{5,37},{6,38},{7,39},{8,40},{9,... | collective-permute-start | bytes 39944 | tf_op jit(solution)/shard_map/ppermute | solution.py:217
  137.7 3.8 %collective-permute-start.20 = (f32[26,128]{1,0:T(8,128)S(1)}, f32[26,128]{1,0:T(8,128)S(1)}, u32[]{:S(2)}, u32[]{:S(2)}) collective-permute-start(f32[26,128]{1,0:T(8,128)S(1)} %get-tuple-element.129), channel_id=1, source_target_pairs={{0,48},{1,49},{2,50},{3,51},{4,52},{5,53},{6,54},{7,55},{8,56},{9,... | collective-permute-start | bytes 39944 | tf_op jit(solution)/shard_map/ppermute | solution.py:217
  141.5 4.0 %collective-permute-start.21 = (f32[104,128]{1,0:T(8,128)S(1)}, f32[104,128]{1,0:T(8,128)S(1)}, u32[]{:S(2)}, u32[]{:S(2)}) collective-permute-start(f32[104,128]{1,0:T(8,128)S(1)} %reshape.193), channel_id=1, source_target_pairs={{0,2},{1,3},{2,0},{3,1},{4,6},{5,7},{6,4},{7,5},{8,10},{9,11},{10,... | collective-permute-start | bytes 159752 | tf_op jit(solution)/shard_map/ppermute | solution.py:217
  141.6 4.6 %collective-permute-start.22 = (f32[104,128]{1,0:T(8,128)S(1)}, f32[104,128]{1,0:T(8,128)S(1)}, u32[]{:S(2)}, u32[]{:S(2)}) collective-permute-start(f32[104,128]{1,0:T(8,128)S(1)} %reshape.193), channel_id=1, source_target_pairs={{0,4},{1,5},{2,6},{3,7},{4,0},{5,1},{6,2},{7,3},{8,12},{9,13},{10,... | collective-permute-start | bytes 159752 | tf_op jit(solution)/shard_map/ppermute | solution.py:217
  143.9 4.2 %collective-permute-start.23 = (f32[104,128]{1,0:T(8,128)S(1)}, f32[104,128]{1,0:T(8,128)S(1)}, u32[]{:S(2)}, u32[]{:S(2)}) collective-permute-start(f32[104,128]{1,0:T(8,128)S(1)} %reshape.193), channel_id=1, source_target_pairs={{0,6},{1,7},{2,4},{3,5},{4,2},{5,3},{6,0},{7,1},{8,14},{9,15},{10,... | collective-permute-start | bytes 159752 | tf_op jit(solution)/shard_map/ppermute | solution.py:217
  148.1 4.8 %collective-permute-start.24 = (f32[416,128]{1,0:T(8,128)S(1)}, f32[416,128]{1,0:T(8,128)S(1)}, u32[]{:S(2)}, u32[]{:S(2)}) collective-permute-start(f32[416,128]{1,0:T(8,128)S(1)} %bitcast.327), channel_id=1, source_target_pairs={{0,64},{1,65},{2,66},{3,67},{4,68},{5,69},{6,70},{7,71},{8,72},{9,... | collective-permute-start | bytes 638984 | tf_op jit(solution)/shard_map/ppermute | solution.py:217
  148.7 8.2 %collective-permute-start.25 = (f32[416,128]{1,0:T(8,128)S(1)}, f32[416,128]{1,0:T(8,128)S(1)}, u32[]{:S(2)}, u32[]{:S(2)}) collective-permute-start(f32[416,128]{1,0:T(8,128)S(1)} %bitcast.328), channel_id=1, source_target_pairs={{0,1},{1,0},{2,3},{3,2},{4,5},{5,4},{6,7},{7,6},{8,9},{9,8},{10,11... | collective-permute-start | bytes 638984 | tf_op jit(solution)/shard_map/ppermute | solution.py:217
  151.4 7.8 %collective-permute-start.26 = (f32[416,128]{1,0:T(8,128)S(1)}, f32[416,128]{1,0:T(8,128)S(1)}, u32[]{:S(2)}, u32[]{:S(2)}) collective-permute-start(f32[416,128]{1,0:T(8,128)S(1)} %bitcast.329), channel_id=1, source_target_pairs={{0,65},{1,64},{2,67},{3,66},{4,69},{5,68},{6,71},{7,70},{8,73},{9,... | collective-permute-start | bytes 638984 | tf_op jit(solution)/shard_map/ppermute | solution.py:217
  159.2 10.5 %collective-permute-start.27 = (f32[1664,128]{1,0:T(8,128)S(1)}, f32[1664,128]{1,0:T(8,128)S(1)}, u32[]{:S(2)}, u32[]{:S(2)}) collective-permute-start(f32[1664,128]{1,0:T(8,128)S(1)} %bitcast.318), channel_id=1, source_target_pairs={{0,8},{1,9},{2,10},{3,11},{4,12},{5,13},{6,14},{7,15},{8,0},{9,1},... | collective-permute-start | bytes 2555912 | tf_op jit(solution)/shard_map/ppermute | solution.py:217
  (84 other events, 452.5 us)

commit v4 on v3

--- a/solution.py
+++ b/solution.py
@@ -15,10 +15,11 @@
         count, length = (lax.axis_size(axis), x.shape[dim])
         up = [(i, (i + 1) % count) for i in range(count - 1)]
         down = [(j, i) for i, j in up]
-        last = lax.slice_in_dim(x, length - width, length, axis=dim)
-        leading = lax.slice_in_dim(x, 0, width, axis=dim)
-        before = lax.ppermute(last, axis, up)
-        after = lax.ppermute(leading, axis, down)
+        order = (1, 0, 2) if dim == 1 else (2, 1, 0)
+        last = jnp.transpose(lax.slice_in_dim(x, length - width, length, axis=dim), order)
+        leading = jnp.transpose(lax.slice_in_dim(x, 0, width, axis=dim), order)
+        before = jnp.transpose(lax.ppermute(last, axis, up), order)
+        after = jnp.transpose(lax.ppermute(leading, axis, down), order)
         x = jnp.concatenate([before, x, after], axis=dim)
     return x
 

time: 179 us -> 181 us (1.011)
    reshape x4, local copies, waits for them, and re-layouts: 2.62 us -> 5.23 us  [pack_rows(): rows.append(flat.reshape(padded_rows, LANES))]
    transpose x0 -> x8, local copies, waits for them, and re-layouts: none -> 2.16 us  [the longest x5 1.37 us: padded_2(): leading = jnp.transpose(lax.slice_in_dim(x, 0, width, axis=dim), order)]
    slice x8 -> x0, local copies, waits for them, and re-layouts: 2.16 us -> none  [the longest x5 1.37 us: padded_2(): leading = lax.slice_in_dim(x, 0, width, axis=dim)]
    unnamed x218 -> x202, local copies, waits for them, and re-layouts: 10.7 us -> 9.86 us
  transfers between devices with their start and end apart: 28 -> 28, of which waited for: 17 -> 18; matrix products, arithmetic and copies ran while one was open for 9% -> 10% of each run, Pallas kernels for 0% -> 0%
where the time goes in v4:
time: 181 us; the launch traced here: 180 us
  starting transfers between devices  64.3 us (36%)
  other arithmetic  38.4 us (21%)
  local copies, waits for them, and re-layouts  35.1 us (19%)
  waiting for transfers between devices  26.1 us (14%)
  matrix products  13.9 us (8%)
  between operations  2.65 us (1%)
    ppermute x4, starting transfers between devices, padded_2(): before = jnp.transpose(lax.ppermute(last, axis, up), order)  20.5 us
    ppermute x10, starting transfers between devices, butterfly_psum(): other = lax.ppermute(buffer, axes, pairs)  20.3 us
    ppermute x10, starting transfers between devices, butterfly_psum(): total = total + lax.ppermute(send, axes, pairs)  15.7 us
    dot_general x12, matrix products, product(): jnp.einsum(form, left_side, right_side, preferred_element_type=jnp.float32)  13.9 us
    ppermute x10, waiting for transfers between devices, butterfly_psum(): other = lax.ppermute(buffer, axes, pairs)  12.7 us
    reduce_sum x4, other arithmetic, conv_backward(): columns.append(jnp.sum(window * conv_float, axis=(1, 2)))  12.2 us
    unnamed x202, local copies, waits for them, and re-layouts  9.86 us
    add x1, other arithmetic, conv_backward(): grad_out.astype(jnp.float32)  9.11 us
  transfers between devices with their start and end apart: 28, of which 18 were waited for; matrix products, arithmetic and copies ran while one was open for 10% of the time, Pallas kernels for 0%

profile of v4, /device:TPU:1, one launch (start us, length us, event | category | flops | bytes accessed | tf_op | source)
XLA Modules:
  0.0 180.4 jit_solution(6271434097470500960)
XLA Ops:
  0.7 1.1 copy-done
  1.9 3.3 %collective-permute-start.1 = (bf16[3,192,128]{2,1,0:T(8,128)(2,1)S(1)}, bf16[3,192,128]{2,1,0:T(8,128)(2,1)S(1)}, u32[]{:S(2)}, u32[]{:S(2)}) collective-permute-start(bf16[3,192,128]{2,1,0:T(8,128)(2,1)S(1)} %get-tuple-element.154), channel_id=1, source_target_pairs={{8,0},{16,8},{24,16},{32,24},{40,32},{48,40},{56,48},{9,1},{17,9},... | collective-permute-start | bytes 442376 | tf_op jit(solution)/shard_map/ppermute | solution.py:22
  5.2 3.1 %collective-permute-start = (bf16[3,192,128]{2,1,0:T(8,128)(2,1)S(1)}, bf16[3,192,128]{2,1,0:T(8,128)(2,1)S(1)}, u32[]{:S(2)}, u32[]{:S(2)}) collective-permute-start(bf16[3,192,128]{2,1,0:T(8,128)(2,1)S(1)} %get-tuple-element.153), channel_id=1, source_target_pairs={{0,8},{8,16},{16,24},{24,32},{32,40},{40,48},{48,56},{1,9},{9,17},... | collective-permute-start | bytes 442376 | tf_op jit(solution)/shard_map/ppermute | solution.py:21
  11.2 1.3 collective-permute-start.3
  12.9 5.5 %collective-permute-start.2 = (bf16[3,14,192]{2,1,0:T(8,128)(2,1)S(1)}, bf16[3,14,192]{2,1,0:T(8,128)(2,1)S(1)}, u32[]{:S(2)}, u32[]{:S(2)}) collective-permute-start(bf16[3,14,192]{2,1,0:T(8,128)(2,1)S(1)} %copy.57), channel_id=1, source_target_pairs={{0,1},{1,2},{2,3},{3,4},{4,5},{5,6},{6,7},{8,9},{9,10},{10,11},{11... | collective-permute-start | bytes 48392 | tf_op jit(solution)/shard_map/ppermute | solution.py:21
  19.7 1.3 pad_maximum_fusion
  21.4 9.0 %fusion.180 = (f32[8,128]{1,0:T(8,128)S(1)}, f32[192,8,128]{2,0,1:T(8,128)S(1)}) fusion(f32[192]{0:T(256)S(1)} %copy-done.93, bf16[192,14,131]{2,0,1:T(8,128)(2,1)S(1)} %get-tuple-element.147, f32[192]{0:T(256)} %bitcast.57, f32[192]{0:T(256)} %bitcast.56, f32[192]{0:T(256)S(1)} %bitcast.373, bf16[192,3,128]{2,0,1:T(8,128)(2,1)S(1)} %bitcast.353, ...), kind=kLoop, calls=%fused_computation.391 | loop fusion | flops 30276608 | bytes 18032128 | tf_op jit(solution)/shard_map/reduce_sum | solution.py:65
  34.4 1.9 %convert_reduce_fusion.2 = (f32[512]{0:T(512)}, bf16[512,8,128]{0,2,1:T(8,128)(2,1)S(1)}) fusion(f32[8,128,512]{2,1,0:T(8,128)S(1)} %get-tuple-element.220, f32[512]{0:T(512)S(1)} %copy-done.91, bf16[16,8,128]{2,0,1:T(8,128)(2,1)S(1)} %get-tuple-element.132, bf16[512,16]{0,1:T(8,128)(2,1)S(1)} %copy-done.12), kind=kOutput, calls=%fused_computation.78 | convolution fusion | flops 23592448 | bytes 3198976 | tf_op jit(solution)/shard_map/khw,lk->lhw/dot_general | solution.py:34
  36.2 1.3 convert_reduce_fusion.3
  37.5 2.4 %convert_reduce_fusion.1 = (f32[768]{0:T(1024)}, bf16[768,8,128]{0,2,1:T(8,128)(2,1)S(1)}) fusion(f32[8,128,768]{2,1,0:T(8,128)S(1)} %get-tuple-element.216, f32[768]{0:T(1024)S(1)} %copy-done.90, bf16[192,8,128]{2,0,1:T(8,128)(2,1)S(1)} %get-tuple-element.134, bf16[768,192]{0,1:T(8,128)(2,1)S(1)} %copy-done.9), kind=kOutput, calls=%fused_computation.64 | convolution fusion | flops 312212736 | bytes 5412864 | tf_op jit(solution)/shard_map/chw,dc->dhw/dot_general | solution.py:34
  39.9 1.3 fusion.147
  41.2 4.1 %fusion.117 = (f32[192]{0:T(256)}, f32[192]{0:T(256)}, f32[192]{0:T(256)}, f32[192]{0:T(256)}, f32[192]{0:T(256)}, /*index=5*/f32[192]{0:T(256)}, f32[192]{0:T(2...) fusion(bf16[192,14,131]{2,0,1:T(8,128)(2,1)S(1)} %get-tuple-ele, ...), kind=kLoop, calls=%fused_computation.241 | loop fusion | flops 12382848 | bytes 9074944 | tf_op jit(solution)/shard_map/reduce_sum | solution.py:122
  45.3 4.4 %fusion.121 = (f32[192]{0:T(256)}, f32[192]{0:T(256)}, f32[192]{0:T(256)}, f32[192]{0:T(256)}, f32[192]{0:T(256)}, /*index=5*/f32[192]{0:T(256)}, f32[192]{0:T(2...) fusion(bf16[192,8,128]{2,0,1:T(8,128)(2,1)S(1)} %get-tuple-elem, ...), kind=kLoop, calls=%fused_computation.245 | loop fusion | flops 11006400 | bytes 7485696 | tf_op jit(solution)/shard_map/reduce_sum | solution.py:122
  50.7 2.7 %fusion.120 = (f32[192]{0:T(256)}, f32[192]{0:T(256)}, f32[192]{0:T(256)}, f32[192]{0:T(256)}, f32[192]{0:T(256)}, /*index=5*/f32[192]{0:T(256)}, f32[192]{0:T(256)}, f32[192]{0:T(256)}, f32[192]{0:T(256)}, f32[192]{0:T(256)}) fusion(bf16[192,8,128]{2,0,1:T(8,128)(2,1)S(1)} %get-tuple-element.130, bf16[192,14,131]{2,0,1:T(8,128)(2,1)S(1)} %get-tuple-element.147, ...), kind=kLoop, calls=%fused_computation.244 | loop fusion | flops 7272576 | bytes 2661888 | tf_op jit(solution)/shard_map/reduce_sum | solution.py:122
  53.4 1.4 convolution_bitcast_fusion.1
  55.4 1.1 convolution_bitcast_fusion.2
  56.5 1.2 convolution_bitcast_fusion.3
  59.0 1.5 concatenate.131
  61.0 5.0 %stack.199 = f32[192,49]{0,1:T(8,128)S(1)} concatenate(f32[192,1]{0,1:T(1,128)} %bitcast.477, f32[192,1]{0,1:T(1,128)} %bitcast.476, f32[192,1]{0,1:T(1,128)} %bitcast.475, f32[192,1]{0,1:T(1,128)} %bitcast.471, f32[192,1]{0,1:T(1,128)} %bitcast.448, f32[192,1]{0,1:T(1,128)} %bitcast.449, f32[192,1]{0,1:T(1,128)} %bitcast.450, f32[192,1]{0,1:T(1,128)} %bitcast.479, ...), dimensions={1} | concatenate | bytes 75264 | tf_op jit(solution)/shard_map/stack | solution.py:123
  66.4 1.1 reshape.185
  67.5 1.2 reshape.186
  68.7 1.8 %reshape.187 = f32[768,128]{1,0:T(8,128)} reshape(f32[192,512]{1,0:T(8,128)} %convolution_bitcast_fusion.2) | data formatting | bytes 786432 | tf_op jit(solution)/shard_map/reshape | solution.py:160
  75.9 2.1 %dynamic-slice_bitcast_fusion = f32[1664,128]{1,0:T(8,128)} fusion(f32[2,1664,128]{2,1,0:T(8,128)} %bitcast.359, s32[]{:T(128)S(6)} %select_n.76), kind=kLoop, calls=%fused_computation.147 | loop fusion | bytes 1703940 | tf_op jit(solution)/shard_map/jit(dynamic_index_in_dim)/squeeze | solution.py:200
  78.1 5.5 %collective-permute-start.8 = (bf16[3,192,128]{2,1,0:T(8,128)(2,1)S(1)}, bf16[3,192,128]{2,1,0:T(8,128)(2,1)S(1)}, u32[]{:S(2)}, u32[]{:S(2)}) collective-permute-start(bf16[3,192,128]{2,1,0:T(8,128)(2,1)S(1)} %get-tuple-element.152), channel_id=1, source_target_pairs={{0,8},{8,16},{16,24},{24,32},{32,40},{40,48},{48,56},{1,9},{9,17},... | collective-permute-start | bytes 442376 | tf_op jit(solution)/shard_map/ppermute | solution.py:21
  83.6 1.9 %collective-permute-start.9 = (bf16[3,192,128]{2,1,0:T(8,128)(2,1)S(1)}, bf16[3,192,128]{2,1,0:T(8,128)(2,1)}, u32[]{:S(2)}, u32[]{:S(2)}) collective-permute-start(bf16[3,192,128]{2,1,0:T(8,128)(2,1)S(1)} %get-tuple-element.151), channel_id=1, source_target_pairs={{8,0},{16,8},{24,16},{32,24},{40,32},{48,40},{56,48},{9,1},{17,9},... | collective-permute-start | bytes 442376 | tf_op jit(solution)/shard_map/ppermute | solution.py:22
  85.7 4.5 %collective-permute-done.9 = bf16[3,192,128]{2,1,0:T(8,128)(2,1)} collective-permute-done((bf16[3,192,128]{2,1,0:T(8,128)(2,1)S(1)}, bf16[3,192,128]{2,1,0:T(8,128)(2,1)}, u32[]{:S(2)}, u32[]{:S(2)}) %collective-permute-start.9) | collective-permute-done | bytes 147488 | tf_op jit(solution)/shard_map/ppermute | solution.py:22
  91.8 1.3 collective-permute-start.10
  93.5 6.4 %collective-permute-start.11 = (bf16[3,14,192]{2,1,0:T(8,128)(2,1)S(1)}, bf16[3,14,192]{2,1,0:T(8,128)(2,1)S(1)}, u32[]{:S(2)}, u32[]{:S(2)}) collective-permute-start(bf16[3,14,192]{2,1,0:T(8,128)(2,1)S(1)} %copy.74), channel_id=1, source_target_pairs={{0,1},{1,2},{2,3},{3,4},{4,5},{5,6},{6,7},{8,9},{9,10},{10,11},{11... | collective-permute-start | bytes 48392 | tf_op jit(solution)/shard_map/ppermute | solution.py:21
  101.2 2.3 %pad_maximum_fusion.1 = (bf16[192,14,131]{2,0,1:T(8,128)(2,1)S(1)}, bf16[192,14,131]{2,0,1:T(8,128)(2,1)S(1)}) fusion(bf16[192,14,3]{2,0,1:T(8,128)(2,1)S(1)} %bitcast.348, bf16[192,3,128]{2,0,1:T(8,128)(2,1)} %bitcast.138, bf16[192,8,128]{2,0,1:T(8,128)(2,1)S(1)} %get-tuple-element.130, bf16[192,3,128]{2,0,1:T(8,128)(2,1)S(1)} %bitcast.362, ...), kind=kLoop, calls=%fused_computation.81 | loop fusion | flops 5634048 | bytes 2128896 | tf_op jit(solution)/shard_map/concatenate | solution.py:23
  103.9 1.3 bitcast_add_fusion
  105.3 4.4 %collective-permute-start.7 = (f32[416,128]{1,0:T(8,128)S(1)}, f32[416,128]{1,0:T(8,128)S(1)}, u32[]{:S(2)}, u32[]{:S(2)}) collective-permute-start(f32[416,128]{1,0:T(8,128)S(1)} %get-tuple-element.140), channel_id=1, source_target_pairs={{0,65},{1,64},{2,67},{3,66},{4,69},{5,68},{6,71},{7,70},{8,73},{9,... | collective-permute-start | bytes 638984 | tf_op jit(solution)/shard_map/ppermute | solution.py:201
  110.6 9.1 %fusion.148 = f32[192,8,128]{2,0,1:T(8,128)S(1)} fusion(f32[192,8,128]{2,0,1:T(8,128)S(1)} %get-tuple-element.223, bf16[192,8,128]{2,0,1:T(8,128)(2,1)S(1)} %get-tuple-element.130, bf16[192,3,128]{2,0,1:T(8,128)(2,1)S(1)} %bitcast.363, bf16[192,3,128]{2,0,1:T(8,128)(2,1)} %bitcast.138, bf16[192,14,131]{2,0,1:T(8,128)(2,1)S(1)} %get-tuple-element.144, ...), kind=kLoop, calls=%fused_computation.281 | loop fusion | flops 30081024 | bytes 18813696 | tf_op jit(solution)/shard_map/add | solution.py:113
  119.9 6.7 %collective-permute-start.14 = (f32[104,128]{1,0:T(8,128)S(1)}, f32[104,128]{1,0:T(8,128)S(1)}, u32[]{:S(2)}, u32[]{:S(2)}) collective-permute-start(f32[104,128]{1,0:T(8,128)S(1)} %get-tuple-element.156), channel_id=1, source_target_pairs={{0,6},{1,7},{2,4},{3,5},{4,2},{5,3},{6,0},{7,1},{8,14},{9,15},{10,... | collective-permute-start | bytes 159752 | tf_op jit(solution)/shard_map/ppermute | solution.py:201
  127.2 1.4 collective-permute-done.14
  128.6 3.0 %collective-permute-done.13 = f32[104,128]{1,0:T(8,128)S(1)} collective-permute-done((f32[104,128]{1,0:T(8,128)S(1)}, f32[104,128]{1,0:T(8,128)S(1)}, u32[]{:S(2)}, u32[]{:S(2)}) %collective-permute-start.13) | collective-permute-done | bytes 53280 | tf_op jit(solution)/shard_map/ppermute | solution.py:201
  131.8 2.8 %collective-permute-start.16 = (f32[26,128]{1,0:T(8,128)S(1)}, f32[26,128]{1,0:T(8,128)S(1)}, u32[]{:S(2)}, u32[]{:S(2)}) collective-permute-start(f32[26,128]{1,0:T(8,128)S(1)} %get-tuple-element.160), channel_id=1, source_target_pairs={{0,32},{1,33},{2,34},{3,35},{4,36},{5,37},{6,38},{7,39},{8,40},{9,... | collective-permute-start | bytes 39944 | tf_op jit(solution)/shard_map/ppermute | solution.py:201
  135.9 1.5 collective-permute-done.15
  138.1 2.1 %collective-permute-start.19 = (f32[26,128]{1,0:T(8,128)S(1)}, f32[26,128]{1,0:T(8,128)S(1)}, u32[]{:S(2)}, u32[]{:S(2)}) collective-permute-start(f32[26,128]{1,0:T(8,128)S(1)} %get-tuple-element.129), channel_id=1, source_target_pairs={{0,32},{1,33},{2,34},{3,35},{4,36},{5,37},{6,38},{7,39},{8,40},{9,... | collective-permute-start | bytes 39944 | tf_op jit(solution)/shard_map/ppermute | solution.py:218
  140.2 1.2 collective-permute-start.20
  142.2 1.8 collective-permute-done.20
  144.1 2.3 %collective-permute-start.22 = (f32[104,128]{1,0:T(8,128)S(1)}, f32[104,128]{1,0:T(8,128)S(1)}, u32[]{:S(2)}, u32[]{:S(2)}) collective-permute-start(f32[104,128]{1,0:T(8,128)S(1)} %reshape.193), channel_id=1, source_target_pairs={{0,4},{1,5},{2,6},{3,7},{4,0},{5,1},{6,2},{7,3},{8,12},{9,13},{10,... | collective-permute-start | bytes 159752 | tf_op jit(solution)/shard_map/ppermute | solution.py:218
  146.4 1.5 collective-permute-start.23
  148.7 1.9 %collective-permute-done.23 = f32[104,128]{1,0:T(8,128)S(1)} collective-permute-done((f32[104,128]{1,0:T(8,128)S(1)}, f32[104,128]{1,0:T(8,128)S(1)}, u32[]{:S(2)}, u32[]{:S(2)}) %collective-permute-start.23) | collective-permute-done | bytes 53280 | tf_op jit(solution)/shard_map/ppermute | solution.py:218
  151.5 2.6 %collective-permute-start.25 = (f32[416,128]{1,0:T(8,128)S(1)}, f32[416,128]{1,0:T(8,128)S(1)}, u32[]{:S(2)}, u32[]{:S(2)}) collective-permute-start(f32[416,128]{1,0:T(8,128)S(1)} %bitcast.367), channel_id=1, source_target_pairs={{0,1},{1,0},{2,3},{3,2},{4,5},{5,4},{6,7},{7,6},{8,9},{9,8},{10,11... | collective-permute-start | bytes 638984 | tf_op jit(solution)/shard_map/ppermute | solution.py:218
  155.6 4.1 %collective-permute-done.25 = f32[416,128]{1,0:T(8,128)S(1)} collective-permute-done((f32[416,128]{1,0:T(8,128)S(1)}, f32[416,128]{1,0:T(8,128)S(1)}, u32[]{:S(2)}, u32[]{:S(2)}) %collective-permute-start.25) | collective-permute-done | bytes 213024 | tf_op jit(solution)/shard_map/ppermute | solution.py:218
  159.7 2.2 %collective-permute-done.26 = f32[416,128]{1,0:T(8,128)S(1)} collective-permute-done((f32[416,128]{1,0:T(8,128)S(1)}, f32[416,128]{1,0:T(8,128)S(1)}, u32[]{:S(2)}, u32[]{:S(2)}) %collective-permute-start.26) | collective-permute-done | bytes 213024 | tf_op jit(solution)/shard_map/ppermute | solution.py:218
  161.9 8.3 %collective-permute-start.27 = (f32[1664,128]{1,0:T(8,128)S(1)}, f32[1664,128]{1,0:T(8,128)S(1)}, u32[]{:S(2)}, u32[]{:S(2)}) collective-permute-start(f32[1664,128]{1,0:T(8,128)S(1)} %bitcast.342), channel_id=1, source_target_pairs={{0,8},{1,9},{2,10},{3,11},{4,12},{5,13},{6,14},{7,15},{8,0},{9,1},... | collective-permute-start | bytes 2555912 | tf_op jit(solution)/shard_map/ppermute | solution.py:218
  170.3 1.3 copy.76
  (311 shorter events, 37.5 us)
Async XLA Ops:
  1.9 7.5 %collective-permute-start.1 = (bf16[3,192,128]{2,1,0:T(8,128)(2,1)S(1)}, bf16[3,192,128]{2,1,0:T(8,128)(2,1)S(1)}, u32[]{:S(2)}, u32[]{:S(2)}) collective-permute-start(bf16[3,192,128]{2,1,0:T(8,128)(2,1)S(1)} %get-tuple-element.154), channel_id=1, source_target_pairs={{8,0},{16,8},{24,16},{32,24},{40,32},{48,40},{56,48},{9,1},{17,9},... | collective-permute-start | bytes 442376 | tf_op jit(solution)/shard_map/ppermute | solution.py:22
  5.2 5.2 %collective-permute-start = (bf16[3,192,128]{2,1,0:T(8,128)(2,1)S(1)}, bf16[3,192,128]{2,1,0:T(8,128)(2,1)S(1)}, u32[]{:S(2)}, u32[]{:S(2)}) collective-permute-start(bf16[3,192,128]{2,1,0:T(8,128)(2,1)S(1)} %get-tuple-element.153), channel_id=1, source_target_pairs={{0,8},{8,16},{16,24},{24,32},{32,40},{40,48},{48,56},{1,9},{9,17},... | collective-permute-start | bytes 442376 | tf_op jit(solution)/shard_map/ppermute | solution.py:21
  8.4 12.6 %copy-start.13 = (f32[192,1]{0,1:T(1,128)}, f32[192,1]{0,1:T(1,128)S(1)}, u32[]{:S(2)}) copy-start(f32[192,1]{0,1:T(1,128)S(1)} %get-tuple-element.162) | copy-start | bytes 2308
  8.4 12.6 %copy-start.15 = (f32[192,1]{0,1:T(1,128)}, f32[192,1]{0,1:T(1,128)S(1)}, u32[]{:S(2)}) copy-start(f32[192,1]{0,1:T(1,128)S(1)} %get-tuple-element.163) | copy-start | bytes 2308
  8.4 12.6 %copy-start.17 = (f32[192,1]{0,1:T(1,128)}, f32[192,1]{0,1:T(1,128)S(1)}, u32[]{:S(2)}) copy-start(f32[192,1]{0,1:T(1,128)S(1)} %get-tuple-element.164) | copy-start | bytes 2308
  8.4 12.6 %copy-start.19 = (f32[192,1]{0,1:T(1,128)}, f32[192,1]{0,1:T(1,128)S(1)}, u32[]{:S(2)}) copy-start(f32[192,1]{0,1:T(1,128)S(1)} %get-tuple-element.165) | copy-start | bytes 2308
  8.4 12.6 %copy-start.21 = (f32[192,1]{0,1:T(1,128)}, f32[192,1]{0,1:T(1,128)S(1)}, u32[]{:S(2)}) copy-start(f32[192,1]{0,1:T(1,128)S(1)} %get-tuple-element.166) | copy-start | bytes 2308
  8.4 12.6 %copy-start.23 = (f32[192,1]{0,1:T(1,128)}, f32[192,1]{0,1:T(1,128)S(1)}, u32[]{:S(2)}) copy-start(f32[192,1]{0,1:T(1,128)S(1)} %get-tuple-element.167) | copy-start | bytes 2308
  8.4 12.6 %copy-start.25 = (f32[192,1]{0,1:T(1,128)}, f32[192,1]{0,1:T(1,128)S(1)}, u32[]{:S(2)}) copy-start(f32[192,1]{0,1:T(1,128)S(1)} %get-tuple-element.168) | copy-start | bytes 2308
  8.4 12.6 %copy-start.27 = (f32[192,1]{0,1:T(1,128)}, f32[192,1]{0,1:T(1,128)S(1)}, u32[]{:S(2)}) copy-start(f32[192,1]{0,1:T(1,128)S(1)} %get-tuple-element.169) | copy-start | bytes 2308
  8.5 12.6 %copy-start.29 = (f32[192,1]{0,1:T(1,128)}, f32[192,1]{0,1:T(1,128)S(1)}, u32[]{:S(2)}) copy-start(f32[192,1]{0,1:T(1,128)S(1)} %get-tuple-element.170) | copy-start | bytes 2308
  8.5 12.6 %copy-start.31 = (f32[192,1]{0,1:T(1,128)}, f32[192,1]{0,1:T(1,128)S(1)}, u32[]{:S(2)}) copy-start(f32[192,1]{0,1:T(1,128)S(1)} %get-tuple-element.171) | copy-start | bytes 2308
  8.5 12.6 %copy-start.33 = (f32[192,1]{0,1:T(1,128)}, f32[192,1]{0,1:T(1,128)S(1)}, u32[]{:S(2)}) copy-start(f32[192,1]{0,1:T(1,128)S(1)} %get-tuple-element.172) | copy-start | bytes 2308
  8.5 12.6 %copy-start.35 = (f32[192,1]{0,1:T(1,128)}, f32[192,1]{0,1:T(1,128)S(1)}, u32[]{:S(2)}) copy-start(f32[192,1]{0,1:T(1,128)S(1)} %get-tuple-element.173) | copy-start | bytes 2308
  8.5 12.6 %copy-start.37 = (f32[192,1]{0,1:T(1,128)}, f32[192,1]{0,1:T(1,128)S(1)}, u32[]{:S(2)}) copy-start(f32[192,1]{0,1:T(1,128)S(1)} %get-tuple-element.174) | copy-start | bytes 2308
  8.5 12.6 %copy-start.39 = (f32[192,1]{0,1:T(1,128)}, f32[192,1]{0,1:T(1,128)S(1)}, u32[]{:S(2)}) copy-start(f32[192,1]{0,1:T(1,128)S(1)} %get-tuple-element.175) | copy-start | bytes 2308
  8.5 12.6 %copy-start.41 = (f32[192,1]{0,1:T(1,128)}, f32[192,1]{0,1:T(1,128)S(1)}, u32[]{:S(2)}) copy-start(f32[192,1]{0,1:T(1,128)S(1)} %get-tuple-element.176) | copy-start | bytes 2308
  8.5 12.6 %copy-start.43 = (f32[192,1]{0,1:T(1,128)}, f32[192,1]{0,1:T(1,128)S(1)}, u32[]{:S(2)}) copy-start(f32[192,1]{0,1:T(1,128)S(1)} %get-tuple-element.177) | copy-start | bytes 2308
  8.5 12.6 %copy-start.45 = (f32[192,1]{0,1:T(1,128)}, f32[192,1]{0,1:T(1,128)S(1)}, u32[]{:S(2)}) copy-start(f32[192,1]{0,1:T(1,128)S(1)} %get-tuple-element.178) | copy-start | bytes 2308
  8.5 12.6 %copy-start.47 = (f32[192,1]{0,1:T(1,128)}, f32[192,1]{0,1:T(1,128)S(1)}, u32[]{:S(2)}) copy-start(f32[192,1]{0,1:T(1,128)S(1)} %get-tuple-element.179) | copy-start | bytes 2308
  8.6 12.6 %copy-start.49 = (f32[192,1]{0,1:T(1,128)}, f32[192,1]{0,1:T(1,128)S(1)}, u32[]{:S(2)}) copy-start(f32[192,1]{0,1:T(1,128)S(1)} %get-tuple-element.180) | copy-start | bytes 2308
  8.6 12.6 %copy-start.51 = (f32[192,1]{0,1:T(1,128)}, f32[192,1]{0,1:T(1,128)S(1)}, u32[]{:S(2)}) copy-start(f32[192,1]{0,1:T(1,128)S(1)} %get-tuple-element.181) | copy-start | bytes 2308
  11.2 7.2 %collective-permute-start.3 = (bf16[3,14,192]{2,1,0:T(8,128)(2,1)S(1)}, bf16[3,14,192]{2,1,0:T(8,128)(2,1)S(1)}, u32[]{:S(2)}, u32[]{:S(2)}) collective-permute-start(bf16[3,14,192]{2,1,0:T(8,128)(2,1)S(1)} %copy.59), channel_id=1, source_target_pairs={{1,0},{2,1},{3,2},{4,3},{5,4},{6,5},{7,6},{9,8},{10,9},{11,10},{12... | collective-permute-start | bytes 48392 | tf_op jit(solution)/shard_map/ppermute | solution.py:22
  12.9 6.4 %collective-permute-start.2 = (bf16[3,14,192]{2,1,0:T(8,128)(2,1)S(1)}, bf16[3,14,192]{2,1,0:T(8,128)(2,1)S(1)}, u32[]{:S(2)}, u32[]{:S(2)}) collective-permute-start(bf16[3,14,192]{2,1,0:T(8,128)(2,1)S(1)} %copy.57), channel_id=1, source_target_pairs={{0,1},{1,2},{2,3},{3,4},{4,5},{5,6},{6,7},{8,9},{9,10},{10,11},{11... | collective-permute-start | bytes 48392 | tf_op jit(solution)/shard_map/ppermute | solution.py:21
  78.1 25.8 %collective-permute-start.4 = (f32[1664,128]{1,0:T(8,128)}, f32[1664,128]{1,0:T(8,128)}, u32[]{:S(2)}, u32[]{:S(2)}) collective-permute-start(f32[1664,128]{1,0:T(8,128)} %dynamic-slice_bitcast_fusion), channel_id=1, source_target_pairs={{0,8},{1,9},{2,10},{3,11},{4,12},{5,13},{6,14},{7,15},{8,0},{9,1},... | collective-permute-start | bytes 2555912 | tf_op jit(solution)/shard_map/ppermute | solution.py:201
  78.1 7.6 %collective-permute-start.8 = (bf16[3,192,128]{2,1,0:T(8,128)(2,1)S(1)}, bf16[3,192,128]{2,1,0:T(8,128)(2,1)S(1)}, u32[]{:S(2)}, u32[]{:S(2)}) collective-permute-start(bf16[3,192,128]{2,1,0:T(8,128)(2,1)S(1)} %get-tuple-element.152), channel_id=1, source_target_pairs={{0,8},{8,16},{16,24},{24,32},{32,40},{40,48},{48,56},{1,9},{9,17},... | collective-permute-start | bytes 442376 | tf_op jit(solution)/shard_map/ppermute | solution.py:21
  83.6 6.6 %collective-permute-start.9 = (bf16[3,192,128]{2,1,0:T(8,128)(2,1)S(1)}, bf16[3,192,128]{2,1,0:T(8,128)(2,1)}, u32[]{:S(2)}, u32[]{:S(2)}) collective-permute-start(bf16[3,192,128]{2,1,0:T(8,128)(2,1)S(1)} %get-tuple-element.151), channel_id=1, source_target_pairs={{8,0},{16,8},{24,16},{32,24},{40,32},{48,40},{56,48},{9,1},{17,9},... | collective-permute-start | bytes 442376 | tf_op jit(solution)/shard_map/ppermute | solution.py:22
  91.8 8.1 %collective-permute-start.10 = (bf16[3,14,192]{2,1,0:T(8,128)(2,1)S(1)}, bf16[3,14,192]{2,1,0:T(8,128)(2,1)S(1)}, u32[]{:S(2)}, u32[]{:S(2)}) collective-permute-start(bf16[3,14,192]{2,1,0:T(8,128)(2,1)S(1)} %copy.72), channel_id=1, source_target_pairs={{1,0},{2,1},{3,2},{4,3},{5,4},{6,5},{7,6},{9,8},{10,9},{11,10},{12... | collective-permute-start | bytes 48392 | tf_op jit(solution)/shard_map/ppermute | solution.py:22
  93.5 7.3 %collective-permute-start.11 = (bf16[3,14,192]{2,1,0:T(8,128)(2,1)S(1)}, bf16[3,14,192]{2,1,0:T(8,128)(2,1)S(1)}, u32[]{:S(2)}, u32[]{:S(2)}) collective-permute-start(bf16[3,14,192]{2,1,0:T(8,128)(2,1)S(1)} %copy.74), channel_id=1, source_target_pairs={{0,1},{1,2},{2,3},{3,4},{4,5},{5,6},{6,7},{8,9},{9,10},{10,11},{11... | collective-permute-start | bytes 48392 | tf_op jit(solution)/shard_map/ppermute | solution.py:21
  105.3 14.5 %collective-permute-start.7 = (f32[416,128]{1,0:T(8,128)S(1)}, f32[416,128]{1,0:T(8,128)S(1)}, u32[]{:S(2)}, u32[]{:S(2)}) collective-permute-start(f32[416,128]{1,0:T(8,128)S(1)} %get-tuple-element.140), channel_id=1, source_target_pairs={{0,65},{1,64},{2,67},{3,66},{4,69},{5,68},{6,71},{7,70},{8,73},{9,... | collective-permute-start | bytes 638984 | tf_op jit(solution)/shard_map/ppermute | solution.py:201
  109.6 10.1 %collective-permute-start.6 = (f32[416,128]{1,0:T(8,128)S(1)}, f32[416,128]{1,0:T(8,128)S(1)}, u32[]{:S(2)}, u32[]{:S(2)}) collective-permute-start(f32[416,128]{1,0:T(8,128)S(1)} %get-tuple-element.141), channel_id=1, source_target_pairs={{0,1},{1,0},{2,3},{3,2},{4,5},{5,4},{6,7},{7,6},{8,9},{9,8},{10,11... | collective-permute-start | bytes 638984 | tf_op jit(solution)/shard_map/ppermute | solution.py:201
  109.9 9.9 %collective-permute-start.5 = (f32[416,128]{1,0:T(8,128)S(1)}, f32[416,128]{1,0:T(8,128)S(1)}, u32[]{:S(2)}, u32[]{:S(2)}) collective-permute-start(f32[416,128]{1,0:T(8,128)S(1)} %get-tuple-element.139), channel_id=1, source_target_pairs={{0,64},{1,65},{2,66},{3,67},{4,68},{5,69},{6,70},{7,71},{8,72},{9,... | collective-permute-start | bytes 638984 | tf_op jit(solution)/shard_map/ppermute | solution.py:201
  119.9 8.8 %collective-permute-start.14 = (f32[104,128]{1,0:T(8,128)S(1)}, f32[104,128]{1,0:T(8,128)S(1)}, u32[]{:S(2)}, u32[]{:S(2)}) collective-permute-start(f32[104,128]{1,0:T(8,128)S(1)} %get-tuple-element.156), channel_id=1, source_target_pairs={{0,6},{1,7},{2,4},{3,5},{4,2},{5,3},{6,0},{7,1},{8,14},{9,15},{10,... | collective-permute-start | bytes 159752 | tf_op jit(solution)/shard_map/ppermute | solution.py:201
  126.6 5.1 %collective-permute-start.13 = (f32[104,128]{1,0:T(8,128)S(1)}, f32[104,128]{1,0:T(8,128)S(1)}, u32[]{:S(2)}, u32[]{:S(2)}) collective-permute-start(f32[104,128]{1,0:T(8,128)S(1)} %get-tuple-element.157), channel_id=1, source_target_pairs={{0,4},{1,5},{2,6},{3,7},{4,0},{5,1},{6,2},{7,3},{8,12},{9,13},{10,... | collective-permute-start | bytes 159752 | tf_op jit(solution)/shard_map/ppermute | solution.py:201
  126.6 5.1 %collective-permute-start.12 = (f32[104,128]{1,0:T(8,128)S(1)}, f32[104,128]{1,0:T(8,128)S(1)}, u32[]{:S(2)}, u32[]{:S(2)}) collective-permute-start(f32[104,128]{1,0:T(8,128)S(1)} %get-tuple-element.155), channel_id=1, source_target_pairs={{0,2},{1,3},{2,0},{3,1},{4,6},{5,7},{6,4},{7,5},{8,10},{9,11},{10,... | collective-permute-start | bytes 159752 | tf_op jit(solution)/shard_map/ppermute | solution.py:201
  131.7 3.9 %collective-permute-start.17 = (f32[26,128]{1,0:T(8,128)S(1)}, f32[26,128]{1,0:T(8,128)S(1)}, u32[]{:S(2)}, u32[]{:S(2)}) collective-permute-start(f32[26,128]{1,0:T(8,128)S(1)} %get-tuple-element.159), channel_id=1, source_target_pairs={{0,48},{1,49},{2,50},{3,51},{4,52},{5,53},{6,54},{7,55},{8,56},{9,... | collective-permute-start | bytes 39944 | tf_op jit(solution)/shard_map/ppermute | solution.py:201
  131.8 4.2 %collective-permute-start.16 = (f32[26,128]{1,0:T(8,128)S(1)}, f32[26,128]{1,0:T(8,128)S(1)}, u32[]{:S(2)}, u32[]{:S(2)}) collective-permute-start(f32[26,128]{1,0:T(8,128)S(1)} %get-tuple-element.160), channel_id=1, source_target_pairs={{0,32},{1,33},{2,34},{3,35},{4,36},{5,37},{6,38},{7,39},{8,40},{9,... | collective-permute-start | bytes 39944 | tf_op jit(solution)/shard_map/ppermute | solution.py:201
  134.5 2.9 %collective-permute-start.15 = (f32[26,128]{1,0:T(8,128)S(1)}, f32[26,128]{1,0:T(8,128)S(1)}, u32[]{:S(2)}, u32[]{:S(2)}) collective-permute-start(f32[26,128]{1,0:T(8,128)S(1)} %get-tuple-element.158), channel_id=1, source_target_pairs={{0,16},{1,17},{2,18},{3,19},{4,20},{5,21},{6,22},{7,23},{8,24},{9,... | collective-permute-start | bytes 39944 | tf_op jit(solution)/shard_map/ppermute | solution.py:201
  137.5 3.9 %collective-permute-start.18 = (f32[26,128]{1,0:T(8,128)S(1)}, f32[26,128]{1,0:T(8,128)S(1)}, u32[]{:S(2)}, u32[]{:S(2)}) collective-permute-start(f32[26,128]{1,0:T(8,128)S(1)} %get-tuple-element.129), channel_id=1, source_target_pairs={{0,16},{1,17},{2,18},{3,19},{4,20},{5,21},{6,22},{7,23},{8,24},{9,... | collective-permute-start | bytes 39944 | tf_op jit(solution)/shard_map/ppermute | solution.py:218
  138.1 4.1 %collective-permute-start.19 = (f32[26,128]{1,0:T(8,128)S(1)}, f32[26,128]{1,0:T(8,128)S(1)}, u32[]{:S(2)}, u32[]{:S(2)}) collective-permute-start(f32[26,128]{1,0:T(8,128)S(1)} %get-tuple-element.129), channel_id=1, source_target_pairs={{0,32},{1,33},{2,34},{3,35},{4,36},{5,37},{6,38},{7,39},{8,40},{9,... | collective-permute-start | bytes 39944 | tf_op jit(solution)/shard_map/ppermute | solution.py:218
  140.2 3.8 %collective-permute-start.20 = (f32[26,128]{1,0:T(8,128)S(1)}, f32[26,128]{1,0:T(8,128)S(1)}, u32[]{:S(2)}, u32[]{:S(2)}) collective-permute-start(f32[26,128]{1,0:T(8,128)S(1)} %get-tuple-element.129), channel_id=1, source_target_pairs={{0,48},{1,49},{2,50},{3,51},{4,52},{5,53},{6,54},{7,55},{8,56},{9,... | collective-permute-start | bytes 39944 | tf_op jit(solution)/shard_map/ppermute | solution.py:218
  144.0 4.0 %collective-permute-start.21 = (f32[104,128]{1,0:T(8,128)S(1)}, f32[104,128]{1,0:T(8,128)S(1)}, u32[]{:S(2)}, u32[]{:S(2)}) collective-permute-start(f32[104,128]{1,0:T(8,128)S(1)} %reshape.193), channel_id=1, source_target_pairs={{0,2},{1,3},{2,0},{3,1},{4,6},{5,7},{6,4},{7,5},{8,10},{9,11},{10,... | collective-permute-start | bytes 159752 | tf_op jit(solution)/shard_map/ppermute | solution.py:218
  144.1 4.6 %collective-permute-start.22 = (f32[104,128]{1,0:T(8,128)S(1)}, f32[104,128]{1,0:T(8,128)S(1)}, u32[]{:S(2)}, u32[]{:S(2)}) collective-permute-start(f32[104,128]{1,0:T(8,128)S(1)} %reshape.193), channel_id=1, source_target_pairs={{0,4},{1,5},{2,6},{3,7},{4,0},{5,1},{6,2},{7,3},{8,12},{9,13},{10,... | collective-permute-start | bytes 159752 | tf_op jit(solution)/shard_map/ppermute | solution.py:218
  146.4 4.2 %collective-permute-start.23 = (f32[104,128]{1,0:T(8,128)S(1)}, f32[104,128]{1,0:T(8,128)S(1)}, u32[]{:S(2)}, u32[]{:S(2)}) collective-permute-start(f32[104,128]{1,0:T(8,128)S(1)} %reshape.193), channel_id=1, source_target_pairs={{0,6},{1,7},{2,4},{3,5},{4,2},{5,3},{6,0},{7,1},{8,14},{9,15},{10,... | collective-permute-start | bytes 159752 | tf_op jit(solution)/shard_map/ppermute | solution.py:218
  150.6 5.0 %collective-permute-start.24 = (f32[416,128]{1,0:T(8,128)S(1)}, f32[416,128]{1,0:T(8,128)S(1)}, u32[]{:S(2)}, u32[]{:S(2)}) collective-permute-start(f32[416,128]{1,0:T(8,128)S(1)} %bitcast.366), channel_id=1, source_target_pairs={{0,64},{1,65},{2,66},{3,67},{4,68},{5,69},{6,70},{7,71},{8,72},{9,... | collective-permute-start | bytes 638984 | tf_op jit(solution)/shard_map/ppermute | solution.py:218
  151.5 8.2 %collective-permute-start.25 = (f32[416,128]{1,0:T(8,128)S(1)}, f32[416,128]{1,0:T(8,128)S(1)}, u32[]{:S(2)}, u32[]{:S(2)}) collective-permute-start(f32[416,128]{1,0:T(8,128)S(1)} %bitcast.367), channel_id=1, source_target_pairs={{0,1},{1,0},{2,3},{3,2},{4,5},{5,4},{6,7},{7,6},{8,9},{9,8},{10,11... | collective-permute-start | bytes 638984 | tf_op jit(solution)/shard_map/ppermute | solution.py:218
  154.1 7.8 %collective-permute-start.26 = (f32[416,128]{1,0:T(8,128)S(1)}, f32[416,128]{1,0:T(8,128)S(1)}, u32[]{:S(2)}, u32[]{:S(2)}) collective-permute-start(f32[416,128]{1,0:T(8,128)S(1)} %bitcast.368), channel_id=1, source_target_pairs={{0,65},{1,64},{2,67},{3,66},{4,69},{5,68},{6,71},{7,70},{8,73},{9,... | collective-permute-start | bytes 638984 | tf_op jit(solution)/shard_map/ppermute | solution.py:218
  161.9 10.3 %collective-permute-start.27 = (f32[1664,128]{1,0:T(8,128)S(1)}, f32[1664,128]{1,0:T(8,128)S(1)}, u32[]{:S(2)}, u32[]{:S(2)}) collective-permute-start(f32[1664,128]{1,0:T(8,128)S(1)} %bitcast.342), channel_id=1, source_target_pairs={{0,8},{1,9},{2,10},{3,11},{4,12},{5,13},{6,14},{7,15},{8,0},{9,1},... | collective-permute-start | bytes 2555912 | tf_op jit(solution)/shard_map/ppermute | solution.py:218
  (76 other events, 568.5 us)

commit v5 on v4

--- a/solution.py
+++ b/solution.py
@@ -150,15 +150,34 @@
 LANES = 128
 
 
+def tile_order(x):
+    rows, cols = x.shape
+    x = x.reshape(rows // 8, 8, cols // LANES, LANES).transpose(0, 2, 1, 3)
+    return x.reshape(rows * cols // LANES, LANES)
+
+
+def from_tile_order(x, shape):
+    rows, cols = shape
+    x = x.reshape(rows // 8, cols // LANES, 8, LANES).transpose(0, 2, 1, 3)
+    return x.reshape(rows, cols)
+
+
+def tiled(shape):
+    return len(shape) == 2 and shape[0] % 8 == 0 and shape[1] % LANES == 0
+
+
 def pack_rows(parts, multiple):
     shapes, rows = [], []
     for part in parts:
+        shapes.append(part.shape)
+        if tiled(part.shape):
+            rows.append(tile_order(part))
+            continue
         flat = part.reshape(-1)
         size = flat.shape[0]
         padded_rows = -(-size // (8 * LANES)) * 8
         flat = jnp.pad(flat, (0, padded_rows * LANES - size))
         rows.append(flat.reshape(padded_rows, LANES))
-        shapes.append(part.shape)
     total = sum(r.shape[0] for r in rows)
     extra = -total % multiple
     if extra:
@@ -171,7 +190,11 @@
     for shape in shapes:
         size = math.prod(shape)
         padded_rows = -(-size // (8 * LANES)) * 8
-        out.append(buffer[at : at + padded_rows].reshape(-1)[:size].reshape(shape))
+        piece = buffer[at : at + padded_rows]
+        if tiled(shape):
+            out.append(from_tile_order(piece, shape))
+        else:
+            out.append(piece.reshape(-1)[:size].reshape(shape))
         at += padded_rows
     return out
 
@@ -269,7 +292,7 @@
     vectors = [convbias_grad, gain_grad, normbias_grad, expbias_grad, projbias_grad]
     vectors += [layerscale_grad, latbias_grad, clsbias_grad, loss_sum.reshape(1)]
     joined = jnp.concatenate(vectors)
-    parts = [joined, kernel_grad, expand_grad, project_grad, lateral_grad, classify_grad]
+    parts = [joined, kernel_grad, expand_grad, project_grad.T, lateral_grad, classify_grad]
     count = math.prod(lax.axis_size(a) for a in axes)
     buffer, shapes = pack_rows(parts, count * 2)
     cell_count = micro_count * height * width * lax.axis_size("row") * lax.axis_size("col")
@@ -285,6 +308,7 @@
     joined, kernel_grad, expand_grad, project_grad, lateral_grad, classify_grad = unpack_rows(
         buffer, shapes
     )
+    project_grad = project_grad.T
     sizes = [v.shape[0] for v in vectors]
     cuts = [sum(sizes[:k]) for k in range(len(sizes) + 1)]
     (

time: 181 us -> 174 us (0.961)
  local copies, waits for them, and re-layouts: 35.1 us -> 28.4 us
    reshape x4 -> x1, local copies, waits for them, and re-layouts: 5.23 us -> 1.08 us  [pack_rows(): rows.append(flat.reshape(padded_rows, LANES))]
    another operation x4 -> x1, local copies, waits for them, and re-layouts: 2.04 us -> 0.12 us  [unpack_rows(): out.append(piece.reshape(-1)[:size].reshape(shape))]
    unnamed x202 -> x271, local copies, waits for them, and re-layouts: 9.86 us -> 8.94 us
where the time goes in v5:
time: 174 us; the launch traced here: 173 us
  starting transfers between devices  63.9 us (37%)
  other arithmetic  38.2 us (22%)
  local copies, waits for them, and re-layouts  28.4 us (16%)
  waiting for transfers between devices  26 us (15%)
  matrix products  13.8 us (8%)
  between operations  3.12 us (2%)
    ppermute x4, starting transfers between devices, padded_2(): before = jnp.transpose(lax.ppermute(last, axis, up), order)  20.5 us
    ppermute x10, starting transfers between devices, butterfly_psum(): other = lax.ppermute(buffer, axes, pairs)  20 us
    ppermute x10, starting transfers between devices, butterfly_psum(): total = total + lax.ppermute(send, axes, pairs)  15.7 us
    dot_general x12, matrix products, product(): jnp.einsum(form, left_side, right_side, preferred_element_type=jnp.float32)  13.8 us
    ppermute x10, waiting for transfers between devices, butterfly_psum(): other = lax.ppermute(buffer, axes, pairs)  12.8 us
    reduce_sum x4, other arithmetic, conv_backward(): columns.append(jnp.sum(window * conv_float, axis=(1, 2)))  12.2 us
    add x1, other arithmetic, conv_backward(): grad_out.astype(jnp.float32)  9.27 us
    reduce_sum x1, other arithmetic, encoder_forward(): centre = conv - jnp.mean(conv, axis=0, keepdims=True)  9.01 us
  transfers between devices with their start and end apart: 28, of which 18 were waited for; matrix products, arithmetic and copies ran while one was open for 10% of the time, Pallas kernels for 0%

profile of v5, /device:TPU:1, one launch (start us, length us, event | category | flops | bytes accessed | tf_op | source)
XLA Modules:
  0.0 173.4 jit_solution(6423767548858648807)
XLA Ops:
  0.7 1.1 copy-done
  1.9 3.3 %collective-permute-start.1 = (bf16[3,192,128]{2,1,0:T(8,128)(2,1)S(1)}, bf16[3,192,128]{2,1,0:T(8,128)(2,1)S(1)}, u32[]{:S(2)}, u32[]{:S(2)}) collective-permute-start(bf16[3,192,128]{2,1,0:T(8,128)(2,1)S(1)} %get-tuple-element.154), channel_id=1, source_target_pairs={{8,0},{16,8},{24,16},{32,24},{40,32},{48,40},{56,48},{9,1},{17,9},... | collective-permute-start | bytes 442376 | tf_op jit(solution)/shard_map/ppermute | solution.py:22
  5.2 3.1 %collective-permute-start = (bf16[3,192,128]{2,1,0:T(8,128)(2,1)S(1)}, bf16[3,192,128]{2,1,0:T(8,128)(2,1)S(1)}, u32[]{:S(2)}, u32[]{:S(2)}) collective-permute-start(bf16[3,192,128]{2,1,0:T(8,128)(2,1)S(1)} %get-tuple-element.153), channel_id=1, source_target_pairs={{0,8},{8,16},{16,24},{24,32},{32,40},{40,48},{48,56},{1,9},{9,17},... | collective-permute-start | bytes 442376 | tf_op jit(solution)/shard_map/ppermute | solution.py:21
  11.2 1.3 collective-permute-start.3
  12.9 5.5 %collective-permute-start.2 = (bf16[3,14,192]{2,1,0:T(8,128)(2,1)S(1)}, bf16[3,14,192]{2,1,0:T(8,128)(2,1)S(1)}, u32[]{:S(2)}, u32[]{:S(2)}) collective-permute-start(bf16[3,14,192]{2,1,0:T(8,128)(2,1)S(1)} %copy.55), channel_id=1, source_target_pairs={{0,1},{1,2},{2,3},{3,4},{4,5},{5,6},{6,7},{8,9},{9,10},{10,11},{11... | collective-permute-start | bytes 48392 | tf_op jit(solution)/shard_map/ppermute | solution.py:21
  19.7 1.3 pad_maximum_fusion
  21.4 9.0 %fusion.181 = (f32[8,128]{1,0:T(8,128)S(1)}, f32[192,8,128]{2,0,1:T(8,128)S(1)}) fusion(f32[192]{0:T(256)S(1)} %copy-done.127, bf16[192,14,131]{2,0,1:T(8,128)(2,1)S(1)} %get-tuple-element.147, f32[192]{0:T(256)} %bitcast.57, f32[192]{0:T(256)} %bitcast.56, f32[192]{0:T(256)S(1)} %bitcast.408, bf16[192,3,128]{2,0,1:T(8,128)(2,1)S(1)} %bitcast.385, ...), kind=kLoop, calls=%fused_computation.389 | loop fusion | flops 30276608 | bytes 18032128 | tf_op jit(solution)/shard_map/reduce_sum | solution.py:65
  34.4 1.9 %convert_reduce_fusion.2 = (f32[512]{0:T(512)}, bf16[512,8,128]{0,2,1:T(8,128)(2,1)S(1)}) fusion(f32[8,128,512]{2,1,0:T(8,128)S(1)} %get-tuple-element.220, f32[512]{0:T(512)S(1)} %copy-done.123, bf16[16,8,128]{2,0,1:T(8,128)(2,1)S(1)} %get-tuple-element.132, bf16[512,16]{0,1:T(8,128)(2,1)S(1)} %copy-done.12), kind=kOutput, calls=%fused_computation.78 | convolution fusion | flops 23592448 | bytes 3198976 | tf_op jit(solution)/shard_map/khw,lk->lhw/dot_general | solution.py:34
  36.2 1.3 convert_reduce_fusion.3
  37.5 2.4 %convert_reduce_fusion.1 = (f32[768]{0:T(1024)}, bf16[768,8,128]{0,2,1:T(8,128)(2,1)S(1)}) fusion(f32[8,128,768]{2,1,0:T(8,128)S(1)} %get-tuple-element.216, f32[768]{0:T(1024)S(1)} %copy-done.92, bf16[192,8,128]{2,0,1:T(8,128)(2,1)S(1)} %get-tuple-element.134, bf16[768,192]{0,1:T(8,128)(2,1)S(1)} %copy-done.9), kind=kOutput, calls=%fused_computation.64 | convolution fusion | flops 312212736 | bytes 5412864 | tf_op jit(solution)/shard_map/chw,dc->dhw/dot_general | solution.py:34
  39.9 1.4 fusion.147
  41.3 4.1 %fusion.117 = (f32[192]{0:T(256)}, f32[192]{0:T(256)}, f32[192]{0:T(256)}, f32[192]{0:T(256)}, f32[192]{0:T(256)}, /*index=5*/f32[192]{0:T(256)}, f32[192]{0:T(2...) fusion(bf16[192,14,131]{2,0,1:T(8,128)(2,1)S(1)} %get-tuple-ele, ...), kind=kLoop, calls=%fused_computation.238 | loop fusion | flops 12382848 | bytes 9074944 | tf_op jit(solution)/shard_map/reduce_sum | solution.py:122
  45.3 4.4 %fusion.121 = (f32[192]{0:T(256)}, f32[192]{0:T(256)}, f32[192]{0:T(256)}, f32[192]{0:T(256)}, f32[192]{0:T(256)}, /*index=5*/f32[192]{0:T(256)}, f32[192]{0:T(2...) fusion(bf16[192,8,128]{2,0,1:T(8,128)(2,1)S(1)} %get-tuple-elem, ...), kind=kLoop, calls=%fused_computation.242 | loop fusion | flops 11006400 | bytes 7485696 | tf_op jit(solution)/shard_map/reduce_sum | solution.py:122
  49.7 1.1 fusion.75
  50.8 2.7 %fusion.120 = (f32[192]{0:T(256)}, f32[192]{0:T(256)}, f32[192]{0:T(256)}, f32[192]{0:T(256)}, f32[192]{0:T(256)}, /*index=5*/f32[192]{0:T(256)}, f32[192]{0:T(256)}, f32[192]{0:T(256)}, f32[192]{0:T(256)}, f32[192]{0:T(256)}) fusion(bf16[192,8,128]{2,0,1:T(8,128)(2,1)S(1)} %get-tuple-element.130, bf16[192,14,131]{2,0,1:T(8,128)(2,1)S(1)} %get-tuple-element.147, ...), kind=kLoop, calls=%fused_computation.241 | loop fusion | flops 7272576 | bytes 2661888 | tf_op jit(solution)/shard_map/reduce_sum | solution.py:122
  54.0 1.3 fusion.189
  55.7 1.1 fusion.190
  56.8 1.2 convolution_bitcast_fusion
  60.3 4.3 %stack.199 = f32[192,49]{0,1:T(8,128)S(1)} concatenate(f32[192,1]{0,1:T(1,128)} %bitcast.512, f32[192,1]{0,1:T(1,128)} %bitcast.511, f32[192,1]{0,1:T(1,128)} %bitcast.510, f32[192,1]{0,1:T(1,128)S(1)} %bitcast.506, f32[192,1]{0,1:T(1,128)S(1)} %bitcast.483, f32[192,1]{0,1:T(1,128)S(1)} %bitcast.484, f32[192,1]{0,1:T(1,128)S(1)} %bitcast.485, f32[192,1]{0,1:T(1,128)} %bitcast.514, ...), dimensions={1} | concatenate | bytes 75264 | tf_op jit(solution)/shard_map/stack | solution.py:123
  64.9 1.1 reshape.212
  70.4 2.1 %dynamic-slice_bitcast_fusion = f32[1664,128]{1,0:T(8,128)} fusion(f32[2,1664,128]{2,1,0:T(8,128)} %bitcast.393, s32[]{:T(128)S(6)} %select_n.76), kind=kLoop, calls=%fused_computation.144 | loop fusion | bytes 1703940 | tf_op jit(solution)/shard_map/jit(dynamic_index_in_dim)/squeeze | solution.py:223
  72.5 5.5 %collective-permute-start.8 = (bf16[3,192,128]{2,1,0:T(8,128)(2,1)S(1)}, bf16[3,192,128]{2,1,0:T(8,128)(2,1)}, u32[]{:S(2)}, u32[]{:S(2)}) collective-permute-start(bf16[3,192,128]{2,1,0:T(8,128)(2,1)S(1)} %get-tuple-element.152), channel_id=1, source_target_pairs={{0,8},{8,16},{16,24},{24,32},{32,40},{40,48},{48,56},{1,9},{9,17},... | collective-permute-start | bytes 442376 | tf_op jit(solution)/shard_map/ppermute | solution.py:21
  78.1 1.9 %collective-permute-start.9 = (bf16[3,192,128]{2,1,0:T(8,128)(2,1)S(1)}, bf16[3,192,128]{2,1,0:T(8,128)(2,1)}, u32[]{:S(2)}, u32[]{:S(2)}) collective-permute-start(bf16[3,192,128]{2,1,0:T(8,128)(2,1)S(1)} %get-tuple-element.151), channel_id=1, source_target_pairs={{8,0},{16,8},{24,16},{32,24},{40,32},{48,40},{56,48},{9,1},{17,9},... | collective-permute-start | bytes 442376 | tf_op jit(solution)/shard_map/ppermute | solution.py:22
  80.1 4.5 %collective-permute-done.9 = bf16[3,192,128]{2,1,0:T(8,128)(2,1)} collective-permute-done((bf16[3,192,128]{2,1,0:T(8,128)(2,1)S(1)}, bf16[3,192,128]{2,1,0:T(8,128)(2,1)}, u32[]{:S(2)}, u32[]{:S(2)}) %collective-permute-start.9) | collective-permute-done | bytes 147488 | tf_op jit(solution)/shard_map/ppermute | solution.py:22
  84.6 1.1 pad_maximum_fusion.3
  86.4 1.3 collective-permute-start.10
  88.1 6.3 %collective-permute-start.11 = (bf16[3,14,192]{2,1,0:T(8,128)(2,1)S(1)}, bf16[3,14,192]{2,1,0:T(8,128)(2,1)S(1)}, u32[]{:S(2)}, u32[]{:S(2)}) collective-permute-start(bf16[3,14,192]{2,1,0:T(8,128)(2,1)S(1)} %copy.71), channel_id=1, source_target_pairs={{0,1},{1,2},{2,3},{3,4},{4,5},{5,6},{6,7},{8,9},{9,10},{10,11},{11... | collective-permute-start | bytes 48392 | tf_op jit(solution)/shard_map/ppermute | solution.py:21
  95.7 2.4 %pad_maximum_fusion.1 = (bf16[192,14,131]{2,0,1:T(8,128)(2,1)S(1)}, bf16[192,14,131]{2,0,1:T(8,128)(2,1)S(1)}) fusion(bf16[192,14,3]{2,0,1:T(8,128)(2,1)S(1)} %bitcast.380, bf16[192,3,128]{2,0,1:T(8,128)(2,1)} %bitcast.147, bf16[192,8,128]{2,0,1:T(8,128)(2,1)S(1)} %get-tuple-element.130, bf16[192,3,128]{2,0,1:T(8,128)(2,1)} %bitcast.145, ...), kind=kLoop, calls=%fused_computation.81 | loop fusion | flops 5634048 | bytes 2128896 | tf_op jit(solution)/shard_map/concatenate | solution.py:23
  98.5 1.3 bitcast_add_fusion
  99.8 4.4 %collective-permute-start.7 = (f32[416,128]{1,0:T(8,128)S(1)}, f32[416,128]{1,0:T(8,128)S(1)}, u32[]{:S(2)}, u32[]{:S(2)}) collective-permute-start(f32[416,128]{1,0:T(8,128)S(1)} %get-tuple-element.140), channel_id=1, source_target_pairs={{0,65},{1,64},{2,67},{3,66},{4,69},{5,68},{6,71},{7,70},{8,73},{9,... | collective-permute-start | bytes 638984 | tf_op jit(solution)/shard_map/ppermute | solution.py:224
  105.2 9.3 %fusion.148 = f32[192,8,128]{2,0,1:T(8,128)S(1)} fusion(f32[192,8,128]{2,0,1:T(8,128)S(1)} %get-tuple-element.223, bf16[192,8,128]{2,0,1:T(8,128)(2,1)S(1)} %get-tuple-element.130, bf16[192,3,128]{2,0,1:T(8,128)(2,1)} %bitcast.145, bf16[192,3,128]{2,0,1:T(8,128)(2,1)} %bitcast.147, bf16[192,14,131]{2,0,1:T(8,128)(2,1)S(1)} %get-tuple-element.144, ...), kind=kLoop, calls=%fused_computation.278 | loop fusion | flops 30081024 | bytes 18813696 | tf_op jit(solution)/shard_map/add | solution.py:113
  114.6 6.7 %collective-permute-start.14 = (f32[104,128]{1,0:T(8,128)S(1)}, f32[104,128]{1,0:T(8,128)S(1)}, u32[]{:S(2)}, u32[]{:S(2)}) collective-permute-start(f32[104,128]{1,0:T(8,128)S(1)} %get-tuple-element.156), channel_id=1, source_target_pairs={{0,6},{1,7},{2,4},{3,5},{4,2},{5,3},{6,0},{7,1},{8,14},{9,15},{10,... | collective-permute-start | bytes 159752 | tf_op jit(solution)/shard_map/ppermute | solution.py:224
  121.9 1.4 collective-permute-done.14
  123.4 3.0 %collective-permute-done.13 = f32[104,128]{1,0:T(8,128)S(1)} collective-permute-done((f32[104,128]{1,0:T(8,128)S(1)}, f32[104,128]{1,0:T(8,128)S(1)}, u32[]{:S(2)}, u32[]{:S(2)}) %collective-permute-start.13) | collective-permute-done | bytes 53280 | tf_op jit(solution)/shard_map/ppermute | solution.py:224
  126.5 2.6 %collective-permute-start.16 = (f32[26,128]{1,0:T(8,128)S(1)}, f32[26,128]{1,0:T(8,128)S(1)}, u32[]{:S(2)}, u32[]{:S(2)}) collective-permute-start(f32[26,128]{1,0:T(8,128)S(1)} %get-tuple-element.160), channel_id=1, source_target_pairs={{0,32},{1,33},{2,34},{3,35},{4,36},{5,37},{6,38},{7,39},{8,40},{9,... | collective-permute-start | bytes 39944 | tf_op jit(solution)/shard_map/ppermute | solution.py:224
  130.7 1.3 collective-permute-done.15
  132.7 2.1 %collective-permute-start.19 = (f32[26,128]{1,0:T(8,128)S(1)}, f32[26,128]{1,0:T(8,128)S(1)}, u32[]{:S(2)}, u32[]{:S(2)}) collective-permute-start(f32[26,128]{1,0:T(8,128)S(1)} %get-tuple-element.129), channel_id=1, source_target_pairs={{0,32},{1,33},{2,34},{3,35},{4,36},{5,37},{6,38},{7,39},{8,40},{9,... | collective-permute-start | bytes 39944 | tf_op jit(solution)/shard_map/ppermute | solution.py:241
  134.7 1.2 collective-permute-start.20
  136.8 1.8 %collective-permute-done.20 = f32[26,128]{1,0:T(8,128)S(1)} collective-permute-done((f32[26,128]{1,0:T(8,128)S(1)}, f32[26,128]{1,0:T(8,128)S(1)}, u32[]{:S(2)}, u32[]{:S(2)}) %collective-permute-start.20) | collective-permute-done | bytes 13344 | tf_op jit(solution)/shard_map/ppermute | solution.py:241
  138.6 2.3 %collective-permute-start.22 = (f32[104,128]{1,0:T(8,128)S(1)}, f32[104,128]{1,0:T(8,128)S(1)}, u32[]{:S(2)}, u32[]{:S(2)}) collective-permute-start(f32[104,128]{1,0:T(8,128)S(1)} %reshape.217), channel_id=1, source_target_pairs={{0,4},{1,5},{2,6},{3,7},{4,0},{5,1},{6,2},{7,3},{8,12},{9,13},{10,... | collective-permute-start | bytes 159752 | tf_op jit(solution)/shard_map/ppermute | solution.py:241
  141.0 1.5 collective-permute-start.23
  143.2 1.9 %collective-permute-done.23 = f32[104,128]{1,0:T(8,128)S(1)} collective-permute-done((f32[104,128]{1,0:T(8,128)S(1)}, f32[104,128]{1,0:T(8,128)S(1)}, u32[]{:S(2)}, u32[]{:S(2)}) %collective-permute-start.23) | collective-permute-done | bytes 53280 | tf_op jit(solution)/shard_map/ppermute | solution.py:241
  145.9 2.6 %collective-permute-start.25 = (f32[416,128]{1,0:T(8,128)S(1)}, f32[416,128]{1,0:T(8,128)S(1)}, u32[]{:S(2)}, u32[]{:S(2)}) collective-permute-start(f32[416,128]{1,0:T(8,128)S(1)} %bitcast.399), channel_id=1, source_target_pairs={{0,1},{1,0},{2,3},{3,2},{4,5},{5,4},{6,7},{7,6},{8,9},{9,8},{10,11... | collective-permute-start | bytes 638984 | tf_op jit(solution)/shard_map/ppermute | solution.py:241
  150.0 4.2 %collective-permute-done.25 = f32[416,128]{1,0:T(8,128)S(1)} collective-permute-done((f32[416,128]{1,0:T(8,128)S(1)}, f32[416,128]{1,0:T(8,128)S(1)}, u32[]{:S(2)}, u32[]{:S(2)}) %collective-permute-start.25) | collective-permute-done | bytes 213024 | tf_op jit(solution)/shard_map/ppermute | solution.py:241
  154.2 2.2 %collective-permute-done.26 = f32[416,128]{1,0:T(8,128)S(1)} collective-permute-done((f32[416,128]{1,0:T(8,128)S(1)}, f32[416,128]{1,0:T(8,128)S(1)}, u32[]{:S(2)}, u32[]{:S(2)}) %collective-permute-start.26) | collective-permute-done | bytes 213024 | tf_op jit(solution)/shard_map/ppermute | solution.py:241
  156.4 8.2 %collective-permute-start.27 = (f32[1664,128]{1,0:T(8,128)S(1)}, f32[1664,128]{1,0:T(8,128)S(1)}, u32[]{:S(2)}, u32[]{:S(2)}) collective-permute-start(f32[1664,128]{1,0:T(8,128)S(1)} %bitcast.374), channel_id=1, source_target_pairs={{0,8},{1,9},{2,10},{3,11},{4,12},{5,13},{6,14},{7,15},{8,0},{9,1},... | collective-permute-start | bytes 2555912 | tf_op jit(solution)/shard_map/ppermute | solution.py:241
  164.6 1.3 copy.73
  167.9 1.1 fusion.183
  (374 shorter events, 32.2 us)
Async XLA Ops:
  1.9 7.5 %collective-permute-start.1 = (bf16[3,192,128]{2,1,0:T(8,128)(2,1)S(1)}, bf16[3,192,128]{2,1,0:T(8,128)(2,1)S(1)}, u32[]{:S(2)}, u32[]{:S(2)}) collective-permute-start(bf16[3,192,128]{2,1,0:T(8,128)(2,1)S(1)} %get-tuple-element.154), channel_id=1, source_target_pairs={{8,0},{16,8},{24,16},{32,24},{40,32},{48,40},{56,48},{9,1},{17,9},... | collective-permute-start | bytes 442376 | tf_op jit(solution)/shard_map/ppermute | solution.py:22
  5.2 5.2 %collective-permute-start = (bf16[3,192,128]{2,1,0:T(8,128)(2,1)S(1)}, bf16[3,192,128]{2,1,0:T(8,128)(2,1)S(1)}, u32[]{:S(2)}, u32[]{:S(2)}) collective-permute-start(bf16[3,192,128]{2,1,0:T(8,128)(2,1)S(1)} %get-tuple-element.153), channel_id=1, source_target_pairs={{0,8},{8,16},{16,24},{24,32},{32,40},{40,48},{48,56},{1,9},{9,17},... | collective-permute-start | bytes 442376 | tf_op jit(solution)/shard_map/ppermute | solution.py:21
  8.4 12.6 %copy-start.13 = (f32[192,1]{0,1:T(1,128)}, f32[192,1]{0,1:T(1,128)S(1)}, u32[]{:S(2)}) copy-start(f32[192,1]{0,1:T(1,128)S(1)} %get-tuple-element.162) | copy-start | bytes 2308
  8.4 12.6 %copy-start.15 = (f32[192,1]{0,1:T(1,128)}, f32[192,1]{0,1:T(1,128)S(1)}, u32[]{:S(2)}) copy-start(f32[192,1]{0,1:T(1,128)S(1)} %get-tuple-element.163) | copy-start | bytes 2308
  8.4 12.6 %copy-start.17 = (f32[192,1]{0,1:T(1,128)}, f32[192,1]{0,1:T(1,128)S(1)}, u32[]{:S(2)}) copy-start(f32[192,1]{0,1:T(1,128)S(1)} %get-tuple-element.164) | copy-start | bytes 2308
  8.4 12.6 %copy-start.19 = (f32[192,1]{0,1:T(1,128)}, f32[192,1]{0,1:T(1,128)S(1)}, u32[]{:S(2)}) copy-start(f32[192,1]{0,1:T(1,128)S(1)} %get-tuple-element.165) | copy-start | bytes 2308
  8.4 12.6 %copy-start.21 = (f32[192,1]{0,1:T(1,128)}, f32[192,1]{0,1:T(1,128)S(1)}, u32[]{:S(2)}) copy-start(f32[192,1]{0,1:T(1,128)S(1)} %get-tuple-element.166) | copy-start | bytes 2308
  8.4 12.6 %copy-start.23 = (f32[192,1]{0,1:T(1,128)}, f32[192,1]{0,1:T(1,128)S(1)}, u32[]{:S(2)}) copy-start(f32[192,1]{0,1:T(1,128)S(1)} %get-tuple-element.167) | copy-start | bytes 2308
  8.4 12.6 %copy-start.25 = (f32[192,1]{0,1:T(1,128)}, f32[192,1]{0,1:T(1,128)S(1)}, u32[]{:S(2)}) copy-start(f32[192,1]{0,1:T(1,128)S(1)} %get-tuple-element.168) | copy-start | bytes 2308
  8.4 12.6 %copy-start.27 = (f32[192,1]{0,1:T(1,128)}, f32[192,1]{0,1:T(1,128)S(1)}, u32[]{:S(2)}) copy-start(f32[192,1]{0,1:T(1,128)S(1)} %get-tuple-element.169) | copy-start | bytes 2308
  8.5 12.6 %copy-start.29 = (f32[192,1]{0,1:T(1,128)}, f32[192,1]{0,1:T(1,128)S(1)}, u32[]{:S(2)}) copy-start(f32[192,1]{0,1:T(1,128)S(1)} %get-tuple-element.170) | copy-start | bytes 2308
  8.5 12.6 %copy-start.31 = (f32[192,1]{0,1:T(1,128)}, f32[192,1]{0,1:T(1,128)S(1)}, u32[]{:S(2)}) copy-start(f32[192,1]{0,1:T(1,128)S(1)} %get-tuple-element.171) | copy-start | bytes 2308
  8.5 12.6 %copy-start.33 = (f32[192,1]{0,1:T(1,128)}, f32[192,1]{0,1:T(1,128)S(1)}, u32[]{:S(2)}) copy-start(f32[192,1]{0,1:T(1,128)S(1)} %get-tuple-element.172) | copy-start | bytes 2308
  8.5 12.6 %copy-start.35 = (f32[192,1]{0,1:T(1,128)}, f32[192,1]{0,1:T(1,128)S(1)}, u32[]{:S(2)}) copy-start(f32[192,1]{0,1:T(1,128)S(1)} %get-tuple-element.173) | copy-start | bytes 2308
  8.5 12.6 %copy-start.37 = (f32[192,1]{0,1:T(1,128)}, f32[192,1]{0,1:T(1,128)S(1)}, u32[]{:S(2)}) copy-start(f32[192,1]{0,1:T(1,128)S(1)} %get-tuple-element.174) | copy-start | bytes 2308
  8.5 12.6 %copy-start.39 = (f32[192,1]{0,1:T(1,128)}, f32[192,1]{0,1:T(1,128)S(1)}, u32[]{:S(2)}) copy-start(f32[192,1]{0,1:T(1,128)S(1)} %get-tuple-element.175) | copy-start | bytes 2308
  8.5 12.6 %copy-start.41 = (f32[192,1]{0,1:T(1,128)}, f32[192,1]{0,1:T(1,128)S(1)}, u32[]{:S(2)}) copy-start(f32[192,1]{0,1:T(1,128)S(1)} %get-tuple-element.176) | copy-start | bytes 2308
  8.5 12.6 %copy-start.43 = (f32[192,1]{0,1:T(1,128)}, f32[192,1]{0,1:T(1,128)S(1)}, u32[]{:S(2)}) copy-start(f32[192,1]{0,1:T(1,128)S(1)} %get-tuple-element.177) | copy-start | bytes 2308
  8.5 12.6 %copy-start.45 = (f32[192,1]{0,1:T(1,128)}, f32[192,1]{0,1:T(1,128)S(1)}, u32[]{:S(2)}) copy-start(f32[192,1]{0,1:T(1,128)S(1)} %get-tuple-element.178) | copy-start | bytes 2308
  8.5 12.6 %copy-start.47 = (f32[192,1]{0,1:T(1,128)}, f32[192,1]{0,1:T(1,128)S(1)}, u32[]{:S(2)}) copy-start(f32[192,1]{0,1:T(1,128)S(1)} %get-tuple-element.179) | copy-start | bytes 2308
  8.6 12.6 %copy-start.49 = (f32[192,1]{0,1:T(1,128)}, f32[192,1]{0,1:T(1,128)S(1)}, u32[]{:S(2)}) copy-start(f32[192,1]{0,1:T(1,128)S(1)} %get-tuple-element.180) | copy-start | bytes 2308
  8.6 12.6 %copy-start.51 = (f32[192,1]{0,1:T(1,128)}, f32[192,1]{0,1:T(1,128)S(1)}, u32[]{:S(2)}) copy-start(f32[192,1]{0,1:T(1,128)S(1)} %get-tuple-element.181) | copy-start | bytes 2308
  11.2 7.2 %collective-permute-start.3 = (bf16[3,14,192]{2,1,0:T(8,128)(2,1)S(1)}, bf16[3,14,192]{2,1,0:T(8,128)(2,1)S(1)}, u32[]{:S(2)}, u32[]{:S(2)}) collective-permute-start(bf16[3,14,192]{2,1,0:T(8,128)(2,1)S(1)} %copy.57), channel_id=1, source_target_pairs={{1,0},{2,1},{3,2},{4,3},{5,4},{6,5},{7,6},{9,8},{10,9},{11,10},{12... | collective-permute-start | bytes 48392 | tf_op jit(solution)/shard_map/ppermute | solution.py:22
  12.9 6.4 %collective-permute-start.2 = (bf16[3,14,192]{2,1,0:T(8,128)(2,1)S(1)}, bf16[3,14,192]{2,1,0:T(8,128)(2,1)S(1)}, u32[]{:S(2)}, u32[]{:S(2)}) collective-permute-start(bf16[3,14,192]{2,1,0:T(8,128)(2,1)S(1)} %copy.55), channel_id=1, source_target_pairs={{0,1},{1,2},{2,3},{3,4},{4,5},{5,6},{6,7},{8,9},{9,10},{10,11},{11... | collective-permute-start | bytes 48392 | tf_op jit(solution)/shard_map/ppermute | solution.py:21
  72.5 26.0 %collective-permute-start.4 = (f32[1664,128]{1,0:T(8,128)}, f32[1664,128]{1,0:T(8,128)}, u32[]{:S(2)}, u32[]{:S(2)}) collective-permute-start(f32[1664,128]{1,0:T(8,128)} %dynamic-slice_bitcast_fusion), channel_id=1, source_target_pairs={{0,8},{1,9},{2,10},{3,11},{4,12},{5,13},{6,14},{7,15},{8,0},{9,1},... | collective-permute-start | bytes 2555912 | tf_op jit(solution)/shard_map/ppermute | solution.py:224
  72.5 7.6 %collective-permute-start.8 = (bf16[3,192,128]{2,1,0:T(8,128)(2,1)S(1)}, bf16[3,192,128]{2,1,0:T(8,128)(2,1)}, u32[]{:S(2)}, u32[]{:S(2)}) collective-permute-start(bf16[3,192,128]{2,1,0:T(8,128)(2,1)S(1)} %get-tuple-element.152), channel_id=1, source_target_pairs={{0,8},{8,16},{16,24},{24,32},{32,40},{40,48},{48,56},{1,9},{9,17},... | collective-permute-start | bytes 442376 | tf_op jit(solution)/shard_map/ppermute | solution.py:21
  78.1 6.6 %collective-permute-start.9 = (bf16[3,192,128]{2,1,0:T(8,128)(2,1)S(1)}, bf16[3,192,128]{2,1,0:T(8,128)(2,1)}, u32[]{:S(2)}, u32[]{:S(2)}) collective-permute-start(bf16[3,192,128]{2,1,0:T(8,128)(2,1)S(1)} %get-tuple-element.151), channel_id=1, source_target_pairs={{8,0},{16,8},{24,16},{32,24},{40,32},{48,40},{56,48},{9,1},{17,9},... | collective-permute-start | bytes 442376 | tf_op jit(solution)/shard_map/ppermute | solution.py:22
  86.4 8.1 %collective-permute-start.10 = (bf16[3,14,192]{2,1,0:T(8,128)(2,1)S(1)}, bf16[3,14,192]{2,1,0:T(8,128)(2,1)S(1)}, u32[]{:S(2)}, u32[]{:S(2)}) collective-permute-start(bf16[3,14,192]{2,1,0:T(8,128)(2,1)S(1)} %copy.69), channel_id=1, source_target_pairs={{1,0},{2,1},{3,2},{4,3},{5,4},{6,5},{7,6},{9,8},{10,9},{11,10},{12... | collective-permute-start | bytes 48392 | tf_op jit(solution)/shard_map/ppermute | solution.py:22
  88.1 7.3 %collective-permute-start.11 = (bf16[3,14,192]{2,1,0:T(8,128)(2,1)S(1)}, bf16[3,14,192]{2,1,0:T(8,128)(2,1)S(1)}, u32[]{:S(2)}, u32[]{:S(2)}) collective-permute-start(bf16[3,14,192]{2,1,0:T(8,128)(2,1)S(1)} %copy.71), channel_id=1, source_target_pairs={{0,1},{1,2},{2,3},{3,4},{4,5},{5,6},{6,7},{8,9},{9,10},{10,11},{11... | collective-permute-start | bytes 48392 | tf_op jit(solution)/shard_map/ppermute | solution.py:21
  99.8 14.7 %collective-permute-start.7 = (f32[416,128]{1,0:T(8,128)S(1)}, f32[416,128]{1,0:T(8,128)S(1)}, u32[]{:S(2)}, u32[]{:S(2)}) collective-permute-start(f32[416,128]{1,0:T(8,128)S(1)} %get-tuple-element.140), channel_id=1, source_target_pairs={{0,65},{1,64},{2,67},{3,66},{4,69},{5,68},{6,71},{7,70},{8,73},{9,... | collective-permute-start | bytes 638984 | tf_op jit(solution)/shard_map/ppermute | solution.py:224
  104.2 10.3 %collective-permute-start.6 = (f32[416,128]{1,0:T(8,128)S(1)}, f32[416,128]{1,0:T(8,128)S(1)}, u32[]{:S(2)}, u32[]{:S(2)}) collective-permute-start(f32[416,128]{1,0:T(8,128)S(1)} %get-tuple-element.141), channel_id=1, source_target_pairs={{0,1},{1,0},{2,3},{3,2},{4,5},{5,4},{6,7},{7,6},{8,9},{9,8},{10,11... | collective-permute-start | bytes 638984 | tf_op jit(solution)/shard_map/ppermute | solution.py:224
  104.4 10.1 %collective-permute-start.5 = (f32[416,128]{1,0:T(8,128)S(1)}, f32[416,128]{1,0:T(8,128)S(1)}, u32[]{:S(2)}, u32[]{:S(2)}) collective-permute-start(f32[416,128]{1,0:T(8,128)S(1)} %get-tuple-element.139), channel_id=1, source_target_pairs={{0,64},{1,65},{2,66},{3,67},{4,68},{5,69},{6,70},{7,71},{8,72},{9,... | collective-permute-start | bytes 638984 | tf_op jit(solution)/shard_map/ppermute | solution.py:224
  114.6 8.7 %collective-permute-start.14 = (f32[104,128]{1,0:T(8,128)S(1)}, f32[104,128]{1,0:T(8,128)S(1)}, u32[]{:S(2)}, u32[]{:S(2)}) collective-permute-start(f32[104,128]{1,0:T(8,128)S(1)} %get-tuple-element.156), channel_id=1, source_target_pairs={{0,6},{1,7},{2,4},{3,5},{4,2},{5,3},{6,0},{7,1},{8,14},{9,15},{10,... | collective-permute-start | bytes 159752 | tf_op jit(solution)/shard_map/ppermute | solution.py:224
  121.3 5.1 %collective-permute-start.13 = (f32[104,128]{1,0:T(8,128)S(1)}, f32[104,128]{1,0:T(8,128)S(1)}, u32[]{:S(2)}, u32[]{:S(2)}) collective-permute-start(f32[104,128]{1,0:T(8,128)S(1)} %get-tuple-element.157), channel_id=1, source_target_pairs={{0,4},{1,5},{2,6},{3,7},{4,0},{5,1},{6,2},{7,3},{8,12},{9,13},{10,... | collective-permute-start | bytes 159752 | tf_op jit(solution)/shard_map/ppermute | solution.py:224
  121.3 5.1 %collective-permute-start.12 = (f32[104,128]{1,0:T(8,128)S(1)}, f32[104,128]{1,0:T(8,128)S(1)}, u32[]{:S(2)}, u32[]{:S(2)}) collective-permute-start(f32[104,128]{1,0:T(8,128)S(1)} %get-tuple-element.155), channel_id=1, source_target_pairs={{0,2},{1,3},{2,0},{3,1},{4,6},{5,7},{6,4},{7,5},{8,10},{9,11},{10,... | collective-permute-start | bytes 159752 | tf_op jit(solution)/shard_map/ppermute | solution.py:224
  126.4 3.9 %collective-permute-start.17 = (f32[26,128]{1,0:T(8,128)S(1)}, f32[26,128]{1,0:T(8,128)S(1)}, u32[]{:S(2)}, u32[]{:S(2)}) collective-permute-start(f32[26,128]{1,0:T(8,128)S(1)} %get-tuple-element.159), channel_id=1, source_target_pairs={{0,48},{1,49},{2,50},{3,51},{4,52},{5,53},{6,54},{7,55},{8,56},{9,... | collective-permute-start | bytes 39944 | tf_op jit(solution)/shard_map/ppermute | solution.py:224
  126.5 4.2 %collective-permute-start.16 = (f32[26,128]{1,0:T(8,128)S(1)}, f32[26,128]{1,0:T(8,128)S(1)}, u32[]{:S(2)}, u32[]{:S(2)}) collective-permute-start(f32[26,128]{1,0:T(8,128)S(1)} %get-tuple-element.160), channel_id=1, source_target_pairs={{0,32},{1,33},{2,34},{3,35},{4,36},{5,37},{6,38},{7,39},{8,40},{9,... | collective-permute-start | bytes 39944 | tf_op jit(solution)/shard_map/ppermute | solution.py:224
  129.1 2.9 %collective-permute-start.15 = (f32[26,128]{1,0:T(8,128)S(1)}, f32[26,128]{1,0:T(8,128)S(1)}, u32[]{:S(2)}, u32[]{:S(2)}) collective-permute-start(f32[26,128]{1,0:T(8,128)S(1)} %get-tuple-element.158), channel_id=1, source_target_pairs={{0,16},{1,17},{2,18},{3,19},{4,20},{5,21},{6,22},{7,23},{8,24},{9,... | collective-permute-start | bytes 39944 | tf_op jit(solution)/shard_map/ppermute | solution.py:224
  132.1 3.9 %collective-permute-start.18 = (f32[26,128]{1,0:T(8,128)S(1)}, f32[26,128]{1,0:T(8,128)S(1)}, u32[]{:S(2)}, u32[]{:S(2)}) collective-permute-start(f32[26,128]{1,0:T(8,128)S(1)} %get-tuple-element.129), channel_id=1, source_target_pairs={{0,16},{1,17},{2,18},{3,19},{4,20},{5,21},{6,22},{7,23},{8,24},{9,... | collective-permute-start | bytes 39944 | tf_op jit(solution)/shard_map/ppermute | solution.py:241
  132.7 4.1 %collective-permute-start.19 = (f32[26,128]{1,0:T(8,128)S(1)}, f32[26,128]{1,0:T(8,128)S(1)}, u32[]{:S(2)}, u32[]{:S(2)}) collective-permute-start(f32[26,128]{1,0:T(8,128)S(1)} %get-tuple-element.129), channel_id=1, source_target_pairs={{0,32},{1,33},{2,34},{3,35},{4,36},{5,37},{6,38},{7,39},{8,40},{9,... | collective-permute-start | bytes 39944 | tf_op jit(solution)/shard_map/ppermute | solution.py:241
  134.7 3.8 %collective-permute-start.20 = (f32[26,128]{1,0:T(8,128)S(1)}, f32[26,128]{1,0:T(8,128)S(1)}, u32[]{:S(2)}, u32[]{:S(2)}) collective-permute-start(f32[26,128]{1,0:T(8,128)S(1)} %get-tuple-element.129), channel_id=1, source_target_pairs={{0,48},{1,49},{2,50},{3,51},{4,52},{5,53},{6,54},{7,55},{8,56},{9,... | collective-permute-start | bytes 39944 | tf_op jit(solution)/shard_map/ppermute | solution.py:241
  138.5 4.0 %collective-permute-start.21 = (f32[104,128]{1,0:T(8,128)S(1)}, f32[104,128]{1,0:T(8,128)S(1)}, u32[]{:S(2)}, u32[]{:S(2)}) collective-permute-start(f32[104,128]{1,0:T(8,128)S(1)} %reshape.217), channel_id=1, source_target_pairs={{0,2},{1,3},{2,0},{3,1},{4,6},{5,7},{6,4},{7,5},{8,10},{9,11},{10,... | collective-permute-start | bytes 159752 | tf_op jit(solution)/shard_map/ppermute | solution.py:241
  138.6 4.6 %collective-permute-start.22 = (f32[104,128]{1,0:T(8,128)S(1)}, f32[104,128]{1,0:T(8,128)S(1)}, u32[]{:S(2)}, u32[]{:S(2)}) collective-permute-start(f32[104,128]{1,0:T(8,128)S(1)} %reshape.217), channel_id=1, source_target_pairs={{0,4},{1,5},{2,6},{3,7},{4,0},{5,1},{6,2},{7,3},{8,12},{9,13},{10,... | collective-permute-start | bytes 159752 | tf_op jit(solution)/shard_map/ppermute | solution.py:241
  141.0 4.2 %collective-permute-start.23 = (f32[104,128]{1,0:T(8,128)S(1)}, f32[104,128]{1,0:T(8,128)S(1)}, u32[]{:S(2)}, u32[]{:S(2)}) collective-permute-start(f32[104,128]{1,0:T(8,128)S(1)} %reshape.217), channel_id=1, source_target_pairs={{0,6},{1,7},{2,4},{3,5},{4,2},{5,3},{6,0},{7,1},{8,14},{9,15},{10,... | collective-permute-start | bytes 159752 | tf_op jit(solution)/shard_map/ppermute | solution.py:241
  145.2 4.8 %collective-permute-start.24 = (f32[416,128]{1,0:T(8,128)S(1)}, f32[416,128]{1,0:T(8,128)S(1)}, u32[]{:S(2)}, u32[]{:S(2)}) collective-permute-start(f32[416,128]{1,0:T(8,128)S(1)} %bitcast.398), channel_id=1, source_target_pairs={{0,64},{1,65},{2,66},{3,67},{4,68},{5,69},{6,70},{7,71},{8,72},{9,... | collective-permute-start | bytes 638984 | tf_op jit(solution)/shard_map/ppermute | solution.py:241
  145.9 8.2 %collective-permute-start.25 = (f32[416,128]{1,0:T(8,128)S(1)}, f32[416,128]{1,0:T(8,128)S(1)}, u32[]{:S(2)}, u32[]{:S(2)}) collective-permute-start(f32[416,128]{1,0:T(8,128)S(1)} %bitcast.399), channel_id=1, source_target_pairs={{0,1},{1,0},{2,3},{3,2},{4,5},{5,4},{6,7},{7,6},{8,9},{9,8},{10,11... | collective-permute-start | bytes 638984 | tf_op jit(solution)/shard_map/ppermute | solution.py:241
  148.5 7.8 %collective-permute-start.26 = (f32[416,128]{1,0:T(8,128)S(1)}, f32[416,128]{1,0:T(8,128)S(1)}, u32[]{:S(2)}, u32[]{:S(2)}) collective-permute-start(f32[416,128]{1,0:T(8,128)S(1)} %bitcast.400), channel_id=1, source_target_pairs={{0,65},{1,64},{2,67},{3,66},{4,69},{5,68},{6,71},{7,70},{8,73},{9,... | collective-permute-start | bytes 638984 | tf_op jit(solution)/shard_map/ppermute | solution.py:241
  156.4 10.2 %collective-permute-start.27 = (f32[1664,128]{1,0:T(8,128)S(1)}, f32[1664,128]{1,0:T(8,128)S(1)}, u32[]{:S(2)}, u32[]{:S(2)}) collective-permute-start(f32[1664,128]{1,0:T(8,128)S(1)} %bitcast.374), channel_id=1, source_target_pairs={{0,8},{1,9},{2,10},{3,11},{4,12},{5,13},{6,14},{7,15},{8,0},{9,1},... | collective-permute-start | bytes 2555912 | tf_op jit(solution)/shard_map/ppermute | solution.py:241
  (111 other events, 728.6 us)

commit v6 on v5

--- a/solution.py
+++ b/solution.py
@@ -11,17 +11,51 @@
 
 
 def padded_2(x, sides, width):
-    for axis, dim in sides:
-        count, length = (lax.axis_size(axis), x.shape[dim])
-        up = [(i, (i + 1) % count) for i in range(count - 1)]
-        down = [(j, i) for i, j in up]
-        order = (1, 0, 2) if dim == 1 else (2, 1, 0)
-        last = jnp.transpose(lax.slice_in_dim(x, length - width, length, axis=dim), order)
-        leading = jnp.transpose(lax.slice_in_dim(x, 0, width, axis=dim), order)
-        before = jnp.transpose(lax.ppermute(last, axis, up), order)
-        after = jnp.transpose(lax.ppermute(leading, axis, down), order)
-        x = jnp.concatenate([before, x, after], axis=dim)
-    return x
+    (row_axis, row_dim), (col_axis, col_dim) = sides
+    rows, cols = lax.axis_size(row_axis), lax.axis_size(col_axis)
+    height, length = x.shape[row_dim], x.shape[col_dim]
+    both = (row_axis, col_axis)
+
+    def moved(block, dr, dc, order):
+        pairs = []
+        for r in range(rows):
+            for c in range(cols):
+                if 0 <= r + dr < rows and 0 <= c + dc < cols:
+                    pairs.append((r * cols + c, (r + dr) * cols + c + dc))
+        block = jnp.transpose(block, order)
+        if dc == 0:
+            sent = lax.ppermute(block, row_axis, [(a // cols, b // cols) for a, b in pairs[::cols]])
+        elif dr == 0:
+            sent = lax.ppermute(block, col_axis, [(a % cols, b % cols) for a, b in pairs[:cols - 1]])
+        else:
+            sent = lax.ppermute(block, both, pairs)
+        return jnp.transpose(sent, order)
+
+    top = lax.slice_in_dim(x, 0, width, axis=row_dim)
+    bottom = lax.slice_in_dim(x, height - width, height, axis=row_dim)
+    left = lax.slice_in_dim(x, 0, width, axis=col_dim)
+    right = lax.slice_in_dim(x, length - width, length, axis=col_dim)
+    strips = (1, 0, 2)
+    thin = (2, 1, 0)
+    above = moved(bottom, 1, 0, strips)
+    below = moved(top, -1, 0, strips)
+    before = moved(right, 0, 1, thin)
+    after = moved(left, 0, -1, thin)
+
+    def corner(block_rows, block_cols, dr, dc):
+        block = lax.slice_in_dim(lax.slice_in_dim(x, *block_rows, axis=row_dim), *block_cols, axis=col_dim)
+        return moved(block, dr, dc, thin)
+
+    low, high = (0, width), (height - width, height)
+    first, last = (0, width), (length - width, length)
+    above_before = corner(high, last, 1, 1)
+    above_after = corner(high, first, 1, -1)
+    below_before = corner(low, last, -1, 1)
+    below_after = corner(low, first, -1, -1)
+    upper = jnp.concatenate([above_before, above, above_after], axis=col_dim)
+    middle = jnp.concatenate([before, x, after], axis=col_dim)
+    lower = jnp.concatenate([below_before, below, below_after], axis=col_dim)
+    return jnp.concatenate([upper, middle, lower], axis=row_dim)
 
 
 def from_behind(block, axis, distance):

time: 174 us -> 224 us (1.29)
  starting transfers between devices: 63.9 us -> 98.2 us
  waiting for transfers between devices: 26 us -> 41.2 us
    ppermute x8 -> x16, starting transfers between devices: 28.3 us -> 63 us  [the longest x8 34.8 us: moved(): sent = lax.ppermute(block, both, pairs)]
    ppermute x8 -> x16, waiting for transfers between devices: 6.61 us -> 23.5 us  [the longest x4 17.6 us: moved(): lax.ppermute(block, col_axis, [(a % cols, b % cols) for a, b in pairs[:co...]
    another operation x2, local copies, waits for them, and re-layouts: 4.39 us -> 0.96 us  [conv_backward(): kernel_grad = jnp.stack(columns, axis=1)]
    ppermute x10, starting transfers between devices: 15.7 us -> 13.3 us  [butterfly_psum(): total = total + lax.ppermute(send, axes, pairs)]
    unnamed x271 -> x253, local copies, waits for them, and re-layouts: 8.94 us -> 10.9 us
    concatenate x4 -> x2, other arithmetic: 4.77 us -> 6.12 us  [padded_2(): return jnp.concatenate([upper, middle, lower], axis=row_dim)]
  transfers between devices with their start and end apart: 28 -> 36, of which waited for: 18 -> 18; matrix products, arithmetic and copies ran while one was open for 10% -> 8% of each run, Pallas kernels for 0% -> 0%
where the time goes in v6:
time: 224 us; the launch traced here: 223 us
  starting transfers between devices  98.2 us (44%)
  waiting for transfers between devices  41.2 us (18%)
  other arithmetic  39.8 us (18%)
  local copies, waits for them, and re-layouts  27.3 us (12%)
  matrix products  13.7 us (6%)
  between operations  2.96 us (1%)
    ppermute x8, starting transfers between devices, moved(): sent = lax.ppermute(block, both, pairs)  34.8 us
    ppermute x10, starting transfers between devices, butterfly_psum(): other = lax.ppermute(buffer, axes, pairs)  21.9 us
    ppermute x4, waiting for transfers between devices, moved(): lax.ppermute(block, col_axis, [(a % cols, b % cols) for a, b in pairs[:co...  17.6 us
    ppermute x4, starting transfers between devices, moved(): lax.ppermute(block, col_axis, [(a % cols, b % cols) for a, b in pairs[:co...  16.1 us
    dot_general x12, matrix products, product(): jnp.einsum(form, left_side, right_side, preferred_element_type=jnp.float32)  13.7 us
    ppermute x10, starting transfers between devices, butterfly_psum(): total = total + lax.ppermute(send, axes, pairs)  13.3 us
    ppermute x4, starting transfers between devices, moved(): lax.ppermute(block, row_axis, [(a // cols, b // cols) for a, b in pairs[:...  12 us
    reduce_sum x4, other arithmetic, conv_backward(): columns.append(jnp.sum(window * conv_float, axis=(1, 2)))  11.9 us
  transfers between devices with their start and end apart: 36, of which 18 were waited for; matrix products, arithmetic and copies ran while one was open for 8% of the time, Pallas kernels for 0%

profile of v6, /device:TPU:1, one launch (start us, length us, event | category | flops | bytes accessed | tf_op | source)
XLA Modules:
  0.0 223.2 jit_solution(9857827323801422825)
XLA Ops:
  4.7 4.5 %collective-permute-start.1 = (bf16[3,192,128]{2,1,0:T(8,128)(2,1)}, bf16[3,192,128]{2,1,0:T(8,128)(2,1)S(1)}, u32[]{:S(2)}, u32[]{:S(2)}) collective-permute-start(bf16[3,192,128]{2,1,0:T(8,128)(2,1)} %get-tuple-element.144), channel_id=1, source_target_pairs={{0,8},{8,16},{16,24},{24,32},{32,40},{40,48},{48,56},{1,9},{9,17},... | collective-permute-start | bytes 442376 | tf_op jit(solution)/shard_map/ppermute | solution.py:27
  9.2 7.2 %collective-permute-start = (bf16[3,3,192]{0,2,1:T(8,128)(2,1)S(1)}, bf16[3,3,192]{0,2,1:T(8,128)(2,1)}, u32[]{:S(2)}, u32[]{:S(2)}) collective-permute-start(bf16[3,3,192]{0,2,1:T(8,128)(2,1)S(1)} %get-tuple-element.140), channel_id=1, source_target_pairs={{0,9},{1,10},{2,11},{3,12},{4,13},{5,14},{6,15},{8,17},{9,18},{10,... | collective-permute-start | bytes 10376 | tf_op jit(solution)/shard_map/ppermute | solution.py:31
  17.7 1.9 collective-permute-start.6
  21.4 1.3 collective-permute-start.4
  22.7 6.4 %collective-permute-start.3 = (bf16[3,8,192]{0,2,1:T(8,128)(2,1)S(1)}, bf16[3,8,192]{0,2,1:T(8,128)(2,1)S(1)}, u32[]{:S(2)}, u32[]{:S(2)}) collective-permute-start(bf16[3,8,192]{0,2,1:T(8,128)(2,1)S(1)} %get-tuple-element.146), channel_id=1, source_target_pairs={{0,1},{1,2},{2,3},{3,4},{4,5},{5,6},{6,7},{8,9},{9,10},{10,11},{11... | collective-permute-start | bytes 27656 | tf_op jit(solution)/shard_map/ppermute | solution.py:29
  29.1 5.3 %collective-permute-start.5 = (bf16[3,3,192]{0,2,1:T(8,128)(2,1)}, bf16[3,3,192]{0,2,1:T(8,128)(2,1)}, u32[]{:S(2)}, u32[]{:S(2)}) collective-permute-start(bf16[3,3,192]{0,2,1:T(8,128)(2,1)} %get-tuple-element.142), channel_id=1, source_target_pairs={{8,1},{9,2},{10,3},{11,4},{12,5},{13,6},{14,7},{16,9},{17,10},{18,... | collective-permute-start | bytes 10376 | tf_op jit(solution)/shard_map/ppermute | solution.py:31
  34.4 5.8 %collective-permute-done.5 = bf16[3,3,192]{0,2,1:T(8,128)(2,1)} collective-permute-done((bf16[3,3,192]{0,2,1:T(8,128)(2,1)}, bf16[3,3,192]{0,2,1:T(8,128)(2,1)}, u32[]{:S(2)}, u32[]{:S(2)}) %collective-permute-start.5) | collective-permute-done | bytes 3488 | tf_op jit(solution)/shard_map/ppermute | solution.py:31
  40.4 2.9 %maximum_maximum_fusion = (bf16[192,11,134]{2,0,1:T(8,128)(2,1)S(1)}, bf16[192,11,134]{2,0,1:T(8,128)(2,1)S(1)}) fusion(bf16[192,8,3]{2,0,1:T(8,128)(2,1)S(1)} %bitcast.399, bf16[192,8,128]{2,0,1:T(8,128)(2,1)S(1)} %bitcast.391, bf16[192,8,3]{2,0,1:T(8,128)(2,1)S(1)} %bitcast.402, bf16[192,3,3]{2,0,1:T(8,128)(2,1)S(1)} %bitcast.429, ...), kind=kLoop, calls=%fused_computation.89 | loop fusion | flops 6792192 | bytes 1852416 | tf_op jit(solution)/shard_map/concatenate | solution.py:58
  43.9 8.9 %fusion.181 = (f32[8,128]{1,0:T(8,128)S(1)}, f32[192,8,128]{2,0,1:T(8,128)S(1)}) fusion(f32[192]{0:T(256)S(1)} %copy-done.119, bf16[192,11,134]{2,0,1:T(8,128)(2,1)S(1)} %get-tuple-element.127, f32[192]{0:T(256)S(1)} %bitcast.529, f32[192]{0:T(256)S(1)} %bitcast.531, f32[192]{0:T(256)S(1)} %bitcast.436, f32[192]{0:T(256)S(1)} %bitcast.438, ...), kind=kLoop, calls=%fused_computation.395 | loop fusion | flops 32635904 | bytes 17755648 | tf_op jit(solution)/shard_map/reduce_sum | solution.py:99
  56.7 1.9 convert_reduce_fusion.2
  59.8 2.4 %convert_reduce_fusion.1 = (f32[768]{0:T(1024)}, bf16[768,8,128]{0,2,1:T(8,128)(2,1)S(1)}) fusion(f32[8,128,768]{2,1,0:T(8,128)S(1)} %get-tuple-element.209, f32[768]{0:T(1024)S(1)} %copy-done.106, bf16[192,8,128]{2,0,1:T(8,128)(2,1)S(1)} %get-tuple-element.119, bf16[768,192]{0,1:T(8,128)(2,1)S(1)} %copy-done.7), kind=kOutput, calls=%fused_computation.64 | convolution fusion | flops 312212736 | bytes 5412864 | tf_op jit(solution)/shard_map/chw,dc->dhw/dot_general | solution.py:68
  62.2 1.4 fusion.147
  63.6 3.6 %fusion.120 = (f32[192]{0:T(256)}, f32[192]{0:T(256)}, f32[192]{0:T(256)}, f32[192]{0:T(256)}, f32[192]{0:T(256)}, /*index=5*/f32[192]{0:T(256)}, f32[192]{0:T(2...) fusion(bf16[192,11,134]{2,0,1:T(8,128)(2,1)S(1)} %get-tuple-element.127, ...), kind=kLoop, calls=%fused_computation.257 | loop fusion | flops 11204736 | bytes 3975424 | tf_op jit(solution)/shard_map/reduce_sum | solution.py:156
  67.2 3.9 %fusion.121 = (f32[192]{0:T(256)S(1)}, f32[192]{0:T(256)S(1)}, f32[192]{0:T(256)S(1)}, f32[192]{0:T(256)S(1)}, f32[192]{0:T(256)S(1)}, /*index=5*/f32[192]{0:T(2...) fusion(bf16[192,8,128]{2,0,1:T(8,128)(2,1)S(1)} %get-tuple-elem, ...), kind=kLoop, calls=%fused_computation.258 | loop fusion | flops 11006400 | bytes 7485696 | tf_op jit(solution)/shard_map/reduce_sum | solution.py:156
  72.2 3.3 %fusion.93 = (f32[192]{0:T(256)S(1)}, f32[192]{0:T(256)S(1)}, f32[192]{0:T(256)S(1)}, f32[192]{0:T(256)S(1)}, f32[192]{0:T(256)S(1)}, /*index=5*/f32[192]{0:T(25...) fusion(bf16[192,8,128]{2,0,1:T(8,128)(2,1)S(1)} %get-tuple-elem, ...), kind=kLoop, calls=%fused_computation.230 | loop fusion | flops 10809984 | bytes 7484928 | tf_op jit(solution)/shard_map/reduce_sum | solution.py:156
  76.0 1.3 fusion.189
  81.0 1.4 concatenate.145
  89.8 2.1 dynamic-slice_bitcast_fusion
  92.0 1.3 collective-permute-start.16
  93.3 8.5 %collective-permute-start.14 = (bf16[3,3,192]{0,2,1:T(8,128)(2,1)S(1)}, bf16[3,3,192]{0,2,1:T(8,128)(2,1)S(1)}, u32[]{:S(2)}, u32[]{:S(2)}) collective-permute-start(bf16[3,3,192]{0,2,1:T(8,128)(2,1)S(1)} %get-tuple-element.132), channel_id=1, source_target_pairs={{8,1},{9,2},{10,3},{11,4},{12,5},{13,6},{14,7},{16,9},{17,10},{18,... | collective-permute-start | bytes 10376 | tf_op jit(solution)/shard_map/ppermute | solution.py:31
  102.6 1.9 collective-permute-start.15
  104.5 1.3 collective-permute-start.19
  105.9 3.6 %collective-permute-start.18 = (bf16[3,192,128]{2,1,0:T(8,128)(2,1)}, bf16[3,192,128]{2,1,0:T(8,128)(2,1)}, u32[]{:S(2)}, u32[]{:S(2)}) collective-permute-start(bf16[3,192,128]{2,1,0:T(8,128)(2,1)} %get-tuple-element.137), channel_id=1, source_target_pairs={{0,8},{8,16},{16,24},{24,32},{32,40},{40,48},{48,56},{1,9},{9,17},... | collective-permute-start | bytes 442376 | tf_op jit(solution)/shard_map/ppermute | solution.py:27
  110.2 8.7 %collective-permute-start.17 = (bf16[3,3,192]{0,2,1:T(8,128)(2,1)S(1)}, bf16[3,3,192]{0,2,1:T(8,128)(2,1)S(1)}, u32[]{:S(2)}, u32[]{:S(2)}) collective-permute-start(bf16[3,3,192]{0,2,1:T(8,128)(2,1)S(1)} %get-tuple-element.134), channel_id=1, source_target_pairs={{0,9},{1,10},{2,11},{3,12},{4,13},{5,14},{6,15},{8,17},{9,18},{10,... | collective-permute-start | bytes 10376 | tf_op jit(solution)/shard_map/ppermute | solution.py:31
  119.8 7.2 %collective-permute-start.12 = (bf16[3,8,192]{0,2,1:T(8,128)(2,1)S(1)}, bf16[3,8,192]{0,2,1:T(8,128)(2,1)S(1)}, u32[]{:S(2)}, u32[]{:S(2)}) collective-permute-start(bf16[3,8,192]{0,2,1:T(8,128)(2,1)S(1)} %get-tuple-element.139), channel_id=1, source_target_pairs={{0,1},{1,2},{2,3},{3,4},{4,5},{5,6},{6,7},{8,9},{9,10},{10,11},{11... | collective-permute-start | bytes 27656 | tf_op jit(solution)/shard_map/ppermute | solution.py:29
  129.0 6.5 %collective-permute-done.12 = bf16[3,8,192]{0,2,1:T(8,128)(2,1)S(1)} collective-permute-done((bf16[3,8,192]{0,2,1:T(8,128)(2,1)S(1)}, bf16[3,8,192]{0,2,1:T(8,128)(2,1)S(1)}, u32[]{:S(2)}, u32[]{:S(2)}) %collective-permute-start.12) | collective-permute-done | bytes 9248 | tf_op jit(solution)/shard_map/ppermute | solution.py:29
  135.5 11.1 %collective-permute-done.13 = bf16[3,8,192]{0,2,1:T(8,128)(2,1)S(1)} collective-permute-done((bf16[3,8,192]{0,2,1:T(8,128)(2,1)S(1)}, bf16[3,8,192]{0,2,1:T(8,128)(2,1)S(1)}, u32[]{:S(2)}, u32[]{:S(2)}) %collective-permute-start.13) | collective-permute-done | bytes 9248 | tf_op jit(solution)/shard_map/ppermute | solution.py:29
  146.6 3.2 %maximum_maximum_fusion.2 = (bf16[192,11,134]{2,0,1:T(8,128)(2,1)S(1)}, bf16[192,11,134]{2,0,1:T(8,128)(2,1)S(1)}) fusion(bf16[192,3,3]{2,0,1:T(8,128)(2,1)} %bitcast.161, bf16[192,3,128]{2,0,1:T(8,128)(2,1)} %bitcast.159, bf16[192,3,3]{2,0,1:T(8,128)(2,1)} %bitcast.431, bf16[192,8,3]{2,0,1:T(8,128)(2,1)S(1)} %bitcast.417, ...), kind=kLoop, calls=%fused_computation.91 | loop fusion | flops 6792192 | bytes 1852416 | tf_op jit(solution)/shard_map/concatenate | solution.py:58
  150.3 1.3 bitcast_add_fusion
  151.6 4.7 %collective-permute-start.11 = (f32[416,128]{1,0:T(8,128)S(1)}, f32[416,128]{1,0:T(8,128)S(1)}, u32[]{:S(2)}, u32[]{:S(2)}) collective-permute-start(f32[416,128]{1,0:T(8,128)S(1)} %get-tuple-element.129), channel_id=1, source_target_pairs={{0,65},{1,64},{2,67},{3,66},{4,69},{5,68},{6,71},{7,70},{8,73},{9,... | collective-permute-start | bytes 638984 | tf_op jit(solution)/shard_map/ppermute | solution.py:258
  157.3 9.4 %fusion.148 = f32[192,8,128]{2,0,1:T(8,128)S(1)} fusion(f32[192,8,128]{2,0,1:T(8,128)S(1)} %get-tuple-element.216, bf16[192,8,128]{2,0,1:T(8,128)(2,1)S(1)} %get-tuple-element.115, bf16[192,8,3]{2,0,1:T(8,128)(2,1)S(1)} %bitcast.416, bf16[192,8,3]{2,0,1:T(8,128)(2,1)S(1)} %bitcast.418, bf16[192,11,134]{2,0,1:T(8,128)(2,1)S(1)} %get-tuple-element.125, ...), kind=kLoop, calls=%fused_computation.294 | loop fusion | flops 32440320 | bytes 18537216 | tf_op jit(solution)/shard_map/add | solution.py:147
  167.2 3.1 %collective-permute-start.21 = (f32[104,128]{1,0:T(8,128)S(1)}, f32[104,128]{1,0:T(8,128)S(1)}, u32[]{:S(2)}, u32[]{:S(2)}) collective-permute-start(f32[104,128]{1,0:T(8,128)S(1)} %get-tuple-element.150), channel_id=1, source_target_pairs={{0,4},{1,5},{2,6},{3,7},{4,0},{5,1},{6,2},{7,3},{8,12},{9,13},{10,... | collective-permute-start | bytes 159752 | tf_op jit(solution)/shard_map/ppermute | solution.py:258
  171.9 1.8 collective-permute-done.20
  173.8 2.8 %collective-permute-start.25 = (f32[26,128]{1,0:T(8,128)S(1)}, f32[26,128]{1,0:T(8,128)S(1)}, u32[]{:S(2)}, u32[]{:S(2)}) collective-permute-start(f32[26,128]{1,0:T(8,128)S(1)} %get-tuple-element.152), channel_id=1, source_target_pairs={{0,48},{1,49},{2,50},{3,51},{4,52},{5,53},{6,54},{7,55},{8,56},{9,... | collective-permute-start | bytes 39944 | tf_op jit(solution)/shard_map/ppermute | solution.py:258
  176.6 1.8 collective-permute-start.24
  178.5 2.3 %collective-permute-done.24 = f32[26,128]{1,0:T(8,128)S(1)} collective-permute-done((f32[26,128]{1,0:T(8,128)S(1)}, f32[26,128]{1,0:T(8,128)S(1)}, u32[]{:S(2)}, u32[]{:S(2)}) %collective-permute-start.24) | collective-permute-done | bytes 13344 | tf_op jit(solution)/shard_map/ppermute | solution.py:258
  181.3 1.7 collective-permute-start.27
  183.0 2.0 collective-permute-start.28
  185.4 1.4 collective-permute-done.28
  188.0 2.4 %collective-permute-start.30 = (f32[104,128]{1,0:T(8,128)S(1)}, f32[104,128]{1,0:T(8,128)S(1)}, u32[]{:S(2)}, u32[]{:S(2)}) collective-permute-start(f32[104,128]{1,0:T(8,128)S(1)} %reshape.217), channel_id=1, source_target_pairs={{0,4},{1,5},{2,6},{3,7},{4,0},{5,1},{6,2},{7,3},{8,12},{9,13},{10,... | collective-permute-start | bytes 159752 | tf_op jit(solution)/shard_map/ppermute | solution.py:275
  191.1 1.4 collective-permute-done.30
  192.5 2.1 collective-permute-done.31
  195.0 1.5 collective-permute-start.33
  196.5 1.9 collective-permute-start.34
  199.6 2.5 %collective-permute-done.33 = f32[416,128]{1,0:T(8,128)S(1)} collective-permute-done((f32[416,128]{1,0:T(8,128)S(1)}, f32[416,128]{1,0:T(8,128)S(1)}, u32[]{:S(2)}, u32[]{:S(2)}) %collective-permute-start.33) | collective-permute-done | bytes 213024 | tf_op jit(solution)/shard_map/ppermute | solution.py:275
  202.2 2.2 collective-permute-done.34
  204.3 10.0 %collective-permute-start.35 = (f32[1664,128]{1,0:T(8,128)S(1)}, f32[1664,128]{1,0:T(8,128)S(1)}, u32[]{:S(2)}, u32[]{:S(2)}) collective-permute-start(f32[1664,128]{1,0:T(8,128)S(1)} %bitcast.405), channel_id=1, source_target_pairs={{0,8},{1,9},{2,10},{3,11},{4,12},{5,13},{6,14},{7,15},{8,0},{9,1},... | collective-permute-start | bytes 2555912 | tf_op jit(solution)/shard_map/ppermute | solution.py:275
  214.3 1.3 copy.51
  (364 shorter events, 43.9 us)
Async XLA Ops:
  1.8 32.5 %copy-start.118 = (s32[2,8,128]{2,1,0:T(8,128)S(1)}, s32[2,8,128]{2,1,0:T(8,128)}, u32[]{:S(2)}) copy-start(s32[2,8,128]{2,1,0:T(8,128)} %param.16) | copy-start | bytes 24580
  2.7 18.7 %collective-permute-start.2 = (bf16[3,3,192]{0,2,1:T(8,128)(2,1)S(1)}, bf16[3,3,192]{0,2,1:T(8,128)(2,1)S(1)}, u32[]{:S(2)}, u32[]{:S(2)}) collective-permute-start(bf16[3,3,192]{0,2,1:T(8,128)(2,1)S(1)} %get-tuple-element.143), channel_id=1, source_target_pairs={{1,8},{2,9},{3,10},{4,11},{5,12},{6,13},{7,14},{9,16},{10,17},{11,... | collective-permute-start | bytes 10376 | tf_op jit(solution)/shard_map/ppermute | solution.py:31
  4.7 35.4 %collective-permute-start.1 = (bf16[3,192,128]{2,1,0:T(8,128)(2,1)}, bf16[3,192,128]{2,1,0:T(8,128)(2,1)S(1)}, u32[]{:S(2)}, u32[]{:S(2)}) collective-permute-start(bf16[3,192,128]{2,1,0:T(8,128)(2,1)} %get-tuple-element.144), channel_id=1, source_target_pairs={{0,8},{8,16},{16,24},{24,32},{32,40},{40,48},{48,56},{1,9},{9,17},... | collective-permute-start | bytes 442376 | tf_op jit(solution)/shard_map/ppermute | solution.py:27
  9.2 13.4 %collective-permute-start = (bf16[3,3,192]{0,2,1:T(8,128)(2,1)S(1)}, bf16[3,3,192]{0,2,1:T(8,128)(2,1)}, u32[]{:S(2)}, u32[]{:S(2)}) collective-permute-start(bf16[3,3,192]{0,2,1:T(8,128)(2,1)S(1)} %get-tuple-element.140), channel_id=1, source_target_pairs={{0,9},{1,10},{2,11},{3,12},{4,13},{5,14},{6,15},{8,17},{9,18},{10,... | collective-permute-start | bytes 10376 | tf_op jit(solution)/shard_map/ppermute | solution.py:31
  16.4 12.6 %collective-permute-start.7 = (bf16[3,3,192]{0,2,1:T(8,128)(2,1)S(1)}, bf16[3,3,192]{0,2,1:T(8,128)(2,1)}, u32[]{:S(2)}, u32[]{:S(2)}) collective-permute-start(bf16[3,3,192]{0,2,1:T(8,128)(2,1)S(1)} %get-tuple-element.141), channel_id=1, source_target_pairs={{9,0},{10,1},{11,2},{12,3},{13,4},{14,5},{15,6},{17,8},{18,9},{19,... | collective-permute-start | bytes 10376 | tf_op jit(solution)/shard_map/ppermute | solution.py:31
  17.7 22.4 %collective-permute-start.6 = (bf16[3,192,128]{2,1,0:T(8,128)(2,1)}, bf16[3,192,128]{2,1,0:T(8,128)(2,1)}, u32[]{:S(2)}, u32[]{:S(2)}) collective-permute-start(bf16[3,192,128]{2,1,0:T(8,128)(2,1)} %get-tuple-element.145), channel_id=1, source_target_pairs={{8,0},{16,8},{24,16},{32,24},{40,32},{48,40},{56,48},{9,1},{17,9},... | collective-permute-start | bytes 442376 | tf_op jit(solution)/shard_map/ppermute | solution.py:27
  19.9 23.5 %copy-start.15 = (f32[192,1]{0,1:T(1,128)}, f32[192,1]{0,1:T(1,128)S(1)}, u32[]{:S(2)}) copy-start(f32[192,1]{0,1:T(1,128)S(1)} %get-tuple-element.155) | copy-start | bytes 2308
  19.9 23.5 %copy-start.17 = (f32[192,1]{0,1:T(1,128)}, f32[192,1]{0,1:T(1,128)S(1)}, u32[]{:S(2)}) copy-start(f32[192,1]{0,1:T(1,128)S(1)} %get-tuple-element.156) | copy-start | bytes 2308
  19.9 23.5 %copy-start.19 = (f32[192,1]{0,1:T(1,128)}, f32[192,1]{0,1:T(1,128)S(1)}, u32[]{:S(2)}) copy-start(f32[192,1]{0,1:T(1,128)S(1)} %get-tuple-element.157) | copy-start | bytes 2308
  19.9 23.5 %copy-start.21 = (f32[192,1]{0,1:T(1,128)}, f32[192,1]{0,1:T(1,128)S(1)}, u32[]{:S(2)}) copy-start(f32[192,1]{0,1:T(1,128)S(1)} %get-tuple-element.158) | copy-start | bytes 2308
  19.9 23.5 %copy-start.23 = (f32[192,1]{0,1:T(1,128)}, f32[192,1]{0,1:T(1,128)S(1)}, u32[]{:S(2)}) copy-start(f32[192,1]{0,1:T(1,128)S(1)} %get-tuple-element.159) | copy-start | bytes 2308
  19.9 23.5 %copy-start.25 = (f32[192,1]{0,1:T(1,128)}, f32[192,1]{0,1:T(1,128)S(1)}, u32[]{:S(2)}) copy-start(f32[192,1]{0,1:T(1,128)S(1)} %get-tuple-element.160) | copy-start | bytes 2308
  19.9 23.5 %copy-start.27 = (f32[192,1]{0,1:T(1,128)}, f32[192,1]{0,1:T(1,128)S(1)}, u32[]{:S(2)}) copy-start(f32[192,1]{0,1:T(1,128)S(1)} %get-tuple-element.161) | copy-start | bytes 2308
  19.9 23.5 %copy-start.29 = (f32[192,1]{0,1:T(1,128)}, f32[192,1]{0,1:T(1,128)S(1)}, u32[]{:S(2)}) copy-start(f32[192,1]{0,1:T(1,128)S(1)} %get-tuple-element.162) | copy-start | bytes 2308
  19.9 23.5 %copy-start.31 = (f32[192,1]{0,1:T(1,128)}, f32[192,1]{0,1:T(1,128)S(1)}, u32[]{:S(2)}) copy-start(f32[192,1]{0,1:T(1,128)S(1)} %get-tuple-element.163) | copy-start | bytes 2308
  19.9 23.5 %copy-start.33 = (f32[192,1]{0,1:T(1,128)}, f32[192,1]{0,1:T(1,128)S(1)}, u32[]{:S(2)}) copy-start(f32[192,1]{0,1:T(1,128)S(1)} %get-tuple-element.164) | copy-start | bytes 2308
  20.0 23.5 %copy-start.35 = (f32[192,1]{0,1:T(1,128)}, f32[192,1]{0,1:T(1,128)S(1)}, u32[]{:S(2)}) copy-start(f32[192,1]{0,1:T(1,128)S(1)} %get-tuple-element.165) | copy-start | bytes 2308
  21.4 18.8 %collective-permute-start.4 = (bf16[3,8,192]{0,2,1:T(8,128)(2,1)S(1)}, bf16[3,8,192]{0,2,1:T(8,128)(2,1)S(1)}, u32[]{:S(2)}, u32[]{:S(2)}) collective-permute-start(bf16[3,8,192]{0,2,1:T(8,128)(2,1)S(1)} %get-tuple-element.147), channel_id=1, source_target_pairs={{1,0},{2,1},{3,2},{4,3},{5,4},{6,5},{7,6},{9,8},{10,9},{11,10},{12... | collective-permute-start | bytes 27656 | tf_op jit(solution)/shard_map/ppermute | solution.py:29
  22.7 17.5 %collective-permute-start.3 = (bf16[3,8,192]{0,2,1:T(8,128)(2,1)S(1)}, bf16[3,8,192]{0,2,1:T(8,128)(2,1)S(1)}, u32[]{:S(2)}, u32[]{:S(2)}) collective-permute-start(bf16[3,8,192]{0,2,1:T(8,128)(2,1)S(1)} %get-tuple-element.146), channel_id=1, source_target_pairs={{0,1},{1,2},{2,3},{3,4},{4,5},{5,6},{6,7},{8,9},{9,10},{10,11},{11... | collective-permute-start | bytes 27656 | tf_op jit(solution)/shard_map/ppermute | solution.py:29
  29.1 11.1 %collective-permute-start.5 = (bf16[3,3,192]{0,2,1:T(8,128)(2,1)}, bf16[3,3,192]{0,2,1:T(8,128)(2,1)}, u32[]{:S(2)}, u32[]{:S(2)}) collective-permute-start(bf16[3,3,192]{0,2,1:T(8,128)(2,1)} %get-tuple-element.142), channel_id=1, source_target_pairs={{8,1},{9,2},{10,3},{11,4},{12,5},{13,6},{14,7},{16,9},{17,10},{18,... | collective-permute-start | bytes 10376 | tf_op jit(solution)/shard_map/ppermute | solution.py:31
  91.9 58.4 %collective-permute-start.8 = (f32[1664,128]{1,0:T(8,128)}, f32[1664,128]{1,0:T(8,128)}, u32[]{:S(2)}, u32[]{:S(2)}) collective-permute-start(f32[1664,128]{1,0:T(8,128)} %dynamic-slice_bitcast_fusion), channel_id=1, source_target_pairs={{0,8},{1,9},{2,10},{3,11},{4,12},{5,13},{6,14},{7,15},{8,0},{9,1},... | collective-permute-start | bytes 2555912 | tf_op jit(solution)/shard_map/ppermute | solution.py:258
  92.0 13.9 %collective-permute-start.16 = (bf16[3,3,192]{0,2,1:T(8,128)(2,1)S(1)}, bf16[3,3,192]{0,2,1:T(8,128)(2,1)}, u32[]{:S(2)}, u32[]{:S(2)}) collective-permute-start(bf16[3,3,192]{0,2,1:T(8,128)(2,1)S(1)} %get-tuple-element.135), channel_id=1, source_target_pairs={{9,0},{10,1},{11,2},{12,3},{13,4},{14,5},{15,6},{17,8},{18,9},{19,... | collective-permute-start | bytes 10376 | tf_op jit(solution)/shard_map/ppermute | solution.py:31
  93.3 16.2 %collective-permute-start.14 = (bf16[3,3,192]{0,2,1:T(8,128)(2,1)S(1)}, bf16[3,3,192]{0,2,1:T(8,128)(2,1)S(1)}, u32[]{:S(2)}, u32[]{:S(2)}) collective-permute-start(bf16[3,3,192]{0,2,1:T(8,128)(2,1)S(1)} %get-tuple-element.132), channel_id=1, source_target_pairs={{8,1},{9,2},{10,3},{11,4},{12,5},{13,6},{14,7},{16,9},{17,10},{18,... | collective-permute-start | bytes 10376 | tf_op jit(solution)/shard_map/ppermute | solution.py:31
  102.6 44.0 %collective-permute-start.15 = (bf16[3,192,128]{2,1,0:T(8,128)(2,1)}, bf16[3,192,128]{2,1,0:T(8,128)(2,1)}, u32[]{:S(2)}, u32[]{:S(2)}) collective-permute-start(bf16[3,192,128]{2,1,0:T(8,128)(2,1)} %get-tuple-element.136), channel_id=1, source_target_pairs={{8,0},{16,8},{24,16},{32,24},{40,32},{48,40},{56,48},{9,1},{17,9},... | collective-permute-start | bytes 442376 | tf_op jit(solution)/shard_map/ppermute | solution.py:27
  104.5 14.6 %collective-permute-start.19 = (bf16[3,3,192]{0,2,1:T(8,128)(2,1)S(1)}, bf16[3,3,192]{0,2,1:T(8,128)(2,1)S(1)}, u32[]{:S(2)}, u32[]{:S(2)}) collective-permute-start(bf16[3,3,192]{0,2,1:T(8,128)(2,1)S(1)} %get-tuple-element.133), channel_id=1, source_target_pairs={{1,8},{2,9},{3,10},{4,11},{5,12},{6,13},{7,14},{9,16},{10,17},{11,... | collective-permute-start | bytes 10376 | tf_op jit(solution)/shard_map/ppermute | solution.py:31
  105.9 40.7 %collective-permute-start.18 = (bf16[3,192,128]{2,1,0:T(8,128)(2,1)}, bf16[3,192,128]{2,1,0:T(8,128)(2,1)}, u32[]{:S(2)}, u32[]{:S(2)}) collective-permute-start(bf16[3,192,128]{2,1,0:T(8,128)(2,1)} %get-tuple-element.137), channel_id=1, source_target_pairs={{0,8},{8,16},{16,24},{24,32},{32,40},{40,48},{48,56},{1,9},{9,17},... | collective-permute-start | bytes 442376 | tf_op jit(solution)/shard_map/ppermute | solution.py:27
  110.2 16.8 %collective-permute-start.17 = (bf16[3,3,192]{0,2,1:T(8,128)(2,1)S(1)}, bf16[3,3,192]{0,2,1:T(8,128)(2,1)S(1)}, u32[]{:S(2)}, u32[]{:S(2)}) collective-permute-start(bf16[3,3,192]{0,2,1:T(8,128)(2,1)S(1)} %get-tuple-element.134), channel_id=1, source_target_pairs={{0,9},{1,10},{2,11},{3,12},{4,13},{5,14},{6,15},{8,17},{9,18},{10,... | collective-permute-start | bytes 10376 | tf_op jit(solution)/shard_map/ppermute | solution.py:31
  119.8 15.7 %collective-permute-start.12 = (bf16[3,8,192]{0,2,1:T(8,128)(2,1)S(1)}, bf16[3,8,192]{0,2,1:T(8,128)(2,1)S(1)}, u32[]{:S(2)}, u32[]{:S(2)}) collective-permute-start(bf16[3,8,192]{0,2,1:T(8,128)(2,1)S(1)} %get-tuple-element.139), channel_id=1, source_target_pairs={{0,1},{1,2},{2,3},{3,4},{4,5},{5,6},{6,7},{8,9},{9,10},{10,11},{11... | collective-permute-start | bytes 27656 | tf_op jit(solution)/shard_map/ppermute | solution.py:29
  127.7 18.9 %collective-permute-start.13 = (bf16[3,8,192]{0,2,1:T(8,128)(2,1)S(1)}, bf16[3,8,192]{0,2,1:T(8,128)(2,1)S(1)}, u32[]{:S(2)}, u32[]{:S(2)}) collective-permute-start(bf16[3,8,192]{0,2,1:T(8,128)(2,1)S(1)} %get-tuple-element.138), channel_id=1, source_target_pairs={{1,0},{2,1},{3,2},{4,3},{5,4},{6,5},{7,6},{9,8},{10,9},{11,10},{12... | collective-permute-start | bytes 27656 | tf_op jit(solution)/shard_map/ppermute | solution.py:29
  151.6 15.1 %collective-permute-start.11 = (f32[416,128]{1,0:T(8,128)S(1)}, f32[416,128]{1,0:T(8,128)S(1)}, u32[]{:S(2)}, u32[]{:S(2)}) collective-permute-start(f32[416,128]{1,0:T(8,128)S(1)} %get-tuple-element.129), channel_id=1, source_target_pairs={{0,65},{1,64},{2,67},{3,66},{4,69},{5,68},{6,71},{7,70},{8,73},{9,... | collective-permute-start | bytes 638984 | tf_op jit(solution)/shard_map/ppermute | solution.py:258
  156.3 10.5 %collective-permute-start.10 = (f32[416,128]{1,0:T(8,128)S(1)}, f32[416,128]{1,0:T(8,128)S(1)}, u32[]{:S(2)}, u32[]{:S(2)}) collective-permute-start(f32[416,128]{1,0:T(8,128)S(1)} %get-tuple-element.130), channel_id=1, source_target_pairs={{0,1},{1,0},{2,3},{3,2},{4,5},{5,4},{6,7},{7,6},{8,9},{9,8},{10,11... | collective-permute-start | bytes 638984 | tf_op jit(solution)/shard_map/ppermute | solution.py:258
  156.5 10.5 %collective-permute-start.9 = (f32[416,128]{1,0:T(8,128)S(1)}, f32[416,128]{1,0:T(8,128)S(1)}, u32[]{:S(2)}, u32[]{:S(2)}) collective-permute-start(f32[416,128]{1,0:T(8,128)S(1)} %get-tuple-element.128), channel_id=1, source_target_pairs={{0,64},{1,65},{2,66},{3,67},{4,68},{5,69},{6,70},{7,71},{8,72},{9,... | collective-permute-start | bytes 638984 | tf_op jit(solution)/shard_map/ppermute | solution.py:258
  167.1 4.3 %collective-permute-start.22 = (f32[104,128]{1,0:T(8,128)S(1)}, f32[104,128]{1,0:T(8,128)S(1)}, u32[]{:S(2)}, u32[]{:S(2)}) collective-permute-start(f32[104,128]{1,0:T(8,128)S(1)} %get-tuple-element.149), channel_id=1, source_target_pairs={{0,6},{1,7},{2,4},{3,5},{4,2},{5,3},{6,0},{7,1},{8,14},{9,15},{10,... | collective-permute-start | bytes 159752 | tf_op jit(solution)/shard_map/ppermute | solution.py:258
  167.2 4.8 %collective-permute-start.21 = (f32[104,128]{1,0:T(8,128)S(1)}, f32[104,128]{1,0:T(8,128)S(1)}, u32[]{:S(2)}, u32[]{:S(2)}) collective-permute-start(f32[104,128]{1,0:T(8,128)S(1)} %get-tuple-element.150), channel_id=1, source_target_pairs={{0,4},{1,5},{2,6},{3,7},{4,0},{5,1},{6,2},{7,3},{8,12},{9,13},{10,... | collective-permute-start | bytes 159752 | tf_op jit(solution)/shard_map/ppermute | solution.py:258
  170.3 3.4 %collective-permute-start.20 = (f32[104,128]{1,0:T(8,128)S(1)}, f32[104,128]{1,0:T(8,128)S(1)}, u32[]{:S(2)}, u32[]{:S(2)}) collective-permute-start(f32[104,128]{1,0:T(8,128)S(1)} %get-tuple-element.148), channel_id=1, source_target_pairs={{0,2},{1,3},{2,0},{3,1},{4,6},{5,7},{6,4},{7,5},{8,10},{9,11},{10,... | collective-permute-start | bytes 159752 | tf_op jit(solution)/shard_map/ppermute | solution.py:258
  173.8 4.7 %collective-permute-start.25 = (f32[26,128]{1,0:T(8,128)S(1)}, f32[26,128]{1,0:T(8,128)S(1)}, u32[]{:S(2)}, u32[]{:S(2)}) collective-permute-start(f32[26,128]{1,0:T(8,128)S(1)} %get-tuple-element.152), channel_id=1, source_target_pairs={{0,48},{1,49},{2,50},{3,51},{4,52},{5,53},{6,54},{7,55},{8,56},{9,... | collective-permute-start | bytes 39944 | tf_op jit(solution)/shard_map/ppermute | solution.py:258
  176.6 4.1 %collective-permute-start.24 = (f32[26,128]{1,0:T(8,128)S(1)}, f32[26,128]{1,0:T(8,128)S(1)}, u32[]{:S(2)}, u32[]{:S(2)}) collective-permute-start(f32[26,128]{1,0:T(8,128)S(1)} %get-tuple-element.153), channel_id=1, source_target_pairs={{0,32},{1,33},{2,34},{3,35},{4,36},{5,37},{6,38},{7,39},{8,40},{9,... | collective-permute-start | bytes 39944 | tf_op jit(solution)/shard_map/ppermute | solution.py:258
  178.4 2.6 %collective-permute-start.23 = (f32[26,128]{1,0:T(8,128)S(1)}, f32[26,128]{1,0:T(8,128)S(1)}, u32[]{:S(2)}, u32[]{:S(2)}) collective-permute-start(f32[26,128]{1,0:T(8,128)S(1)} %get-tuple-element.151), channel_id=1, source_target_pairs={{0,16},{1,17},{2,18},{3,19},{4,20},{5,21},{6,22},{7,23},{8,24},{9,... | collective-permute-start | bytes 39944 | tf_op jit(solution)/shard_map/ppermute | solution.py:258
  181.1 3.9 %collective-permute-start.26 = (f32[26,128]{1,0:T(8,128)S(1)}, f32[26,128]{1,0:T(8,128)S(1)}, u32[]{:S(2)}, u32[]{:S(2)}) collective-permute-start(f32[26,128]{1,0:T(8,128)S(1)} %get-tuple-element.114), channel_id=1, source_target_pairs={{0,16},{1,17},{2,18},{3,19},{4,20},{5,21},{6,22},{7,23},{8,24},{9,... | collective-permute-start | bytes 39944 | tf_op jit(solution)/shard_map/ppermute | solution.py:275
  181.3 4.1 %collective-permute-start.27 = (f32[26,128]{1,0:T(8,128)S(1)}, f32[26,128]{1,0:T(8,128)S(1)}, u32[]{:S(2)}, u32[]{:S(2)}) collective-permute-start(f32[26,128]{1,0:T(8,128)S(1)} %get-tuple-element.114), channel_id=1, source_target_pairs={{0,32},{1,33},{2,34},{3,35},{4,36},{5,37},{6,38},{7,39},{8,40},{9,... | collective-permute-start | bytes 39944 | tf_op jit(solution)/shard_map/ppermute | solution.py:275
  183.0 3.8 %collective-permute-start.28 = (f32[26,128]{1,0:T(8,128)S(1)}, f32[26,128]{1,0:T(8,128)S(1)}, u32[]{:S(2)}, u32[]{:S(2)}) collective-permute-start(f32[26,128]{1,0:T(8,128)S(1)} %get-tuple-element.114), channel_id=1, source_target_pairs={{0,48},{1,49},{2,50},{3,51},{4,52},{5,53},{6,54},{7,55},{8,56},{9,... | collective-permute-start | bytes 39944 | tf_op jit(solution)/shard_map/ppermute | solution.py:275
  186.8 4.2 %collective-permute-start.29 = (f32[104,128]{1,0:T(8,128)S(1)}, f32[104,128]{1,0:T(8,128)S(1)}, u32[]{:S(2)}, u32[]{:S(2)}) collective-permute-start(f32[104,128]{1,0:T(8,128)S(1)} %reshape.217), channel_id=1, source_target_pairs={{0,2},{1,3},{2,0},{3,1},{4,6},{5,7},{6,4},{7,5},{8,10},{9,11},{10,... | collective-permute-start | bytes 159752 | tf_op jit(solution)/shard_map/ppermute | solution.py:275
  188.0 4.5 %collective-permute-start.30 = (f32[104,128]{1,0:T(8,128)S(1)}, f32[104,128]{1,0:T(8,128)S(1)}, u32[]{:S(2)}, u32[]{:S(2)}) collective-permute-start(f32[104,128]{1,0:T(8,128)S(1)} %reshape.217), channel_id=1, source_target_pairs={{0,4},{1,5},{2,6},{3,7},{4,0},{5,1},{6,2},{7,3},{8,12},{9,13},{10,... | collective-permute-start | bytes 159752 | tf_op jit(solution)/shard_map/ppermute | solution.py:275
  190.3 4.2 %collective-permute-start.31 = (f32[104,128]{1,0:T(8,128)S(1)}, f32[104,128]{1,0:T(8,128)S(1)}, u32[]{:S(2)}, u32[]{:S(2)}) collective-permute-start(f32[104,128]{1,0:T(8,128)S(1)} %reshape.217), channel_id=1, source_target_pairs={{0,6},{1,7},{2,4},{3,5},{4,2},{5,3},{6,0},{7,1},{8,14},{9,15},{10,... | collective-permute-start | bytes 159752 | tf_op jit(solution)/shard_map/ppermute | solution.py:275
  194.5 5.1 %collective-permute-start.32 = (f32[416,128]{1,0:T(8,128)S(1)}, f32[416,128]{1,0:T(8,128)S(1)}, u32[]{:S(2)}, u32[]{:S(2)}) collective-permute-start(f32[416,128]{1,0:T(8,128)S(1)} %bitcast.421), channel_id=1, source_target_pairs={{0,64},{1,65},{2,66},{3,67},{4,68},{5,69},{6,70},{7,71},{8,72},{9,... | collective-permute-start | bytes 638984 | tf_op jit(solution)/shard_map/ppermute | solution.py:275
  195.0 7.1 %collective-permute-start.33 = (f32[416,128]{1,0:T(8,128)S(1)}, f32[416,128]{1,0:T(8,128)S(1)}, u32[]{:S(2)}, u32[]{:S(2)}) collective-permute-start(f32[416,128]{1,0:T(8,128)S(1)} %bitcast.422), channel_id=1, source_target_pairs={{0,1},{1,0},{2,3},{3,2},{4,5},{5,4},{6,7},{7,6},{8,9},{9,8},{10,11... | collective-permute-start | bytes 638984 | tf_op jit(solution)/shard_map/ppermute | solution.py:275
  196.5 7.8 %collective-permute-start.34 = (f32[416,128]{1,0:T(8,128)S(1)}, f32[416,128]{1,0:T(8,128)S(1)}, u32[]{:S(2)}, u32[]{:S(2)}) collective-permute-start(f32[416,128]{1,0:T(8,128)S(1)} %bitcast.423), channel_id=1, source_target_pairs={{0,65},{1,64},{2,67},{3,66},{4,69},{5,68},{6,71},{7,70},{8,73},{9,... | collective-permute-start | bytes 638984 | tf_op jit(solution)/shard_map/ppermute | solution.py:275
  204.3 12.0 %collective-permute-start.35 = (f32[1664,128]{1,0:T(8,128)S(1)}, f32[1664,128]{1,0:T(8,128)S(1)}, u32[]{:S(2)}, u32[]{:S(2)}) collective-permute-start(f32[1664,128]{1,0:T(8,128)S(1)} %bitcast.405), channel_id=1, source_target_pairs={{0,8},{1,9},{2,10},{3,11},{4,12},{5,13},{6,14},{7,15},{8,0},{9,1},... | collective-permute-start | bytes 2555912 | tf_op jit(solution)/shard_map/ppermute | solution.py:275
  (110 other events, 849.8 us)

commit v7 on v5

--- a/solution.py
+++ b/solution.py
@@ -303,7 +303,7 @@
         return jnp.where(position == loss_at, 1.0 / cell_count, grad_scale).astype(jnp.float32)
 
     buffer, d_input = butterfly_psum(
-        buffer, axes, [(3,), (6, 0), (1, 2), (4, 5)], scale_of, d_input, 2
+        buffer, axes, [(3,), (6, 0), (1, 2, 4, 5)], scale_of, d_input, 2
     )
     joined, kernel_grad, expand_grad, project_grad, lateral_grad, classify_grad = unpack_rows(
         buffer, shapes

time: 174 us -> 220 us (1.26)
  starting transfers between devices: 63.9 us -> 108 us
  local copies, waits for them, and re-layouts: 28.4 us -> 39 us
  waiting for transfers between devices: 26 us -> 18.9 us
    ppermute x10 -> x19, starting transfers between devices: 20 us -> 45.6 us  [butterfly_psum(): other = lax.ppermute(buffer, axes, pairs)]
    ppermute x10 -> x19, starting transfers between devices: 15.7 us -> 33.8 us  [butterfly_psum(): total = total + lax.ppermute(send, axes, pairs)]
    another operation x2, local copies, waits for them, and re-layouts: 4.39 us -> 10.7 us  [conv_backward(): kernel_grad = jnp.stack(columns, axis=1)]
    ppermute x10 -> x19, waiting for transfers between devices: 12.8 us -> 9.06 us  [butterfly_psum(): other = lax.ppermute(buffer, axes, pairs)]
    ppermute x10 -> x19, waiting for transfers between devices: 6.65 us -> 3.46 us  [butterfly_psum(): total = total + lax.ppermute(send, axes, pairs)]
    unnamed x271 -> x207, local copies, waits for them, and re-layouts: 8.94 us -> 10.2 us
  transfers between devices with their start and end apart: 28 -> 46, of which waited for: 18 -> 12; matrix products, arithmetic and copies ran while one was open for 10% -> 7% of each run, Pallas kernels for 0% -> 0%
where the time goes in v7:
time: 220 us; the launch traced here: 219 us
  starting transfers between devices  108 us (49%)
  local copies, waits for them, and re-layouts  39 us (18%)
  other arithmetic  37.3 us (17%)
  waiting for transfers between devices  18.9 us (9%)
  matrix products  13.7 us (6%)
  between operations  2.79 us (1%)
    ppermute x19, starting transfers between devices, butterfly_psum(): other = lax.ppermute(buffer, axes, pairs)  45.6 us
    ppermute x19, starting transfers between devices, butterfly_psum(): total = total + lax.ppermute(send, axes, pairs)  33.8 us
    ppermute x4, starting transfers between devices, padded_2(): before = jnp.transpose(lax.ppermute(last, axis, up), order)  20.5 us
    dot_general x12, matrix products, product(): jnp.einsum(form, left_side, right_side, preferred_element_type=jnp.float32)  13.7 us
    reduce_sum x4, other arithmetic, conv_backward(): columns.append(jnp.sum(window * conv_float, axis=(1, 2)))  12.2 us
    another operation x2, local copies, waits for them, and re-layouts, conv_backward(): kernel_grad = jnp.stack(columns, axis=1)  10.7 us
    unnamed x207, local copies, waits for them, and re-layouts  10.2 us
    ppermute x19, waiting for transfers between devices, butterfly_psum(): other = lax.ppermute(buffer, axes, pairs)  9.06 us
  transfers between devices with their start and end apart: 46, of which 12 were waited for; matrix products, arithmetic and copies ran while one was open for 7% of the time, Pallas kernels for 0%

profile of v7, /device:TPU:1, one launch (start us, length us, event | category | flops | bytes accessed | tf_op | source)
XLA Modules:
  0.0 219.4 jit_solution(960903561988581867)
XLA Ops:
  1.9 3.3 %collective-permute-start.1 = (bf16[3,192,128]{2,1,0:T(8,128)(2,1)S(1)}, bf16[3,192,128]{2,1,0:T(8,128)(2,1)S(1)}, u32[]{:S(2)}, u32[]{:S(2)}) collective-permute-start(bf16[3,192,128]{2,1,0:T(8,128)(2,1)S(1)} %get-tuple-element.154), channel_id=1, source_target_pairs={{8,0},{16,8},{24,16},{32,24},{40,32},{48,40},{56,48},{9,1},{17,9},... | collective-permute-start | bytes 442376 | tf_op jit(solution)/shard_map/ppermute | solution.py:22
  5.2 3.1 %collective-permute-start = (bf16[3,192,128]{2,1,0:T(8,128)(2,1)S(1)}, bf16[3,192,128]{2,1,0:T(8,128)(2,1)S(1)}, u32[]{:S(2)}, u32[]{:S(2)}) collective-permute-start(bf16[3,192,128]{2,1,0:T(8,128)(2,1)S(1)} %get-tuple-element.153), channel_id=1, source_target_pairs={{0,8},{8,16},{16,24},{24,32},{32,40},{40,48},{48,56},{1,9},{9,17},... | collective-permute-start | bytes 442376 | tf_op jit(solution)/shard_map/ppermute | solution.py:21
  11.2 1.3 collective-permute-start.3
  12.9 5.5 %collective-permute-start.2 = (bf16[3,14,192]{2,1,0:T(8,128)(2,1)S(1)}, bf16[3,14,192]{2,1,0:T(8,128)(2,1)S(1)}, u32[]{:S(2)}, u32[]{:S(2)}) collective-permute-start(bf16[3,14,192]{2,1,0:T(8,128)(2,1)S(1)} %copy.55), channel_id=1, source_target_pairs={{0,1},{1,2},{2,3},{3,4},{4,5},{5,6},{6,7},{8,9},{9,10},{10,11},{11... | collective-permute-start | bytes 48392 | tf_op jit(solution)/shard_map/ppermute | solution.py:21
  21.4 9.0 %fusion.191 = (f32[8,128]{1,0:T(8,128)S(1)}, f32[192,8,128]{2,0,1:T(8,128)S(1)}) fusion(f32[192]{0:T(256)S(1)} %copy-done.96, bf16[192,14,131]{2,0,1:T(8,128)(2,1)S(1)} %get-tuple-element.147, f32[192]{0:T(256)} %bitcast.57, f32[192]{0:T(256)} %bitcast.56, f32[192]{0:T(256)S(1)} %bitcast.457, bf16[192,3,128]{2,0,1:T(8,128)(2,1)S(1)} %bitcast.434, ...), kind=kLoop, calls=%fused_computation.415 | loop fusion | flops 30276608 | bytes 18032128 | tf_op jit(solution)/shard_map/reduce_sum | solution.py:65
  34.3 1.9 convert_reduce_fusion.2
  37.4 2.4 %convert_reduce_fusion.1 = (f32[768]{0:T(1024)}, bf16[768,8,128]{0,2,1:T(8,128)(2,1)S(1)}) fusion(f32[8,128,768]{2,1,0:T(8,128)S(1)} %get-tuple-element.225, f32[768]{0:T(1024)S(1)} %copy-done.93, bf16[192,8,128]{2,0,1:T(8,128)(2,1)S(1)} %get-tuple-element.134, bf16[768,192]{0,1:T(8,128)(2,1)S(1)} %copy-done.11), kind=kOutput, calls=%fused_computation.64 | convolution fusion | flops 312212736 | bytes 5412864 | tf_op jit(solution)/shard_map/chw,dc->dhw/dot_general | solution.py:34
  39.8 1.4 fusion.147
  41.2 4.1 %fusion.117 = (f32[192]{0:T(256)}, f32[192]{0:T(256)}, f32[192]{0:T(256)}, f32[192]{0:T(256)}, f32[192]{0:T(256)}, /*index=5*/f32[192]{0:T(256)}, f32[192]{0:T(2...) fusion(bf16[192,14,131]{2,0,1:T(8,128)(2,1)S(1)} %get-tuple-ele, ...), kind=kLoop, calls=%fused_computation.238 | loop fusion | flops 12382848 | bytes 9074944 | tf_op jit(solution)/shard_map/reduce_sum | solution.py:122
  45.3 4.4 %fusion.121 = (f32[192]{0:T(256)}, f32[192]{0:T(256)}, f32[192]{0:T(256)}, f32[192]{0:T(256)}, f32[192]{0:T(256)}, /*index=5*/f32[192]{0:T(256)}, f32[192]{0:T(2...) fusion(bf16[192,8,128]{2,0,1:T(8,128)(2,1)S(1)} %get-tuple-elem, ...), kind=kLoop, calls=%fused_computation.242 | loop fusion | flops 11006400 | bytes 7485696 | tf_op jit(solution)/shard_map/reduce_sum | solution.py:122
  50.7 2.7 %fusion.120 = (f32[192]{0:T(256)}, f32[192]{0:T(256)}, f32[192]{0:T(256)}, f32[192]{0:T(256)}, f32[192]{0:T(256)}, /*index=5*/f32[192]{0:T(256)}, f32[192]{0:T(256)}, f32[192]{0:T(256)}, f32[192]{0:T(256)}, f32[192]{0:T(256)}) fusion(bf16[192,8,128]{2,0,1:T(8,128)(2,1)S(1)} %get-tuple-element.130, bf16[192,14,131]{2,0,1:T(8,128)(2,1)S(1)} %get-tuple-element.147, ...), kind=kLoop, calls=%fused_computation.241 | loop fusion | flops 7272576 | bytes 2661888 | tf_op jit(solution)/shard_map/reduce_sum | solution.py:122
  54.0 1.3 fusion.199
  58.8 1.5 concatenate.131
  60.9 9.2 %stack.199 = f32[192,49]{0,1:T(8,128)} concatenate(f32[192,1]{0,1:T(1,128)} %bitcast.561, f32[192,1]{0,1:T(1,128)} %bitcast.560, f32[192,1]{0,1:T(1,128)} %bitcast.559, f32[192,1]{0,1:T(1,128)} %bitcast.555, f32[192,1]{0,1:T(1,128)} %bitcast.532, f32[192,1]{0,1:T(1,128)} %bitcast.533, f32[192,1]{0,1:T(1,128)} %bitcast.534, f32[192,1]{0,1:T(1,128)} %bitcast.563, ...), dimensions={1} | concatenate | bytes 75264 | tf_op jit(solution)/shard_map/stack | solution.py:123
  70.1 1.6 copy.63
  71.6 1.7 reshape.197
  73.3 1.7 reshape.205
  75.0 1.4 bitcast_dynamic-update-slice_fusion.5
  80.2 2.1 dynamic-slice_bitcast_fusion
  82.3 5.5 %collective-permute-start.8 = (bf16[3,192,128]{2,1,0:T(8,128)(2,1)S(1)}, bf16[3,192,128]{2,1,0:T(8,128)(2,1)S(1)}, u32[]{:S(2)}, u32[]{:S(2)}) collective-permute-start(bf16[3,192,128]{2,1,0:T(8,128)(2,1)S(1)} %get-tuple-element.152), channel_id=1, source_target_pairs={{0,8},{8,16},{16,24},{24,32},{32,40},{40,48},{48,56},{1,9},{9,17},... | collective-permute-start | bytes 442376 | tf_op jit(solution)/shard_map/ppermute | solution.py:21
  87.8 1.9 collective-permute-start.9
  89.9 4.4 %collective-permute-done.9 = bf16[3,192,128]{2,1,0:T(8,128)(2,1)S(1)} collective-permute-done((bf16[3,192,128]{2,1,0:T(8,128)(2,1)S(1)}, bf16[3,192,128]{2,1,0:T(8,128)(2,1)S(1)}, u32[]{:S(2)}, u32[]{:S(2)}) %collective-permute-start.9) | collective-permute-done | bytes 147488 | tf_op jit(solution)/shard_map/ppermute | solution.py:22
  95.7 1.3 collective-permute-start.10
  97.4 6.4 %collective-permute-start.11 = (bf16[3,14,192]{2,1,0:T(8,128)(2,1)S(1)}, bf16[3,14,192]{2,1,0:T(8,128)(2,1)S(1)}, u32[]{:S(2)}, u32[]{:S(2)}) collective-permute-start(bf16[3,14,192]{2,1,0:T(8,128)(2,1)S(1)} %copy.71), channel_id=1, source_target_pairs={{0,1},{1,2},{2,3},{3,4},{4,5},{5,6},{6,7},{8,9},{9,10},{10,11},{11... | collective-permute-start | bytes 48392 | tf_op jit(solution)/shard_map/ppermute | solution.py:21
  105.1 2.3 %pad_maximum_fusion.1 = (bf16[192,14,131]{2,0,1:T(8,128)(2,1)S(1)}, bf16[192,14,131]{2,0,1:T(8,128)(2,1)S(1)}) fusion(bf16[192,14,3]{2,0,1:T(8,128)(2,1)S(1)} %bitcast.429, bf16[192,3,128]{2,0,1:T(8,128)(2,1)} %bitcast.449, bf16[192,8,128]{2,0,1:T(8,128)(2,1)S(1)} %get-tuple-element.130, bf16[192,3,128]{2,0,1:T(8,128)(2,1)S(1)} %bitcast.446, ...), kind=kLoop, calls=%fused_computation.81 | loop fusion | flops 5634048 | bytes 2128896 | tf_op jit(solution)/shard_map/concatenate | solution.py:23
  109.1 4.4 %collective-permute-start.7 = (f32[416,128]{1,0:T(8,128)S(1)}, f32[416,128]{1,0:T(8,128)S(1)}, u32[]{:S(2)}, u32[]{:S(2)}) collective-permute-start(f32[416,128]{1,0:T(8,128)S(1)} %get-tuple-element.140), channel_id=1, source_target_pairs={{0,65},{1,64},{2,67},{3,66},{4,69},{5,68},{6,71},{7,70},{8,73},{9,... | collective-permute-start | bytes 638984 | tf_op jit(solution)/shard_map/ppermute | solution.py:224
  114.5 8.9 %fusion.148 = f32[192,8,128]{2,0,1:T(8,128)S(1)} fusion(f32[192,8,128]{2,0,1:T(8,128)S(1)} %get-tuple-element.232, bf16[192,8,128]{2,0,1:T(8,128)(2,1)S(1)} %get-tuple-element.130, bf16[192,3,128]{2,0,1:T(8,128)(2,1)S(1)} %bitcast.447, bf16[192,3,128]{2,0,1:T(8,128)(2,1)S(1)} %bitcast.450, bf16[192,14,131]{2,0,1:T(8,128)(2,1)S(1)} %get-tuple-element.144, ...), kind=kLoop, calls=%fused_computation.278 | loop fusion | flops 30081024 | bytes 18813696 | tf_op jit(solution)/shard_map/add | solution.py:113
  123.6 5.0 %collective-permute-start.26 = (f32[26,128]{1,0:T(8,128)S(1)}, f32[26,128]{1,0:T(8,128)S(1)}, u32[]{:S(2)}, u32[]{:S(2)}) collective-permute-start(f32[26,128]{1,0:T(8,128)S(1)} %get-tuple-element.156), channel_id=1, source_target_pairs={{0,54},{1,55},{2,52},{3,53},{4,50},{5,51},{6,48},{7,49},{8,62},{9,... | collective-permute-start | bytes 39944 | tf_op jit(solution)/shard_map/ppermute | solution.py:224
  128.6 3.2 %collective-permute-start.25 = (f32[26,128]{1,0:T(8,128)S(1)}, f32[26,128]{1,0:T(8,128)S(1)}, u32[]{:S(2)}, u32[]{:S(2)}) collective-permute-start(f32[26,128]{1,0:T(8,128)S(1)} %get-tuple-element.157), channel_id=1, source_target_pairs={{0,52},{1,53},{2,54},{3,55},{4,48},{5,49},{6,50},{7,51},{8,60},{9,... | collective-permute-start | bytes 39944 | tf_op jit(solution)/shard_map/ppermute | solution.py:224
  133.1 5.4 %collective-permute-start.22 = (f32[26,128]{1,0:T(8,128)S(1)}, f32[26,128]{1,0:T(8,128)S(1)}, u32[]{:S(2)}, u32[]{:S(2)}) collective-permute-start(f32[26,128]{1,0:T(8,128)S(1)} %get-tuple-element.160), channel_id=1, source_target_pairs={{0,38},{1,39},{2,36},{3,37},{4,34},{5,35},{6,32},{7,33},{8,46},{9,... | collective-permute-start | bytes 39944 | tf_op jit(solution)/shard_map/ppermute | solution.py:224
  138.5 1.3 collective-permute-start.21
  141.8 3.6 %collective-permute-start.18 = (f32[26,128]{1,0:T(8,128)S(1)}, f32[26,128]{1,0:T(8,128)S(1)}, u32[]{:S(2)}, u32[]{:S(2)}) collective-permute-start(f32[26,128]{1,0:T(8,128)S(1)} %get-tuple-element.164), channel_id=1, source_target_pairs={{0,22},{1,23},{2,20},{3,21},{4,18},{5,19},{6,16},{7,17},{8,30},{9,... | collective-permute-start | bytes 39944 | tf_op jit(solution)/shard_map/ppermute | solution.py:224
  148.0 3.8 %collective-permute-start.14 = (f32[26,128]{1,0:T(8,128)S(1)}, f32[26,128]{1,0:T(8,128)S(1)}, u32[]{:S(2)}, u32[]{:S(2)}) collective-permute-start(f32[26,128]{1,0:T(8,128)S(1)} %get-tuple-element.168), channel_id=1, source_target_pairs={{0,6},{1,7},{2,4},{3,5},{4,2},{5,3},{6,0},{7,1},{8,14},{9,15},{10,... | collective-permute-start | bytes 39944 | tf_op jit(solution)/shard_map/ppermute | solution.py:224
  152.9 3.0 %collective-permute-done.13 = f32[26,128]{1,0:T(8,128)S(1)} collective-permute-done((f32[26,128]{1,0:T(8,128)S(1)}, f32[26,128]{1,0:T(8,128)S(1)}, u32[]{:S(2)}, u32[]{:S(2)}) %collective-permute-start.13) | collective-permute-done | bytes 13344 | tf_op jit(solution)/shard_map/ppermute | solution.py:224
  156.2 1.9 collective-permute-start.28
  158.2 1.9 collective-permute-start.29
  160.5 2.6 %collective-permute-start.32 = (f32[26,128]{1,0:T(8,128)S(1)}, f32[26,128]{1,0:T(8,128)S(1)}, u32[]{:S(2)}, u32[]{:S(2)}) collective-permute-start(f32[26,128]{1,0:T(8,128)S(1)} %get-tuple-element.129), channel_id=1, source_target_pairs={{0,20},{1,21},{2,22},{3,23},{4,16},{5,17},{6,18},{7,19},{8,28},{9,... | collective-permute-start | bytes 39944 | tf_op jit(solution)/shard_map/ppermute | solution.py:241
  163.1 3.0 %collective-permute-start.33 = (f32[26,128]{1,0:T(8,128)S(1)}, f32[26,128]{1,0:T(8,128)S(1)}, u32[]{:S(2)}, u32[]{:S(2)}) collective-permute-start(f32[26,128]{1,0:T(8,128)S(1)} %get-tuple-element.129), channel_id=1, source_target_pairs={{0,22},{1,23},{2,20},{3,21},{4,18},{5,19},{6,16},{7,17},{8,30},{9,... | collective-permute-start | bytes 39944 | tf_op jit(solution)/shard_map/ppermute | solution.py:241
  166.8 4.2 %collective-permute-start.36 = (f32[26,128]{1,0:T(8,128)S(1)}, f32[26,128]{1,0:T(8,128)S(1)}, u32[]{:S(2)}, u32[]{:S(2)}) collective-permute-start(f32[26,128]{1,0:T(8,128)S(1)} %get-tuple-element.129), channel_id=1, source_target_pairs={{0,36},{1,37},{2,38},{3,39},{4,32},{5,33},{6,34},{7,35},{8,44},{9,... | collective-permute-start | bytes 39944 | tf_op jit(solution)/shard_map/ppermute | solution.py:241
  171.0 4.0 %collective-permute-start.37 = (f32[26,128]{1,0:T(8,128)S(1)}, f32[26,128]{1,0:T(8,128)S(1)}, u32[]{:S(2)}, u32[]{:S(2)}) collective-permute-start(f32[26,128]{1,0:T(8,128)S(1)} %get-tuple-element.129), channel_id=1, source_target_pairs={{0,38},{1,39},{2,36},{3,37},{4,34},{5,35},{6,32},{7,33},{8,46},{9,... | collective-permute-start | bytes 39944 | tf_op jit(solution)/shard_map/ppermute | solution.py:241
  175.4 4.0 %collective-permute-start.40 = (f32[26,128]{1,0:T(8,128)S(1)}, f32[26,128]{1,0:T(8,128)S(1)}, u32[]{:S(2)}, u32[]{:S(2)}) collective-permute-start(f32[26,128]{1,0:T(8,128)S(1)} %get-tuple-element.129), channel_id=1, source_target_pairs={{0,52},{1,53},{2,54},{3,55},{4,48},{5,49},{6,50},{7,51},{8,60},{9,... | collective-permute-start | bytes 39944 | tf_op jit(solution)/shard_map/ppermute | solution.py:241
  179.4 4.0 %collective-permute-start.41 = (f32[26,128]{1,0:T(8,128)S(1)}, f32[26,128]{1,0:T(8,128)S(1)}, u32[]{:S(2)}, u32[]{:S(2)}) collective-permute-start(f32[26,128]{1,0:T(8,128)S(1)} %get-tuple-element.129), channel_id=1, source_target_pairs={{0,54},{1,55},{2,52},{3,53},{4,50},{5,51},{6,48},{7,49},{8,62},{9,... | collective-permute-start | bytes 39944 | tf_op jit(solution)/shard_map/ppermute | solution.py:241
  183.5 1.8 collective-permute-done.41
  185.9 2.7 %collective-permute-start.43 = (f32[416,128]{1,0:T(8,128)S(1)}, f32[416,128]{1,0:T(8,128)S(1)}, u32[]{:S(2)}, u32[]{:S(2)}) collective-permute-start(f32[416,128]{1,0:T(8,128)S(1)} %reshape.209), channel_id=1, source_target_pairs={{0,1},{1,0},{2,3},{3,2},{4,5},{5,4},{6,7},{7,6},{8,9},{9,8},{10,11... | collective-permute-start | bytes 638984 | tf_op jit(solution)/shard_map/ppermute | solution.py:241
  190.1 3.9 %collective-permute-done.43 = f32[416,128]{1,0:T(8,128)S(1)} collective-permute-done((f32[416,128]{1,0:T(8,128)S(1)}, f32[416,128]{1,0:T(8,128)S(1)}, u32[]{:S(2)}, u32[]{:S(2)}) %collective-permute-start.43) | collective-permute-done | bytes 213024 | tf_op jit(solution)/shard_map/ppermute | solution.py:241
  194.1 2.2 collective-permute-done.44
  196.3 14.3 %collective-permute-start.45 = (f32[1664,128]{1,0:T(8,128)S(1)}, f32[1664,128]{1,0:T(8,128)S(1)}, u32[]{:S(2)}, u32[]{:S(2)}) collective-permute-start(f32[1664,128]{1,0:T(8,128)S(1)} %bitcast.423), channel_id=1, source_target_pairs={{0,8},{1,9},{2,10},{3,11},{4,12},{5,13},{6,14},{7,15},{8,0},{9,1},... | collective-permute-start | bytes 2555912 | tf_op jit(solution)/shard_map/ppermute | solution.py:241
  210.5 1.3 copy.73
  (351 shorter events, 45.1 us)
Async XLA Ops:
  1.9 7.5 %collective-permute-start.1 = (bf16[3,192,128]{2,1,0:T(8,128)(2,1)S(1)}, bf16[3,192,128]{2,1,0:T(8,128)(2,1)S(1)}, u32[]{:S(2)}, u32[]{:S(2)}) collective-permute-start(bf16[3,192,128]{2,1,0:T(8,128)(2,1)S(1)} %get-tuple-element.154), channel_id=1, source_target_pairs={{8,0},{16,8},{24,16},{32,24},{40,32},{48,40},{56,48},{9,1},{17,9},... | collective-permute-start | bytes 442376 | tf_op jit(solution)/shard_map/ppermute | solution.py:22
  5.2 5.2 %collective-permute-start = (bf16[3,192,128]{2,1,0:T(8,128)(2,1)S(1)}, bf16[3,192,128]{2,1,0:T(8,128)(2,1)S(1)}, u32[]{:S(2)}, u32[]{:S(2)}) collective-permute-start(bf16[3,192,128]{2,1,0:T(8,128)(2,1)S(1)} %get-tuple-element.153), channel_id=1, source_target_pairs={{0,8},{8,16},{16,24},{24,32},{32,40},{40,48},{48,56},{1,9},{9,17},... | collective-permute-start | bytes 442376 | tf_op jit(solution)/shard_map/ppermute | solution.py:21
  11.2 7.2 %collective-permute-start.3 = (bf16[3,14,192]{2,1,0:T(8,128)(2,1)S(1)}, bf16[3,14,192]{2,1,0:T(8,128)(2,1)S(1)}, u32[]{:S(2)}, u32[]{:S(2)}) collective-permute-start(bf16[3,14,192]{2,1,0:T(8,128)(2,1)S(1)} %copy.57), channel_id=1, source_target_pairs={{1,0},{2,1},{3,2},{4,3},{5,4},{6,5},{7,6},{9,8},{10,9},{11,10},{12... | collective-permute-start | bytes 48392 | tf_op jit(solution)/shard_map/ppermute | solution.py:22
  12.9 6.4 %collective-permute-start.2 = (bf16[3,14,192]{2,1,0:T(8,128)(2,1)S(1)}, bf16[3,14,192]{2,1,0:T(8,128)(2,1)S(1)}, u32[]{:S(2)}, u32[]{:S(2)}) collective-permute-start(bf16[3,14,192]{2,1,0:T(8,128)(2,1)S(1)} %copy.55), channel_id=1, source_target_pairs={{0,1},{1,2},{2,3},{3,4},{4,5},{5,6},{6,7},{8,9},{9,10},{10,11},{11... | collective-permute-start | bytes 48392 | tf_op jit(solution)/shard_map/ppermute | solution.py:21
  58.2 19.1 %copy-start.5 = (f32[192,768,1]{1,0,2:T(8,128)S(1)}, f32[192,768,1]{1,0,2:T(8,128)}, u32[]{:S(2)}) copy-start(f32[192,768,1]{1,0,2:T(8,128)} %fusion.199) | copy-start | bytes 1769476
  58.2 19.9 %copy-start.7 = (f32[192,512,1]{1,0,2:T(8,128)S(1)}, f32[192,512,1]{1,0,2:T(8,128)}, u32[]{:S(2)}) copy-start(f32[192,512,1]{1,0,2:T(8,128)} %fusion.200) | copy-start | bytes 1179652
  82.3 25.5 %collective-permute-start.4 = (f32[1664,128]{1,0:T(8,128)}, f32[1664,128]{1,0:T(8,128)}, u32[]{:S(2)}, u32[]{:S(2)}) collective-permute-start(f32[1664,128]{1,0:T(8,128)} %dynamic-slice_bitcast_fusion), channel_id=1, source_target_pairs={{0,8},{1,9},{2,10},{3,11},{4,12},{5,13},{6,14},{7,15},{8,0},{9,1},... | collective-permute-start | bytes 2555912 | tf_op jit(solution)/shard_map/ppermute | solution.py:224
  82.3 7.6 %collective-permute-start.8 = (bf16[3,192,128]{2,1,0:T(8,128)(2,1)S(1)}, bf16[3,192,128]{2,1,0:T(8,128)(2,1)S(1)}, u32[]{:S(2)}, u32[]{:S(2)}) collective-permute-start(bf16[3,192,128]{2,1,0:T(8,128)(2,1)S(1)} %get-tuple-element.152), channel_id=1, source_target_pairs={{0,8},{8,16},{16,24},{24,32},{32,40},{40,48},{48,56},{1,9},{9,17},... | collective-permute-start | bytes 442376 | tf_op jit(solution)/shard_map/ppermute | solution.py:21
  87.8 6.5 %collective-permute-start.9 = (bf16[3,192,128]{2,1,0:T(8,128)(2,1)S(1)}, bf16[3,192,128]{2,1,0:T(8,128)(2,1)S(1)}, u32[]{:S(2)}, u32[]{:S(2)}) collective-permute-start(bf16[3,192,128]{2,1,0:T(8,128)(2,1)S(1)} %get-tuple-element.151), channel_id=1, source_target_pairs={{8,0},{16,8},{24,16},{32,24},{40,32},{48,40},{56,48},{9,1},{17,9},... | collective-permute-start | bytes 442376 | tf_op jit(solution)/shard_map/ppermute | solution.py:22
  95.7 8.2 %collective-permute-start.10 = (bf16[3,14,192]{2,1,0:T(8,128)(2,1)S(1)}, bf16[3,14,192]{2,1,0:T(8,128)(2,1)S(1)}, u32[]{:S(2)}, u32[]{:S(2)}) collective-permute-start(bf16[3,14,192]{2,1,0:T(8,128)(2,1)S(1)} %copy.69), channel_id=1, source_target_pairs={{1,0},{2,1},{3,2},{4,3},{5,4},{6,5},{7,6},{9,8},{10,9},{11,10},{12... | collective-permute-start | bytes 48392 | tf_op jit(solution)/shard_map/ppermute | solution.py:22
  97.4 7.3 %collective-permute-start.11 = (bf16[3,14,192]{2,1,0:T(8,128)(2,1)S(1)}, bf16[3,14,192]{2,1,0:T(8,128)(2,1)S(1)}, u32[]{:S(2)}, u32[]{:S(2)}) collective-permute-start(bf16[3,14,192]{2,1,0:T(8,128)(2,1)S(1)} %copy.71), channel_id=1, source_target_pairs={{0,1},{1,2},{2,3},{3,4},{4,5},{5,6},{6,7},{8,9},{9,10},{10,11},{11... | collective-permute-start | bytes 48392 | tf_op jit(solution)/shard_map/ppermute | solution.py:21
  109.1 14.3 %collective-permute-start.7 = (f32[416,128]{1,0:T(8,128)S(1)}, f32[416,128]{1,0:T(8,128)S(1)}, u32[]{:S(2)}, u32[]{:S(2)}) collective-permute-start(f32[416,128]{1,0:T(8,128)S(1)} %get-tuple-element.140), channel_id=1, source_target_pairs={{0,65},{1,64},{2,67},{3,66},{4,69},{5,68},{6,71},{7,70},{8,73},{9,... | collective-permute-start | bytes 638984 | tf_op jit(solution)/shard_map/ppermute | solution.py:224
  113.5 9.9 %collective-permute-start.6 = (f32[416,128]{1,0:T(8,128)S(1)}, f32[416,128]{1,0:T(8,128)S(1)}, u32[]{:S(2)}, u32[]{:S(2)}) collective-permute-start(f32[416,128]{1,0:T(8,128)S(1)} %get-tuple-element.141), channel_id=1, source_target_pairs={{0,1},{1,0},{2,3},{3,2},{4,5},{5,4},{6,7},{7,6},{8,9},{9,8},{10,11... | collective-permute-start | bytes 638984 | tf_op jit(solution)/shard_map/ppermute | solution.py:224
  113.7 9.7 %collective-permute-start.5 = (f32[416,128]{1,0:T(8,128)S(1)}, f32[416,128]{1,0:T(8,128)S(1)}, u32[]{:S(2)}, u32[]{:S(2)}) collective-permute-start(f32[416,128]{1,0:T(8,128)S(1)} %get-tuple-element.139), channel_id=1, source_target_pairs={{0,64},{1,65},{2,66},{3,67},{4,68},{5,69},{6,70},{7,71},{8,72},{9,... | collective-permute-start | bytes 638984 | tf_op jit(solution)/shard_map/ppermute | solution.py:224
  123.6 14.9 %collective-permute-start.26 = (f32[26,128]{1,0:T(8,128)S(1)}, f32[26,128]{1,0:T(8,128)S(1)}, u32[]{:S(2)}, u32[]{:S(2)}) collective-permute-start(f32[26,128]{1,0:T(8,128)S(1)} %get-tuple-element.156), channel_id=1, source_target_pairs={{0,54},{1,55},{2,52},{3,53},{4,50},{5,51},{6,48},{7,49},{8,62},{9,... | collective-permute-start | bytes 39944 | tf_op jit(solution)/shard_map/ppermute | solution.py:224
  128.6 11.2 %collective-permute-start.25 = (f32[26,128]{1,0:T(8,128)S(1)}, f32[26,128]{1,0:T(8,128)S(1)}, u32[]{:S(2)}, u32[]{:S(2)}) collective-permute-start(f32[26,128]{1,0:T(8,128)S(1)} %get-tuple-element.157), channel_id=1, source_target_pairs={{0,52},{1,53},{2,54},{3,55},{4,48},{5,49},{6,50},{7,51},{8,60},{9,... | collective-permute-start | bytes 39944 | tf_op jit(solution)/shard_map/ppermute | solution.py:224
  131.8 9.3 %collective-permute-start.24 = (f32[26,128]{1,0:T(8,128)S(1)}, f32[26,128]{1,0:T(8,128)S(1)}, u32[]{:S(2)}, u32[]{:S(2)}) collective-permute-start(f32[26,128]{1,0:T(8,128)S(1)} %get-tuple-element.158), channel_id=1, source_target_pairs={{0,50},{1,51},{2,48},{3,49},{4,54},{5,55},{6,52},{7,53},{8,58},{9,... | collective-permute-start | bytes 39944 | tf_op jit(solution)/shard_map/ppermute | solution.py:224
  133.1 8.7 %collective-permute-start.23 = (f32[26,128]{1,0:T(8,128)S(1)}, f32[26,128]{1,0:T(8,128)S(1)}, u32[]{:S(2)}, u32[]{:S(2)}) collective-permute-start(f32[26,128]{1,0:T(8,128)S(1)} %get-tuple-element.159), channel_id=1, source_target_pairs={{0,48},{1,49},{2,50},{3,51},{4,52},{5,53},{6,54},{7,55},{8,56},{9,... | collective-permute-start | bytes 39944 | tf_op jit(solution)/shard_map/ppermute | solution.py:224
  133.1 12.3 %collective-permute-start.22 = (f32[26,128]{1,0:T(8,128)S(1)}, f32[26,128]{1,0:T(8,128)S(1)}, u32[]{:S(2)}, u32[]{:S(2)}) collective-permute-start(f32[26,128]{1,0:T(8,128)S(1)} %get-tuple-element.160), channel_id=1, source_target_pairs={{0,38},{1,39},{2,36},{3,37},{4,34},{5,35},{6,32},{7,33},{8,46},{9,... | collective-permute-start | bytes 39944 | tf_op jit(solution)/shard_map/ppermute | solution.py:224
  138.5 8.2 %collective-permute-start.21 = (f32[26,128]{1,0:T(8,128)S(1)}, f32[26,128]{1,0:T(8,128)S(1)}, u32[]{:S(2)}, u32[]{:S(2)}) collective-permute-start(f32[26,128]{1,0:T(8,128)S(1)} %get-tuple-element.161), channel_id=1, source_target_pairs={{0,36},{1,37},{2,38},{3,39},{4,32},{5,33},{6,34},{7,35},{8,44},{9,... | collective-permute-start | bytes 39944 | tf_op jit(solution)/shard_map/ppermute | solution.py:224
  139.8 8.1 %collective-permute-start.20 = (f32[26,128]{1,0:T(8,128)S(1)}, f32[26,128]{1,0:T(8,128)S(1)}, u32[]{:S(2)}, u32[]{:S(2)}) collective-permute-start(f32[26,128]{1,0:T(8,128)S(1)} %get-tuple-element.162), channel_id=1, source_target_pairs={{0,34},{1,35},{2,32},{3,33},{4,38},{5,39},{6,36},{7,37},{8,42},{9,... | collective-permute-start | bytes 39944 | tf_op jit(solution)/shard_map/ppermute | solution.py:224
  141.0 6.9 %collective-permute-start.19 = (f32[26,128]{1,0:T(8,128)S(1)}, f32[26,128]{1,0:T(8,128)S(1)}, u32[]{:S(2)}, u32[]{:S(2)}) collective-permute-start(f32[26,128]{1,0:T(8,128)S(1)} %get-tuple-element.163), channel_id=1, source_target_pairs={{0,32},{1,33},{2,34},{3,35},{4,36},{5,37},{6,38},{7,39},{8,40},{9,... | collective-permute-start | bytes 39944 | tf_op jit(solution)/shard_map/ppermute | solution.py:224
  141.8 10.0 %collective-permute-start.18 = (f32[26,128]{1,0:T(8,128)S(1)}, f32[26,128]{1,0:T(8,128)S(1)}, u32[]{:S(2)}, u32[]{:S(2)}) collective-permute-start(f32[26,128]{1,0:T(8,128)S(1)} %get-tuple-element.164), channel_id=1, source_target_pairs={{0,22},{1,23},{2,20},{3,21},{4,18},{5,19},{6,16},{7,17},{8,30},{9,... | collective-permute-start | bytes 39944 | tf_op jit(solution)/shard_map/ppermute | solution.py:224
  145.4 6.4 %collective-permute-start.17 = (f32[26,128]{1,0:T(8,128)S(1)}, f32[26,128]{1,0:T(8,128)S(1)}, u32[]{:S(2)}, u32[]{:S(2)}) collective-permute-start(f32[26,128]{1,0:T(8,128)S(1)} %get-tuple-element.165), channel_id=1, source_target_pairs={{0,20},{1,21},{2,22},{3,23},{4,16},{5,17},{6,18},{7,19},{8,28},{9,... | collective-permute-start | bytes 39944 | tf_op jit(solution)/shard_map/ppermute | solution.py:224
  146.7 5.7 %collective-permute-start.16 = (f32[26,128]{1,0:T(8,128)S(1)}, f32[26,128]{1,0:T(8,128)S(1)}, u32[]{:S(2)}, u32[]{:S(2)}) collective-permute-start(f32[26,128]{1,0:T(8,128)S(1)} %get-tuple-element.166), channel_id=1, source_target_pairs={{0,18},{1,19},{2,16},{3,17},{4,22},{5,23},{6,20},{7,21},{8,26},{9,... | collective-permute-start | bytes 39944 | tf_op jit(solution)/shard_map/ppermute | solution.py:224
  148.0 4.5 %collective-permute-start.15 = (f32[26,128]{1,0:T(8,128)S(1)}, f32[26,128]{1,0:T(8,128)S(1)}, u32[]{:S(2)}, u32[]{:S(2)}) collective-permute-start(f32[26,128]{1,0:T(8,128)S(1)} %get-tuple-element.167), channel_id=1, source_target_pairs={{0,16},{1,17},{2,18},{3,19},{4,20},{5,21},{6,22},{7,23},{8,24},{9,... | collective-permute-start | bytes 39944 | tf_op jit(solution)/shard_map/ppermute | solution.py:224
  148.0 4.9 %collective-permute-start.14 = (f32[26,128]{1,0:T(8,128)S(1)}, f32[26,128]{1,0:T(8,128)S(1)}, u32[]{:S(2)}, u32[]{:S(2)}) collective-permute-start(f32[26,128]{1,0:T(8,128)S(1)} %get-tuple-element.168), channel_id=1, source_target_pairs={{0,6},{1,7},{2,4},{3,5},{4,2},{5,3},{6,0},{7,1},{8,14},{9,15},{10,... | collective-permute-start | bytes 39944 | tf_op jit(solution)/shard_map/ppermute | solution.py:224
  151.8 4.1 %collective-permute-start.13 = (f32[26,128]{1,0:T(8,128)S(1)}, f32[26,128]{1,0:T(8,128)S(1)}, u32[]{:S(2)}, u32[]{:S(2)}) collective-permute-start(f32[26,128]{1,0:T(8,128)S(1)} %get-tuple-element.169), channel_id=1, source_target_pairs={{0,4},{1,5},{2,6},{3,7},{4,0},{5,1},{6,2},{7,3},{8,12},{9,13},{10,... | collective-permute-start | bytes 39944 | tf_op jit(solution)/shard_map/ppermute | solution.py:224
  151.8 4.1 %collective-permute-start.12 = (f32[26,128]{1,0:T(8,128)S(1)}, f32[26,128]{1,0:T(8,128)S(1)}, u32[]{:S(2)}, u32[]{:S(2)}) collective-permute-start(f32[26,128]{1,0:T(8,128)S(1)} %get-tuple-element.155), channel_id=1, source_target_pairs={{0,2},{1,3},{2,0},{3,1},{4,6},{5,7},{6,4},{7,5},{8,10},{9,11},{10,... | collective-permute-start | bytes 39944 | tf_op jit(solution)/shard_map/ppermute | solution.py:224
  156.0 4.5 %collective-permute-start.27 = (f32[26,128]{1,0:T(8,128)S(1)}, f32[26,128]{1,0:T(8,128)S(1)}, u32[]{:S(2)}, u32[]{:S(2)}) collective-permute-start(f32[26,128]{1,0:T(8,128)S(1)} %get-tuple-element.129), channel_id=1, source_target_pairs={{0,2},{1,3},{2,0},{3,1},{4,6},{5,7},{6,4},{7,5},{8,10},{9,11},{10,... | collective-permute-start | bytes 39944 | tf_op jit(solution)/shard_map/ppermute | solution.py:241
  156.2 6.8 %collective-permute-start.28 = (f32[26,128]{1,0:T(8,128)S(1)}, f32[26,128]{1,0:T(8,128)S(1)}, u32[]{:S(2)}, u32[]{:S(2)}) collective-permute-start(f32[26,128]{1,0:T(8,128)S(1)} %get-tuple-element.129), channel_id=1, source_target_pairs={{0,4},{1,5},{2,6},{3,7},{4,0},{5,1},{6,2},{7,3},{8,12},{9,13},{10,... | collective-permute-start | bytes 39944 | tf_op jit(solution)/shard_map/ppermute | solution.py:241
  158.2 7.9 %collective-permute-start.29 = (f32[26,128]{1,0:T(8,128)S(1)}, f32[26,128]{1,0:T(8,128)S(1)}, u32[]{:S(2)}, u32[]{:S(2)}) collective-permute-start(f32[26,128]{1,0:T(8,128)S(1)} %get-tuple-element.129), channel_id=1, source_target_pairs={{0,6},{1,7},{2,4},{3,5},{4,2},{5,3},{6,0},{7,1},{8,14},{9,15},{10,... | collective-permute-start | bytes 39944 | tf_op jit(solution)/shard_map/ppermute | solution.py:241
  160.1 6.7 %collective-permute-start.30 = (f32[26,128]{1,0:T(8,128)S(1)}, f32[26,128]{1,0:T(8,128)S(1)}, u32[]{:S(2)}, u32[]{:S(2)}) collective-permute-start(f32[26,128]{1,0:T(8,128)S(1)} %get-tuple-element.129), channel_id=1, source_target_pairs={{0,16},{1,17},{2,18},{3,19},{4,20},{5,21},{6,22},{7,23},{8,24},{9,... | collective-permute-start | bytes 39944 | tf_op jit(solution)/shard_map/ppermute | solution.py:241
  160.5 6.3 %collective-permute-start.31 = (f32[26,128]{1,0:T(8,128)S(1)}, f32[26,128]{1,0:T(8,128)S(1)}, u32[]{:S(2)}, u32[]{:S(2)}) collective-permute-start(f32[26,128]{1,0:T(8,128)S(1)} %get-tuple-element.129), channel_id=1, source_target_pairs={{0,18},{1,19},{2,16},{3,17},{4,22},{5,23},{6,20},{7,21},{8,26},{9,... | collective-permute-start | bytes 39944 | tf_op jit(solution)/shard_map/ppermute | solution.py:241
  160.5 10.6 %collective-permute-start.32 = (f32[26,128]{1,0:T(8,128)S(1)}, f32[26,128]{1,0:T(8,128)S(1)}, u32[]{:S(2)}, u32[]{:S(2)}) collective-permute-start(f32[26,128]{1,0:T(8,128)S(1)} %get-tuple-element.129), channel_id=1, source_target_pairs={{0,20},{1,21},{2,22},{3,23},{4,16},{5,17},{6,18},{7,19},{8,28},{9,... | collective-permute-start | bytes 39944 | tf_op jit(solution)/shard_map/ppermute | solution.py:241
  163.1 11.9 %collective-permute-start.33 = (f32[26,128]{1,0:T(8,128)S(1)}, f32[26,128]{1,0:T(8,128)S(1)}, u32[]{:S(2)}, u32[]{:S(2)}) collective-permute-start(f32[26,128]{1,0:T(8,128)S(1)} %get-tuple-element.129), channel_id=1, source_target_pairs={{0,22},{1,23},{2,20},{3,21},{4,18},{5,19},{6,16},{7,17},{8,30},{9,... | collective-permute-start | bytes 39944 | tf_op jit(solution)/shard_map/ppermute | solution.py:241
  166.0 9.3 %collective-permute-start.34 = (f32[26,128]{1,0:T(8,128)S(1)}, f32[26,128]{1,0:T(8,128)S(1)}, u32[]{:S(2)}, u32[]{:S(2)}) collective-permute-start(f32[26,128]{1,0:T(8,128)S(1)} %get-tuple-element.129), channel_id=1, source_target_pairs={{0,32},{1,33},{2,34},{3,35},{4,36},{5,37},{6,38},{7,39},{8,40},{9,... | collective-permute-start | bytes 39944 | tf_op jit(solution)/shard_map/ppermute | solution.py:241
  166.8 8.6 %collective-permute-start.35 = (f32[26,128]{1,0:T(8,128)S(1)}, f32[26,128]{1,0:T(8,128)S(1)}, u32[]{:S(2)}, u32[]{:S(2)}) collective-permute-start(f32[26,128]{1,0:T(8,128)S(1)} %get-tuple-element.129), channel_id=1, source_target_pairs={{0,34},{1,35},{2,32},{3,33},{4,38},{5,39},{6,36},{7,37},{8,42},{9,... | collective-permute-start | bytes 39944 | tf_op jit(solution)/shard_map/ppermute | solution.py:241
  166.8 12.6 %collective-permute-start.36 = (f32[26,128]{1,0:T(8,128)S(1)}, f32[26,128]{1,0:T(8,128)S(1)}, u32[]{:S(2)}, u32[]{:S(2)}) collective-permute-start(f32[26,128]{1,0:T(8,128)S(1)} %get-tuple-element.129), channel_id=1, source_target_pairs={{0,36},{1,37},{2,38},{3,39},{4,32},{5,33},{6,34},{7,35},{8,44},{9,... | collective-permute-start | bytes 39944 | tf_op jit(solution)/shard_map/ppermute | solution.py:241
  171.0 12.4 %collective-permute-start.37 = (f32[26,128]{1,0:T(8,128)S(1)}, f32[26,128]{1,0:T(8,128)S(1)}, u32[]{:S(2)}, u32[]{:S(2)}) collective-permute-start(f32[26,128]{1,0:T(8,128)S(1)} %get-tuple-element.129), channel_id=1, source_target_pairs={{0,38},{1,39},{2,36},{3,37},{4,34},{5,35},{6,32},{7,33},{8,46},{9,... | collective-permute-start | bytes 39944 | tf_op jit(solution)/shard_map/ppermute | solution.py:241
  175.0 8.4 %collective-permute-start.38 = (f32[26,128]{1,0:T(8,128)S(1)}, f32[26,128]{1,0:T(8,128)S(1)}, u32[]{:S(2)}, u32[]{:S(2)}) collective-permute-start(f32[26,128]{1,0:T(8,128)S(1)} %get-tuple-element.129), channel_id=1, source_target_pairs={{0,48},{1,49},{2,50},{3,51},{4,52},{5,53},{6,54},{7,55},{8,56},{9,... | collective-permute-start | bytes 39944 | tf_op jit(solution)/shard_map/ppermute | solution.py:241
  175.3 8.1 %collective-permute-start.39 = (f32[26,128]{1,0:T(8,128)S(1)}, f32[26,128]{1,0:T(8,128)S(1)}, u32[]{:S(2)}, u32[]{:S(2)}) collective-permute-start(f32[26,128]{1,0:T(8,128)S(1)} %get-tuple-element.129), channel_id=1, source_target_pairs={{0,50},{1,51},{2,48},{3,49},{4,54},{5,55},{6,52},{7,53},{8,58},{9,... | collective-permute-start | bytes 39944 | tf_op jit(solution)/shard_map/ppermute | solution.py:241
  175.4 8.1 %collective-permute-start.40 = (f32[26,128]{1,0:T(8,128)S(1)}, f32[26,128]{1,0:T(8,128)S(1)}, u32[]{:S(2)}, u32[]{:S(2)}) collective-permute-start(f32[26,128]{1,0:T(8,128)S(1)} %get-tuple-element.129), channel_id=1, source_target_pairs={{0,52},{1,53},{2,54},{3,55},{4,48},{5,49},{6,50},{7,51},{8,60},{9,... | collective-permute-start | bytes 39944 | tf_op jit(solution)/shard_map/ppermute | solution.py:241
  179.4 5.9 %collective-permute-start.41 = (f32[26,128]{1,0:T(8,128)S(1)}, f32[26,128]{1,0:T(8,128)S(1)}, u32[]{:S(2)}, u32[]{:S(2)}) collective-permute-start(f32[26,128]{1,0:T(8,128)S(1)} %get-tuple-element.129), channel_id=1, source_target_pairs={{0,54},{1,55},{2,52},{3,53},{4,50},{5,51},{6,48},{7,49},{8,62},{9,... | collective-permute-start | bytes 39944 | tf_op jit(solution)/shard_map/ppermute | solution.py:241
  185.3 4.8 %collective-permute-start.42 = (f32[416,128]{1,0:T(8,128)S(1)}, f32[416,128]{1,0:T(8,128)S(1)}, u32[]{:S(2)}, u32[]{:S(2)}) collective-permute-start(f32[416,128]{1,0:T(8,128)S(1)} %reshape.209), channel_id=1, source_target_pairs={{0,64},{1,65},{2,66},{3,67},{4,68},{5,69},{6,70},{7,71},{8,72},{9,... | collective-permute-start | bytes 638984 | tf_op jit(solution)/shard_map/ppermute | solution.py:241
  185.9 8.2 %collective-permute-start.43 = (f32[416,128]{1,0:T(8,128)S(1)}, f32[416,128]{1,0:T(8,128)S(1)}, u32[]{:S(2)}, u32[]{:S(2)}) collective-permute-start(f32[416,128]{1,0:T(8,128)S(1)} %reshape.209), channel_id=1, source_target_pairs={{0,1},{1,0},{2,3},{3,2},{4,5},{5,4},{6,7},{7,6},{8,9},{9,8},{10,11... | collective-permute-start | bytes 638984 | tf_op jit(solution)/shard_map/ppermute | solution.py:241
  188.5 7.7 %collective-permute-start.44 = (f32[416,128]{1,0:T(8,128)S(1)}, f32[416,128]{1,0:T(8,128)S(1)}, u32[]{:S(2)}, u32[]{:S(2)}) collective-permute-start(f32[416,128]{1,0:T(8,128)S(1)} %reshape.209), channel_id=1, source_target_pairs={{0,65},{1,64},{2,67},{3,66},{4,69},{5,68},{6,71},{7,70},{8,73},{9,... | collective-permute-start | bytes 638984 | tf_op jit(solution)/shard_map/ppermute | solution.py:241
  196.3 16.3 %collective-permute-start.45 = (f32[1664,128]{1,0:T(8,128)S(1)}, f32[1664,128]{1,0:T(8,128)S(1)}, u32[]{:S(2)}, u32[]{:S(2)}) collective-permute-start(f32[1664,128]{1,0:T(8,128)S(1)} %bitcast.423), channel_id=1, source_target_pairs={{0,8},{1,9},{2,10},{3,11},{4,12},{5,13},{6,14},{7,15},{8,0},{9,1},... | collective-permute-start | bytes 2555912 | tf_op jit(solution)/shard_map/ppermute | solution.py:241
  (97 other events, 826.1 us)

commit v8 on v7

--- a/solution.py
+++ b/solution.py
@@ -207,7 +207,7 @@
     return out
 
 
-def butterfly_psum(buffer, axes, stages, scale_of, tie, tie_after):
+def butterfly_psum(buffer, axes, stages, scale_of, ties):
     index = lax.axis_index(axes)
     count = math.prod(lax.axis_size(a) for a in axes)
     offset = jnp.zeros((), jnp.int32)
@@ -225,8 +225,8 @@
         offset = offset * ways + mine
         places.append((bits, mine))
         buffer = total
-        if len(places) == tie_after:
-            buffer, tie = lax.optimization_barrier((buffer, tie))
+        if len(places) in ties:
+            buffer, ties[len(places)] = lax.optimization_barrier((buffer, ties[len(places)]))
     rows = buffer.shape[0]
     position = (offset * rows + lax.broadcasted_iota(jnp.int32, buffer.shape, 0)) * buffer.shape[1]
     position = position + lax.broadcasted_iota(jnp.int32, buffer.shape, 1)
@@ -241,7 +241,7 @@
             other = lax.ppermute(buffer, axes, pairs)
             both = lax.dynamic_update_index_in_dim(both, other, mine ^ step, 0)
         buffer = both.reshape(-1, buffer.shape[1])
-    return buffer, tie
+    return buffer, ties
 
 
 def shards(
@@ -302,9 +302,15 @@
     def scale_of(position):
         return jnp.where(position == loss_at, 1.0 / cell_count, grad_scale).astype(jnp.float32)
 
-    buffer, d_input = butterfly_psum(
-        buffer, axes, [(3,), (6, 0), (1, 2, 4, 5)], scale_of, d_input, 2
-    )
+    half = d_conv.shape[0] // 2
+
+    def input_part(low, high):
+        flipped = depthwise(d_padded[low:high], dw_weight[low:high], height, width, True)
+        return returned[low:high].astype(jnp.float32) + flipped
+
+    ties = {2: input_part(0, half), 3: input_part(half, d_conv.shape[0])}
+    buffer, ties = butterfly_psum(buffer, axes, [(3,), (6, 0), (1, 2), (4, 5)], scale_of, ties)
+    d_input = jnp.concatenate([ties[2], ties[3]], axis=0)
     joined, kernel_grad, expand_grad, project_grad, lateral_grad, classify_grad = unpack_rows(
         buffer, shapes
     )

time: 220 us -> 174 us (0.79)
  starting transfers between devices: 108 us -> 63 us
  local copies, waits for them, and re-layouts: 39 us -> 35.3 us
  waiting for transfers between devices: 18.9 us -> 22.2 us
    ppermute x19 -> x10, starting transfers between devices: 45.6 us -> 20.4 us  [butterfly_psum(): other = lax.ppermute(buffer, axes, pairs)]
    ppermute x19 -> x10, starting transfers between devices: 33.8 us -> 16.4 us  [butterfly_psum(): total = total + lax.ppermute(send, axes, pairs)]
    another operation x2, local copies, waits for them, and re-layouts: 10.7 us -> 4.41 us  [conv_backward(): kernel_grad = jnp.stack(columns, axis=1)]
    ppermute x19 -> x10, waiting for transfers between devices: 9.06 us -> 13.8 us  [butterfly_psum(): other = lax.ppermute(buffer, axes, pairs)]
    mul x0 -> x6, local copies, waits for them, and re-layouts: none -> 4.31 us  [depthwise(): total = total + kernel[:, tap_index][:, None, None] * window]
    ppermute x19 -> x10, waiting for transfers between devices: 3.46 us -> 5.42 us  [butterfly_psum(): total = total + lax.ppermute(send, axes, pairs)]
    add x1 -> x2, other arithmetic: 8.89 us -> 10.4 us  [input_part(): return returned[low:high].astype(jnp.float32) + flipped]
    unnamed x207 -> x245, local copies, waits for them, and re-layouts: 10.2 us -> 10.1 us
  transfers between devices with their start and end apart: 46 -> 28, of which waited for: 12 -> 15; matrix products, arithmetic and copies ran while one was open for 7% -> 14% of each run, Pallas kernels for 0% -> 0%
where the time goes in v8:
time: 174 us; the launch traced here: 173 us
  starting transfers between devices  63 us (36%)
  other arithmetic  36.8 us (21%)
  local copies, waits for them, and re-layouts  35.3 us (20%)
  waiting for transfers between devices  22.2 us (13%)
  matrix products  13.1 us (8%)
  between operations  2.89 us (2%)
    ppermute x10, starting transfers between devices, butterfly_psum(): other = lax.ppermute(buffer, axes, pairs)  20.4 us
    ppermute x4, starting transfers between devices, padded_2(): before = jnp.transpose(lax.ppermute(last, axis, up), order)  18.4 us
    ppermute x10, starting transfers between devices, butterfly_psum(): total = total + lax.ppermute(send, axes, pairs)  16.4 us
    ppermute x10, waiting for transfers between devices, butterfly_psum(): other = lax.ppermute(buffer, axes, pairs)  13.8 us
    dot_general x12, matrix products, product(): jnp.einsum(form, left_side, right_side, preferred_element_type=jnp.float32)  13.1 us
    reduce_sum x4, other arithmetic, conv_backward(): columns.append(jnp.sum(window * conv_float, axis=(1, 2)))  12.2 us
    add x2, other arithmetic, input_part(): return returned[low:high].astype(jnp.float32) + flipped  10.4 us
    unnamed x245, local copies, waits for them, and re-layouts  10.1 us
  transfers between devices with their start and end apart: 28, of which 15 were waited for; matrix products, arithmetic and copies ran while one was open for 14% of the time, Pallas kernels for 0%

profile of v8, /device:TPU:1, one launch (start us, length us, event | category | flops | bytes accessed | tf_op | source)
XLA Modules:
  0.0 173.3 jit_solution(1707787491690138131)
XLA Ops:
  0.7 1.1 copy-done
  1.9 3.3 %collective-permute-start.1 = (bf16[3,192,128]{2,1,0:T(8,128)(2,1)S(1)}, bf16[3,192,128]{2,1,0:T(8,128)(2,1)S(1)}, u32[]{:S(2)}, u32[]{:S(2)}) collective-permute-start(bf16[3,192,128]{2,1,0:T(8,128)(2,1)S(1)} %get-tuple-element.157), channel_id=1, source_target_pairs={{8,0},{16,8},{24,16},{32,24},{40,32},{48,40},{56,48},{9,1},{17,9},... | collective-permute-start | bytes 442376 | tf_op jit(solution)/shard_map/ppermute | solution.py:22
  5.2 3.1 %collective-permute-start = (bf16[3,192,128]{2,1,0:T(8,128)(2,1)S(1)}, bf16[3,192,128]{2,1,0:T(8,128)(2,1)S(1)}, u32[]{:S(2)}, u32[]{:S(2)}) collective-permute-start(bf16[3,192,128]{2,1,0:T(8,128)(2,1)S(1)} %get-tuple-element.156), channel_id=1, source_target_pairs={{0,8},{8,16},{16,24},{24,32},{32,40},{40,48},{48,56},{1,9},{9,17},... | collective-permute-start | bytes 442376 | tf_op jit(solution)/shard_map/ppermute | solution.py:21
  14.0 1.3 collective-permute-start.3
  15.7 5.5 %collective-permute-start.2 = (bf16[3,14,192]{2,1,0:T(8,128)(2,1)S(1)}, bf16[3,14,192]{2,1,0:T(8,128)(2,1)S(1)}, u32[]{:S(2)}, u32[]{:S(2)}) collective-permute-start(bf16[3,14,192]{2,1,0:T(8,128)(2,1)S(1)} %copy.55), channel_id=1, source_target_pairs={{0,1},{1,2},{2,3},{3,4},{4,5},{5,6},{6,7},{8,9},{9,10},{10,11},{11... | collective-permute-start | bytes 48392 | tf_op jit(solution)/shard_map/ppermute | solution.py:21
  22.8 1.4 pad_maximum_fusion
  24.6 8.3 %fusion.165 = (f32[8,128]{1,0:T(8,128)S(1)}, f32[192,8,128]{2,0,1:T(8,128)S(1)}) fusion(f32[192]{0:T(256)S(1)} %copy-done.114, bf16[192,14,131]{2,0,1:T(8,128)(2,1)S(1)} %get-tuple-element.150, f32[192]{0:T(256)S(1)} %bitcast.637, f32[192]{0:T(256)S(1)} %bitcast.638, f32[192]{0:T(256)S(1)} %bitcast.639, bf16[192,3,128]{2,0,1:T(8,128)(2,1)S(1)} %bitcast.579, ...), kind=kLoop, calls=%fused_computation.483 | loop fusion | flops 30276608 | bytes 18032128 | tf_op jit(solution)/shard_map/reduce_sum | solution.py:65
  36.8 1.9 %convert_reduce_fusion.2 = (f32[512]{0:T(512)}, bf16[512,8,128]{0,2,1:T(8,128)(2,1)S(1)}) fusion(f32[8,128,512]{2,1,0:T(8,128)S(1)} %get-tuple-element.321, f32[512]{0:T(512)S(1)} %copy-done.70, bf16[16,8,128]{2,0,1:T(8,128)(2,1)S(1)} %get-tuple-element.138, bf16[512,16]{0,1:T(8,128)(2,1)S(1)} %copy-done.10), kind=kOutput, calls=%fused_computation.77 | convolution fusion | flops 23592448 | bytes 3198976 | tf_op jit(solution)/shard_map/khw,lk->lhw/dot_general | solution.py:34
  38.6 1.2 fusion.72
  39.8 2.5 %convert_reduce_fusion.1 = (f32[768]{0:T(1024)}, bf16[768,8,128]{0,2,1:T(8,128)(2,1)S(1)}) fusion(f32[8,128,768]{2,1,0:T(8,128)S(1)} %get-tuple-element.317, f32[768]{0:T(1024)S(1)} %copy-done.15, bf16[768,192]{0,1:T(8,128)(2,1)S(1)} %copy-done.5, bf16[192,8,128]{2,0,1:T(8,128)(2,1)S(1)} %get-tuple-element.327, f32[192]{0:T(256)S(1)} %copy-done.11), kind=kOutput, calls=%fused_computation.63 | convolution fusion | flops 312802560 | bytes 5413632 | tf_op jit(solution)/shard_map/chw,dc->dhw/dot_general | solution.py:34
  42.4 1.4 fusion.123
  43.7 4.1 %fusion.118 = (f32[192]{0:T(256)}, f32[192]{0:T(256)}, f32[192]{0:T(256)}, f32[192]{0:T(256)}, f32[192]{0:T(256)}, /*index=5*/f32[192]{0:T(256)}, f32[192]{0:T(2...) fusion(bf16[192,14,131]{2,0,1:T(8,128)(2,1)S(1)} %get-tuple-ele, ...), kind=kLoop, calls=%fused_computation.250 | loop fusion | flops 12382848 | bytes 9074944 | tf_op jit(solution)/shard_map/reduce_sum | solution.py:122
  47.8 4.4 %fusion.122 = (f32[192]{0:T(256)}, f32[192]{0:T(256)}, f32[192]{0:T(256)}, f32[192]{0:T(256)}, f32[192]{0:T(256)}, /*index=5*/f32[192]{0:T(256)}, f32[192]{0:T(2...) fusion(bf16[192,8,128]{2,0,1:T(8,128)(2,1)S(1)} %get-tuple-elem, ...), kind=kLoop, calls=%fused_computation.254 | loop fusion | flops 11006400 | bytes 7485696 | tf_op jit(solution)/shard_map/reduce_sum | solution.py:122
  52.2 1.1 fusion.76
  53.3 2.7 %fusion.121 = (f32[192]{0:T(256)}, f32[192]{0:T(256)}, f32[192]{0:T(256)}, f32[192]{0:T(256)}, f32[192]{0:T(256)}, /*index=5*/f32[192]{0:T(256)}, f32[192]{0:T(256)}, f32[192]{0:T(256)}, f32[192]{0:T(256)}, f32[192]{0:T(256)}) fusion(bf16[192,8,128]{2,0,1:T(8,128)(2,1)S(1)} %get-tuple-element.136, bf16[192,14,131]{2,0,1:T(8,128)(2,1)S(1)} %get-tuple-element.150, ...), kind=kLoop, calls=%fused_computation.253 | loop fusion | flops 7272576 | bytes 2661888 | tf_op jit(solution)/shard_map/reduce_sum | solution.py:122
  56.5 1.3 fusion.160
  58.6 1.2 convolution_bitcast_fusion
  62.9 4.3 %stack.199 = f32[192,49]{0,1:T(8,128)S(1)} concatenate(f32[192,1]{0,1:T(1,128)} %bitcast.686, f32[192,1]{0,1:T(1,128)} %bitcast.687, f32[192,1]{0,1:T(1,128)} %bitcast.685, f32[192,1]{0,1:T(1,128)S(1)} %bitcast.632, f32[192,1]{0,1:T(1,128)S(1)} %bitcast.609, f32[192,1]{0,1:T(1,128)S(1)} %bitcast.610, f32[192,1]{0,1:T(1,128)S(1)} %bitcast.611, f32[192,1]{0,1:T(1,128)} %bitcast.689, ...), dimensions={1} | concatenate | bytes 75264 | tf_op jit(solution)/shard_map/stack | solution.py:123
  67.6 1.1 reshape.310
  70.1 1.9 %constant_dynamic-update-slice_fusion.2 = f32[3328,128]{1,0:T(8,128)} fusion(f32[3328,128]{1,0:T(8,128)} %constant_dynamic-update-slice_fusion.3, f32[1152,128]{1,0:T(8,128)} %bitcast.586), kind=kLoop, calls=%fused_computation.355 | loop fusion | bytes 1179648
  74.0 3.5 %collective-permute-start.8 = (bf16[3,192,128]{2,1,0:T(8,128)(2,1)S(1)}, bf16[3,192,128]{2,1,0:T(8,128)(2,1)S(1)}, u32[]{:S(2)}, u32[]{:S(2)}) collective-permute-start(bf16[3,192,128]{2,1,0:T(8,128)(2,1)S(1)} %copy-done.9), channel_id=1, source_target_pairs={{0,8},{8,16},{16,24},{24,32},{32,40},{40,48},{48,56},{1,9},{9,17},... | collective-permute-start | bytes 442376 | tf_op jit(solution)/shard_map/ppermute | solution.py:21
  77.5 1.9 %collective-permute-start.9 = (bf16[3,192,128]{2,1,0:T(8,128)(2,1)S(1)}, bf16[3,192,128]{2,1,0:T(8,128)(2,1)S(1)}, u32[]{:S(2)}, u32[]{:S(2)}) collective-permute-start(bf16[3,192,128]{2,1,0:T(8,128)(2,1)S(1)} %copy-done.8), channel_id=1, source_target_pairs={{8,0},{16,8},{24,16},{32,24},{40,32},{48,40},{56,48},{9,1},{17,9},... | collective-permute-start | bytes 442376 | tf_op jit(solution)/shard_map/ppermute | solution.py:22
  79.5 2.1 %dynamic-slice_bitcast_fusion = f32[1664,128]{1,0:T(8,128)} fusion(f32[2,1664,128]{2,1,0:T(8,128)} %bitcast.595, s32[]{:T(128)S(6)} %select_n.76), kind=kLoop, calls=%fused_computation.154 | loop fusion | bytes 1703940 | tf_op jit(solution)/shard_map/jit(dynamic_index_in_dim)/squeeze | solution.py:223
  81.6 2.4 %collective-permute-done.9 = bf16[3,192,128]{2,1,0:T(8,128)(2,1)S(1)} collective-permute-done((bf16[3,192,128]{2,1,0:T(8,128)(2,1)S(1)}, bf16[3,192,128]{2,1,0:T(8,128)(2,1)S(1)}, u32[]{:S(2)}, u32[]{:S(2)}) %collective-permute-start.9) | collective-permute-done | bytes 147488 | tf_op jit(solution)/shard_map/ppermute | solution.py:22
  84.8 1.3 collective-permute-start.10
  86.4 6.3 %collective-permute-start.11 = (bf16[3,14,192]{2,1,0:T(8,128)(2,1)S(1)}, bf16[3,14,192]{2,1,0:T(8,128)(2,1)S(1)}, u32[]{:S(2)}, u32[]{:S(2)}) collective-permute-start(bf16[3,14,192]{2,1,0:T(8,128)(2,1)S(1)} %copy.71), channel_id=1, source_target_pairs={{0,1},{1,2},{2,3},{3,4},{4,5},{5,6},{6,7},{8,9},{9,10},{10,11},{11... | collective-permute-start | bytes 48392 | tf_op jit(solution)/shard_map/ppermute | solution.py:21
  94.4 1.3 pad_maximum_fusion.1
  95.9 1.3 bitcast_add_fusion
  97.2 4.5 %collective-permute-start.7 = (f32[416,128]{1,0:T(8,128)S(1)}, f32[416,128]{1,0:T(8,128)S(1)}, u32[]{:S(2)}, u32[]{:S(2)}) collective-permute-start(f32[416,128]{1,0:T(8,128)S(1)} %get-tuple-element.144), channel_id=1, source_target_pairs={{0,65},{1,64},{2,67},{3,66},{4,69},{5,68},{6,71},{7,70},{8,73},{9,... | collective-permute-start | bytes 638984 | tf_op jit(solution)/shard_map/ppermute | solution.py:224
  102.7 5.6 %add_add_fusion.1 = f32[96,8,128]{2,0,1:T(8,128)S(1)} fusion(bf16[192,8,128]{2,0,1:T(8,128)(2,1)S(1)} %get-tuple-element.136, bf16[192,3,128]{2,0,1:T(8,128)(2,1)S(1)} %bitcast.589, bf16[192,3,128]{2,0,1:T(8,128)(2,1)S(1)} %bitcast.593, bf16[192,14,131]{2,0,1:T(8,128)(2,1)S(1)} %get-tuple-element.147, bf16[192,14,131]{2,0,1:T(8,128)(2,1)S(1)} %get-tuple-element.146, ...), kind=kLoop, calls=%fused_computation.299 | loop fusion | flops 15138816 | bytes 9751296 | tf_op jit(solution)/shard_map/add | solution.py:309
  108.4 2.5 %collective-permute-done.7 = f32[416,128]{1,0:T(8,128)S(1)} collective-permute-done((f32[416,128]{1,0:T(8,128)S(1)}, f32[416,128]{1,0:T(8,128)S(1)}, u32[]{:S(2)}, u32[]{:S(2)}) %collective-permute-start.7) | collective-permute-done | bytes 213024 | tf_op jit(solution)/shard_map/ppermute | solution.py:224
  112.0 7.2 %collective-permute-start.14 = (f32[104,128]{1,0:T(8,128)S(1)}, f32[104,128]{1,0:T(8,128)S(1)}, u32[]{:S(2)}, u32[]{:S(2)}) collective-permute-start(f32[104,128]{1,0:T(8,128)S(1)} %get-tuple-element.159), channel_id=1, source_target_pairs={{0,6},{1,7},{2,4},{3,5},{4,2},{5,3},{6,0},{7,1},{8,14},{9,15},{10,... | collective-permute-start | bytes 159752 | tf_op jit(solution)/shard_map/ppermute | solution.py:224
  120.3 4.8 %add_add_fusion = f32[96,8,128]{2,0,1:T(8,128)S(1)} fusion(bf16[192,8,128]{2,0,1:T(8,128)(2,1)S(1)} %get-tuple-element.136, bf16[192,3,128]{2,0,1:T(8,128)(2,1)S(1)} %bitcast.590, bf16[192,3,128]{2,0,1:T(8,128)(2,1)S(1)} %bitcast.594, bf16[192,14,131]{2,0,1:T(8,128)(2,1)S(1)} %get-tuple-element.147, bf16[192,14,131]{2,0,1:T(8,128)(2,1)S(1)} %get-tuple-element.146, ...), kind=kLoop, calls=%fused_computation.298 | loop fusion | flops 16318464 | bytes 9756032 | tf_op jit(solution)/shard_map/add | solution.py:309
  125.2 2.2 %collective-permute-start.16 = (f32[26,128]{1,0:T(8,128)S(1)}, f32[26,128]{1,0:T(8,128)S(1)}, u32[]{:S(2)}, u32[]{:S(2)}) collective-permute-start(f32[26,128]{1,0:T(8,128)S(1)} %get-tuple-element.163), channel_id=1, source_target_pairs={{0,32},{1,33},{2,34},{3,35},{4,36},{5,37},{6,38},{7,39},{8,40},{9,... | collective-permute-start | bytes 39944 | tf_op jit(solution)/shard_map/ppermute | solution.py:224
  131.2 2.1 %collective-permute-start.19 = (f32[26,128]{1,0:T(8,128)S(1)}, f32[26,128]{1,0:T(8,128)S(1)}, u32[]{:S(2)}, u32[]{:S(2)}) collective-permute-start(f32[26,128]{1,0:T(8,128)S(1)} %get-tuple-element.135), channel_id=1, source_target_pairs={{0,32},{1,33},{2,34},{3,35},{4,36},{5,37},{6,38},{7,39},{8,40},{9,... | collective-permute-start | bytes 39944 | tf_op jit(solution)/shard_map/ppermute | solution.py:241
  133.3 1.0 collective-permute-start.20
  135.3 1.8 %collective-permute-done.20 = f32[26,128]{1,0:T(8,128)S(1)} collective-permute-done((f32[26,128]{1,0:T(8,128)S(1)}, f32[26,128]{1,0:T(8,128)S(1)}, u32[]{:S(2)}, u32[]{:S(2)}) %collective-permute-start.20) | collective-permute-done | bytes 13344 | tf_op jit(solution)/shard_map/ppermute | solution.py:241
  137.1 1.1 collective-permute-start.21
  138.3 3.0 %collective-permute-start.22 = (f32[104,128]{1,0:T(8,128)S(1)}, f32[104,128]{1,0:T(8,128)S(1)}, u32[]{:S(2)}, u32[]{:S(2)}) collective-permute-start(f32[104,128]{1,0:T(8,128)S(1)} %reshape.315), channel_id=1, source_target_pairs={{0,4},{1,5},{2,6},{3,7},{4,0},{5,1},{6,2},{7,3},{8,12},{9,13},{10,... | collective-permute-start | bytes 159752 | tf_op jit(solution)/shard_map/ppermute | solution.py:241
  141.4 1.9 %collective-permute-done.22 = f32[104,128]{1,0:T(8,128)S(1)} collective-permute-done((f32[104,128]{1,0:T(8,128)S(1)}, f32[104,128]{1,0:T(8,128)S(1)}, u32[]{:S(2)}, u32[]{:S(2)}) %collective-permute-start.22) | collective-permute-done | bytes 53280 | tf_op jit(solution)/shard_map/ppermute | solution.py:241
  143.3 2.1 %collective-permute-done.23 = f32[104,128]{1,0:T(8,128)S(1)} collective-permute-done((f32[104,128]{1,0:T(8,128)S(1)}, f32[104,128]{1,0:T(8,128)S(1)}, u32[]{:S(2)}, u32[]{:S(2)}) %collective-permute-start.23) | collective-permute-done | bytes 53280 | tf_op jit(solution)/shard_map/ppermute | solution.py:241
  145.7 2.6 %collective-permute-start.25 = (f32[416,128]{1,0:T(8,128)S(1)}, f32[416,128]{1,0:T(8,128)S(1)}, u32[]{:S(2)}, u32[]{:S(2)}) collective-permute-start(f32[416,128]{1,0:T(8,128)S(1)} %bitcast.601), channel_id=1, source_target_pairs={{0,1},{1,0},{2,3},{3,2},{4,5},{5,4},{6,7},{7,6},{8,9},{9,8},{10,11... | collective-permute-start | bytes 638984 | tf_op jit(solution)/shard_map/ppermute | solution.py:241
  148.3 1.1 collective-permute-start.26
  150.2 3.7 %collective-permute-done.25 = f32[416,128]{1,0:T(8,128)S(1)} collective-permute-done((f32[416,128]{1,0:T(8,128)S(1)}, f32[416,128]{1,0:T(8,128)S(1)}, u32[]{:S(2)}, u32[]{:S(2)}) %collective-permute-start.25) | collective-permute-done | bytes 213024 | tf_op jit(solution)/shard_map/ppermute | solution.py:241
  153.9 2.2 %collective-permute-done.26 = f32[416,128]{1,0:T(8,128)S(1)} collective-permute-done((f32[416,128]{1,0:T(8,128)S(1)}, f32[416,128]{1,0:T(8,128)S(1)}, u32[]{:S(2)}, u32[]{:S(2)}) %collective-permute-start.26) | collective-permute-done | bytes 213024 | tf_op jit(solution)/shard_map/ppermute | solution.py:241
  156.1 8.4 %collective-permute-start.27 = (f32[1664,128]{1,0:T(8,128)S(1)}, f32[1664,128]{1,0:T(8,128)S(1)}, u32[]{:S(2)}, u32[]{:S(2)}) collective-permute-start(f32[1664,128]{1,0:T(8,128)S(1)} %bitcast.569), channel_id=1, source_target_pairs={{0,8},{1,9},{2,10},{3,11},{4,12},{5,13},{6,14},{7,15},{8,0},{9,1},... | collective-permute-start | bytes 2555912 | tf_op jit(solution)/shard_map/ppermute | solution.py:241
  164.5 1.3 copy.73
  167.8 1.1 fusion.167
  (356 shorter events, 36.9 us)
Async XLA Ops:
  1.9 11.3 %collective-permute-start.1 = (bf16[3,192,128]{2,1,0:T(8,128)(2,1)S(1)}, bf16[3,192,128]{2,1,0:T(8,128)(2,1)S(1)}, u32[]{:S(2)}, u32[]{:S(2)}) collective-permute-start(bf16[3,192,128]{2,1,0:T(8,128)(2,1)S(1)} %get-tuple-element.157), channel_id=1, source_target_pairs={{8,0},{16,8},{24,16},{32,24},{40,32},{48,40},{56,48},{9,1},{17,9},... | collective-permute-start | bytes 442376 | tf_op jit(solution)/shard_map/ppermute | solution.py:22
  5.2 8.0 %collective-permute-start = (bf16[3,192,128]{2,1,0:T(8,128)(2,1)S(1)}, bf16[3,192,128]{2,1,0:T(8,128)(2,1)S(1)}, u32[]{:S(2)}, u32[]{:S(2)}) collective-permute-start(bf16[3,192,128]{2,1,0:T(8,128)(2,1)S(1)} %get-tuple-element.156), channel_id=1, source_target_pairs={{0,8},{8,16},{16,24},{24,32},{32,40},{40,48},{48,56},{1,9},{9,17},... | collective-permute-start | bytes 442376 | tf_op jit(solution)/shard_map/ppermute | solution.py:21
  14.0 7.2 %collective-permute-start.3 = (bf16[3,14,192]{2,1,0:T(8,128)(2,1)S(1)}, bf16[3,14,192]{2,1,0:T(8,128)(2,1)S(1)}, u32[]{:S(2)}, u32[]{:S(2)}) collective-permute-start(bf16[3,14,192]{2,1,0:T(8,128)(2,1)S(1)} %copy.57), channel_id=1, source_target_pairs={{1,0},{2,1},{3,2},{4,3},{5,4},{6,5},{7,6},{9,8},{10,9},{11,10},{12... | collective-permute-start | bytes 48392 | tf_op jit(solution)/shard_map/ppermute | solution.py:22
  15.7 6.5 %collective-permute-start.2 = (bf16[3,14,192]{2,1,0:T(8,128)(2,1)S(1)}, bf16[3,14,192]{2,1,0:T(8,128)(2,1)S(1)}, u32[]{:S(2)}, u32[]{:S(2)}) collective-permute-start(bf16[3,14,192]{2,1,0:T(8,128)(2,1)S(1)} %copy.55), channel_id=1, source_target_pairs={{0,1},{1,2},{2,3},{3,4},{4,5},{5,6},{6,7},{8,9},{9,10},{10,11},{11... | collective-permute-start | bytes 48392 | tf_op jit(solution)/shard_map/ppermute | solution.py:21
  74.0 7.6 %collective-permute-start.8 = (bf16[3,192,128]{2,1,0:T(8,128)(2,1)S(1)}, bf16[3,192,128]{2,1,0:T(8,128)(2,1)S(1)}, u32[]{:S(2)}, u32[]{:S(2)}) collective-permute-start(bf16[3,192,128]{2,1,0:T(8,128)(2,1)S(1)} %copy-done.9), channel_id=1, source_target_pairs={{0,8},{8,16},{16,24},{24,32},{32,40},{40,48},{48,56},{1,9},{9,17},... | collective-permute-start | bytes 442376 | tf_op jit(solution)/shard_map/ppermute | solution.py:21
  77.5 6.5 %collective-permute-start.9 = (bf16[3,192,128]{2,1,0:T(8,128)(2,1)S(1)}, bf16[3,192,128]{2,1,0:T(8,128)(2,1)S(1)}, u32[]{:S(2)}, u32[]{:S(2)}) collective-permute-start(bf16[3,192,128]{2,1,0:T(8,128)(2,1)S(1)} %copy-done.8), channel_id=1, source_target_pairs={{8,0},{16,8},{24,16},{32,24},{40,32},{48,40},{56,48},{9,1},{17,9},... | collective-permute-start | bytes 442376 | tf_op jit(solution)/shard_map/ppermute | solution.py:22
  81.6 14.1 %collective-permute-start.4 = (f32[1664,128]{1,0:T(8,128)}, f32[1664,128]{1,0:T(8,128)}, u32[]{:S(2)}, u32[]{:S(2)}) collective-permute-start(f32[1664,128]{1,0:T(8,128)} %dynamic-slice_bitcast_fusion), channel_id=1, source_target_pairs={{0,8},{1,9},{2,10},{3,11},{4,12},{5,13},{6,14},{7,15},{8,0},{9,1},... | collective-permute-start | bytes 2555912 | tf_op jit(solution)/shard_map/ppermute | solution.py:224
  84.8 8.8 %collective-permute-start.10 = (bf16[3,14,192]{2,1,0:T(8,128)(2,1)S(1)}, bf16[3,14,192]{2,1,0:T(8,128)(2,1)S(1)}, u32[]{:S(2)}, u32[]{:S(2)}) collective-permute-start(bf16[3,14,192]{2,1,0:T(8,128)(2,1)S(1)} %copy.69), channel_id=1, source_target_pairs={{1,0},{2,1},{3,2},{4,3},{5,4},{6,5},{7,6},{9,8},{10,9},{11,10},{12... | collective-permute-start | bytes 48392 | tf_op jit(solution)/shard_map/ppermute | solution.py:22
  86.4 7.5 %collective-permute-start.11 = (bf16[3,14,192]{2,1,0:T(8,128)(2,1)S(1)}, bf16[3,14,192]{2,1,0:T(8,128)(2,1)S(1)}, u32[]{:S(2)}, u32[]{:S(2)}) collective-permute-start(bf16[3,14,192]{2,1,0:T(8,128)(2,1)S(1)} %copy.71), channel_id=1, source_target_pairs={{0,1},{1,2},{2,3},{3,4},{4,5},{5,6},{6,7},{8,9},{9,10},{10,11},{11... | collective-permute-start | bytes 48392 | tf_op jit(solution)/shard_map/ppermute | solution.py:21
  97.2 13.7 %collective-permute-start.7 = (f32[416,128]{1,0:T(8,128)S(1)}, f32[416,128]{1,0:T(8,128)S(1)}, u32[]{:S(2)}, u32[]{:S(2)}) collective-permute-start(f32[416,128]{1,0:T(8,128)S(1)} %get-tuple-element.144), channel_id=1, source_target_pairs={{0,65},{1,64},{2,67},{3,66},{4,69},{5,68},{6,71},{7,70},{8,73},{9,... | collective-permute-start | bytes 638984 | tf_op jit(solution)/shard_map/ppermute | solution.py:224
  101.7 9.2 %collective-permute-start.6 = (f32[416,128]{1,0:T(8,128)S(1)}, f32[416,128]{1,0:T(8,128)S(1)}, u32[]{:S(2)}, u32[]{:S(2)}) collective-permute-start(f32[416,128]{1,0:T(8,128)S(1)} %get-tuple-element.145), channel_id=1, source_target_pairs={{0,1},{1,0},{2,3},{3,2},{4,5},{5,4},{6,7},{7,6},{8,9},{9,8},{10,11... | collective-permute-start | bytes 638984 | tf_op jit(solution)/shard_map/ppermute | solution.py:224
  101.9 10.0 %collective-permute-start.5 = (f32[416,128]{1,0:T(8,128)S(1)}, f32[416,128]{1,0:T(8,128)S(1)}, u32[]{:S(2)}, u32[]{:S(2)}) collective-permute-start(f32[416,128]{1,0:T(8,128)S(1)} %get-tuple-element.143), channel_id=1, source_target_pairs={{0,64},{1,65},{2,66},{3,67},{4,68},{5,69},{6,70},{7,71},{8,72},{9,... | collective-permute-start | bytes 638984 | tf_op jit(solution)/shard_map/ppermute | solution.py:224
  102.4 17.5 %copy-start.71 = (f32[96]{0:T(128)S(1)}, f32[96]{0:T(128)}, u32[]{:S(2)}) copy-start(f32[96]{0:T(128)} %get-tuple-element.183) | copy-start | bytes 1156
  102.4 17.5 %copy-start.72 = (f32[96]{0:T(128)S(1)}, f32[96]{0:T(128)}, u32[]{:S(2)}) copy-start(f32[96]{0:T(128)} %get-tuple-element.184) | copy-start | bytes 1156
  102.4 17.5 %copy-start.73 = (f32[96]{0:T(128)S(1)}, f32[96]{0:T(128)}, u32[]{:S(2)}) copy-start(f32[96]{0:T(128)} %get-tuple-element.185) | copy-start | bytes 1156
  102.4 17.5 %copy-start.74 = (f32[96]{0:T(128)S(1)}, f32[96]{0:T(128)}, u32[]{:S(2)}) copy-start(f32[96]{0:T(128)} %get-tuple-element.186) | copy-start | bytes 1156
  102.4 17.5 %copy-start.75 = (f32[96]{0:T(128)S(1)}, f32[96]{0:T(128)}, u32[]{:S(2)}) copy-start(f32[96]{0:T(128)} %get-tuple-element.187) | copy-start | bytes 1156
  102.4 17.5 %copy-start.76 = (f32[96]{0:T(128)S(1)}, f32[96]{0:T(128)}, u32[]{:S(2)}) copy-start(f32[96]{0:T(128)} %get-tuple-element.188) | copy-start | bytes 1156
  102.4 17.5 %copy-start.77 = (f32[96]{0:T(128)S(1)}, f32[96]{0:T(128)}, u32[]{:S(2)}) copy-start(f32[96]{0:T(128)} %get-tuple-element.189) | copy-start | bytes 1156
  102.4 17.5 %copy-start.78 = (f32[96]{0:T(128)S(1)}, f32[96]{0:T(128)}, u32[]{:S(2)}) copy-start(f32[96]{0:T(128)} %get-tuple-element.190) | copy-start | bytes 1156
  102.4 17.5 %copy-start.79 = (f32[96]{0:T(128)S(1)}, f32[96]{0:T(128)}, u32[]{:S(2)}) copy-start(f32[96]{0:T(128)} %get-tuple-element.191) | copy-start | bytes 1156
  102.4 17.5 %copy-start.80 = (f32[96]{0:T(128)S(1)}, f32[96]{0:T(128)}, u32[]{:S(2)}) copy-start(f32[96]{0:T(128)} %get-tuple-element.221) | copy-start | bytes 1156
  102.4 17.5 %copy-start.81 = (f32[96]{0:T(128)S(1)}, f32[96]{0:T(128)}, u32[]{:S(2)}) copy-start(f32[96]{0:T(128)} %get-tuple-element.240) | copy-start | bytes 1156
  102.5 17.5 %copy-start.82 = (f32[96]{0:T(128)S(1)}, f32[96]{0:T(128)}, u32[]{:S(2)}) copy-start(f32[96]{0:T(128)} %get-tuple-element.202) | copy-start | bytes 1156
  102.5 17.5 %copy-start.83 = (f32[96]{0:T(128)S(1)}, f32[96]{0:T(128)}, u32[]{:S(2)}) copy-start(f32[96]{0:T(128)} %get-tuple-element.203) | copy-start | bytes 1156
  102.5 17.5 %copy-start.84 = (f32[96]{0:T(128)S(1)}, f32[96]{0:T(128)}, u32[]{:S(2)}) copy-start(f32[96]{0:T(128)} %get-tuple-element.204) | copy-start | bytes 1156
  102.5 17.5 %copy-start.85 = (f32[96]{0:T(128)S(1)}, f32[96]{0:T(128)}, u32[]{:S(2)}) copy-start(f32[96]{0:T(128)} %get-tuple-element.205) | copy-start | bytes 1156
  102.5 17.5 %copy-start.86 = (f32[96]{0:T(128)S(1)}, f32[96]{0:T(128)}, u32[]{:S(2)}) copy-start(f32[96]{0:T(128)} %get-tuple-element.206) | copy-start | bytes 1156
  102.5 17.5 %copy-start.87 = (f32[96]{0:T(128)S(1)}, f32[96]{0:T(128)}, u32[]{:S(2)}) copy-start(f32[96]{0:T(128)} %get-tuple-element.207) | copy-start | bytes 1156
  102.5 17.5 %copy-start.88 = (f32[96]{0:T(128)S(1)}, f32[96]{0:T(128)}, u32[]{:S(2)}) copy-start(f32[96]{0:T(128)} %get-tuple-element.208) | copy-start | bytes 1156
  102.5 17.5 %copy-start.89 = (f32[96]{0:T(128)S(1)}, f32[96]{0:T(128)}, u32[]{:S(2)}) copy-start(f32[96]{0:T(128)} %get-tuple-element.209) | copy-start | bytes 1156
  102.5 17.5 %copy-start.90 = (f32[96]{0:T(128)S(1)}, f32[96]{0:T(128)}, u32[]{:S(2)}) copy-start(f32[96]{0:T(128)} %get-tuple-element.210) | copy-start | bytes 1156
  112.0 13.1 %collective-permute-start.14 = (f32[104,128]{1,0:T(8,128)S(1)}, f32[104,128]{1,0:T(8,128)S(1)}, u32[]{:S(2)}, u32[]{:S(2)}) collective-permute-start(f32[104,128]{1,0:T(8,128)S(1)} %get-tuple-element.159), channel_id=1, source_target_pairs={{0,6},{1,7},{2,4},{3,5},{4,2},{5,3},{6,0},{7,1},{8,14},{9,15},{10,... | collective-permute-start | bytes 159752 | tf_op jit(solution)/shard_map/ppermute | solution.py:224
  119.2 5.8 %collective-permute-start.13 = (f32[104,128]{1,0:T(8,128)S(1)}, f32[104,128]{1,0:T(8,128)S(1)}, u32[]{:S(2)}, u32[]{:S(2)}) collective-permute-start(f32[104,128]{1,0:T(8,128)S(1)} %get-tuple-element.160), channel_id=1, source_target_pairs={{0,4},{1,5},{2,6},{3,7},{4,0},{5,1},{6,2},{7,3},{8,12},{9,13},{10,... | collective-permute-start | bytes 159752 | tf_op jit(solution)/shard_map/ppermute | solution.py:224
  119.2 5.8 %collective-permute-start.12 = (f32[104,128]{1,0:T(8,128)S(1)}, f32[104,128]{1,0:T(8,128)S(1)}, u32[]{:S(2)}, u32[]{:S(2)}) collective-permute-start(f32[104,128]{1,0:T(8,128)S(1)} %get-tuple-element.158), channel_id=1, source_target_pairs={{0,2},{1,3},{2,0},{3,1},{4,6},{5,7},{6,4},{7,5},{8,10},{9,11},{10,... | collective-permute-start | bytes 159752 | tf_op jit(solution)/shard_map/ppermute | solution.py:224
  125.1 3.9 %collective-permute-start.17 = (f32[26,128]{1,0:T(8,128)S(1)}, f32[26,128]{1,0:T(8,128)S(1)}, u32[]{:S(2)}, u32[]{:S(2)}) collective-permute-start(f32[26,128]{1,0:T(8,128)S(1)} %get-tuple-element.162), channel_id=1, source_target_pairs={{0,48},{1,49},{2,50},{3,51},{4,52},{5,53},{6,54},{7,55},{8,56},{9,... | collective-permute-start | bytes 39944 | tf_op jit(solution)/shard_map/ppermute | solution.py:224
  125.2 4.2 %collective-permute-start.16 = (f32[26,128]{1,0:T(8,128)S(1)}, f32[26,128]{1,0:T(8,128)S(1)}, u32[]{:S(2)}, u32[]{:S(2)}) collective-permute-start(f32[26,128]{1,0:T(8,128)S(1)} %get-tuple-element.163), channel_id=1, source_target_pairs={{0,32},{1,33},{2,34},{3,35},{4,36},{5,37},{6,38},{7,39},{8,40},{9,... | collective-permute-start | bytes 39944 | tf_op jit(solution)/shard_map/ppermute | solution.py:224
  127.5 2.9 %collective-permute-start.15 = (f32[26,128]{1,0:T(8,128)S(1)}, f32[26,128]{1,0:T(8,128)S(1)}, u32[]{:S(2)}, u32[]{:S(2)}) collective-permute-start(f32[26,128]{1,0:T(8,128)S(1)} %get-tuple-element.161), channel_id=1, source_target_pairs={{0,16},{1,17},{2,18},{3,19},{4,20},{5,21},{6,22},{7,23},{8,24},{9,... | collective-permute-start | bytes 39944 | tf_op jit(solution)/shard_map/ppermute | solution.py:224
  130.4 3.9 %collective-permute-start.18 = (f32[26,128]{1,0:T(8,128)S(1)}, f32[26,128]{1,0:T(8,128)S(1)}, u32[]{:S(2)}, u32[]{:S(2)}) collective-permute-start(f32[26,128]{1,0:T(8,128)S(1)} %get-tuple-element.135), channel_id=1, source_target_pairs={{0,16},{1,17},{2,18},{3,19},{4,20},{5,21},{6,22},{7,23},{8,24},{9,... | collective-permute-start | bytes 39944 | tf_op jit(solution)/shard_map/ppermute | solution.py:241
  131.2 4.1 %collective-permute-start.19 = (f32[26,128]{1,0:T(8,128)S(1)}, f32[26,128]{1,0:T(8,128)S(1)}, u32[]{:S(2)}, u32[]{:S(2)}) collective-permute-start(f32[26,128]{1,0:T(8,128)S(1)} %get-tuple-element.135), channel_id=1, source_target_pairs={{0,32},{1,33},{2,34},{3,35},{4,36},{5,37},{6,38},{7,39},{8,40},{9,... | collective-permute-start | bytes 39944 | tf_op jit(solution)/shard_map/ppermute | solution.py:241
  133.3 3.8 %collective-permute-start.20 = (f32[26,128]{1,0:T(8,128)S(1)}, f32[26,128]{1,0:T(8,128)S(1)}, u32[]{:S(2)}, u32[]{:S(2)}) collective-permute-start(f32[26,128]{1,0:T(8,128)S(1)} %get-tuple-element.135), channel_id=1, source_target_pairs={{0,48},{1,49},{2,50},{3,51},{4,52},{5,53},{6,54},{7,55},{8,56},{9,... | collective-permute-start | bytes 39944 | tf_op jit(solution)/shard_map/ppermute | solution.py:241
  137.1 4.2 %collective-permute-start.21 = (f32[104,128]{1,0:T(8,128)S(1)}, f32[104,128]{1,0:T(8,128)S(1)}, u32[]{:S(2)}, u32[]{:S(2)}) collective-permute-start(f32[104,128]{1,0:T(8,128)S(1)} %reshape.315), channel_id=1, source_target_pairs={{0,2},{1,3},{2,0},{3,1},{4,6},{5,7},{6,4},{7,5},{8,10},{9,11},{10,... | collective-permute-start | bytes 159752 | tf_op jit(solution)/shard_map/ppermute | solution.py:241
  138.3 5.1 %collective-permute-start.22 = (f32[104,128]{1,0:T(8,128)S(1)}, f32[104,128]{1,0:T(8,128)S(1)}, u32[]{:S(2)}, u32[]{:S(2)}) collective-permute-start(f32[104,128]{1,0:T(8,128)S(1)} %reshape.315), channel_id=1, source_target_pairs={{0,4},{1,5},{2,6},{3,7},{4,0},{5,1},{6,2},{7,3},{8,12},{9,13},{10,... | collective-permute-start | bytes 159752 | tf_op jit(solution)/shard_map/ppermute | solution.py:241
  141.2 4.2 %collective-permute-start.23 = (f32[104,128]{1,0:T(8,128)S(1)}, f32[104,128]{1,0:T(8,128)S(1)}, u32[]{:S(2)}, u32[]{:S(2)}) collective-permute-start(f32[104,128]{1,0:T(8,128)S(1)} %reshape.315), channel_id=1, source_target_pairs={{0,6},{1,7},{2,4},{3,5},{4,2},{5,3},{6,0},{7,1},{8,14},{9,15},{10,... | collective-permute-start | bytes 159752 | tf_op jit(solution)/shard_map/ppermute | solution.py:241
  145.4 4.8 %collective-permute-start.24 = (f32[416,128]{1,0:T(8,128)S(1)}, f32[416,128]{1,0:T(8,128)S(1)}, u32[]{:S(2)}, u32[]{:S(2)}) collective-permute-start(f32[416,128]{1,0:T(8,128)S(1)} %bitcast.600), channel_id=1, source_target_pairs={{0,64},{1,65},{2,66},{3,67},{4,68},{5,69},{6,70},{7,71},{8,72},{9,... | collective-permute-start | bytes 638984 | tf_op jit(solution)/shard_map/ppermute | solution.py:241
  145.7 8.2 %collective-permute-start.25 = (f32[416,128]{1,0:T(8,128)S(1)}, f32[416,128]{1,0:T(8,128)S(1)}, u32[]{:S(2)}, u32[]{:S(2)}) collective-permute-start(f32[416,128]{1,0:T(8,128)S(1)} %bitcast.601), channel_id=1, source_target_pairs={{0,1},{1,0},{2,3},{3,2},{4,5},{5,4},{6,7},{7,6},{8,9},{9,8},{10,11... | collective-permute-start | bytes 638984 | tf_op jit(solution)/shard_map/ppermute | solution.py:241
  148.3 7.8 %collective-permute-start.26 = (f32[416,128]{1,0:T(8,128)S(1)}, f32[416,128]{1,0:T(8,128)S(1)}, u32[]{:S(2)}, u32[]{:S(2)}) collective-permute-start(f32[416,128]{1,0:T(8,128)S(1)} %bitcast.602), channel_id=1, source_target_pairs={{0,65},{1,64},{2,67},{3,66},{4,69},{5,68},{6,71},{7,70},{8,73},{9,... | collective-permute-start | bytes 638984 | tf_op jit(solution)/shard_map/ppermute | solution.py:241
  156.1 10.4 %collective-permute-start.27 = (f32[1664,128]{1,0:T(8,128)S(1)}, f32[1664,128]{1,0:T(8,128)S(1)}, u32[]{:S(2)}, u32[]{:S(2)}) collective-permute-start(f32[1664,128]{1,0:T(8,128)S(1)} %bitcast.569), channel_id=1, source_target_pairs={{0,8},{1,9},{2,10},{3,11},{4,12},{5,13},{6,14},{7,15},{8,0},{9,1},... | collective-permute-start | bytes 2555912 | tf_op jit(solution)/shard_map/ppermute | solution.py:241
  (98 other events, 648.6 us)

commit v9 on v8

--- a/solution.py
+++ b/solution.py
@@ -185,6 +185,33 @@
     return jnp.concatenate(rows, axis=0), shapes
 
 
+def pack_rotated(parts, multiple, turn):
+    blocks, shapes = [], []
+    for part in parts:
+        shapes.append(part.shape)
+        if tiled(part.shape):
+            blocks.append(tile_order(part))
+            continue
+        flat = part.reshape(-1)
+        size = flat.shape[0]
+        padded_rows = -(-size // (8 * LANES)) * 8
+        blocks.append(jnp.pad(flat, (0, padded_rows * LANES - size)).reshape(padded_rows, LANES))
+    total = sum(b.shape[0] for b in blocks)
+    total += -total % multiple
+    half = total // 2
+    buffer = jnp.zeros((total, LANES), jnp.float32)
+    at = 0
+    for block in blocks:
+        pieces = [(block, at)]
+        if at < half < at + block.shape[0]:
+            pieces = [(block[: half - at], at), (block[half - at :], half)]
+        for piece, start in pieces:
+            place = (start + turn * half) % total
+            buffer = lax.dynamic_update_slice_in_dim(buffer, piece, place, 0)
+        at += block.shape[0]
+    return buffer, shapes
+
+
 def unpack_rows(buffer, shapes):
     out, at = [], 0
     for shape in shapes:
@@ -216,11 +243,15 @@
         ways = 1 << len(bits)
         mine = sum(((index >> bit_at) & 1) << k for k, bit_at in enumerate(bits))
         pieces = buffer.reshape(ways, buffer.shape[0] // ways, buffer.shape[1])
-        total = lax.dynamic_index_in_dim(pieces, mine, 0, keepdims=False)
+        turned = not places
+        total = pieces[0] if turned else lax.dynamic_index_in_dim(pieces, mine, 0, keepdims=False)
         for step in range(1, ways):
             flip = spread(step, bits)
             pairs = [(i, i ^ flip) for i in range(count)]
-            send = lax.dynamic_index_in_dim(pieces, mine ^ step, 0, keepdims=False)
+            if turned:
+                send = pieces[step]
+            else:
+                send = lax.dynamic_index_in_dim(pieces, mine ^ step, 0, keepdims=False)
             total = total + lax.ppermute(send, axes, pairs)
         offset = offset * ways + mine
         places.append((bits, mine))
@@ -294,7 +325,8 @@
     joined = jnp.concatenate(vectors)
     parts = [joined, kernel_grad, expand_grad, project_grad.T, lateral_grad, classify_grad]
     count = math.prod(lax.axis_size(a) for a in axes)
-    buffer, shapes = pack_rows(parts, count * 2)
+    turn = (lax.axis_index(axes) >> 3) & 1
+    buffer, shapes = pack_rotated(parts, count * 2, turn)
     cell_count = micro_count * height * width * lax.axis_size("row") * lax.axis_size("col")
     grad_scale = 1.0 / math.sqrt(cell_count)
     loss_at = joined.shape[0] - 1

time: 174 us -> 182 us (1.046)
  local copies, waits for them, and re-layouts: 35.3 us -> 40.2 us
    dynamic_update_slice x0 -> x7, local copies, waits for them, and re-layouts: none -> 11.3 us  [pack_rotated(): buffer = lax.dynamic_update_slice_in_dim(buffer, piece, place, 0)]
    unnamed x245 -> x189, local copies, waits for them, and re-layouts: 10.1 us -> 4.52 us
    ppermute x10, waiting for transfers between devices: 5.42 us -> 9.6 us  [butterfly_psum(): total = total + lax.ppermute(send, axes, pairs)]
    another operation x2, local copies, waits for them, and re-layouts: 4.41 us -> 0.28 us  [conv_backward(): kernel_grad = jnp.stack(columns, axis=1)]
    ppermute x4, starting transfers between devices: 18.4 us -> 21.1 us  [padded_2(): before = jnp.transpose(lax.ppermute(last, axis, up), order)]
    slice x0 -> x3, local copies, waits for them, and re-layouts: none -> 2.45 us  [the longest x2 1.48 us: pack_rotated(): pieces = [(block[:half - at], at), (block[half - at:], half)]]
    ppermute x4, waiting for transfers between devices: 2.41 us -> 0.01 us  [padded_2(): after = jnp.transpose(lax.ppermute(leading, axis, down), order)]
    ppermute x10, waiting for transfers between devices: 13.8 us -> 11.5 us  [butterfly_psum(): other = lax.ppermute(buffer, axes, pairs)]
  transfers between devices with their start and end apart: 28 -> 28, of which waited for: 15 -> 13; matrix products, arithmetic and copies ran while one was open for 14% -> 25% of each run, Pallas kernels for 0% -> 0%
where the time goes in v9:
time: 182 us; the launch traced here: 181 us
  starting transfers between devices  64.8 us (36%)
  local copies, waits for them, and re-layouts  40.2 us (22%)
  other arithmetic  37.5 us (21%)
  waiting for transfers between devices  21.4 us (12%)
  matrix products  14.6 us (8%)
  between operations  2.84 us (2%)
    ppermute x4, starting transfers between devices, padded_2(): before = jnp.transpose(lax.ppermute(last, axis, up), order)  21.1 us
    ppermute x10, starting transfers between devices, butterfly_psum(): other = lax.ppermute(buffer, axes, pairs)  20.3 us
    ppermute x10, starting transfers between devices, butterfly_psum(): total = total + lax.ppermute(send, axes, pairs)  17 us
    dot_general x12, matrix products, product(): jnp.einsum(form, left_side, right_side, preferred_element_type=jnp.float32)  14.6 us
    ppermute x10, waiting for transfers between devices, butterfly_psum(): other = lax.ppermute(buffer, axes, pairs)  11.5 us
    dynamic_update_slice x7, local copies, waits for them, and re-layouts, pack_rotated(): buffer = lax.dynamic_update_slice_in_dim(buffer, piece, place, 0)  11.3 us
    add x2, other arithmetic, input_part(): return returned[low:high].astype(jnp.float32) + flipped  10.6 us
    reduce_sum x4, other arithmetic, conv_backward(): columns.append(jnp.sum(window * conv_float, axis=(1, 2)))  10.3 us
  transfers between devices with their start and end apart: 28, of which 13 were waited for; matrix products, arithmetic and copies ran while one was open for 25% of the time, Pallas kernels for 0%

profile of v9, /device:TPU:1, one launch (start us, length us, event | category | flops | bytes accessed | tf_op | source)
XLA Modules:
  0.0 181.4 jit_solution(7171742957769761356)
XLA Ops:
  1.9 4.5 %collective-permute-start = (bf16[3,192,128]{2,1,0:T(8,128)(2,1)S(1)}, bf16[3,192,128]{2,1,0:T(8,128)(2,1)S(1)}, u32[]{:S(2)}, u32[]{:S(2)}) collective-permute-start(bf16[3,192,128]{2,1,0:T(8,128)(2,1)S(1)} %get-tuple-element.156), channel_id=1, source_target_pairs={{0,8},{8,16},{16,24},{24,32},{32,40},{40,48},{48,56},{1,9},{9,17},... | collective-permute-start | bytes 442376 | tf_op jit(solution)/shard_map/ppermute | solution.py:21
  6.4 1.9 %collective-permute-start.1 = (bf16[3,192,128]{2,1,0:T(8,128)(2,1)S(1)}, bf16[3,192,128]{2,1,0:T(8,128)(2,1)S(1)}, u32[]{:S(2)}, u32[]{:S(2)}) collective-permute-start(bf16[3,192,128]{2,1,0:T(8,128)(2,1)S(1)} %get-tuple-element.157), channel_id=1, source_target_pairs={{8,0},{16,8},{24,16},{32,24},{40,32},{48,40},{56,48},{9,1},{17,9},... | collective-permute-start | bytes 442376 | tf_op jit(solution)/shard_map/ppermute | solution.py:22
  13.9 1.3 collective-permute-start.3
  15.6 5.5 %collective-permute-start.2 = (bf16[3,14,192]{2,1,0:T(8,128)(2,1)S(1)}, bf16[3,14,192]{2,1,0:T(8,128)(2,1)S(1)}, u32[]{:S(2)}, u32[]{:S(2)}) collective-permute-start(bf16[3,14,192]{2,1,0:T(8,128)(2,1)S(1)} %copy.55), channel_id=1, source_target_pairs={{0,1},{1,2},{2,3},{3,4},{4,5},{5,6},{6,7},{8,9},{9,10},{10,11},{11... | collective-permute-start | bytes 48392 | tf_op jit(solution)/shard_map/ppermute | solution.py:21
  22.7 1.3 pad_maximum_fusion
  24.3 8.3 %fusion.165 = (f32[8,128]{1,0:T(8,128)S(1)}, f32[192,8,128]{2,0,1:T(8,128)S(1)}) fusion(f32[192]{0:T(256)S(1)} %copy-done.89, bf16[192,14,131]{2,0,1:T(8,128)(2,1)S(1)} %get-tuple-element.150, f32[192]{0:T(256)S(1)} %bitcast.627, f32[192]{0:T(256)S(1)} %bitcast.628, f32[192]{0:T(256)S(1)} %bitcast.629, bf16[192,3,128]{2,0,1:T(8,128)(2,1)S(1)} %bitcast.578, ...), kind=kLoop, calls=%fused_computation.477 | loop fusion | flops 30276608 | bytes 18032128 | tf_op jit(solution)/shard_map/reduce_sum | solution.py:65
  38.2 1.9 %convert_reduce_fusion.2 = (f32[512]{0:T(512)}, bf16[512,8,128]{0,2,1:T(8,128)(2,1)S(1)}) fusion(f32[8,128,512]{2,1,0:T(8,128)S(1)} %get-tuple-element.321, f32[512]{0:T(512)S(1)} %copy-done.46, bf16[16,8,128]{2,0,1:T(8,128)(2,1)S(1)} %get-tuple-element.138, bf16[512,16]{0,1:T(8,128)(2,1)S(1)} %copy-done.12), kind=kOutput, calls=%fused_computation.77 | convolution fusion | flops 23592448 | bytes 3198976 | tf_op jit(solution)/shard_map/khw,lk->lhw/dot_general | solution.py:34
  41.3 2.6 %convert_reduce_fusion.1 = (f32[768]{0:T(1024)}, bf16[768,8,128]{0,2,1:T(8,128)(2,1)S(1)}) fusion(f32[8,128,768]{2,1,0:T(8,128)S(1)} %get-tuple-element.317, f32[768]{0:T(1024)S(1)} %copy-done.17, bf16[768,192]{0,1:T(8,128)(2,1)S(1)} %copy-done.8, bf16[192,8,128]{2,0,1:T(8,128)(2,1)S(1)} %get-tuple-element.327, f32[192]{0:T(256)S(1)} %copy-done.14), kind=kOutput, calls=%fused_computation.63 | convolution fusion | flops 312802560 | bytes 5413632 | tf_op jit(solution)/shard_map/chw,dc->dhw/dot_general | solution.py:34
  43.9 1.4 fusion.123
  45.2 1.4 fusion.163
  46.6 4.0 %fusion.118 = (f32[192]{0:T(256)S(1)}, f32[192]{0:T(256)S(1)}, f32[192]{0:T(256)S(1)}, f32[192]{0:T(256)S(1)}, f32[192]{0:T(256)S(1)}, /*index=5*/f32[192]{0:T(2...) fusion(bf16[192,14,131]{2,0,1:T(8,128)(2,1)S(1)} %get-tuple-ele, ...), kind=kLoop, calls=%fused_computation.249 | loop fusion | flops 12382848 | bytes 9074944 | tf_op jit(solution)/shard_map/reduce_sum | solution.py:122
  51.3 1.9 %fusion.121 = (f32[192]{0:T(256)S(1)}, f32[192]{0:T(256)S(1)}, f32[192]{0:T(256)S(1)}, f32[192]{0:T(256)S(1)}, f32[192]{0:T(256)S(1)}, /*index=5*/f32[192]{0:T(2...) fusion(bf16[192,8,128]{2,0,1:T(8,128)(2,1)S(1)} %get-tuple-element.136, ...), kind=kLoop, calls=%fused_computation.252 | loop fusion | flops 7272576 | bytes 2661888 | tf_op jit(solution)/shard_map/reduce_sum | solution.py:122
  53.8 3.9 %fusion.122 = (f32[192]{0:T(256)S(1)}, f32[192]{0:T(256)S(1)}, f32[192]{0:T(256)S(1)}, f32[192]{0:T(256)S(1)}, f32[192]{0:T(256)S(1)}, /*index=5*/f32[192]{0:T(2...) fusion(bf16[192,8,128]{2,0,1:T(8,128)(2,1)S(1)} %get-tuple-elem, ...), kind=kLoop, calls=%fused_computation.253 | loop fusion | flops 11006400 | bytes 7485696 | tf_op jit(solution)/shard_map/reduce_sum | solution.py:122
  59.3 4.8 %collective-permute-start.8 = (bf16[3,192,128]{2,1,0:T(8,128)(2,1)}, bf16[3,192,128]{2,1,0:T(8,128)(2,1)S(1)}, u32[]{:S(2)}, u32[]{:S(2)}) collective-permute-start(bf16[3,192,128]{2,1,0:T(8,128)(2,1)} %get-tuple-element.155), channel_id=1, source_target_pairs={{0,8},{8,16},{16,24},{24,32},{32,40},{40,48},{48,56},{1,9},{9,17},... | collective-permute-start | bytes 442376 | tf_op jit(solution)/shard_map/ppermute | solution.py:21
  64.0 1.9 %collective-permute-start.9 = (bf16[3,192,128]{2,1,0:T(8,128)(2,1)}, bf16[3,192,128]{2,1,0:T(8,128)(2,1)}, u32[]{:S(2)}, u32[]{:S(2)}) collective-permute-start(bf16[3,192,128]{2,1,0:T(8,128)(2,1)} %get-tuple-element.154), channel_id=1, source_target_pairs={{8,0},{16,8},{24,16},{32,24},{40,32},{48,40},{56,48},{9,1},{17,9},... | collective-permute-start | bytes 442376 | tf_op jit(solution)/shard_map/ppermute | solution.py:22
  69.6 3.7 %dynamic_update_slice.69 = f32[3328,128]{1,0:T(8,128)S(1)} dynamic-update-slice(f32[3328,128]{1,0:T(8,128)S(1)} %dynamic_update_slice.68, f32[1152,128]{1,0:T(8,128)} %bitcast.580, s32[]{:T(128)S(6)} %select_n.129, s32[]{:T(128)} %constant.151.clone.1) | dynamic-update-slice | bytes 1179652 | tf_op jit(solution)/shard_map/dynamic_update_slice | solution.py:210
  73.3 1.8 dynamic_update_slice.70
  75.1 2.4 %dynamic_update_slice.71 = f32[3328,128]{1,0:T(8,128)S(1)} dynamic-update-slice(f32[3328,128]{1,0:T(8,128)S(1)} %dynamic_update_slice.70, f32[744,128]{1,0:T(8,128)} %slice.1767, s32[]{:T(128)S(6)} %select_n.133, s32[]{:T(128)} %constant.151.clone.1) | dynamic-update-slice | bytes 761860 | tf_op jit(solution)/shard_map/dynamic_update_slice | solution.py:210
  77.5 2.3 %fusion.173 = f32[192,512,1]{1,0,2:T(8,128)} fusion(bf16[192,8,128]{2,0,1:T(8,128)(2,1)S(1)} %get-tuple-element.318, bf16[512,8,128]{0,2,1:T(8,128)(2,1)} %copy-done.1), kind=kOutput, calls=%fused_computation.484 | convolution fusion | flops 201326592 | bytes 1835008 | tf_op jit(solution)/shard_map/chw,lhw->cl/dot_general | solution.py:34
  79.9 2.3 %dynamic_update_slice.72 = f32[3328,128]{1,0:T(8,128)S(1)} dynamic-update-slice(f32[3328,128]{1,0:T(8,128)S(1)} %dynamic_update_slice.71, f32[768,128]{1,0:T(8,128)} %bitcast.587, s32[]{:T(128)S(6)} %select_n.135, s32[]{:T(128)} %constant.151.clone.1) | dynamic-update-slice | bytes 786436 | tf_op jit(solution)/shard_map/dynamic_update_slice | solution.py:210
  84.5 1.4 slice_bitcast_fusion.1
  85.9 1.5 copy.69
  87.4 1.3 collective-permute-start.10
  88.7 1.5 copy.71
  90.1 6.3 %collective-permute-start.11 = (bf16[3,14,192]{2,1,0:T(8,128)(2,1)S(1)}, bf16[3,14,192]{2,1,0:T(8,128)(2,1)S(1)}, u32[]{:S(2)}, u32[]{:S(2)}) collective-permute-start(bf16[3,14,192]{2,1,0:T(8,128)(2,1)S(1)} %copy.71), channel_id=1, source_target_pairs={{0,1},{1,2},{2,3},{3,4},{4,5},{5,6},{6,7},{8,9},{9,10},{10,11},{11... | collective-permute-start | bytes 48392 | tf_op jit(solution)/shard_map/ppermute | solution.py:21
  98.9 2.4 %pad_maximum_fusion.1 = (bf16[192,14,131]{2,0,1:T(8,128)(2,1)S(1)}, bf16[192,14,131]{2,0,1:T(8,128)(2,1)S(1)}) fusion(bf16[192,14,3]{2,0,1:T(8,128)(2,1)} %bitcast.569, bf16[192,3,128]{2,0,1:T(8,128)(2,1)} %bitcast.148, bf16[192,8,128]{2,0,1:T(8,128)(2,1)S(1)} %get-tuple-element.136, bf16[192,3,128]{2,0,1:T(8,128)(2,1)S(1)} %bitcast.584, ...), kind=kLoop, calls=%fused_computation.80 | loop fusion | flops 5634048 | bytes 2128896 | tf_op jit(solution)/shard_map/concatenate | solution.py:23
  101.4 1.3 slice_add_fusion
  103.8 4.5 %collective-permute-start.6 = (f32[416,128]{1,0:T(8,128)S(1)}, f32[416,128]{1,0:T(8,128)S(1)}, u32[]{:S(2)}, u32[]{:S(2)}) collective-permute-start(f32[416,128]{1,0:T(8,128)S(1)} %get-tuple-element.145), channel_id=1, source_target_pairs={{0,1},{1,0},{2,3},{3,2},{4,5},{5,4},{6,7},{7,6},{8,9},{9,8},{10,11... | collective-permute-start | bytes 638984 | tf_op jit(solution)/shard_map/ppermute | solution.py:255
  108.7 5.6 %add_add_fusion.1 = f32[96,8,128]{2,0,1:T(8,128)S(1)} fusion(bf16[192,8,128]{2,0,1:T(8,128)(2,1)S(1)} %get-tuple-element.136, bf16[192,3,128]{2,0,1:T(8,128)(2,1)S(1)} %bitcast.585, bf16[192,3,128]{2,0,1:T(8,128)(2,1)} %bitcast.148, bf16[192,14,131]{2,0,1:T(8,128)(2,1)S(1)} %get-tuple-element.147, bf16[192,14,131]{2,0,1:T(8,128)(2,1)S(1)} %get-tuple-element.146, ...), kind=kLoop, calls=%fused_computation.298 | loop fusion | flops 15138816 | bytes 9751296 | tf_op jit(solution)/shard_map/add | solution.py:341
  114.3 2.6 %collective-permute-done.6 = f32[416,128]{1,0:T(8,128)S(1)} collective-permute-done((f32[416,128]{1,0:T(8,128)S(1)}, f32[416,128]{1,0:T(8,128)S(1)}, u32[]{:S(2)}, u32[]{:S(2)}) %collective-permute-start.6) | collective-permute-done | bytes 213024 | tf_op jit(solution)/shard_map/ppermute | solution.py:255
  117.0 3.2 %collective-permute-done.7 = f32[416,128]{1,0:T(8,128)S(1)} collective-permute-done((f32[416,128]{1,0:T(8,128)S(1)}, f32[416,128]{1,0:T(8,128)S(1)}, u32[]{:S(2)}, u32[]{:S(2)}) %collective-permute-start.7) | collective-permute-done | bytes 213024 | tf_op jit(solution)/shard_map/ppermute | solution.py:255
  120.2 2.7 %collective-permute-start.12 = (f32[104,128]{1,0:T(8,128)S(1)}, f32[104,128]{1,0:T(8,128)S(1)}, u32[]{:S(2)}, u32[]{:S(2)}) collective-permute-start(f32[104,128]{1,0:T(8,128)S(1)} %get-tuple-element.158), channel_id=1, source_target_pairs={{0,2},{1,3},{2,0},{3,1},{4,6},{5,7},{6,4},{7,5},{8,10},{9,11},{10,... | collective-permute-start | bytes 159752 | tf_op jit(solution)/shard_map/ppermute | solution.py:255
  122.9 3.6 %collective-permute-start.13 = (f32[104,128]{1,0:T(8,128)S(1)}, f32[104,128]{1,0:T(8,128)S(1)}, u32[]{:S(2)}, u32[]{:S(2)}) collective-permute-start(f32[104,128]{1,0:T(8,128)S(1)} %get-tuple-element.160), channel_id=1, source_target_pairs={{0,4},{1,5},{2,6},{3,7},{4,0},{5,1},{6,2},{7,3},{8,12},{9,13},{10,... | collective-permute-start | bytes 159752 | tf_op jit(solution)/shard_map/ppermute | solution.py:255
  126.9 5.0 %add_add_fusion = f32[96,8,128]{2,0,1:T(8,128)S(1)} fusion(bf16[192,8,128]{2,0,1:T(8,128)(2,1)S(1)} %get-tuple-element.136, bf16[192,3,128]{2,0,1:T(8,128)(2,1)S(1)} %bitcast.586, bf16[192,3,128]{2,0,1:T(8,128)(2,1)} %bitcast.148, bf16[192,14,131]{2,0,1:T(8,128)(2,1)S(1)} %get-tuple-element.147, bf16[192,14,131]{2,0,1:T(8,128)(2,1)S(1)} %get-tuple-element.146, ...), kind=kLoop, calls=%fused_computation.297 | loop fusion | flops 16318464 | bytes 9755904 | tf_op jit(solution)/shard_map/add | solution.py:341
  131.9 2.7 %collective-permute-start.15 = (f32[26,128]{1,0:T(8,128)S(1)}, f32[26,128]{1,0:T(8,128)S(1)}, u32[]{:S(2)}, u32[]{:S(2)}) collective-permute-start(f32[26,128]{1,0:T(8,128)S(1)} %get-tuple-element.161), channel_id=1, source_target_pairs={{0,16},{1,17},{2,18},{3,19},{4,20},{5,21},{6,22},{7,23},{8,24},{9,... | collective-permute-start | bytes 39944 | tf_op jit(solution)/shard_map/ppermute | solution.py:255
  134.6 2.5 %collective-permute-start.16 = (f32[26,128]{1,0:T(8,128)S(1)}, f32[26,128]{1,0:T(8,128)S(1)}, u32[]{:S(2)}, u32[]{:S(2)}) collective-permute-start(f32[26,128]{1,0:T(8,128)S(1)} %get-tuple-element.163), channel_id=1, source_target_pairs={{0,32},{1,33},{2,34},{3,35},{4,36},{5,37},{6,38},{7,39},{8,40},{9,... | collective-permute-start | bytes 39944 | tf_op jit(solution)/shard_map/ppermute | solution.py:255
  137.1 1.6 collective-permute-done.16
  138.7 2.2 %collective-permute-done.17 = f32[26,128]{1,0:T(8,128)S(1)} collective-permute-done((f32[26,128]{1,0:T(8,128)S(1)}, f32[26,128]{1,0:T(8,128)S(1)}, u32[]{:S(2)}, u32[]{:S(2)}) %collective-permute-start.17) | collective-permute-done | bytes 13344 | tf_op jit(solution)/shard_map/ppermute | solution.py:255
  142.2 2.6 %collective-permute-start.20 = (f32[26,128]{1,0:T(8,128)S(1)}, f32[26,128]{1,0:T(8,128)S(1)}, u32[]{:S(2)}, u32[]{:S(2)}) collective-permute-start(f32[26,128]{1,0:T(8,128)S(1)} %get-tuple-element.135), channel_id=1, source_target_pairs={{0,48},{1,49},{2,50},{3,51},{4,52},{5,53},{6,54},{7,55},{8,56},{9,... | collective-permute-start | bytes 39944 | tf_op jit(solution)/shard_map/ppermute | solution.py:272
  146.1 3.8 %collective-permute-start.22 = (f32[104,128]{1,0:T(8,128)S(1)}, f32[104,128]{1,0:T(8,128)S(1)}, u32[]{:S(2)}, u32[]{:S(2)}) collective-permute-start(f32[104,128]{1,0:T(8,128)S(1)} %reshape.316), channel_id=1, source_target_pairs={{0,4},{1,5},{2,6},{3,7},{4,0},{5,1},{6,2},{7,3},{8,12},{9,13},{10,... | collective-permute-start | bytes 159752 | tf_op jit(solution)/shard_map/ppermute | solution.py:272
  150.0 2.0 %collective-permute-done.22 = f32[104,128]{1,0:T(8,128)S(1)} collective-permute-done((f32[104,128]{1,0:T(8,128)S(1)}, f32[104,128]{1,0:T(8,128)S(1)}, u32[]{:S(2)}, u32[]{:S(2)}) %collective-permute-start.22) | collective-permute-done | bytes 53280 | tf_op jit(solution)/shard_map/ppermute | solution.py:272
  152.0 2.1 %collective-permute-done.23 = f32[104,128]{1,0:T(8,128)S(1)} collective-permute-done((f32[104,128]{1,0:T(8,128)S(1)}, f32[104,128]{1,0:T(8,128)S(1)}, u32[]{:S(2)}, u32[]{:S(2)}) %collective-permute-start.23) | collective-permute-done | bytes 53280 | tf_op jit(solution)/shard_map/ppermute | solution.py:272
  154.2 2.0 %collective-permute-start.25 = (f32[416,128]{1,0:T(8,128)S(1)}, f32[416,128]{1,0:T(8,128)S(1)}, u32[]{:S(2)}, u32[]{:S(2)}) collective-permute-start(f32[416,128]{1,0:T(8,128)S(1)} %bitcast.591), channel_id=1, source_target_pairs={{0,1},{1,0},{2,3},{3,2},{4,5},{5,4},{6,7},{7,6},{8,9},{9,8},{10,11... | collective-permute-start | bytes 638984 | tf_op jit(solution)/shard_map/ppermute | solution.py:272
  156.2 1.9 %collective-permute-start.26 = (f32[416,128]{1,0:T(8,128)S(1)}, f32[416,128]{1,0:T(8,128)S(1)}, u32[]{:S(2)}, u32[]{:S(2)}) collective-permute-start(f32[416,128]{1,0:T(8,128)S(1)} %bitcast.592), channel_id=1, source_target_pairs={{0,65},{1,64},{2,67},{3,66},{4,69},{5,68},{6,71},{7,70},{8,73},{9,... | collective-permute-start | bytes 638984 | tf_op jit(solution)/shard_map/ppermute | solution.py:272
  158.9 2.9 %collective-permute-done.25 = f32[416,128]{1,0:T(8,128)S(1)} collective-permute-done((f32[416,128]{1,0:T(8,128)S(1)}, f32[416,128]{1,0:T(8,128)S(1)}, u32[]{:S(2)}, u32[]{:S(2)}) %collective-permute-start.25) | collective-permute-done | bytes 213024 | tf_op jit(solution)/shard_map/ppermute | solution.py:272
  161.8 2.2 %collective-permute-done.26 = f32[416,128]{1,0:T(8,128)S(1)} collective-permute-done((f32[416,128]{1,0:T(8,128)S(1)}, f32[416,128]{1,0:T(8,128)S(1)}, u32[]{:S(2)}, u32[]{:S(2)}) %collective-permute-start.26) | collective-permute-done | bytes 213024 | tf_op jit(solution)/shard_map/ppermute | solution.py:272
  164.0 8.5 %collective-permute-start.27 = (f32[1664,128]{1,0:T(8,128)S(1)}, f32[1664,128]{1,0:T(8,128)S(1)}, u32[]{:S(2)}, u32[]{:S(2)}) collective-permute-start(f32[1664,128]{1,0:T(8,128)S(1)} %bitcast.566), channel_id=1, source_target_pairs={{0,8},{1,9},{2,10},{3,11},{4,12},{5,13},{6,14},{7,15},{8,0},{9,1},... | collective-permute-start | bytes 2555912 | tf_op jit(solution)/shard_map/ppermute | solution.py:272
  172.6 1.3 copy.73
  (311 shorter events, 38.6 us)
Async XLA Ops:
  1.9 11.2 %collective-permute-start = (bf16[3,192,128]{2,1,0:T(8,128)(2,1)S(1)}, bf16[3,192,128]{2,1,0:T(8,128)(2,1)S(1)}, u32[]{:S(2)}, u32[]{:S(2)}) collective-permute-start(bf16[3,192,128]{2,1,0:T(8,128)(2,1)S(1)} %get-tuple-element.156), channel_id=1, source_target_pairs={{0,8},{8,16},{16,24},{24,32},{32,40},{40,48},{48,56},{1,9},{9,17},... | collective-permute-start | bytes 442376 | tf_op jit(solution)/shard_map/ppermute | solution.py:21
  6.4 6.7 %collective-permute-start.1 = (bf16[3,192,128]{2,1,0:T(8,128)(2,1)S(1)}, bf16[3,192,128]{2,1,0:T(8,128)(2,1)S(1)}, u32[]{:S(2)}, u32[]{:S(2)}) collective-permute-start(bf16[3,192,128]{2,1,0:T(8,128)(2,1)S(1)} %get-tuple-element.157), channel_id=1, source_target_pairs={{8,0},{16,8},{24,16},{32,24},{40,32},{48,40},{56,48},{9,1},{17,9},... | collective-permute-start | bytes 442376 | tf_op jit(solution)/shard_map/ppermute | solution.py:22
  13.9 7.4 %collective-permute-start.3 = (bf16[3,14,192]{2,1,0:T(8,128)(2,1)S(1)}, bf16[3,14,192]{2,1,0:T(8,128)(2,1)S(1)}, u32[]{:S(2)}, u32[]{:S(2)}) collective-permute-start(bf16[3,14,192]{2,1,0:T(8,128)(2,1)S(1)} %copy.57), channel_id=1, source_target_pairs={{1,0},{2,1},{3,2},{4,3},{5,4},{6,5},{7,6},{9,8},{10,9},{11,10},{12... | collective-permute-start | bytes 48392 | tf_op jit(solution)/shard_map/ppermute | solution.py:22
  15.6 6.4 %collective-permute-start.2 = (bf16[3,14,192]{2,1,0:T(8,128)(2,1)S(1)}, bf16[3,14,192]{2,1,0:T(8,128)(2,1)S(1)}, u32[]{:S(2)}, u32[]{:S(2)}) collective-permute-start(bf16[3,14,192]{2,1,0:T(8,128)(2,1)S(1)} %copy.55), channel_id=1, source_target_pairs={{0,1},{1,2},{2,3},{3,4},{4,5},{5,6},{6,7},{8,9},{9,10},{10,11},{11... | collective-permute-start | bytes 48392 | tf_op jit(solution)/shard_map/ppermute | solution.py:21
  59.3 24.3 %collective-permute-start.8 = (bf16[3,192,128]{2,1,0:T(8,128)(2,1)}, bf16[3,192,128]{2,1,0:T(8,128)(2,1)S(1)}, u32[]{:S(2)}, u32[]{:S(2)}) collective-permute-start(bf16[3,192,128]{2,1,0:T(8,128)(2,1)} %get-tuple-element.155), channel_id=1, source_target_pairs={{0,8},{8,16},{16,24},{24,32},{32,40},{40,48},{48,56},{1,9},{9,17},... | collective-permute-start | bytes 442376 | tf_op jit(solution)/shard_map/ppermute | solution.py:21
  64.0 19.5 %collective-permute-start.9 = (bf16[3,192,128]{2,1,0:T(8,128)(2,1)}, bf16[3,192,128]{2,1,0:T(8,128)(2,1)}, u32[]{:S(2)}, u32[]{:S(2)}) collective-permute-start(bf16[3,192,128]{2,1,0:T(8,128)(2,1)} %get-tuple-element.154), channel_id=1, source_target_pairs={{8,0},{16,8},{24,16},{32,24},{40,32},{48,40},{56,48},{9,1},{17,9},... | collective-permute-start | bytes 442376 | tf_op jit(solution)/shard_map/ppermute | solution.py:22
  83.5 17.8 %collective-permute-start.4 = (f32[1664,128]{1,0:T(8,128)}, f32[1664,128]{1,0:T(8,128)}, u32[]{:S(2)}, u32[]{:S(2)}) collective-permute-start(f32[1664,128]{1,0:T(8,128)} %slice.1769), channel_id=1, source_target_pairs={{0,8},{1,9},{2,10},{3,11},{4,12},{5,13},{6,14},{7,15},{8,0},{9,1},... | collective-permute-start | bytes 2555912 | tf_op jit(solution)/shard_map/ppermute | solution.py:255
  87.4 9.2 %collective-permute-start.10 = (bf16[3,14,192]{2,1,0:T(8,128)(2,1)S(1)}, bf16[3,14,192]{2,1,0:T(8,128)(2,1)S(1)}, u32[]{:S(2)}, u32[]{:S(2)}) collective-permute-start(bf16[3,14,192]{2,1,0:T(8,128)(2,1)S(1)} %copy.69), channel_id=1, source_target_pairs={{1,0},{2,1},{3,2},{4,3},{5,4},{6,5},{7,6},{9,8},{10,9},{11,10},{12... | collective-permute-start | bytes 48392 | tf_op jit(solution)/shard_map/ppermute | solution.py:22
  90.1 7.6 %collective-permute-start.11 = (bf16[3,14,192]{2,1,0:T(8,128)(2,1)S(1)}, bf16[3,14,192]{2,1,0:T(8,128)(2,1)S(1)}, u32[]{:S(2)}, u32[]{:S(2)}) collective-permute-start(bf16[3,14,192]{2,1,0:T(8,128)(2,1)S(1)} %copy.71), channel_id=1, source_target_pairs={{0,1},{1,2},{2,3},{3,4},{4,5},{5,6},{6,7},{8,9},{9,10},{10,11},{11... | collective-permute-start | bytes 48392 | tf_op jit(solution)/shard_map/ppermute | solution.py:21
  102.7 11.6 %collective-permute-start.5 = (f32[416,128]{1,0:T(8,128)S(1)}, f32[416,128]{1,0:T(8,128)S(1)}, u32[]{:S(2)}, u32[]{:S(2)}) collective-permute-start(f32[416,128]{1,0:T(8,128)S(1)} %get-tuple-element.143), channel_id=1, source_target_pairs={{0,64},{1,65},{2,66},{3,67},{4,68},{5,69},{6,70},{7,71},{8,72},{9,... | collective-permute-start | bytes 638984 | tf_op jit(solution)/shard_map/ppermute | solution.py:255
  103.8 13.1 %collective-permute-start.6 = (f32[416,128]{1,0:T(8,128)S(1)}, f32[416,128]{1,0:T(8,128)S(1)}, u32[]{:S(2)}, u32[]{:S(2)}) collective-permute-start(f32[416,128]{1,0:T(8,128)S(1)} %get-tuple-element.145), channel_id=1, source_target_pairs={{0,1},{1,0},{2,3},{3,2},{4,5},{5,4},{6,7},{7,6},{8,9},{9,8},{10,11... | collective-permute-start | bytes 638984 | tf_op jit(solution)/shard_map/ppermute | solution.py:255
  108.3 11.8 %collective-permute-start.7 = (f32[416,128]{1,0:T(8,128)S(1)}, f32[416,128]{1,0:T(8,128)S(1)}, u32[]{:S(2)}, u32[]{:S(2)}) collective-permute-start(f32[416,128]{1,0:T(8,128)S(1)} %get-tuple-element.144), channel_id=1, source_target_pairs={{0,65},{1,64},{2,67},{3,66},{4,69},{5,68},{6,71},{7,70},{8,73},{9,... | collective-permute-start | bytes 638984 | tf_op jit(solution)/shard_map/ppermute | solution.py:255
  108.3 18.2 %copy-start.48 = (f32[96]{0:T(128)S(1)}, f32[96]{0:T(128)}, u32[]{:S(2)}) copy-start(f32[96]{0:T(128)} %get-tuple-element.165) | copy-start | bytes 1156
  108.3 18.2 %copy-start.49 = (f32[96]{0:T(128)S(1)}, f32[96]{0:T(128)}, u32[]{:S(2)}) copy-start(f32[96]{0:T(128)} %get-tuple-element.166) | copy-start | bytes 1156
  108.3 18.2 %copy-start.50 = (f32[96]{0:T(128)S(1)}, f32[96]{0:T(128)}, u32[]{:S(2)}) copy-start(f32[96]{0:T(128)} %get-tuple-element.167) | copy-start | bytes 1156
  108.3 18.2 %copy-start.51 = (f32[96]{0:T(128)S(1)}, f32[96]{0:T(128)}, u32[]{:S(2)}) copy-start(f32[96]{0:T(128)} %get-tuple-element.168) | copy-start | bytes 1156
  108.3 18.2 %copy-start.52 = (f32[96]{0:T(128)S(1)}, f32[96]{0:T(128)}, u32[]{:S(2)}) copy-start(f32[96]{0:T(128)} %get-tuple-element.169) | copy-start | bytes 1156
  108.4 18.2 %copy-start.53 = (f32[96]{0:T(128)S(1)}, f32[96]{0:T(128)}, u32[]{:S(2)}) copy-start(f32[96]{0:T(128)} %get-tuple-element.170) | copy-start | bytes 1156
  108.4 18.2 %copy-start.54 = (f32[96]{0:T(128)S(1)}, f32[96]{0:T(128)}, u32[]{:S(2)}) copy-start(f32[96]{0:T(128)} %get-tuple-element.171) | copy-start | bytes 1156
  108.4 18.2 %copy-start.55 = (f32[96]{0:T(128)S(1)}, f32[96]{0:T(128)}, u32[]{:S(2)}) copy-start(f32[96]{0:T(128)} %get-tuple-element.172) | copy-start | bytes 1156
  108.4 18.2 %copy-start.56 = (f32[96]{0:T(128)S(1)}, f32[96]{0:T(128)}, u32[]{:S(2)}) copy-start(f32[96]{0:T(128)} %get-tuple-element.173) | copy-start | bytes 1156
  108.4 18.2 %copy-start.57 = (f32[96]{0:T(128)S(1)}, f32[96]{0:T(128)}, u32[]{:S(2)}) copy-start(f32[96]{0:T(128)} %get-tuple-element.174) | copy-start | bytes 1156
  108.4 18.2 %copy-start.58 = (f32[96]{0:T(128)S(1)}, f32[96]{0:T(128)}, u32[]{:S(2)}) copy-start(f32[96]{0:T(128)} %get-tuple-element.175) | copy-start | bytes 1156
  108.4 18.2 %copy-start.59 = (f32[96]{0:T(128)S(1)}, f32[96]{0:T(128)}, u32[]{:S(2)}) copy-start(f32[96]{0:T(128)} %get-tuple-element.176) | copy-start | bytes 1156
  108.4 18.2 %copy-start.60 = (f32[96]{0:T(128)S(1)}, f32[96]{0:T(128)}, u32[]{:S(2)}) copy-start(f32[96]{0:T(128)} %get-tuple-element.177) | copy-start | bytes 1156
  108.4 18.2 %copy-start.61 = (f32[96]{0:T(128)S(1)}, f32[96]{0:T(128)}, u32[]{:S(2)}) copy-start(f32[96]{0:T(128)} %get-tuple-element.178) | copy-start | bytes 1156
  108.4 18.2 %copy-start.62 = (f32[96]{0:T(128)S(1)}, f32[96]{0:T(128)}, u32[]{:S(2)}) copy-start(f32[96]{0:T(128)} %get-tuple-element.179) | copy-start | bytes 1156
  108.5 18.2 %copy-start.63 = (f32[96]{0:T(128)S(1)}, f32[96]{0:T(128)}, u32[]{:S(2)}) copy-start(f32[96]{0:T(128)} %get-tuple-element.180) | copy-start | bytes 1156
  108.5 18.2 %copy-start.64 = (f32[96]{0:T(128)S(1)}, f32[96]{0:T(128)}, u32[]{:S(2)}) copy-start(f32[96]{0:T(128)} %get-tuple-element.181) | copy-start | bytes 1156
  108.5 18.2 %copy-start.65 = (f32[96]{0:T(128)S(1)}, f32[96]{0:T(128)}, u32[]{:S(2)}) copy-start(f32[96]{0:T(128)} %get-tuple-element.182) | copy-start | bytes 1156
  108.5 18.2 %copy-start.66 = (f32[96]{0:T(128)S(1)}, f32[96]{0:T(128)}, u32[]{:S(2)}) copy-start(f32[96]{0:T(128)} %get-tuple-element.183) | copy-start | bytes 1156
  108.5 18.2 %copy-start.67 = (f32[96]{0:T(128)S(1)}, f32[96]{0:T(128)}, u32[]{:S(2)}) copy-start(f32[96]{0:T(128)} %get-tuple-element.184) | copy-start | bytes 1156
  120.2 11.6 %collective-permute-start.12 = (f32[104,128]{1,0:T(8,128)S(1)}, f32[104,128]{1,0:T(8,128)S(1)}, u32[]{:S(2)}, u32[]{:S(2)}) collective-permute-start(f32[104,128]{1,0:T(8,128)S(1)} %get-tuple-element.158), channel_id=1, source_target_pairs={{0,2},{1,3},{2,0},{3,1},{4,6},{5,7},{6,4},{7,5},{8,10},{9,11},{10,... | collective-permute-start | bytes 159752 | tf_op jit(solution)/shard_map/ppermute | solution.py:255
  122.9 8.9 %collective-permute-start.13 = (f32[104,128]{1,0:T(8,128)S(1)}, f32[104,128]{1,0:T(8,128)S(1)}, u32[]{:S(2)}, u32[]{:S(2)}) collective-permute-start(f32[104,128]{1,0:T(8,128)S(1)} %get-tuple-element.160), channel_id=1, source_target_pairs={{0,4},{1,5},{2,6},{3,7},{4,0},{5,1},{6,2},{7,3},{8,12},{9,13},{10,... | collective-permute-start | bytes 159752 | tf_op jit(solution)/shard_map/ppermute | solution.py:255
  126.5 5.4 %collective-permute-start.14 = (f32[104,128]{1,0:T(8,128)S(1)}, f32[104,128]{1,0:T(8,128)S(1)}, u32[]{:S(2)}, u32[]{:S(2)}) collective-permute-start(f32[104,128]{1,0:T(8,128)S(1)} %get-tuple-element.159), channel_id=1, source_target_pairs={{0,6},{1,7},{2,4},{3,5},{4,2},{5,3},{6,0},{7,1},{8,14},{9,15},{10,... | collective-permute-start | bytes 159752 | tf_op jit(solution)/shard_map/ppermute | solution.py:255
  131.9 5.2 %collective-permute-start.15 = (f32[26,128]{1,0:T(8,128)S(1)}, f32[26,128]{1,0:T(8,128)S(1)}, u32[]{:S(2)}, u32[]{:S(2)}) collective-permute-start(f32[26,128]{1,0:T(8,128)S(1)} %get-tuple-element.161), channel_id=1, source_target_pairs={{0,16},{1,17},{2,18},{3,19},{4,20},{5,21},{6,22},{7,23},{8,24},{9,... | collective-permute-start | bytes 39944 | tf_op jit(solution)/shard_map/ppermute | solution.py:255
  134.6 4.1 %collective-permute-start.16 = (f32[26,128]{1,0:T(8,128)S(1)}, f32[26,128]{1,0:T(8,128)S(1)}, u32[]{:S(2)}, u32[]{:S(2)}) collective-permute-start(f32[26,128]{1,0:T(8,128)S(1)} %get-tuple-element.163), channel_id=1, source_target_pairs={{0,32},{1,33},{2,34},{3,35},{4,36},{5,37},{6,38},{7,39},{8,40},{9,... | collective-permute-start | bytes 39944 | tf_op jit(solution)/shard_map/ppermute | solution.py:255
  137.0 3.8 %collective-permute-start.17 = (f32[26,128]{1,0:T(8,128)S(1)}, f32[26,128]{1,0:T(8,128)S(1)}, u32[]{:S(2)}, u32[]{:S(2)}) collective-permute-start(f32[26,128]{1,0:T(8,128)S(1)} %get-tuple-element.162), channel_id=1, source_target_pairs={{0,48},{1,49},{2,50},{3,51},{4,52},{5,53},{6,54},{7,55},{8,56},{9,... | collective-permute-start | bytes 39944 | tf_op jit(solution)/shard_map/ppermute | solution.py:255
  140.9 3.9 %collective-permute-start.18 = (f32[26,128]{1,0:T(8,128)S(1)}, f32[26,128]{1,0:T(8,128)S(1)}, u32[]{:S(2)}, u32[]{:S(2)}) collective-permute-start(f32[26,128]{1,0:T(8,128)S(1)} %get-tuple-element.135), channel_id=1, source_target_pairs={{0,16},{1,17},{2,18},{3,19},{4,20},{5,21},{6,22},{7,23},{8,24},{9,... | collective-permute-start | bytes 39944 | tf_op jit(solution)/shard_map/ppermute | solution.py:272
  141.0 4.2 %collective-permute-start.19 = (f32[26,128]{1,0:T(8,128)S(1)}, f32[26,128]{1,0:T(8,128)S(1)}, u32[]{:S(2)}, u32[]{:S(2)}) collective-permute-start(f32[26,128]{1,0:T(8,128)S(1)} %get-tuple-element.135), channel_id=1, source_target_pairs={{0,32},{1,33},{2,34},{3,35},{4,36},{5,37},{6,38},{7,39},{8,40},{9,... | collective-permute-start | bytes 39944 | tf_op jit(solution)/shard_map/ppermute | solution.py:272
  142.2 3.8 %collective-permute-start.20 = (f32[26,128]{1,0:T(8,128)S(1)}, f32[26,128]{1,0:T(8,128)S(1)}, u32[]{:S(2)}, u32[]{:S(2)}) collective-permute-start(f32[26,128]{1,0:T(8,128)S(1)} %get-tuple-element.135), channel_id=1, source_target_pairs={{0,48},{1,49},{2,50},{3,51},{4,52},{5,53},{6,54},{7,55},{8,56},{9,... | collective-permute-start | bytes 39944 | tf_op jit(solution)/shard_map/ppermute | solution.py:272
  146.0 4.0 %collective-permute-start.21 = (f32[104,128]{1,0:T(8,128)S(1)}, f32[104,128]{1,0:T(8,128)S(1)}, u32[]{:S(2)}, u32[]{:S(2)}) collective-permute-start(f32[104,128]{1,0:T(8,128)S(1)} %reshape.316), channel_id=1, source_target_pairs={{0,2},{1,3},{2,0},{3,1},{4,6},{5,7},{6,4},{7,5},{8,10},{9,11},{10,... | collective-permute-start | bytes 159752 | tf_op jit(solution)/shard_map/ppermute | solution.py:272
  146.1 5.9 %collective-permute-start.22 = (f32[104,128]{1,0:T(8,128)S(1)}, f32[104,128]{1,0:T(8,128)S(1)}, u32[]{:S(2)}, u32[]{:S(2)}) collective-permute-start(f32[104,128]{1,0:T(8,128)S(1)} %reshape.316), channel_id=1, source_target_pairs={{0,4},{1,5},{2,6},{3,7},{4,0},{5,1},{6,2},{7,3},{8,12},{9,13},{10,... | collective-permute-start | bytes 159752 | tf_op jit(solution)/shard_map/ppermute | solution.py:272
  149.9 4.2 %collective-permute-start.23 = (f32[104,128]{1,0:T(8,128)S(1)}, f32[104,128]{1,0:T(8,128)S(1)}, u32[]{:S(2)}, u32[]{:S(2)}) collective-permute-start(f32[104,128]{1,0:T(8,128)S(1)} %reshape.316), channel_id=1, source_target_pairs={{0,6},{1,7},{2,4},{3,5},{4,2},{5,3},{6,0},{7,1},{8,14},{9,15},{10,... | collective-permute-start | bytes 159752 | tf_op jit(solution)/shard_map/ppermute | solution.py:272
  154.1 4.8 %collective-permute-start.24 = (f32[416,128]{1,0:T(8,128)S(1)}, f32[416,128]{1,0:T(8,128)S(1)}, u32[]{:S(2)}, u32[]{:S(2)}) collective-permute-start(f32[416,128]{1,0:T(8,128)S(1)} %bitcast.590), channel_id=1, source_target_pairs={{0,64},{1,65},{2,66},{3,67},{4,68},{5,69},{6,70},{7,71},{8,72},{9,... | collective-permute-start | bytes 638984 | tf_op jit(solution)/shard_map/ppermute | solution.py:272
  154.2 7.6 %collective-permute-start.25 = (f32[416,128]{1,0:T(8,128)S(1)}, f32[416,128]{1,0:T(8,128)S(1)}, u32[]{:S(2)}, u32[]{:S(2)}) collective-permute-start(f32[416,128]{1,0:T(8,128)S(1)} %bitcast.591), channel_id=1, source_target_pairs={{0,1},{1,0},{2,3},{3,2},{4,5},{5,4},{6,7},{7,6},{8,9},{9,8},{10,11... | collective-permute-start | bytes 638984 | tf_op jit(solution)/shard_map/ppermute | solution.py:272
  156.2 7.8 %collective-permute-start.26 = (f32[416,128]{1,0:T(8,128)S(1)}, f32[416,128]{1,0:T(8,128)S(1)}, u32[]{:S(2)}, u32[]{:S(2)}) collective-permute-start(f32[416,128]{1,0:T(8,128)S(1)} %bitcast.592), channel_id=1, source_target_pairs={{0,65},{1,64},{2,67},{3,66},{4,69},{5,68},{6,71},{7,70},{8,73},{9,... | collective-permute-start | bytes 638984 | tf_op jit(solution)/shard_map/ppermute | solution.py:272
  164.0 10.5 %collective-permute-start.27 = (f32[1664,128]{1,0:T(8,128)S(1)}, f32[1664,128]{1,0:T(8,128)S(1)}, u32[]{:S(2)}, u32[]{:S(2)}) collective-permute-start(f32[1664,128]{1,0:T(8,128)S(1)} %bitcast.566), channel_id=1, source_target_pairs={{0,8},{1,9},{2,10},{3,11},{4,12},{5,13},{6,14},{7,15},{8,0},{9,1},... | collective-permute-start | bytes 2555912 | tf_op jit(solution)/shard_map/ppermute | solution.py:272
  (73 other events, 589.5 us)

commit v10 on v8

--- a/solution.py
+++ b/solution.py
@@ -302,7 +302,7 @@
     def scale_of(position):
         return jnp.where(position == loss_at, 1.0 / cell_count, grad_scale).astype(jnp.float32)
 
-    half = d_conv.shape[0] // 2
+    half = d_conv.shape[0] * 2 // 3
 
     def input_part(low, high):
         flipped = depthwise(d_padded[low:high], dw_weight[low:high], height, width, True)

time: 174 us -> 172 us (0.989)
  transfers between devices with their start and end apart: 28 -> 28, of which waited for: 15 -> 16; matrix products, arithmetic and copies ran while one was open for 14% -> 13% of each run, Pallas kernels for 0% -> 0%
where the time goes in v10:
time: 172 us
  starting transfers between devices  62.8 us (37%)
  other arithmetic  36 us (21%)
  local copies, waits for them, and re-layouts  35 us (20%)
  waiting for transfers between devices  21.6 us (13%)
  matrix products  13.1 us (8%)
  between operations  2.97 us (2%)
    ppermute x10, starting transfers between devices, butterfly_psum(): other = lax.ppermute(buffer, axes, pairs)  20.1 us
    ppermute x4, starting transfers between devices, padded_2(): before = jnp.transpose(lax.ppermute(last, axis, up), order)  18.4 us
    ppermute x10, starting transfers between devices, butterfly_psum(): total = total + lax.ppermute(send, axes, pairs)  16.4 us
    ppermute x10, waiting for transfers between devices, butterfly_psum(): other = lax.ppermute(buffer, axes, pairs)  13.9 us
    dot_general x12, matrix products, product(): jnp.einsum(form, left_side, right_side, preferred_element_type=jnp.float32)  13.1 us
    reduce_sum x4, other arithmetic, conv_backward(): columns.append(jnp.sum(window * conv_float, axis=(1, 2)))  12.2 us
    unnamed x245, local copies, waits for them, and re-layouts  9.97 us
    add x2, other arithmetic, input_part(): return returned[low:high].astype(jnp.float32) + flipped  9.58 us
  transfers between devices with their start and end apart: 28, of which 16 were waited for; matrix products, arithmetic and copies ran while one was open for 13% of the time, Pallas kernels for 0%

profile of v10, /device:TPU:1, one launch (start us, length us, event | category | flops | bytes accessed | tf_op | source)
XLA Modules:
  0.0 171.6 jit_solution(13387067253801865876)
XLA Ops:
  0.7 1.1 copy-done
  1.9 3.3 %collective-permute-start.1 = (bf16[3,192,128]{2,1,0:T(8,128)(2,1)S(1)}, bf16[3,192,128]{2,1,0:T(8,128)(2,1)S(1)}, u32[]{:S(2)}, u32[]{:S(2)}) collective-permute-start(bf16[3,192,128]{2,1,0:T(8,128)(2,1)S(1)} %get-tuple-element.157), channel_id=1, source_target_pairs={{8,0},{16,8},{24,16},{32,24},{40,32},{48,40},{56,48},{9,1},{17,9},... | collective-permute-start | bytes 442376 | tf_op jit(solution)/shard_map/ppermute | solution.py:22
  5.2 3.1 %collective-permute-start = (bf16[3,192,128]{2,1,0:T(8,128)(2,1)S(1)}, bf16[3,192,128]{2,1,0:T(8,128)(2,1)S(1)}, u32[]{:S(2)}, u32[]{:S(2)}) collective-permute-start(bf16[3,192,128]{2,1,0:T(8,128)(2,1)S(1)} %get-tuple-element.156), channel_id=1, source_target_pairs={{0,8},{8,16},{16,24},{24,32},{32,40},{40,48},{48,56},{1,9},{9,17},... | collective-permute-start | bytes 442376 | tf_op jit(solution)/shard_map/ppermute | solution.py:21
  13.7 1.3 collective-permute-start.3
  15.4 5.5 %collective-permute-start.2 = (bf16[3,14,192]{2,1,0:T(8,128)(2,1)S(1)}, bf16[3,14,192]{2,1,0:T(8,128)(2,1)S(1)}, u32[]{:S(2)}, u32[]{:S(2)}) collective-permute-start(bf16[3,14,192]{2,1,0:T(8,128)(2,1)S(1)} %copy.55), channel_id=1, source_target_pairs={{0,1},{1,2},{2,3},{3,4},{4,5},{5,6},{6,7},{8,9},{9,10},{10,11},{11... | collective-permute-start | bytes 48392 | tf_op jit(solution)/shard_map/ppermute | solution.py:21
  22.6 1.4 pad_maximum_fusion
  24.3 8.3 %fusion.165 = (f32[8,128]{1,0:T(8,128)S(1)}, f32[192,8,128]{2,0,1:T(8,128)S(1)}) fusion(f32[192]{0:T(256)S(1)} %copy-done.114, bf16[192,14,131]{2,0,1:T(8,128)(2,1)S(1)} %get-tuple-element.150, f32[192]{0:T(256)S(1)} %bitcast.637, f32[192]{0:T(256)S(1)} %bitcast.638, f32[192]{0:T(256)S(1)} %bitcast.639, bf16[192,3,128]{2,0,1:T(8,128)(2,1)S(1)} %bitcast.579, ...), kind=kLoop, calls=%fused_computation.483 | loop fusion | flops 30276608 | bytes 18032128 | tf_op jit(solution)/shard_map/reduce_sum | solution.py:65
  36.5 1.9 %convert_reduce_fusion.2 = (f32[512]{0:T(512)}, bf16[512,8,128]{0,2,1:T(8,128)(2,1)S(1)}) fusion(f32[8,128,512]{2,1,0:T(8,128)S(1)} %get-tuple-element.321, f32[512]{0:T(512)S(1)} %copy-done.70, bf16[16,8,128]{2,0,1:T(8,128)(2,1)S(1)} %get-tuple-element.138, bf16[512,16]{0,1:T(8,128)(2,1)S(1)} %copy-done.10), kind=kOutput, calls=%fused_computation.77 | convolution fusion | flops 23592448 | bytes 3198976 | tf_op jit(solution)/shard_map/khw,lk->lhw/dot_general | solution.py:34
  38.4 1.2 fusion.72
  39.5 2.5 %convert_reduce_fusion.1 = (f32[768]{0:T(1024)}, bf16[768,8,128]{0,2,1:T(8,128)(2,1)S(1)}) fusion(f32[8,128,768]{2,1,0:T(8,128)S(1)} %get-tuple-element.317, f32[768]{0:T(1024)S(1)} %copy-done.15, bf16[768,192]{0,1:T(8,128)(2,1)S(1)} %copy-done.5, bf16[192,8,128]{2,0,1:T(8,128)(2,1)S(1)} %get-tuple-element.327, f32[192]{0:T(256)S(1)} %copy-done.11), kind=kOutput, calls=%fused_computation.63 | convolution fusion | flops 312802560 | bytes 5413632 | tf_op jit(solution)/shard_map/chw,dc->dhw/dot_general | solution.py:34
  42.1 1.4 fusion.123
  43.5 4.1 %fusion.118 = (f32[192]{0:T(256)}, f32[192]{0:T(256)}, f32[192]{0:T(256)}, f32[192]{0:T(256)}, f32[192]{0:T(256)}, /*index=5*/f32[192]{0:T(256)}, f32[192]{0:T(2...) fusion(bf16[192,14,131]{2,0,1:T(8,128)(2,1)S(1)} %get-tuple-ele, ...), kind=kLoop, calls=%fused_computation.250 | loop fusion | flops 12382848 | bytes 9074944 | tf_op jit(solution)/shard_map/reduce_sum | solution.py:122
  47.5 4.4 %fusion.122 = (f32[192]{0:T(256)}, f32[192]{0:T(256)}, f32[192]{0:T(256)}, f32[192]{0:T(256)}, f32[192]{0:T(256)}, /*index=5*/f32[192]{0:T(256)}, f32[192]{0:T(2...) fusion(bf16[192,8,128]{2,0,1:T(8,128)(2,1)S(1)} %get-tuple-elem, ...), kind=kLoop, calls=%fused_computation.254 | loop fusion | flops 11006400 | bytes 7485696 | tf_op jit(solution)/shard_map/reduce_sum | solution.py:122
  51.9 1.1 fusion.76
  53.0 2.7 %fusion.121 = (f32[192]{0:T(256)}, f32[192]{0:T(256)}, f32[192]{0:T(256)}, f32[192]{0:T(256)}, f32[192]{0:T(256)}, /*index=5*/f32[192]{0:T(256)}, f32[192]{0:T(256)}, f32[192]{0:T(256)}, f32[192]{0:T(256)}, f32[192]{0:T(256)}) fusion(bf16[192,8,128]{2,0,1:T(8,128)(2,1)S(1)} %get-tuple-element.136, bf16[192,14,131]{2,0,1:T(8,128)(2,1)S(1)} %get-tuple-element.150, ...), kind=kLoop, calls=%fused_computation.253 | loop fusion | flops 7272576 | bytes 2661888 | tf_op jit(solution)/shard_map/reduce_sum | solution.py:122
  56.3 1.3 fusion.160
  58.3 1.2 convolution_bitcast_fusion
  62.7 4.3 %stack.199 = f32[192,49]{0,1:T(8,128)S(1)} concatenate(f32[192,1]{0,1:T(1,128)} %bitcast.687, f32[192,1]{0,1:T(1,128)} %bitcast.686, f32[192,1]{0,1:T(1,128)} %bitcast.685, f32[192,1]{0,1:T(1,128)S(1)} %bitcast.632, f32[192,1]{0,1:T(1,128)S(1)} %bitcast.609, f32[192,1]{0,1:T(1,128)S(1)} %bitcast.610, f32[192,1]{0,1:T(1,128)S(1)} %bitcast.611, f32[192,1]{0,1:T(1,128)} %bitcast.689, ...), dimensions={1} | concatenate | bytes 75264 | tf_op jit(solution)/shard_map/stack | solution.py:123
  67.3 1.1 reshape.310
  69.8 1.9 %constant_dynamic-update-slice_fusion.2 = f32[3328,128]{1,0:T(8,128)} fusion(f32[3328,128]{1,0:T(8,128)} %constant_dynamic-update-slice_fusion.3, f32[1152,128]{1,0:T(8,128)} %bitcast.586), kind=kLoop, calls=%fused_computation.355 | loop fusion | bytes 1179648
  73.8 3.5 %collective-permute-start.8 = (bf16[3,192,128]{2,1,0:T(8,128)(2,1)S(1)}, bf16[3,192,128]{2,1,0:T(8,128)(2,1)S(1)}, u32[]{:S(2)}, u32[]{:S(2)}) collective-permute-start(bf16[3,192,128]{2,1,0:T(8,128)(2,1)S(1)} %copy-done.9), channel_id=1, source_target_pairs={{0,8},{8,16},{16,24},{24,32},{32,40},{40,48},{48,56},{1,9},{9,17},... | collective-permute-start | bytes 442376 | tf_op jit(solution)/shard_map/ppermute | solution.py:21
  77.3 1.9 %collective-permute-start.9 = (bf16[3,192,128]{2,1,0:T(8,128)(2,1)S(1)}, bf16[3,192,128]{2,1,0:T(8,128)(2,1)S(1)}, u32[]{:S(2)}, u32[]{:S(2)}) collective-permute-start(bf16[3,192,128]{2,1,0:T(8,128)(2,1)S(1)} %copy-done.8), channel_id=1, source_target_pairs={{8,0},{16,8},{24,16},{32,24},{40,32},{48,40},{56,48},{9,1},{17,9},... | collective-permute-start | bytes 442376 | tf_op jit(solution)/shard_map/ppermute | solution.py:22
  79.2 2.1 %dynamic-slice_bitcast_fusion = f32[1664,128]{1,0:T(8,128)} fusion(f32[2,1664,128]{2,1,0:T(8,128)} %bitcast.595, s32[]{:T(128)S(6)} %select_n.76), kind=kLoop, calls=%fused_computation.154 | loop fusion | bytes 1703940 | tf_op jit(solution)/shard_map/jit(dynamic_index_in_dim)/squeeze | solution.py:223
  81.3 2.4 %collective-permute-done.9 = bf16[3,192,128]{2,1,0:T(8,128)(2,1)S(1)} collective-permute-done((bf16[3,192,128]{2,1,0:T(8,128)(2,1)S(1)}, bf16[3,192,128]{2,1,0:T(8,128)(2,1)S(1)}, u32[]{:S(2)}, u32[]{:S(2)}) %collective-permute-start.9) | collective-permute-done | bytes 147488 | tf_op jit(solution)/shard_map/ppermute | solution.py:22
  84.5 1.3 collective-permute-start.10
  86.2 6.3 %collective-permute-start.11 = (bf16[3,14,192]{2,1,0:T(8,128)(2,1)S(1)}, bf16[3,14,192]{2,1,0:T(8,128)(2,1)S(1)}, u32[]{:S(2)}, u32[]{:S(2)}) collective-permute-start(bf16[3,14,192]{2,1,0:T(8,128)(2,1)S(1)} %copy.71), channel_id=1, source_target_pairs={{0,1},{1,2},{2,3},{3,4},{4,5},{5,6},{6,7},{8,9},{9,10},{10,11},{11... | collective-permute-start | bytes 48392 | tf_op jit(solution)/shard_map/ppermute | solution.py:21
  94.4 1.3 pad_maximum_fusion.1
  96.0 1.3 bitcast_add_fusion
  97.4 4.5 %collective-permute-start.7 = (f32[416,128]{1,0:T(8,128)S(1)}, f32[416,128]{1,0:T(8,128)S(1)}, u32[]{:S(2)}, u32[]{:S(2)}) collective-permute-start(f32[416,128]{1,0:T(8,128)S(1)} %get-tuple-element.144), channel_id=1, source_target_pairs={{0,65},{1,64},{2,67},{3,66},{4,69},{5,68},{6,71},{7,70},{8,73},{9,... | collective-permute-start | bytes 638984 | tf_op jit(solution)/shard_map/ppermute | solution.py:224
  102.9 5.9 %add_add_fusion = f32[128,8,128]{2,0,1:T(8,128)S(1)} fusion(bf16[192,8,128]{2,0,1:T(8,128)(2,1)S(1)} %get-tuple-element.136, bf16[192,3,128]{2,0,1:T(8,128)(2,1)S(1)} %bitcast.589, bf16[192,3,128]{2,0,1:T(8,128)(2,1)S(1)} %bitcast.593, bf16[192,14,131]{2,0,1:T(8,128)(2,1)S(1)} %get-tuple-element.147, bf16[192,14,131]{2,0,1:T(8,128)(2,1)S(1)} %get-tuple-element.146, ...), kind=kLoop, calls=%fused_computation.291 | loop fusion | flops 20185088 | bytes 12771840 | tf_op jit(solution)/shard_map/add | solution.py:309
  108.9 2.0 %collective-permute-done.7 = f32[416,128]{1,0:T(8,128)S(1)} collective-permute-done((f32[416,128]{1,0:T(8,128)S(1)}, f32[416,128]{1,0:T(8,128)S(1)}, u32[]{:S(2)}, u32[]{:S(2)}) %collective-permute-start.7) | collective-permute-done | bytes 213024 | tf_op jit(solution)/shard_map/ppermute | solution.py:224
  112.0 7.2 %collective-permute-start.14 = (f32[104,128]{1,0:T(8,128)S(1)}, f32[104,128]{1,0:T(8,128)S(1)}, u32[]{:S(2)}, u32[]{:S(2)}) collective-permute-start(f32[104,128]{1,0:T(8,128)S(1)} %get-tuple-element.159), channel_id=1, source_target_pairs={{0,6},{1,7},{2,4},{3,5},{4,2},{5,3},{6,0},{7,1},{8,14},{9,15},{10,... | collective-permute-start | bytes 159752 | tf_op jit(solution)/shard_map/ppermute | solution.py:224
  119.9 3.6 %add_add_fusion.1 = f32[64,8,128]{2,0,1:T(8,128)S(1)} fusion(bf16[192,8,128]{2,0,1:T(8,128)(2,1)S(1)} %get-tuple-element.136, bf16[192,3,128]{2,0,1:T(8,128)(2,1)S(1)} %bitcast.590, bf16[192,3,128]{2,0,1:T(8,128)(2,1)S(1)} %bitcast.594, bf16[192,14,131]{2,0,1:T(8,128)(2,1)S(1)} %get-tuple-element.147, bf16[192,14,131]{2,0,1:T(8,128)(2,1)S(1)} %get-tuple-element.146, ...), kind=kLoop, calls=%fused_computation.311 | loop fusion | flops 10878976 | bytes 6733056 | tf_op jit(solution)/shard_map/add | solution.py:309
  123.9 2.3 %collective-permute-start.16 = (f32[26,128]{1,0:T(8,128)S(1)}, f32[26,128]{1,0:T(8,128)S(1)}, u32[]{:S(2)}, u32[]{:S(2)}) collective-permute-start(f32[26,128]{1,0:T(8,128)S(1)} %get-tuple-element.163), channel_id=1, source_target_pairs={{0,32},{1,33},{2,34},{3,35},{4,36},{5,37},{6,38},{7,39},{8,40},{9,... | collective-permute-start | bytes 39944 | tf_op jit(solution)/shard_map/ppermute | solution.py:224
  128.8 1.0 collective-permute-start.18
  129.8 2.2 %collective-permute-start.19 = (f32[26,128]{1,0:T(8,128)S(1)}, f32[26,128]{1,0:T(8,128)S(1)}, u32[]{:S(2)}, u32[]{:S(2)}) collective-permute-start(f32[26,128]{1,0:T(8,128)S(1)} %get-tuple-element.135), channel_id=1, source_target_pairs={{0,32},{1,33},{2,34},{3,35},{4,36},{5,37},{6,38},{7,39},{8,40},{9,... | collective-permute-start | bytes 39944 | tf_op jit(solution)/shard_map/ppermute | solution.py:241
  132.7 1.2 collective-permute-done.19
  133.9 1.9 %collective-permute-done.20 = f32[26,128]{1,0:T(8,128)S(1)} collective-permute-done((f32[26,128]{1,0:T(8,128)S(1)}, f32[26,128]{1,0:T(8,128)S(1)}, u32[]{:S(2)}, u32[]{:S(2)}) %collective-permute-start.20) | collective-permute-done | bytes 13344 | tf_op jit(solution)/shard_map/ppermute | solution.py:241
  136.5 3.0 %collective-permute-start.22 = (f32[104,128]{1,0:T(8,128)S(1)}, f32[104,128]{1,0:T(8,128)S(1)}, u32[]{:S(2)}, u32[]{:S(2)}) collective-permute-start(f32[104,128]{1,0:T(8,128)S(1)} %reshape.315), channel_id=1, source_target_pairs={{0,4},{1,5},{2,6},{3,7},{4,0},{5,1},{6,2},{7,3},{8,12},{9,13},{10,... | collective-permute-start | bytes 159752 | tf_op jit(solution)/shard_map/ppermute | solution.py:241
  139.8 1.7 collective-permute-done.22
  141.6 2.1 %collective-permute-done.23 = f32[104,128]{1,0:T(8,128)S(1)} collective-permute-done((f32[104,128]{1,0:T(8,128)S(1)}, f32[104,128]{1,0:T(8,128)S(1)}, u32[]{:S(2)}, u32[]{:S(2)}) %collective-permute-start.23) | collective-permute-done | bytes 53280 | tf_op jit(solution)/shard_map/ppermute | solution.py:241
  143.9 2.6 %collective-permute-start.25 = (f32[416,128]{1,0:T(8,128)S(1)}, f32[416,128]{1,0:T(8,128)S(1)}, u32[]{:S(2)}, u32[]{:S(2)}) collective-permute-start(f32[416,128]{1,0:T(8,128)S(1)} %bitcast.601), channel_id=1, source_target_pairs={{0,1},{1,0},{2,3},{3,2},{4,5},{5,4},{6,7},{7,6},{8,9},{9,8},{10,11... | collective-permute-start | bytes 638984 | tf_op jit(solution)/shard_map/ppermute | solution.py:241
  146.5 1.1 collective-permute-start.26
  148.5 3.7 %collective-permute-done.25 = f32[416,128]{1,0:T(8,128)S(1)} collective-permute-done((f32[416,128]{1,0:T(8,128)S(1)}, f32[416,128]{1,0:T(8,128)S(1)}, u32[]{:S(2)}, u32[]{:S(2)}) %collective-permute-start.25) | collective-permute-done | bytes 213024 | tf_op jit(solution)/shard_map/ppermute | solution.py:241
  152.1 2.2 %collective-permute-done.26 = f32[416,128]{1,0:T(8,128)S(1)} collective-permute-done((f32[416,128]{1,0:T(8,128)S(1)}, f32[416,128]{1,0:T(8,128)S(1)}, u32[]{:S(2)}, u32[]{:S(2)}) %collective-permute-start.26) | collective-permute-done | bytes 213024 | tf_op jit(solution)/shard_map/ppermute | solution.py:241
  154.3 8.4 %collective-permute-start.27 = (f32[1664,128]{1,0:T(8,128)S(1)}, f32[1664,128]{1,0:T(8,128)S(1)}, u32[]{:S(2)}, u32[]{:S(2)}) collective-permute-start(f32[1664,128]{1,0:T(8,128)S(1)} %bitcast.569), channel_id=1, source_target_pairs={{0,8},{1,9},{2,10},{3,11},{4,12},{5,13},{6,14},{7,15},{8,0},{9,1},... | collective-permute-start | bytes 2555912 | tf_op jit(solution)/shard_map/ppermute | solution.py:241
  162.8 1.3 copy.73
  166.0 1.1 fusion.167
  (356 shorter events, 36.4 us)
Async XLA Ops:
  0.7 7.7 %copy-start.7 = (f32[192,49]{0,1:T(8,128)S(1)}, f32[192,49]{0,1:T(8,128)}, u32[]{:S(2)}) copy-start(f32[192,49]{0,1:T(8,128)} %param.17) | copy-start | bytes 112900
  1.9 11.0 %collective-permute-start.1 = (bf16[3,192,128]{2,1,0:T(8,128)(2,1)S(1)}, bf16[3,192,128]{2,1,0:T(8,128)(2,1)S(1)}, u32[]{:S(2)}, u32[]{:S(2)}) collective-permute-start(bf16[3,192,128]{2,1,0:T(8,128)(2,1)S(1)} %get-tuple-element.157), channel_id=1, source_target_pairs={{8,0},{16,8},{24,16},{32,24},{40,32},{48,40},{56,48},{9,1},{17,9},... | collective-permute-start | bytes 442376 | tf_op jit(solution)/shard_map/ppermute | solution.py:22
  5.2 7.7 %collective-permute-start = (bf16[3,192,128]{2,1,0:T(8,128)(2,1)S(1)}, bf16[3,192,128]{2,1,0:T(8,128)(2,1)S(1)}, u32[]{:S(2)}, u32[]{:S(2)}) collective-permute-start(bf16[3,192,128]{2,1,0:T(8,128)(2,1)S(1)} %get-tuple-element.156), channel_id=1, source_target_pairs={{0,8},{8,16},{16,24},{24,32},{32,40},{40,48},{48,56},{1,9},{9,17},... | collective-permute-start | bytes 442376 | tf_op jit(solution)/shard_map/ppermute | solution.py:21
  12.9 11.1 %copy-start.1 = (bf16[3,192,128]{2,1,0:T(8,128)(2,1)}, bf16[3,192,128]{2,1,0:T(8,128)(2,1)S(1)}, u32[]{:S(2)}) copy-start(bf16[3,192,128]{2,1,0:T(8,128)(2,1)S(1)} %collective-permute-done) | copy-start | bytes 442372
  13.0 7.9 %copy-start.112 = (s32[2,8,128]{2,1,0:T(8,128)S(1)}, s32[2,8,128]{2,1,0:T(8,128)}, u32[]{:S(2)}) copy-start(s32[2,8,128]{2,1,0:T(8,128)} %param.16) | copy-start | bytes 24580
  13.7 7.2 %collective-permute-start.3 = (bf16[3,14,192]{2,1,0:T(8,128)(2,1)S(1)}, bf16[3,14,192]{2,1,0:T(8,128)(2,1)S(1)}, u32[]{:S(2)}, u32[]{:S(2)}) collective-permute-start(bf16[3,14,192]{2,1,0:T(8,128)(2,1)S(1)} %copy.57), channel_id=1, source_target_pairs={{1,0},{2,1},{3,2},{4,3},{5,4},{6,5},{7,6},{9,8},{10,9},{11,10},{12... | collective-permute-start | bytes 48392 | tf_op jit(solution)/shard_map/ppermute | solution.py:22
  15.4 6.5 %collective-permute-start.2 = (bf16[3,14,192]{2,1,0:T(8,128)(2,1)S(1)}, bf16[3,14,192]{2,1,0:T(8,128)(2,1)S(1)}, u32[]{:S(2)}, u32[]{:S(2)}) collective-permute-start(bf16[3,14,192]{2,1,0:T(8,128)(2,1)S(1)} %copy.55), channel_id=1, source_target_pairs={{0,1},{1,2},{2,3},{3,4},{4,5},{5,6},{6,7},{8,9},{9,10},{10,11},{11... | collective-permute-start | bytes 48392 | tf_op jit(solution)/shard_map/ppermute | solution.py:21
  24.3 8.4 %copy-start.6 = (bf16[192,768]{1,0:T(8,128)(2,1)S(1)}, bf16[192,768]{1,0:T(8,128)(2,1)}, u32[]{:S(2)}) copy-start(bf16[192,768]{1,0:T(8,128)(2,1)} %param.21) | copy-start | bytes 884740
  24.3 8.4 %copy-start.12 = (f32[192]{0:T(256)S(1)}, f32[192]{0:T(256)}, u32[]{:S(2)}) copy-start(f32[192]{0:T(256)} %param.19) | copy-start | bytes 2308
  24.3 8.4 %copy-start.13 = (f32[192]{0:T(256)S(1)}, f32[192]{0:T(256)}, u32[]{:S(2)}) copy-start(f32[192]{0:T(256)} %param.20) | copy-start | bytes 2308
  24.3 8.4 %copy-start.15 = (f32[768]{0:T(1024)S(1)}, f32[768]{0:T(1024)}, u32[]{:S(2)}) copy-start(f32[768]{0:T(1024)} %param.22) | copy-start | bytes 9220
  62.4 11.4 %copy-start.9 = (bf16[3,192,128]{2,1,0:T(8,128)(2,1)S(1)}, bf16[3,192,128]{2,1,0:T(8,128)(2,1)}, u32[]{:S(2)}) copy-start(bf16[3,192,128]{2,1,0:T(8,128)(2,1)} %get-tuple-element.155) | copy-start | bytes 442372
  62.4 14.8 %copy-start.8 = (bf16[3,192,128]{2,1,0:T(8,128)(2,1)S(1)}, bf16[3,192,128]{2,1,0:T(8,128)(2,1)}, u32[]{:S(2)}) copy-start(bf16[3,192,128]{2,1,0:T(8,128)(2,1)} %get-tuple-element.154) | copy-start | bytes 442372
  73.8 7.6 %collective-permute-start.8 = (bf16[3,192,128]{2,1,0:T(8,128)(2,1)S(1)}, bf16[3,192,128]{2,1,0:T(8,128)(2,1)S(1)}, u32[]{:S(2)}, u32[]{:S(2)}) collective-permute-start(bf16[3,192,128]{2,1,0:T(8,128)(2,1)S(1)} %copy-done.9), channel_id=1, source_target_pairs={{0,8},{8,16},{16,24},{24,32},{32,40},{40,48},{48,56},{1,9},{9,17},... | collective-permute-start | bytes 442376 | tf_op jit(solution)/shard_map/ppermute | solution.py:21
  77.3 6.5 %collective-permute-start.9 = (bf16[3,192,128]{2,1,0:T(8,128)(2,1)S(1)}, bf16[3,192,128]{2,1,0:T(8,128)(2,1)S(1)}, u32[]{:S(2)}, u32[]{:S(2)}) collective-permute-start(bf16[3,192,128]{2,1,0:T(8,128)(2,1)S(1)} %copy-done.8), channel_id=1, source_target_pairs={{8,0},{16,8},{24,16},{32,24},{40,32},{48,40},{56,48},{9,1},{17,9},... | collective-permute-start | bytes 442376 | tf_op jit(solution)/shard_map/ppermute | solution.py:22
  81.3 14.7 %collective-permute-start.4 = (f32[1664,128]{1,0:T(8,128)}, f32[1664,128]{1,0:T(8,128)}, u32[]{:S(2)}, u32[]{:S(2)}) collective-permute-start(f32[1664,128]{1,0:T(8,128)} %dynamic-slice_bitcast_fusion), channel_id=1, source_target_pairs={{0,8},{1,9},{2,10},{3,11},{4,12},{5,13},{6,14},{7,15},{8,0},{9,1},... | collective-permute-start | bytes 2555912 | tf_op jit(solution)/shard_map/ppermute | solution.py:224
  84.5 9.1 %collective-permute-start.10 = (bf16[3,14,192]{2,1,0:T(8,128)(2,1)S(1)}, bf16[3,14,192]{2,1,0:T(8,128)(2,1)S(1)}, u32[]{:S(2)}, u32[]{:S(2)}) collective-permute-start(bf16[3,14,192]{2,1,0:T(8,128)(2,1)S(1)} %copy.69), channel_id=1, source_target_pairs={{1,0},{2,1},{3,2},{4,3},{5,4},{6,5},{7,6},{9,8},{10,9},{11,10},{12... | collective-permute-start | bytes 48392 | tf_op jit(solution)/shard_map/ppermute | solution.py:22
  86.2 7.8 %collective-permute-start.11 = (bf16[3,14,192]{2,1,0:T(8,128)(2,1)S(1)}, bf16[3,14,192]{2,1,0:T(8,128)(2,1)S(1)}, u32[]{:S(2)}, u32[]{:S(2)}) collective-permute-start(bf16[3,14,192]{2,1,0:T(8,128)(2,1)S(1)} %copy.71), channel_id=1, source_target_pairs={{0,1},{1,2},{2,3},{3,4},{4,5},{5,6},{6,7},{8,9},{9,10},{10,11},{11... | collective-permute-start | bytes 48392 | tf_op jit(solution)/shard_map/ppermute | solution.py:21
  95.6 6.9 %copy-start.71 = (f32[128]{0:T(128)S(1)}, f32[128]{0:T(128)}, u32[]{:S(2)}) copy-start(f32[128]{0:T(128)} %get-tuple-element.213) | copy-start | bytes 1540
  95.6 6.9 %copy-start.72 = (f32[128]{0:T(128)S(1)}, f32[128]{0:T(128)}, u32[]{:S(2)}) copy-start(f32[128]{0:T(128)} %get-tuple-element.214) | copy-start | bytes 1540
  95.7 6.9 %copy-start.73 = (f32[128]{0:T(128)S(1)}, f32[128]{0:T(128)}, u32[]{:S(2)}) copy-start(f32[128]{0:T(128)} %get-tuple-element.215) | copy-start | bytes 1540
  95.7 6.9 %copy-start.74 = (f32[128]{0:T(128)S(1)}, f32[128]{0:T(128)}, u32[]{:S(2)}) copy-start(f32[128]{0:T(128)} %get-tuple-element.216) | copy-start | bytes 1540
  95.7 6.9 %copy-start.75 = (f32[128]{0:T(128)S(1)}, f32[128]{0:T(128)}, u32[]{:S(2)}) copy-start(f32[128]{0:T(128)} %get-tuple-element.217) | copy-start | bytes 1540
  95.7 6.9 %copy-start.76 = (f32[128]{0:T(128)S(1)}, f32[128]{0:T(128)}, u32[]{:S(2)}) copy-start(f32[128]{0:T(128)} %get-tuple-element.218) | copy-start | bytes 1540
  95.7 6.9 %copy-start.77 = (f32[128]{0:T(128)S(1)}, f32[128]{0:T(128)}, u32[]{:S(2)}) copy-start(f32[128]{0:T(128)} %get-tuple-element.219) | copy-start | bytes 1540
  95.7 6.9 %copy-start.78 = (f32[128]{0:T(128)S(1)}, f32[128]{0:T(128)}, u32[]{:S(2)}) copy-start(f32[128]{0:T(128)} %get-tuple-element.220) | copy-start | bytes 1540
  95.7 6.9 %copy-start.79 = (f32[128]{0:T(128)S(1)}, f32[128]{0:T(128)}, u32[]{:S(2)}) copy-start(f32[128]{0:T(128)} %get-tuple-element.221) | copy-start | bytes 1540
  95.7 6.9 %copy-start.80 = (f32[128]{0:T(128)S(1)}, f32[128]{0:T(128)}, u32[]{:S(2)}) copy-start(f32[128]{0:T(128)} %get-tuple-element.222) | copy-start | bytes 1540
  97.4 13.5 %collective-permute-start.7 = (f32[416,128]{1,0:T(8,128)S(1)}, f32[416,128]{1,0:T(8,128)S(1)}, u32[]{:S(2)}, u32[]{:S(2)}) collective-permute-start(f32[416,128]{1,0:T(8,128)S(1)} %get-tuple-element.144), channel_id=1, source_target_pairs={{0,65},{1,64},{2,67},{3,66},{4,69},{5,68},{6,71},{7,70},{8,73},{9,... | collective-permute-start | bytes 638984 | tf_op jit(solution)/shard_map/ppermute | solution.py:224
  101.9 9.0 %collective-permute-start.6 = (f32[416,128]{1,0:T(8,128)S(1)}, f32[416,128]{1,0:T(8,128)S(1)}, u32[]{:S(2)}, u32[]{:S(2)}) collective-permute-start(f32[416,128]{1,0:T(8,128)S(1)} %get-tuple-element.145), channel_id=1, source_target_pairs={{0,1},{1,0},{2,3},{3,2},{4,5},{5,4},{6,7},{7,6},{8,9},{9,8},{10,11... | collective-permute-start | bytes 638984 | tf_op jit(solution)/shard_map/ppermute | solution.py:224
  102.1 9.8 %collective-permute-start.5 = (f32[416,128]{1,0:T(8,128)S(1)}, f32[416,128]{1,0:T(8,128)S(1)}, u32[]{:S(2)}, u32[]{:S(2)}) collective-permute-start(f32[416,128]{1,0:T(8,128)S(1)} %get-tuple-element.143), channel_id=1, source_target_pairs={{0,64},{1,65},{2,66},{3,67},{4,68},{5,69},{6,70},{7,71},{8,72},{9,... | collective-permute-start | bytes 638984 | tf_op jit(solution)/shard_map/ppermute | solution.py:224
  102.9 17.0 %copy-start.113 = (f32[64]{0:T(128)S(1)}, f32[64]{0:T(128)}, u32[]{:S(2)}) copy-start(f32[64]{0:T(128)} %get-tuple-element.194) | copy-start | bytes 772
  112.0 11.6 %collective-permute-start.14 = (f32[104,128]{1,0:T(8,128)S(1)}, f32[104,128]{1,0:T(8,128)S(1)}, u32[]{:S(2)}, u32[]{:S(2)}) collective-permute-start(f32[104,128]{1,0:T(8,128)S(1)} %get-tuple-element.159), channel_id=1, source_target_pairs={{0,6},{1,7},{2,4},{3,5},{4,2},{5,3},{6,0},{7,1},{8,14},{9,15},{10,... | collective-permute-start | bytes 159752 | tf_op jit(solution)/shard_map/ppermute | solution.py:224
  119.2 4.5 %collective-permute-start.13 = (f32[104,128]{1,0:T(8,128)S(1)}, f32[104,128]{1,0:T(8,128)S(1)}, u32[]{:S(2)}, u32[]{:S(2)}) collective-permute-start(f32[104,128]{1,0:T(8,128)S(1)} %get-tuple-element.160), channel_id=1, source_target_pairs={{0,4},{1,5},{2,6},{3,7},{4,0},{5,1},{6,2},{7,3},{8,12},{9,13},{10,... | collective-permute-start | bytes 159752 | tf_op jit(solution)/shard_map/ppermute | solution.py:224
  119.2 4.5 %collective-permute-start.12 = (f32[104,128]{1,0:T(8,128)S(1)}, f32[104,128]{1,0:T(8,128)S(1)}, u32[]{:S(2)}, u32[]{:S(2)}) collective-permute-start(f32[104,128]{1,0:T(8,128)S(1)} %get-tuple-element.158), channel_id=1, source_target_pairs={{0,2},{1,3},{2,0},{3,1},{4,6},{5,7},{6,4},{7,5},{8,10},{9,11},{10,... | collective-permute-start | bytes 159752 | tf_op jit(solution)/shard_map/ppermute | solution.py:224
  123.8 3.9 %collective-permute-start.17 = (f32[26,128]{1,0:T(8,128)S(1)}, f32[26,128]{1,0:T(8,128)S(1)}, u32[]{:S(2)}, u32[]{:S(2)}) collective-permute-start(f32[26,128]{1,0:T(8,128)S(1)} %get-tuple-element.162), channel_id=1, source_target_pairs={{0,48},{1,49},{2,50},{3,51},{4,52},{5,53},{6,54},{7,55},{8,56},{9,... | collective-permute-start | bytes 39944 | tf_op jit(solution)/shard_map/ppermute | solution.py:224
  123.9 4.2 %collective-permute-start.16 = (f32[26,128]{1,0:T(8,128)S(1)}, f32[26,128]{1,0:T(8,128)S(1)}, u32[]{:S(2)}, u32[]{:S(2)}) collective-permute-start(f32[26,128]{1,0:T(8,128)S(1)} %get-tuple-element.163), channel_id=1, source_target_pairs={{0,32},{1,33},{2,34},{3,35},{4,36},{5,37},{6,38},{7,39},{8,40},{9,... | collective-permute-start | bytes 39944 | tf_op jit(solution)/shard_map/ppermute | solution.py:224
  126.1 2.6 %collective-permute-start.15 = (f32[26,128]{1,0:T(8,128)S(1)}, f32[26,128]{1,0:T(8,128)S(1)}, u32[]{:S(2)}, u32[]{:S(2)}) collective-permute-start(f32[26,128]{1,0:T(8,128)S(1)} %get-tuple-element.161), channel_id=1, source_target_pairs={{0,16},{1,17},{2,18},{3,19},{4,20},{5,21},{6,22},{7,23},{8,24},{9,... | collective-permute-start | bytes 39944 | tf_op jit(solution)/shard_map/ppermute | solution.py:224
  128.8 3.9 %collective-permute-start.18 = (f32[26,128]{1,0:T(8,128)S(1)}, f32[26,128]{1,0:T(8,128)S(1)}, u32[]{:S(2)}, u32[]{:S(2)}) collective-permute-start(f32[26,128]{1,0:T(8,128)S(1)} %get-tuple-element.135), channel_id=1, source_target_pairs={{0,16},{1,17},{2,18},{3,19},{4,20},{5,21},{6,22},{7,23},{8,24},{9,... | collective-permute-start | bytes 39944 | tf_op jit(solution)/shard_map/ppermute | solution.py:241
  129.8 4.1 %collective-permute-start.19 = (f32[26,128]{1,0:T(8,128)S(1)}, f32[26,128]{1,0:T(8,128)S(1)}, u32[]{:S(2)}, u32[]{:S(2)}) collective-permute-start(f32[26,128]{1,0:T(8,128)S(1)} %get-tuple-element.135), channel_id=1, source_target_pairs={{0,32},{1,33},{2,34},{3,35},{4,36},{5,37},{6,38},{7,39},{8,40},{9,... | collective-permute-start | bytes 39944 | tf_op jit(solution)/shard_map/ppermute | solution.py:241
  132.0 3.8 %collective-permute-start.20 = (f32[26,128]{1,0:T(8,128)S(1)}, f32[26,128]{1,0:T(8,128)S(1)}, u32[]{:S(2)}, u32[]{:S(2)}) collective-permute-start(f32[26,128]{1,0:T(8,128)S(1)} %get-tuple-element.135), channel_id=1, source_target_pairs={{0,48},{1,49},{2,50},{3,51},{4,52},{5,53},{6,54},{7,55},{8,56},{9,... | collective-permute-start | bytes 39944 | tf_op jit(solution)/shard_map/ppermute | solution.py:241
  135.8 4.0 %collective-permute-start.21 = (f32[104,128]{1,0:T(8,128)S(1)}, f32[104,128]{1,0:T(8,128)S(1)}, u32[]{:S(2)}, u32[]{:S(2)}) collective-permute-start(f32[104,128]{1,0:T(8,128)S(1)} %reshape.315), channel_id=1, source_target_pairs={{0,2},{1,3},{2,0},{3,1},{4,6},{5,7},{6,4},{7,5},{8,10},{9,11},{10,... | collective-permute-start | bytes 159752 | tf_op jit(solution)/shard_map/ppermute | solution.py:241
  136.5 5.1 %collective-permute-start.22 = (f32[104,128]{1,0:T(8,128)S(1)}, f32[104,128]{1,0:T(8,128)S(1)}, u32[]{:S(2)}, u32[]{:S(2)}) collective-permute-start(f32[104,128]{1,0:T(8,128)S(1)} %reshape.315), channel_id=1, source_target_pairs={{0,4},{1,5},{2,6},{3,7},{4,0},{5,1},{6,2},{7,3},{8,12},{9,13},{10,... | collective-permute-start | bytes 159752 | tf_op jit(solution)/shard_map/ppermute | solution.py:241
  139.5 4.2 %collective-permute-start.23 = (f32[104,128]{1,0:T(8,128)S(1)}, f32[104,128]{1,0:T(8,128)S(1)}, u32[]{:S(2)}, u32[]{:S(2)}) collective-permute-start(f32[104,128]{1,0:T(8,128)S(1)} %reshape.315), channel_id=1, source_target_pairs={{0,6},{1,7},{2,4},{3,5},{4,2},{5,3},{6,0},{7,1},{8,14},{9,15},{10,... | collective-permute-start | bytes 159752 | tf_op jit(solution)/shard_map/ppermute | solution.py:241
  143.7 4.8 %collective-permute-start.24 = (f32[416,128]{1,0:T(8,128)S(1)}, f32[416,128]{1,0:T(8,128)S(1)}, u32[]{:S(2)}, u32[]{:S(2)}) collective-permute-start(f32[416,128]{1,0:T(8,128)S(1)} %bitcast.600), channel_id=1, source_target_pairs={{0,64},{1,65},{2,66},{3,67},{4,68},{5,69},{6,70},{7,71},{8,72},{9,... | collective-permute-start | bytes 638984 | tf_op jit(solution)/shard_map/ppermute | solution.py:241
  143.9 8.2 %collective-permute-start.25 = (f32[416,128]{1,0:T(8,128)S(1)}, f32[416,128]{1,0:T(8,128)S(1)}, u32[]{:S(2)}, u32[]{:S(2)}) collective-permute-start(f32[416,128]{1,0:T(8,128)S(1)} %bitcast.601), channel_id=1, source_target_pairs={{0,1},{1,0},{2,3},{3,2},{4,5},{5,4},{6,7},{7,6},{8,9},{9,8},{10,11... | collective-permute-start | bytes 638984 | tf_op jit(solution)/shard_map/ppermute | solution.py:241
  146.5 7.8 %collective-permute-start.26 = (f32[416,128]{1,0:T(8,128)S(1)}, f32[416,128]{1,0:T(8,128)S(1)}, u32[]{:S(2)}, u32[]{:S(2)}) collective-permute-start(f32[416,128]{1,0:T(8,128)S(1)} %bitcast.602), channel_id=1, source_target_pairs={{0,65},{1,64},{2,67},{3,66},{4,69},{5,68},{6,71},{7,70},{8,73},{9,... | collective-permute-start | bytes 638984 | tf_op jit(solution)/shard_map/ppermute | solution.py:241
  154.3 10.4 %collective-permute-start.27 = (f32[1664,128]{1,0:T(8,128)S(1)}, f32[1664,128]{1,0:T(8,128)S(1)}, u32[]{:S(2)}, u32[]{:S(2)}) collective-permute-start(f32[1664,128]{1,0:T(8,128)S(1)} %bitcast.569), channel_id=1, source_target_pairs={{0,8},{1,9},{2,10},{3,11},{4,12},{5,13},{6,14},{7,15},{8,0},{9,1},... | collective-permute-start | bytes 2555912 | tf_op jit(solution)/shard_map/ppermute | solution.py:241
  (98 other events, 411.7 us)
